TPU v7x, 32 devices: a whole 2x2x4 slice. The times are simulated.
32 devices in a mesh: rep: 2 (over x), member: 4 (over y, core), tp: 4 (over z).
Axes of the slice: x: 2, y: 2, z: 4, core: 2. Of those that a mesh axis runs over, the one named last changes fastest.
Arguments:
- states: bfloat16 [4096, 1024], P(('rep', 'member', 'tp')), parts along dimension 0, may hold values from -6 to 6
- member_of: int32 [4096, 1], P(('rep', 'member', 'tp')), parts along dimension 0, may hold values from 0 to 1; in each aligned block of 128 rows (0 to 127, 128 to 255, ...) at most 128 rows name the same one
- place: int32 [4096], P(('rep', 'member', 'tp')), parts along dimension 0, may hold values from 0 to 2047, as said below
- norm_gain: float32 [2, 1024], replicated, may hold values from 0.5 to 2
- w_up: bfloat16 [4, 1024, 2048], P('member', None, 'tp'), may hold values from -0.1875 to 0.1875
- w_down: bfloat16 [4, 2048, 1024], P('member', 'tp'), may hold values from -0.09375 to 0.09375
- policy_gain: float32 [1024], replicated, may hold values from 0.5 to 2
- w_policy: bfloat16 [1024, 128], replicated, may hold values from -0.1875 to 0.1875
Outputs:
- imagined: bfloat16 [4096, 1024], P(('rep', 'member', 'tp')), parts along dimension 0
- action: bfloat16 [4096, 128], P(('rep', 'member', 'tp')), parts along dimension 0
There are 2 independent parts, one for each index of `rep`. A program takes and returns all parts, laid end to end along the dimension named above; an argument that names none is the same for every part. Nothing has to cross between parts.
Inputs may be any that keep to these rules, and one draw needn't show every extreme that they name: `member_of`: at most 128 of the rows of one device name any one member, and that count is reached on some device. `place`: A permutation of the 2048 learner positions; learner device k holds positions k * 128 to (k + 1) * 128 - 1, and the rows of each device go exactly 8 to every learner device.
All inputs are finite; a program needn't handle non-finite values.
Results may differ from a plain program's by a relative error of at most 0.0069.
Values may be sent and summed in bfloat16 or wider, within the bound.
No kernel may reach another device: no remote copies, remote signals or barrier semaphores. Data moves between devices by JAX's collectives and lax.ppermute only.
A program may use at most 128 MiB of HBM per device.

v0:
```python
import jax
import jax.numpy as jnp
from jax import lax
from jax.sharding import PartitionSpec as P


def from_partner(value, axis, distance):
    return lax.ppermute(value, axis, [(i, i ^ 1 << distance) for i in range(lax.axis_size(axis))])


def rms_scale(values, gain):
    mean_square = jnp.mean(values * values, axis=-1, keepdims=True)
    return values * lax.rsqrt(mean_square + 1e-06) * gain


def running_rank(member_hits):
    return jnp.sum((jnp.cumsum(member_hits, axis=0) - member_hits) * member_hits, axis=1)


def local(states, member_of, place, norm_gain, w_up, w_down, policy_gain, w_policy):
    n_member = lax.axis_size("member")
    n_tp = lax.axis_size("tp")
    n_dev = n_member * n_tp
    group_width = 2 * n_tp
    member_total = n_member // 2
    rows_here = states.shape[0]
    feature_width = states.shape[1]
    slot_count = 2 * rows_here // n_dev
    member = member_of[:, 0]
    member_hits = (member[:, None] == jnp.arange(member_total, dtype=jnp.int32)[None, :]).astype(
        jnp.int32
    )
    earlier = running_rank(member_hits)
    target = (member * group_width + earlier % group_width) * slot_count + earlier // group_width
    picker = (jnp.arange(n_dev * slot_count, dtype=jnp.int32)[:, None] == target[None, :]).astype(
        jnp.bfloat16
    )
    outgoing = jnp.dot(picker, states, preferred_element_type=jnp.float32).astype(jnp.bfloat16)
    arrived = lax.all_to_all(
        outgoing.reshape(n_dev, slot_count, feature_width),
        ("member", "tp"),
        split_axis=0,
        concat_axis=0,
        tiled=True,
    )
    arrived = arrived.reshape(n_dev * slot_count, feature_width)
    arrived_count = arrived.shape[0]
    own_member = lax.axis_index("member") // 2
    gain_here = lax.dynamic_index_in_dim(norm_gain, own_member, 0, keepdims=False)
    normed = rms_scale(arrived.astype(jnp.float32), gain_here).astype(jnp.bfloat16)
    partner_normed = from_partner(normed, "member", 0)
    both_rows = jnp.concatenate([normed, partner_normed], axis=0)
    up_local = w_up[0]
    down_local = w_down[0]
    hidden = jax.nn.gelu(
        jnp.dot(
            lax.all_gather(both_rows, "tp", axis=0, tiled=True),
            up_local,
            preferred_element_type=jnp.float32,
        )
    ).astype(jnp.bfloat16)
    half_change = lax.psum_scatter(
        jnp.dot(hidden, down_local, preferred_element_type=jnp.float32),
        "tp",
        scatter_dimension=0,
        tiled=True,
    )
    partner_part = from_partner(half_change[arrived_count:], "member", 0)
    change = half_change[:arrived_count] + partner_part
    predicted = (arrived.astype(jnp.float32) + change).astype(jnp.bfloat16)
    returned = lax.all_to_all(
        predicted.reshape(n_dev, slot_count, feature_width),
        ("member", "tp"),
        split_axis=0,
        concat_axis=0,
        tiled=True,
    )
    returned = returned.reshape(n_dev * slot_count, feature_width)
    own_rows = jnp.einsum("sr,sd->rd", picker, returned, preferred_element_type=jnp.float32).astype(
        jnp.bfloat16
    )
    per_learner = rows_here // n_dev
    learner = place // rows_here
    spot_index = place % rows_here
    learner_hits = (learner[:, None] == jnp.arange(n_dev, dtype=jnp.int32)[None, :]).astype(
        jnp.int32
    )
    lane_index = learner * per_learner + running_rank(learner_hits)
    placer = jnp.arange(rows_here, dtype=jnp.int32)[:, None] == lane_index[None, :]
    packed = jnp.dot(
        placer.astype(jnp.bfloat16), own_rows, preferred_element_type=jnp.float32
    ).astype(jnp.bfloat16)
    packed_spot = jnp.sum(placer.astype(jnp.int32) * spot_index[None, :], axis=1)
    arrivals, arrival_spots = (
        lax.all_to_all(
            packed.reshape(n_dev, per_learner, feature_width),
            ("member", "tp"),
            split_axis=0,
            concat_axis=0,
            tiled=True,
        ),
        lax.all_to_all(
            packed_spot.reshape(n_dev, per_learner),
            ("member", "tp"),
            split_axis=0,
            concat_axis=0,
            tiled=True,
        ),
    )
    arrivals = arrivals.reshape(rows_here, feature_width)
    arrival_spots = arrival_spots.reshape(rows_here)
    settle = (jnp.arange(rows_here, dtype=jnp.int32)[:, None] == arrival_spots[None, :]).astype(
        jnp.bfloat16
    )
    imagined = jnp.dot(settle, arrivals, preferred_element_type=jnp.float32).astype(jnp.bfloat16)
    policy_normed = rms_scale(imagined.astype(jnp.float32), policy_gain).astype(jnp.bfloat16)
    action = jnp.tanh(jnp.dot(policy_normed, w_policy, preferred_element_type=jnp.float32)).astype(
        jnp.bfloat16
    )
    return (imagined, action)


def solution(mesh):
    in_specs = (
        P(("rep", "member", "tp"), None),
        P(("rep", "member", "tp"), None),
        P(("rep", "member", "tp")),
        P(),
        P("member", None, "tp"),
        P("member", "tp", None),
        P(),
        P(),
    )
    out_specs = (P(("rep", "member", "tp"), None), P(("rep", "member", "tp"), None))
    return jax.shard_map(local, mesh=mesh, in_specs=in_specs, out_specs=out_specs, check_vma=False)
```

profile of v0, /device:TPU:0, one launch (start us, length us, event | category | flops | bytes accessed | tf_op | source)
XLA Modules:
  0.0 330.6 jit_solution(9997030250772812439)
XLA Ops:
  7.2 0.9 fusion.38
  8.3 0.8 select_reduce_fusion
  9.1 0.7 multiply_add_fusion
  9.8 2.0 convolution_convert_fusion
  11.8 7.4 %all-to-all-start.1 = ((bf16[16,16,1024]{2,1,0:T(8,128)(2,1)}), bf16[16,16,1024]{2,1,0:T(8,128)(2,1)S(1)}, u32[]{:S(2)}, u32[]{:S(2)}) async-start(bf16[16,16,1024]{2,1,0:T(8,128)(2,1)} %bitcast.2), calls=%async_computation.1 | async-start | bytes 1048576 | tf_op jit(solution)/shard_map/all_to_all | solution.py:39
  19.3 0.7 constant_dynamic-slice_fusion
  20.0 14.9 %all-to-all-done.1 = bf16[16,16,1024]{2,1,0:T(8,128)(2,1)S(1)} async-done(((bf16[16,16,1024]{2,1,0:T(8,128)(2,1)}), bf16[16,16,1024]{2,1,0:T(8,128)(2,1)S(1)}, u32[]{:S(2)}, u32[]{:S(2)}) %all-to-all-start.1) | async-done | bytes 524320 | tf_op jit(solution)/shard_map/all_to_all | solution.py:39
  35.4 1.9 collective-permute-done
  37.3 1.1 pad_maximum_fusion
  38.5 79.5 %all-gather.2.cloned.1.call-done = bf16[2048,1024]{1,0:T(8,128)(2,1)} async-done(((bf16[512,1024]{1,0:T(8,128)(2,1)}), bf16[2048,1024]{1,0:T(8,128)(2,1)}) %all-gather.2.cloned.1.call-update) | async-done | bytes 4194320 | tf_op jit(solution)/shard_map/all_gather | solution.py:57
  118.0 10.6 %fusion.8 = f32[2048,1024]{1,0:T(8,128)} fusion(bf16[1,512,1024]{2,1,0:T(8,128)(2,1)S(1)} %copy-done, bf16[2048,1024]{1,0:T(8,128)(2,1)} %all-gather.2.cloned.1.call-done, bf16[1,1024,512]{2,1,0:T(8,128)(2,1)S(1)} %copy-done.2), kind=kOutput, calls=%fused_computation.9 | convolution fusion | flops 4304404480 | bytes 14680064 | tf_op jit(solution)/shard_map/dot_general | solution.py:63
  128.7 143.1 %reduce-scatter.2.cloned.1.call-done = f32[512,1024]{1,0:T(8,128)} async-done(((f32[2048,1024]{1,0:T(8,128)}), f32[512,1024]{1,0:T(8,128)}) %reduce-scatter.2.cloned.1.call-update) | async-done | bytes 2097168 | tf_op jit(solution)/shard_map/reduce_scatter | solution.py:62
  271.8 1.3 slice.9
  273.2 2.6 collective-permute-done.1
  275.9 2.2 fusion.17
  278.1 5.4 %all-to-all-start.2 = ((bf16[16,16,1024]{2,1,0:T(8,128)(2,1)}), bf16[16,16,1024]{2,1,0:T(8,128)(2,1)S(1)}, u32[]{:S(2)}, u32[]{:S(2)}) async-start(bf16[16,16,1024]{2,1,0:T(8,128)(2,1)} %bitcast.7), calls=%async_computation.3 | async-start | bytes 1048576 | tf_op jit(solution)/shard_map/all_to_all | solution.py:71
  284.1 0.7 all_to_all.15
  284.8 14.4 %all-to-all-done.2 = bf16[16,16,1024]{2,1,0:T(8,128)(2,1)S(1)} async-done(((bf16[16,16,1024]{2,1,0:T(8,128)(2,1)}), bf16[16,16,1024]{2,1,0:T(8,128)(2,1)S(1)}, u32[]{:S(2)}, u32[]{:S(2)}) %all-to-all-start.2) | async-done | bytes 524320 | tf_op jit(solution)/shard_map/all_to_all | solution.py:71
  299.2 3.5 %all-to-all-start = ((s32[16,1,8]{2,1,0:T(1,128)}), s32[16,1,8]{2,1,0:T(1,128)S(1)}, u32[]{:S(2)}, u32[]{:S(2)}) async-start(s32[16,1,8]{2,1,0:T(1,128)} %bitcast), calls=%async_computation | async-start | bytes 16384 | tf_op jit(solution)/shard_map/all_to_all | solution.py:102
  302.7 1.1 fusion.14
  303.8 5.1 %all-to-all-done = s32[16,1,8]{2,1,0:T(1,128)S(1)} async-done(((s32[16,1,8]{2,1,0:T(1,128)}), s32[16,1,8]{2,1,0:T(1,128)S(1)}, u32[]{:S(2)}, u32[]{:S(2)}) %all-to-all-start) | async-done | bytes 544 | tf_op jit(solution)/shard_map/all_to_all | solution.py:102
  308.9 3.5 %all-to-all-start.3 = ((bf16[16,8,1024]{2,1,0:T(8,128)(2,1)}), bf16[16,8,1024]{2,1,0:T(8,128)(2,1)S(1)}, u32[]{:S(2)}, u32[]{:S(2)}) async-start(bf16[16,8,1024]{2,1,0:T(8,128)(2,1)} %fusion.14), calls=%async_computation.4 | async-start | bytes 524288 | tf_op jit(solution)/shard_map/all_to_all | solution.py:95
  313.7 8.7 %all-to-all-done.3 = bf16[16,8,1024]{2,1,0:T(8,128)(2,1)S(1)} async-done(((bf16[16,8,1024]{2,1,0:T(8,128)(2,1)}), bf16[16,8,1024]{2,1,0:T(8,128)(2,1)S(1)}, u32[]{:S(2)}, u32[]{:S(2)}) %all-to-all-start.3) | async-done | bytes 262176 | tf_op jit(solution)/shard_map/all_to_all | solution.py:95
  322.8 0.9 fusion.15
  (34 shorter events, 3.1 us)
Async XLA Ops:
  7.2 110.8 %copy-start = (bf16[1,512,1024]{2,1,0:T(8,128)(2,1)S(1)}, bf16[1,512,1024]{2,1,0:T(8,128)(2,1)}, u32[]{:S(2)}) copy-start(bf16[1,512,1024]{2,1,0:T(8,128)(2,1)} %param.13) | copy-start | bytes 3145732
  7.2 110.8 %copy-start.2 = (bf16[1,1024,512]{2,1,0:T(8,128)(2,1)S(1)}, bf16[1,1024,512]{2,1,0:T(8,128)(2,1)}, u32[]{:S(2)}) copy-start(bf16[1,1024,512]{2,1,0:T(8,128)(2,1)} %param.12) | copy-start | bytes 3145732
  11.8 23.1 %all-to-all-start.1 = ((bf16[16,16,1024]{2,1,0:T(8,128)(2,1)}), bf16[16,16,1024]{2,1,0:T(8,128)(2,1)S(1)}, u32[]{:S(2)}, u32[]{:S(2)}) async-start(bf16[16,16,1024]{2,1,0:T(8,128)(2,1)} %bitcast.2), calls=%async_computation.1 | async-start | bytes 1048576 | tf_op jit(solution)/shard_map/all_to_all | solution.py:39
  19.2 98.8 %all-gather.2.cloned.1.call-start = ((), (), s32[]{:S(2)}) async-start(), calls=%async_computation.5 | async-start | bytes 5242880 | tf_op jit(solution)/shard_map/all_gather | solution.py:57
  35.3 2.0 collective-permute-start
  38.4 233.4 %reduce-scatter.2.cloned.1.call-start = ((), (), s32[]{:S(2)}) async-start(), calls=%async_computation.6 | async-start | bytes 10485760 | tf_op jit(solution)/shard_map/reduce_scatter | solution.py:62
  128.6 154.9 %copy-start.5 = (s32[128]{0:T(128)S(1)}, s32[128]{0:T(128)}, u32[]{:S(2)}) copy-start(s32[128]{0:T(128)} %param.10) | copy-start | bytes 1540
  128.6 194.2 %copy-start.3 = (bf16[1024,128]{1,0:T(8,128)(2,1)S(1)}, bf16[1024,128]{1,0:T(8,128)(2,1)}, u32[]{:S(2)}) copy-start(bf16[1024,128]{1,0:T(8,128)(2,1)} %param.15) | copy-start | bytes 786436
  128.6 194.2 %copy-start.4 = (f32[1024]{0:T(1024)S(1)}, f32[1024]{0:T(1024)}, u32[]{:S(2)}) copy-start(f32[1024]{0:T(1024)} %param.14) | copy-start | bytes 12292
  273.1 2.7 collective-permute-start.1
  278.1 21.1 %all-to-all-start.2 = ((bf16[16,16,1024]{2,1,0:T(8,128)(2,1)}), bf16[16,16,1024]{2,1,0:T(8,128)(2,1)S(1)}, u32[]{:S(2)}, u32[]{:S(2)}) async-start(bf16[16,16,1024]{2,1,0:T(8,128)(2,1)} %bitcast.7), calls=%async_computation.3 | async-start | bytes 1048576 | tf_op jit(solution)/shard_map/all_to_all | solution.py:71
  299.2 9.7 %all-to-all-start = ((s32[16,1,8]{2,1,0:T(1,128)}), s32[16,1,8]{2,1,0:T(1,128)S(1)}, u32[]{:S(2)}, u32[]{:S(2)}) async-start(s32[16,1,8]{2,1,0:T(1,128)} %bitcast), calls=%async_computation | async-start | bytes 16384 | tf_op jit(solution)/shard_map/all_to_all | solution.py:102
  308.9 13.6 %all-to-all-start.3 = ((bf16[16,8,1024]{2,1,0:T(8,128)(2,1)}), bf16[16,8,1024]{2,1,0:T(8,128)(2,1)S(1)}, u32[]{:S(2)}, u32[]{:S(2)}) async-start(bf16[16,8,1024]{2,1,0:T(8,128)(2,1)} %fusion.14), calls=%async_computation.4 | async-start | bytes 524288 | tf_op jit(solution)/shard_map/all_to_all | solution.py:95
  322.8 1.0 copy-start.1
Sparse Core Ops, SparseCore 0:
  38.5 79.4 all-gather.1
  128.7 143.0 reduce-scatter.1
where the time goes:
time: 331 us
  waiting for transfers between devices  270 us (82%)
  starting transfers between devices  20 us (6%)
  matrix products  15 us (5%)
  between operations  14.3 us (4%)
  other arithmetic  7.45 us (2%)
  local copies, waits for them, and re-layouts  3.45 us (1%)
    reduce_scatter x1, waiting for transfers between devices, local(): lax.psum_scatter(jnp.dot(hidden, down_local, preferred_element_type=jnp.f...  143 us
    all_gather x1, waiting for transfers between devices, local(): lax.all_gather(both_rows, 'tp', axis=0, tiled=True)  79.5 us
    all_to_all x1, waiting for transfers between devices, local(): lax.all_to_all(outgoing.reshape(n_dev, slot_count, feature_width), ('memb...  14.9 us
    all_to_all x1, waiting for transfers between devices, local(): lax.all_to_all(predicted.reshape(n_dev, slot_count, feature_width), ('mem...  14.4 us
    dot_general x1, matrix products, local(): jnp.dot(hidden, down_local, preferred_element_type=jnp.float32)  10.6 us
    all_to_all x1, waiting for transfers between devices, local(): lax.all_to_all(packed.reshape(n_dev, per_learner, feature_width), ('membe...  8.74 us
    all_to_all x1, starting transfers between devices, local(): lax.all_to_all(outgoing.reshape(n_dev, slot_count, feature_width), ('memb...  7.39 us
  transfers between devices with their start and end apart: 8, of which 8 were waited for; matrix products, arithmetic and copies ran while one was open for 1% of the time, Pallas kernels for 0%

commit v1 on v0

--- a/solution.py
+++ b/solution.py
@@ -44,29 +44,24 @@
         tiled=True,
     )
     arrived = arrived.reshape(n_dev * slot_count, feature_width)
-    arrived_count = arrived.shape[0]
     own_member = lax.axis_index("member") // 2
     gain_here = lax.dynamic_index_in_dim(norm_gain, own_member, 0, keepdims=False)
     normed = rms_scale(arrived.astype(jnp.float32), gain_here).astype(jnp.bfloat16)
-    partner_normed = from_partner(normed, "member", 0)
-    both_rows = jnp.concatenate([normed, partner_normed], axis=0)
-    up_local = w_up[0]
-    down_local = w_down[0]
+    up_local = jnp.concatenate([w_up[0], from_partner(w_up[0], "member", 0)], axis=1)
+    down_local = jnp.concatenate([w_down[0], from_partner(w_down[0], "member", 0)], axis=0)
     hidden = jax.nn.gelu(
         jnp.dot(
-            lax.all_gather(both_rows, "tp", axis=0, tiled=True),
+            lax.all_gather(normed, "tp", axis=0, tiled=True),
             up_local,
             preferred_element_type=jnp.float32,
         )
     ).astype(jnp.bfloat16)
-    half_change = lax.psum_scatter(
+    change = lax.psum_scatter(
         jnp.dot(hidden, down_local, preferred_element_type=jnp.float32),
         "tp",
         scatter_dimension=0,
         tiled=True,
     )
-    partner_part = from_partner(half_change[arrived_count:], "member", 0)
-    change = half_change[:arrived_count] + partner_part
     predicted = (arrived.astype(jnp.float32) + change).astype(jnp.bfloat16)
     returned = lax.all_to_all(
         predicted.reshape(n_dev, slot_count, feature_width),

time: 331 us -> 219 us (0.66)
  waiting for transfers between devices: 270 us -> 162 us
    reduce_scatter x1, waiting for transfers between devices: 143 us -> 75.6 us  [local(): lax.psum_scatter(jnp.dot(hidden, down_local, preferred_element_type=jnp.f...]
    all_gather x1, waiting for transfers between devices: 79.5 us -> 40.4 us  [local(): lax.all_gather(normed, 'tp', axis=0, tiled=True)]
  transfers between devices with their start and end apart: 8 -> 8, of which waited for: 8 -> 7; matrix products, arithmetic and copies ran while one was open for 1% -> 2% of each run, Pallas kernels for 0% -> 0%
where the time goes in v1:
time: 219 us
  waiting for transfers between devices  162 us (74%)
  starting transfers between devices  20.2 us (9%)
  between operations  14.2 us (6%)
  matrix products  12.2 us (6%)
  other arithmetic  7.14 us (3%)
  local copies, waits for them, and re-layouts  3.1 us (1%)
    reduce_scatter x1, waiting for transfers between devices, local(): lax.psum_scatter(jnp.dot(hidden, down_local, preferred_element_type=jnp.f...  75.6 us
    all_gather x1, waiting for transfers between devices, local(): lax.all_gather(normed, 'tp', axis=0, tiled=True)  40.4 us
    all_to_all x1, waiting for transfers between devices, local(): lax.all_to_all(outgoing.reshape(n_dev, slot_count, feature_width), ('memb...  14.9 us
    all_to_all x1, waiting for transfers between devices, local(): lax.all_to_all(predicted.reshape(n_dev, slot_count, feature_width), ('mem...  14.4 us
    all_to_all x1, waiting for transfers between devices, local(): lax.all_to_all(packed.reshape(n_dev, per_learner, feature_width), ('membe...  8.74 us
    dot_general x1, matrix products, local(): jnp.dot(hidden, down_local, preferred_element_type=jnp.float32)  8.7 us
    all_to_all x1, starting transfers between devices, local(): lax.all_to_all(outgoing.reshape(n_dev, slot_count, feature_width), ('memb...  7.39 us
    all_to_all x1, starting transfers between devices, local(): lax.all_to_all(predicted.reshape(n_dev, slot_count, feature_width), ('mem...  5.21 us
  transfers between devices with their start and end apart: 8, of which 7 were waited for; matrix products, arithmetic and copies ran while one was open for 2% of the time, Pallas kernels for 0%

profile of v1, /device:TPU:0, one launch (start us, length us, event | category | flops | bytes accessed | tf_op | source)
XLA Modules:
  0.0 218.8 jit_solution(4283796861576501177)
XLA Ops:
  7.2 0.9 fusion.41
  8.3 0.8 select_reduce_fusion
  9.1 0.7 multiply_add_fusion
  9.8 1.1 convolution_convert_fusion
  10.9 7.4 %all-to-all-start.1 = ((bf16[16,16,1024]{2,1,0:T(8,128)(2,1)}), bf16[16,16,1024]{2,1,0:T(8,128)(2,1)S(1)}, u32[]{:S(2)}, u32[]{:S(2)}) async-start(bf16[16,16,1024]{2,1,0:T(8,128)(2,1)} %bitcast.2), calls=%async_computation.1 | async-start | bytes 1048576 | tf_op jit(solution)/shard_map/all_to_all | solution.py:39
  18.3 0.7 constant_dynamic-slice_fusion
  19.0 14.9 %all-to-all-done.1 = bf16[16,16,1024]{2,1,0:T(8,128)(2,1)S(1)} async-done(((bf16[16,16,1024]{2,1,0:T(8,128)(2,1)}), bf16[16,16,1024]{2,1,0:T(8,128)(2,1)S(1)}, u32[]{:S(2)}, u32[]{:S(2)}) %all-to-all-start.1) | async-done | bytes 524320 | tf_op jit(solution)/shard_map/all_to_all | solution.py:39
  34.2 1.0 fusion.29
  35.9 2.8 %collective-permute-done = bf16[1024,512]{1,0:T(8,128)(2,1)S(1)} collective-permute-done((bf16[1024,512]{1,0:T(8,128)(2,1)S(1)}, bf16[1024,512]{1,0:T(8,128)(2,1)S(1)}, u32[]{:S(2)}, u32[]{:S(2)}) %collective-permute-start) | collective-permute-done | bytes 1048608 | tf_op jit(solution)/shard_map/ppermute | solution.py:8
  38.6 1.0 copy-done.4
  39.6 40.4 %all-gather.2.cloned.1.call-done = bf16[1024,1024]{1,0:T(8,128)(2,1)} async-done(((bf16[256,1024]{1,0:T(8,128)(2,1)}), bf16[1024,1024]{1,0:T(8,128)(2,1)}) %all-gather.2.cloned.1.call-update) | async-done | bytes 2097168 | tf_op jit(solution)/shard_map/all_gather | solution.py:54
  80.0 8.7 %fusion.8 = f32[1024,1024]{1,0:T(8,128)} fusion(bf16[512,1024]{1,0:T(8,128)(2,1)} %collective-permute-done.1, bf16[512,1024]{1,0:T(8,128)(2,1)S(1)} %bitcast.34, bf16[1024,1024]{1,0:T(8,128)(2,1)} %all-gather.2.cloned.1.call-done, bf16[1024,512]{1,0:T(8,128)(2,1)} %copy-done.4, bf16[1024,512]{1,0:T(8,128)(2,1)S(1)} %bitcast.36), kind=kOutput, calls=%fused_computation.9 | convolution fusion | flops 4312793088 | bytes 10485760 | tf_op jit(solution)/shard_map/dot_general | solution.py:60
  88.7 75.6 %reduce-scatter.2.cloned.1.call-done = f32[256,1024]{1,0:T(8,128)} async-done(((f32[1024,1024]{1,0:T(8,128)}), f32[256,1024]{1,0:T(8,128)}) %reduce-scatter.2.cloned.1.call-update) | async-done | bytes 1048592 | tf_op jit(solution)/shard_map/reduce_scatter | solution.py:59
  164.4 2.2 fusion.30
  166.5 5.2 %all-to-all-start.2 = ((bf16[16,16,1024]{2,1,0:T(8,128)(2,1)}), bf16[16,16,1024]{2,1,0:T(8,128)(2,1)S(1)}, u32[]{:S(2)}, u32[]{:S(2)}) async-start(bf16[16,16,1024]{2,1,0:T(8,128)(2,1)} %bitcast.7), calls=%async_computation.3 | async-start | bytes 1048576 | tf_op jit(solution)/shard_map/all_to_all | solution.py:66
  172.4 0.7 all_to_all.15
  173.1 14.4 %all-to-all-done.2 = bf16[16,16,1024]{2,1,0:T(8,128)(2,1)S(1)} async-done(((bf16[16,16,1024]{2,1,0:T(8,128)(2,1)}), bf16[16,16,1024]{2,1,0:T(8,128)(2,1)S(1)}, u32[]{:S(2)}, u32[]{:S(2)}) %all-to-all-start.2) | async-done | bytes 524320 | tf_op jit(solution)/shard_map/all_to_all | solution.py:66
  187.5 3.5 %all-to-all-start = ((s32[16,1,8]{2,1,0:T(1,128)}), s32[16,1,8]{2,1,0:T(1,128)S(1)}, u32[]{:S(2)}, u32[]{:S(2)}) async-start(s32[16,1,8]{2,1,0:T(1,128)} %bitcast), calls=%async_computation | async-start | bytes 16384 | tf_op jit(solution)/shard_map/all_to_all | solution.py:97
  190.9 1.2 fusion.25
  192.1 5.1 %all-to-all-done = s32[16,1,8]{2,1,0:T(1,128)S(1)} async-done(((s32[16,1,8]{2,1,0:T(1,128)}), s32[16,1,8]{2,1,0:T(1,128)S(1)}, u32[]{:S(2)}, u32[]{:S(2)}) %all-to-all-start) | async-done | bytes 544 | tf_op jit(solution)/shard_map/all_to_all | solution.py:97
  197.2 3.5 %all-to-all-start.3 = ((bf16[16,8,1024]{2,1,0:T(8,128)(2,1)}), bf16[16,8,1024]{2,1,0:T(8,128)(2,1)S(1)}, u32[]{:S(2)}, u32[]{:S(2)}) async-start(bf16[16,8,1024]{2,1,0:T(8,128)(2,1)} %fusion.25), calls=%async_computation.4 | async-start | bytes 524288 | tf_op jit(solution)/shard_map/all_to_all | solution.py:90
  201.2 0.7 reduce.4
  202.0 8.7 %all-to-all-done.3 = bf16[16,8,1024]{2,1,0:T(8,128)(2,1)S(1)} async-done(((bf16[16,8,1024]{2,1,0:T(8,128)(2,1)}), bf16[16,8,1024]{2,1,0:T(8,128)(2,1)S(1)}, u32[]{:S(2)}, u32[]{:S(2)}) %all-to-all-start.3) | async-done | bytes 262176 | tf_op jit(solution)/shard_map/all_to_all | solution.py:90
  211.1 0.9 fusion.26
  (36 shorter events, 2.7 us)
Async XLA Ops:
  7.2 2.6 %copy-start = (bf16[128,1024]{1,0:T(8,128)(2,1)S(1)}, bf16[128,1024]{1,0:T(8,128)(2,1)}, u32[]{:S(2)}) copy-start(bf16[128,1024]{1,0:T(8,128)(2,1)} %param.8) | copy-start | bytes 786436
  7.2 28.1 %copy-start.3 = (bf16[1,1024,512]{2,1,0:T(8,128)(2,1)S(1)}, bf16[1,1024,512]{2,1,0:T(8,128)(2,1)}, u32[]{:S(2)}) copy-start(bf16[1,1024,512]{2,1,0:T(8,128)(2,1)} %param.12) | copy-start | bytes 3145732
  7.2 28.2 %copy-start.2 = (bf16[1,512,1024]{2,1,0:T(8,128)(2,1)S(1)}, bf16[1,512,1024]{2,1,0:T(8,128)(2,1)}, u32[]{:S(2)}) copy-start(bf16[1,512,1024]{2,1,0:T(8,128)(2,1)} %param.13) | copy-start | bytes 3145732
  10.9 23.1 %all-to-all-start.1 = ((bf16[16,16,1024]{2,1,0:T(8,128)(2,1)}), bf16[16,16,1024]{2,1,0:T(8,128)(2,1)S(1)}, u32[]{:S(2)}, u32[]{:S(2)}) async-start(bf16[16,16,1024]{2,1,0:T(8,128)(2,1)} %bitcast.2), calls=%async_computation.1 | async-start | bytes 1048576 | tf_op jit(solution)/shard_map/all_to_all | solution.py:39
  18.3 61.7 %all-gather.2.cloned.1.call-start = ((), (), s32[]{:S(2)}) async-start(), calls=%async_computation.5 | async-start | bytes 2621440 | tf_op jit(solution)/shard_map/all_gather | solution.py:54
  35.2 129.1 %reduce-scatter.2.cloned.1.call-start = ((), (), s32[]{:S(2)}) async-start(), calls=%async_computation.6 | async-start | bytes 5242880 | tf_op jit(solution)/shard_map/reduce_scatter | solution.py:59
  35.3 3.3 %collective-permute-start = (bf16[1024,512]{1,0:T(8,128)(2,1)S(1)}, bf16[1024,512]{1,0:T(8,128)(2,1)S(1)}, u32[]{:S(2)}, u32[]{:S(2)}) collective-permute-start(bf16[1024,512]{1,0:T(8,128)(2,1)S(1)} %bitcast.35), channel_id=1, source_target_pairs={{0,4},{4,0},{8,12},{12,8},{1,5},{5,1},{9,13},{13,9},{2,6},{6,2},{1... | collective-permute-start | bytes 3145736 | tf_op jit(solution)/shard_map/ppermute | solution.py:8
  35.4 4.3 %collective-permute-start.1 = (bf16[512,1024]{1,0:T(8,128)(2,1)S(1)}, bf16[512,1024]{1,0:T(8,128)(2,1)}, u32[]{:S(2)}, u32[]{:S(2)}) collective-permute-start(bf16[512,1024]{1,0:T(8,128)(2,1)S(1)} %bitcast.33), channel_id=1, source_target_pairs={{0,4},{4,0},{8,12},{12,8},{1,5},{5,1},{9,13},{13,9},{2,6},{6,2},{1... | collective-permute-start | bytes 3145736 | tf_op jit(solution)/shard_map/ppermute | solution.py:8
  38.6 1.0 copy-start.4
  88.7 83.1 %copy-start.7 = (s32[128]{0:T(128)S(1)}, s32[128]{0:T(128)}, u32[]{:S(2)}) copy-start(s32[128]{0:T(128)} %param.10) | copy-start | bytes 1540
  88.7 122.4 %copy-start.5 = (bf16[1024,128]{1,0:T(8,128)(2,1)S(1)}, bf16[1024,128]{1,0:T(8,128)(2,1)}, u32[]{:S(2)}) copy-start(bf16[1024,128]{1,0:T(8,128)(2,1)} %param.15) | copy-start | bytes 786436
  88.7 122.4 %copy-start.6 = (f32[1024]{0:T(1024)S(1)}, f32[1024]{0:T(1024)}, u32[]{:S(2)}) copy-start(f32[1024]{0:T(1024)} %param.14) | copy-start | bytes 12292
  166.5 20.9 %all-to-all-start.2 = ((bf16[16,16,1024]{2,1,0:T(8,128)(2,1)}), bf16[16,16,1024]{2,1,0:T(8,128)(2,1)S(1)}, u32[]{:S(2)}, u32[]{:S(2)}) async-start(bf16[16,16,1024]{2,1,0:T(8,128)(2,1)} %bitcast.7), calls=%async_computation.3 | async-start | bytes 1048576 | tf_op jit(solution)/shard_map/all_to_all | solution.py:66
  187.5 9.7 %all-to-all-start = ((s32[16,1,8]{2,1,0:T(1,128)}), s32[16,1,8]{2,1,0:T(1,128)S(1)}, u32[]{:S(2)}, u32[]{:S(2)}) async-start(s32[16,1,8]{2,1,0:T(1,128)} %bitcast), calls=%async_computation | async-start | bytes 16384 | tf_op jit(solution)/shard_map/all_to_all | solution.py:97
  197.2 13.6 %all-to-all-start.3 = ((bf16[16,8,1024]{2,1,0:T(8,128)(2,1)}), bf16[16,8,1024]{2,1,0:T(8,128)(2,1)S(1)}, u32[]{:S(2)}, u32[]{:S(2)}) async-start(bf16[16,8,1024]{2,1,0:T(8,128)(2,1)} %fusion.25), calls=%async_computation.4 | async-start | bytes 524288 | tf_op jit(solution)/shard_map/all_to_all | solution.py:90
  211.0 1.0 copy-start.1
Sparse Core Ops, SparseCore 0:
  35.4 44.6 all-gather.1
  88.9 75.4 reduce-scatter.1

commit v2 on v1

--- a/solution.py
+++ b/solution.py
@@ -57,11 +57,11 @@
         )
     ).astype(jnp.bfloat16)
     change = lax.psum_scatter(
-        jnp.dot(hidden, down_local, preferred_element_type=jnp.float32),
+        jnp.dot(hidden, down_local, preferred_element_type=jnp.float32).astype(jnp.bfloat16),
         "tp",
         scatter_dimension=0,
         tiled=True,
-    )
+    ).astype(jnp.float32)
     predicted = (arrived.astype(jnp.float32) + change).astype(jnp.bfloat16)
     returned = lax.all_to_all(
         predicted.reshape(n_dev, slot_count, feature_width),

time: 219 us -> 185 us (0.84)
  waiting for transfers between devices: 162 us -> 130 us
    reduce_scatter x1, waiting for transfers between devices: 75.6 us -> 42.7 us  [local(): lax.psum_scatter(jnp.dot(hidden, down_local, preferred_element_type=jnp.f...]
where the time goes in v2:
time: 185 us; the launch traced here: 184 us
  waiting for transfers between devices  130 us (70%)
  starting transfers between devices  19.1 us (10%)
  between operations  14.3 us (8%)
  matrix products  11.5 us (6%)
  other arithmetic  7.02 us (4%)
  local copies, waits for them, and re-layouts  2.45 us (1%)
    reduce_scatter x1, waiting for transfers between devices, local(): lax.psum_scatter(jnp.dot(hidden, down_local, preferred_element_type=jnp.f...  42.7 us
    all_gather x1, waiting for transfers between devices, local(): lax.all_gather(normed, 'tp', axis=0, tiled=True)  40.4 us
    all_to_all x1, waiting for transfers between devices, local(): lax.all_to_all(outgoing.reshape(n_dev, slot_count, feature_width), ('memb...  15.6 us
    all_to_all x1, waiting for transfers between devices, local(): lax.all_to_all(predicted.reshape(n_dev, slot_count, feature_width), ('mem...  14.4 us
    all_to_all x1, waiting for transfers between devices, local(): lax.all_to_all(packed.reshape(n_dev, per_learner, feature_width), ('membe...  8.74 us
    dot_general x1, matrix products, local(): jnp.dot(hidden, down_local, preferred_element_type=jnp.float32)  8.09 us
    all_to_all x1, starting transfers between devices, local(): lax.all_to_all(outgoing.reshape(n_dev, slot_count, feature_width), ('memb...  7.39 us
    all_to_all x1, waiting for transfers between devices, local(): lax.all_to_all(packed_spot.reshape(n_dev, per_learner), ('member', 'tp'),...  5.1 us
  transfers between devices with their start and end apart: 8, of which 7 were waited for; matrix products, arithmetic and copies ran while one was open for 2% of the time, Pallas kernels for 0%

profile of v2, /device:TPU:0, one launch (start us, length us, event | category | flops | bytes accessed | tf_op | source)
XLA Modules:
  0.0 184.0 jit_solution(679460454926450507)
XLA Ops:
  7.2 0.8 fusion.46
  8.2 0.9 select_reduce_fusion
  9.1 0.7 multiply_add_fusion
  9.8 1.1 convolution_convert_fusion
  10.9 7.4 %all-to-all-start.1 = ((bf16[16,16,1024]{2,1,0:T(8,128)(2,1)}), bf16[16,16,1024]{2,1,0:T(8,128)(2,1)S(1)}, u32[]{:S(2)}, u32[]{:S(2)}) async-start(bf16[16,16,1024]{2,1,0:T(8,128)(2,1)} %bitcast.2), calls=%async_computation.1 | async-start | bytes 1048576 | tf_op jit(solution)/shard_map/all_to_all | solution.py:39
  18.4 15.6 %all-to-all-done.1 = bf16[16,16,1024]{2,1,0:T(8,128)(2,1)S(1)} async-done(((bf16[16,16,1024]{2,1,0:T(8,128)(2,1)}), bf16[16,16,1024]{2,1,0:T(8,128)(2,1)S(1)}, u32[]{:S(2)}, u32[]{:S(2)}) %all-to-all-start.1) | async-done | bytes 524320 | tf_op jit(solution)/shard_map/all_to_all | solution.py:39
  34.2 1.0 fusion.34
  35.9 2.8 %collective-permute-done = bf16[1024,512]{1,0:T(8,128)(2,1)S(1)} collective-permute-done((bf16[1024,512]{1,0:T(8,128)(2,1)S(1)}, bf16[1024,512]{1,0:T(8,128)(2,1)S(1)}, u32[]{:S(2)}, u32[]{:S(2)}) %collective-permute-start) | collective-permute-done | bytes 1048608 | tf_op jit(solution)/shard_map/ppermute | solution.py:8
  38.6 1.0 copy-done.5
  39.7 40.4 %all-gather.2.cloned.1.call-done = bf16[1024,1024]{1,0:T(8,128)(2,1)} async-done(((bf16[256,1024]{1,0:T(8,128)(2,1)}), bf16[1024,1024]{1,0:T(8,128)(2,1)}) %all-gather.2.cloned.1.call-update) | async-done | bytes 2097168 | tf_op jit(solution)/shard_map/all_gather | solution.py:54
  80.0 8.1 %fusion.21 = bf16[1024,1024]{1,0:T(8,128)(2,1)} fusion(bf16[512,1024]{1,0:T(8,128)(2,1)} %collective-permute-done.1, bf16[512,1024]{1,0:T(8,128)(2,1)S(1)} %bitcast.34, bf16[1024,1024]{1,0:T(8,128)(2,1)} %all-gather.2.cloned.1.call-done, bf16[1024,512]{1,0:T(8,128)(2,1)} %copy-done.5, bf16[1024,512]{1,0:T(8,128)(2,1)S(1)} %bitcast.36), kind=kOutput, calls=%fused_computation.21 | convolution fusion | flops 4313841664 | bytes 8388608 | tf_op jit(solution)/shard_map/dot_general | solution.py:60
  88.2 42.7 %reduce-scatter.2.cloned.1.call-done = bf16[256,1024]{1,0:T(8,128)(2,1)} async-done(((bf16[1024,1024]{1,0:T(8,128)(2,1)}), bf16[256,1024]{1,0:T(8,128)(2,1)}) %reduce-scatter.2.cloned.1.call-update) | async-done | bytes 524304 | tf_op jit(solution)/shard_map/reduce_scatter | solution.py:59
  130.9 2.0 %fusion.35 = bf16[256,1024]{1,0:T(8,128)(2,1)} fusion(bf16[16,16,1024]{2,1,0:T(8,128)(2,1)S(1)} %all-to-all-done.1, bf16[256,1024]{1,0:T(8,128)(2,1)} %reduce-scatter.2.cloned.1.call-done), kind=kLoop, calls=%fused_computation.35 | loop fusion | flops 1048576 | bytes 1572864 | tf_op jit(solution)/shard_map/convert_element_type | solution.py:65
  132.9 4.0 %all-to-all-start.2 = ((bf16[16,16,1024]{2,1,0:T(8,128)(2,1)}), bf16[16,16,1024]{2,1,0:T(8,128)(2,1)S(1)}, u32[]{:S(2)}, u32[]{:S(2)}) async-start(bf16[16,16,1024]{2,1,0:T(8,128)(2,1)} %bitcast.7), calls=%async_computation.3 | async-start | bytes 1048576 | tf_op jit(solution)/shard_map/all_to_all | solution.py:66
  137.5 0.7 all_to_all.15
  138.2 14.4 %all-to-all-done.2 = bf16[16,16,1024]{2,1,0:T(8,128)(2,1)S(1)} async-done(((bf16[16,16,1024]{2,1,0:T(8,128)(2,1)}), bf16[16,16,1024]{2,1,0:T(8,128)(2,1)S(1)}, u32[]{:S(2)}, u32[]{:S(2)}) %all-to-all-start.2) | async-done | bytes 524320 | tf_op jit(solution)/shard_map/all_to_all | solution.py:66
  152.6 3.5 %all-to-all-start = ((s32[16,1,8]{2,1,0:T(1,128)}), s32[16,1,8]{2,1,0:T(1,128)S(1)}, u32[]{:S(2)}, u32[]{:S(2)}) async-start(s32[16,1,8]{2,1,0:T(1,128)} %bitcast), calls=%async_computation | async-start | bytes 16384 | tf_op jit(solution)/shard_map/all_to_all | solution.py:97
  156.1 1.1 fusion.30
  157.3 5.1 %all-to-all-done = s32[16,1,8]{2,1,0:T(1,128)S(1)} async-done(((s32[16,1,8]{2,1,0:T(1,128)}), s32[16,1,8]{2,1,0:T(1,128)S(1)}, u32[]{:S(2)}, u32[]{:S(2)}) %all-to-all-start) | async-done | bytes 544 | tf_op jit(solution)/shard_map/all_to_all | solution.py:97
  162.4 3.5 %all-to-all-start.3 = ((bf16[16,8,1024]{2,1,0:T(8,128)(2,1)}), bf16[16,8,1024]{2,1,0:T(8,128)(2,1)S(1)}, u32[]{:S(2)}, u32[]{:S(2)}) async-start(bf16[16,8,1024]{2,1,0:T(8,128)(2,1)} %fusion.30), calls=%async_computation.4 | async-start | bytes 524288 | tf_op jit(solution)/shard_map/all_to_all | solution.py:90
  165.9 0.5 broadcast.140
  166.4 0.7 reduce.4
  167.2 8.7 %all-to-all-done.3 = bf16[16,8,1024]{2,1,0:T(8,128)(2,1)S(1)} async-done(((bf16[16,8,1024]{2,1,0:T(8,128)(2,1)}), bf16[16,8,1024]{2,1,0:T(8,128)(2,1)S(1)}, u32[]{:S(2)}, u32[]{:S(2)}) %all-to-all-start.3) | async-done | bytes 262176 | tf_op jit(solution)/shard_map/all_to_all | solution.py:90
  176.3 0.9 fusion.31
  (38 shorter events, 2.1 us)
Async XLA Ops:
  7.2 2.6 %copy-start = (bf16[128,1024]{1,0:T(8,128)(2,1)S(1)}, bf16[128,1024]{1,0:T(8,128)(2,1)}, u32[]{:S(2)}) copy-start(bf16[128,1024]{1,0:T(8,128)(2,1)} %param.8) | copy-start | bytes 786436
  7.2 11.2 %copy-start.2 = (f32[2,1024]{1,0:T(2,128)S(1)}, f32[2,1024]{1,0:T(2,128)}, u32[]{:S(2)}) copy-start(f32[2,1024]{1,0:T(2,128)} %param.11) | copy-start | bytes 24580
  8.0 27.3 %copy-start.4 = (bf16[1,1024,512]{2,1,0:T(8,128)(2,1)S(1)}, bf16[1,1024,512]{2,1,0:T(8,128)(2,1)}, u32[]{:S(2)}) copy-start(bf16[1,1024,512]{2,1,0:T(8,128)(2,1)} %param.12) | copy-start | bytes 3145732
  8.0 27.4 %copy-start.3 = (bf16[1,512,1024]{2,1,0:T(8,128)(2,1)S(1)}, bf16[1,512,1024]{2,1,0:T(8,128)(2,1)}, u32[]{:S(2)}) copy-start(bf16[1,512,1024]{2,1,0:T(8,128)(2,1)} %param.13) | copy-start | bytes 3145732
  10.9 23.1 %all-to-all-start.1 = ((bf16[16,16,1024]{2,1,0:T(8,128)(2,1)}), bf16[16,16,1024]{2,1,0:T(8,128)(2,1)S(1)}, u32[]{:S(2)}, u32[]{:S(2)}) async-start(bf16[16,16,1024]{2,1,0:T(8,128)(2,1)} %bitcast.2), calls=%async_computation.1 | async-start | bytes 1048576 | tf_op jit(solution)/shard_map/all_to_all | solution.py:39
  18.3 61.8 %all-gather.2.cloned.1.call-start = ((), (), s32[]{:S(2)}) async-start(), calls=%async_computation.5 | async-start | bytes 2621440 | tf_op jit(solution)/shard_map/all_gather | solution.py:54
  35.2 95.6 %reduce-scatter.2.cloned.1.call-start = ((), (), s32[]{:S(2)}) async-start(), calls=%async_computation.6 | async-start | bytes 2621440 | tf_op jit(solution)/shard_map/reduce_scatter | solution.py:59
  35.3 3.3 %collective-permute-start = (bf16[1024,512]{1,0:T(8,128)(2,1)S(1)}, bf16[1024,512]{1,0:T(8,128)(2,1)S(1)}, u32[]{:S(2)}, u32[]{:S(2)}) collective-permute-start(bf16[1024,512]{1,0:T(8,128)(2,1)S(1)} %bitcast.35), channel_id=1, source_target_pairs={{0,4},{4,0},{8,12},{12,8},{1,5},{5,1},{9,13},{13,9},{2,6},{6,2},{1... | collective-permute-start | bytes 3145736 | tf_op jit(solution)/shard_map/ppermute | solution.py:8
  35.4 4.3 %collective-permute-start.1 = (bf16[512,1024]{1,0:T(8,128)(2,1)S(1)}, bf16[512,1024]{1,0:T(8,128)(2,1)}, u32[]{:S(2)}, u32[]{:S(2)}) collective-permute-start(bf16[512,1024]{1,0:T(8,128)(2,1)S(1)} %bitcast.33), channel_id=1, source_target_pairs={{0,4},{4,0},{8,12},{12,8},{1,5},{5,1},{9,13},{13,9},{2,6},{6,2},{1... | collective-permute-start | bytes 3145736 | tf_op jit(solution)/shard_map/ppermute | solution.py:8
  38.6 1.0 copy-start.5
  88.1 48.8 %copy-start.8 = (s32[128]{0:T(128)S(1)}, s32[128]{0:T(128)}, u32[]{:S(2)}) copy-start(s32[128]{0:T(128)} %param.10) | copy-start | bytes 1540
  88.1 88.1 %copy-start.6 = (bf16[1024,128]{1,0:T(8,128)(2,1)S(1)}, bf16[1024,128]{1,0:T(8,128)(2,1)}, u32[]{:S(2)}) copy-start(bf16[1024,128]{1,0:T(8,128)(2,1)} %param.15) | copy-start | bytes 786436
  88.1 88.1 %copy-start.7 = (f32[1024]{0:T(1024)S(1)}, f32[1024]{0:T(1024)}, u32[]{:S(2)}) copy-start(f32[1024]{0:T(1024)} %param.14) | copy-start | bytes 12292
  132.9 19.7 %all-to-all-start.2 = ((bf16[16,16,1024]{2,1,0:T(8,128)(2,1)}), bf16[16,16,1024]{2,1,0:T(8,128)(2,1)S(1)}, u32[]{:S(2)}, u32[]{:S(2)}) async-start(bf16[16,16,1024]{2,1,0:T(8,128)(2,1)} %bitcast.7), calls=%async_computation.3 | async-start | bytes 1048576 | tf_op jit(solution)/shard_map/all_to_all | solution.py:66
  152.6 9.7 %all-to-all-start = ((s32[16,1,8]{2,1,0:T(1,128)}), s32[16,1,8]{2,1,0:T(1,128)S(1)}, u32[]{:S(2)}, u32[]{:S(2)}) async-start(s32[16,1,8]{2,1,0:T(1,128)} %bitcast), calls=%async_computation | async-start | bytes 16384 | tf_op jit(solution)/shard_map/all_to_all | solution.py:97
  162.4 13.6 %all-to-all-start.3 = ((bf16[16,8,1024]{2,1,0:T(8,128)(2,1)}), bf16[16,8,1024]{2,1,0:T(8,128)(2,1)S(1)}, u32[]{:S(2)}, u32[]{:S(2)}) async-start(bf16[16,8,1024]{2,1,0:T(8,128)(2,1)} %fusion.30), calls=%async_computation.4 | async-start | bytes 524288 | tf_op jit(solution)/shard_map/all_to_all | solution.py:90
  176.2 1.0 copy-start.1
Sparse Core Ops, SparseCore 0:
  35.4 44.6 all-gather.1
  88.3 42.5 reduce-scatter.1

commit v3 on v2

v3 whole, which is shorter than its diff:
```python
import jax
import jax.numpy as jnp
from jax import lax
from jax.sharding import PartitionSpec as P


PARTIAL_DTYPE = jnp.float32


def from_partner(value, axis, distance):
    return lax.ppermute(value, axis, [(i, i ^ 1 << distance) for i in range(lax.axis_size(axis))])


def rms_scale(values, gain):
    mean_square = jnp.mean(values * values, axis=-1, keepdims=True)
    return values * lax.rsqrt(mean_square + 1e-06) * gain


def running_rank(member_hits):
    return jnp.sum((jnp.cumsum(member_hits, axis=0) - member_hits) * member_hits, axis=1)


def local(states, member_of, place, norm_gain, w_up, w_down, policy_gain, w_policy):
    n_member = lax.axis_size("member")
    n_tp = lax.axis_size("tp")
    n_dev = n_member * n_tp
    member_total = n_member // 2
    rows_here = states.shape[0]
    feature_width = states.shape[1]
    pair_slots = rows_here // member_total
    all_place = lax.all_gather(place, ("member", "tp"), axis=0, tiled=True)
    up_local = jnp.concatenate([w_up[0], from_partner(w_up[0], "member", 0)], axis=1)
    down_local = jnp.concatenate([w_down[0], from_partner(w_down[0], "member", 0)], axis=0)
    member = member_of[:, 0]
    member_hits = (member[:, None] == jnp.arange(member_total, dtype=jnp.int32)[None, :]).astype(
        jnp.int32
    )
    earlier = running_rank(member_hits)
    target = (2 * member + earlier % 2) * pair_slots + earlier // 2
    picker = (jnp.arange(n_member * pair_slots, dtype=jnp.int32)[:, None] == target[None, :]).astype(
        jnp.bfloat16
    )
    outgoing = jnp.dot(picker, states, preferred_element_type=jnp.float32).astype(jnp.bfloat16)
    arrived = lax.all_to_all(
        outgoing.reshape(n_member, pair_slots, feature_width),
        "member",
        split_axis=0,
        concat_axis=0,
        tiled=True,
    )
    arrived = arrived.reshape(n_member * pair_slots, feature_width)
    own_member = lax.axis_index("member") // 2
    gain_here = lax.dynamic_index_in_dim(norm_gain, own_member, 0, keepdims=False)
    normed = rms_scale(arrived.astype(jnp.float32), gain_here).astype(jnp.bfloat16)
    hidden = jax.nn.gelu(
        jnp.dot(
            lax.all_gather(normed, "tp", axis=0, tiled=True),
            up_local,
            preferred_element_type=jnp.float32,
        )
    ).astype(jnp.bfloat16)
    change = lax.psum_scatter(
        jnp.dot(hidden, down_local, preferred_element_type=jnp.float32).astype(PARTIAL_DTYPE),
        "tp",
        scatter_dimension=0,
        tiled=True,
    ).astype(jnp.float32)
    predicted = (arrived.astype(jnp.float32) + change).astype(jnp.bfloat16)
    returned = lax.all_to_all(
        predicted.reshape(n_member, pair_slots, feature_width),
        "member",
        split_axis=0,
        concat_axis=0,
        tiled=True,
    )
    returned = returned.reshape(n_member * pair_slots, feature_width)
    own_rows = jnp.einsum("sr,sd->rd", picker, returned, preferred_element_type=jnp.float32).astype(
        jnp.bfloat16
    )
    per_learner = rows_here // n_dev
    learner = place // rows_here
    learner_hits = (learner[:, None] == jnp.arange(n_dev, dtype=jnp.int32)[None, :]).astype(
        jnp.int32
    )
    lane_index = learner * per_learner + running_rank(learner_hits)
    placer = jnp.arange(rows_here, dtype=jnp.int32)[:, None] == lane_index[None, :]
    packed = jnp.dot(
        placer.astype(jnp.bfloat16), own_rows, preferred_element_type=jnp.float32
    ).astype(jnp.bfloat16)
    arrivals = lax.all_to_all(
        packed.reshape(n_dev, per_learner, feature_width),
        ("member", "tp"),
        split_axis=0,
        concat_axis=0,
        tiled=True,
    )
    arrivals = arrivals.reshape(n_dev * per_learner, feature_width)
    me = lax.axis_index("member") * n_tp + lax.axis_index("tp")
    source_place = all_place.reshape(n_dev, rows_here)
    mine = (source_place // rows_here == me).astype(jnp.int32)
    slot_of = (
        jnp.arange(n_dev, dtype=jnp.int32)[:, None] * per_learner
        + jnp.cumsum(mine, axis=1)
        - mine
    ).reshape(-1)
    spot_of = (source_place % rows_here).reshape(-1)
    mine = mine.reshape(-1)
    spot_pick = (
        (jnp.arange(rows_here, dtype=jnp.int32)[:, None] == spot_of[None, :]) & (mine[None, :] > 0)
    ).astype(jnp.bfloat16)
    slot_pick = (slot_of[:, None] == jnp.arange(n_dev * per_learner, dtype=jnp.int32)[None, :]).astype(
        jnp.bfloat16
    )
    settle = jnp.dot(spot_pick, slot_pick, preferred_element_type=jnp.float32).astype(jnp.bfloat16)
    imagined = jnp.dot(settle, arrivals, preferred_element_type=jnp.float32).astype(jnp.bfloat16)
    policy_normed = rms_scale(imagined.astype(jnp.float32), policy_gain).astype(jnp.bfloat16)
    action = jnp.tanh(jnp.dot(policy_normed, w_policy, preferred_element_type=jnp.float32)).astype(
        jnp.bfloat16
    )
    return (imagined, action)


def solution(mesh):
    in_specs = (
        P(("rep", "member", "tp"), None),
        P(("rep", "member", "tp"), None),
        P(("rep", "member", "tp")),
        P(),
        P("member", None, "tp"),
        P("member", "tp", None),
        P(),
        P(),
    )
    out_specs = (P(("rep", "member", "tp"), None), P(("rep", "member", "tp"), None))
    return jax.shard_map(local, mesh=mesh, in_specs=in_specs, out_specs=out_specs, check_vma=False)
```

time: 185 us -> 196 us (1.059)
  blocking collectives: 0 us -> 30.9 us
  waiting for transfers between devices: 130 us -> 116 us
  starting transfers between devices: 19.1 us -> 12.6 us
    all_gather x0 -> x1, blocking collectives: none -> 30.9 us  [local(): all_place = lax.all_gather(place, ('member', 'tp'), axis=0, tiled=True)]
    all_to_all x3 -> x2, waiting for transfers between devices: 35.1 us -> 16.9 us  [the longest x1 8.78 us: local(): lax.all_to_all(predicted.reshape(n_member, pair_slots, feature_width), 'm...]
    all_to_all x3 -> x2, starting transfers between devices: 14.9 us -> 7.7 us  [the longest x1 4.24 us: local(): lax.all_to_all(outgoing.reshape(n_member, pair_slots, feature_width), 'me...]
    all_gather x1, waiting for transfers between devices: 40.4 us -> 42.6 us  [local(): lax.all_gather(normed, 'tp', axis=0, tiled=True)]
  transfers between devices with their start and end apart: 8 -> 7, of which waited for: 7 -> 6; matrix products, arithmetic and copies ran while one was open for 2% -> 1% of each run, Pallas kernels for 0% -> 0%
where the time goes in v3:
time: 196 us; the launch traced here: 195 us
  waiting for transfers between devices  116 us (59%)
  blocking collectives  30.9 us (16%)
  between operations  14.2 us (7%)
  matrix products  12.7 us (6%)
  starting transfers between devices  12.6 us (6%)
  other arithmetic  6.73 us (3%)
  local copies, waits for them, and re-layouts  2.41 us (1%)
    reduce_scatter x1, waiting for transfers between devices, local(): lax.psum_scatter(jnp.dot(hidden, down_local, preferred_element_type=jnp.f...  43.8 us
    all_gather x1, waiting for transfers between devices, local(): lax.all_gather(normed, 'tp', axis=0, tiled=True)  42.6 us
    all_gather x1, blocking collectives, local(): all_place = lax.all_gather(place, ('member', 'tp'), axis=0, tiled=True)  30.9 us
    all_to_all x1, waiting for transfers between devices, local(): lax.all_to_all(packed.reshape(n_dev, per_learner, feature_width), ('membe...  9.68 us
    all_to_all x1, waiting for transfers between devices, local(): lax.all_to_all(predicted.reshape(n_member, pair_slots, feature_width), 'm...  8.78 us
    dot_general x1, matrix products, local(): jnp.dot(hidden, down_local, preferred_element_type=jnp.float32)  8.72 us
    all_to_all x1, waiting for transfers between devices, local(): lax.all_to_all(outgoing.reshape(n_member, pair_slots, feature_width), 'me...  8.14 us
    all_to_all x1, starting transfers between devices, local(): lax.all_to_all(packed.reshape(n_dev, per_learner, feature_width), ('membe...  4.3 us
  transfers between devices with their start and end apart: 7, of which 6 were waited for; matrix products, arithmetic and copies ran while one was open for 1% of the time, Pallas kernels for 0%

profile of v3, /device:TPU:0, one launch (start us, length us, event | category | flops | bytes accessed | tf_op | source)
XLA Modules:
  0.0 195.4 jit_solution(8012934174027632554)
XLA Ops:
  7.2 0.9 fusion.50
  8.3 0.8 select_reduce_fusion
  9.1 0.7 multiply_add_fusion
  9.8 1.1 convolution_convert_fusion
  10.9 4.2 %all-to-all-start = ((bf16[4,64,1024]{2,1,0:T(8,128)(2,1)}), bf16[4,64,1024]{2,1,0:T(8,128)(2,1)S(1)}, u32[]{:S(2)}, u32[]{:S(2)}) async-start(bf16[4,64,1024]{2,1,0:T(8,128)(2,1)} %bitcast.5), calls=%async_computation | async-start | bytes 1048576 | tf_op jit(solution)/shard_map/all_to_all | solution.py:44
  15.1 0.7 constant_dynamic-slice_fusion
  15.8 8.1 %all-to-all-done = bf16[4,64,1024]{2,1,0:T(8,128)(2,1)S(1)} async-done(((bf16[4,64,1024]{2,1,0:T(8,128)(2,1)}), bf16[4,64,1024]{2,1,0:T(8,128)(2,1)S(1)}, u32[]{:S(2)}, u32[]{:S(2)}) %all-to-all-start) | async-done | bytes 524320 | tf_op jit(solution)/shard_map/all_to_all | solution.py:44
  24.2 1.0 fusion.29
  25.4 0.5 collective-permute-start.1
  25.9 2.8 %collective-permute-done = bf16[1024,512]{1,0:T(8,128)(2,1)S(1)} collective-permute-done((bf16[1024,512]{1,0:T(8,128)(2,1)S(1)}, bf16[1024,512]{1,0:T(8,128)(2,1)S(1)}, u32[]{:S(2)}, u32[]{:S(2)}) %collective-permute-start) | collective-permute-done | bytes 1048608 | tf_op jit(solution)/shard_map/ppermute | solution.py:11
  28.6 1.0 copy-done.4
  29.6 42.6 %all-gather.3.cloned.1.call-done = bf16[1024,1024]{1,0:T(8,128)(2,1)} async-done(((bf16[256,1024]{1,0:T(8,128)(2,1)}), bf16[1024,1024]{1,0:T(8,128)(2,1)}) %all-gather.3.cloned.1.call-update) | async-done | bytes 2097168 | tf_op jit(solution)/shard_map/all_gather | solution.py:57
  72.3 8.7 %fusion.8 = f32[1024,1024]{1,0:T(8,128)} fusion(bf16[512,1024]{1,0:T(8,128)(2,1)} %collective-permute-done.1, bf16[512,1024]{1,0:T(8,128)(2,1)S(1)} %bitcast.42, bf16[1024,1024]{1,0:T(8,128)(2,1)} %all-gather.3.cloned.1.call-done, bf16[1024,512]{1,0:T(8,128)(2,1)} %copy-done.4, bf16[1024,512]{1,0:T(8,128)(2,1)S(1)} %bitcast.44), kind=kOutput, calls=%fused_computation.9 | convolution fusion | flops 4312793088 | bytes 10485760 | tf_op jit(solution)/shard_map/dot_general | solution.py:63
  81.0 0.6 copy-done.1
  81.9 30.9 %all-gather = s32[16,1,128]{2,1,0:T(1,128)S(1)} all-gather(s32[1,1,128]{2,1,0:T(1,128)S(1)} %bitcast.40), channel_id=1, replica_groups=mesh['rep'=2,'member'=4,'tp'=4] {'member','tp'}, dimensions={0}, use_global_device_ids=true | all-gather | bytes 8704 | tf_op jit(solution)/shard_map/all_gather | solution.py:31
  113.0 43.8 %reduce-scatter.2.cloned.1.call-done = f32[256,1024]{1,0:T(8,128)} async-done(((f32[1024,1024]{1,0:T(8,128)}), f32[256,1024]{1,0:T(8,128)}) %reduce-scatter.2.cloned.1.call-update) | async-done | bytes 1048592 | tf_op jit(solution)/shard_map/reduce_scatter | solution.py:62
  156.8 2.2 %fusion.30 = bf16[256,1024]{1,0:T(8,128)(2,1)} fusion(f32[256,1024]{1,0:T(8,128)} %reduce-scatter.2.cloned.1.call-done, bf16[4,64,1024]{2,1,0:T(8,128)(2,1)S(1)} %all-to-all-done), kind=kLoop, calls=%fused_computation.35 | loop fusion | flops 786432 | bytes 2097152 | tf_op jit(solution)/shard_map/convert_element_type | solution.py:68
  158.9 3.5 %all-to-all-start.1 = ((bf16[4,64,1024]{2,1,0:T(8,128)(2,1)}), bf16[4,64,1024]{2,1,0:T(8,128)(2,1)S(1)}, u32[]{:S(2)}, u32[]{:S(2)}) async-start(bf16[4,64,1024]{2,1,0:T(8,128)(2,1)} %bitcast.10), calls=%async_computation.2 | async-start | bytes 1048576 | tf_op jit(solution)/shard_map/all_to_all | solution.py:69
  162.5 8.8 %all-to-all-done.1 = bf16[4,64,1024]{2,1,0:T(8,128)(2,1)S(1)} async-done(((bf16[4,64,1024]{2,1,0:T(8,128)(2,1)}), bf16[4,64,1024]{2,1,0:T(8,128)(2,1)S(1)}, u32[]{:S(2)}, u32[]{:S(2)}) %all-to-all-start.1) | async-done | bytes 524320 | tf_op jit(solution)/shard_map/all_to_all | solution.py:69
  171.2 1.2 fusion.25
  172.4 4.3 %all-to-all-start.2 = ((bf16[16,8,1024]{2,1,0:T(8,128)(2,1)}), bf16[16,8,1024]{2,1,0:T(8,128)(2,1)S(1)}, u32[]{:S(2)}, u32[]{:S(2)}) async-start(bf16[16,8,1024]{2,1,0:T(8,128)(2,1)} %fusion.25), calls=%async_computation.3 | async-start | bytes 524288 | tf_op jit(solution)/shard_map/all_to_all | solution.py:90
  177.1 9.7 %all-to-all-done.2 = bf16[16,8,1024]{2,1,0:T(8,128)(2,1)S(1)} async-done(((bf16[16,8,1024]{2,1,0:T(8,128)(2,1)}), bf16[16,8,1024]{2,1,0:T(8,128)(2,1)S(1)}, u32[]{:S(2)}, u32[]{:S(2)}) %all-to-all-start.2) | async-done | bytes 262176 | tf_op jit(solution)/shard_map/all_to_all | solution.py:90
  186.8 0.8 fusion.34
  187.6 0.9 fusion.26
  (35 shorter events, 1.5 us)
Async XLA Ops:
  7.2 2.6 %copy-start = (bf16[128,1024]{1,0:T(8,128)(2,1)S(1)}, bf16[128,1024]{1,0:T(8,128)(2,1)}, u32[]{:S(2)}) copy-start(bf16[128,1024]{1,0:T(8,128)(2,1)} %param.8) | copy-start | bytes 786436
  7.2 18.1 %copy-start.3 = (bf16[1,1024,512]{2,1,0:T(8,128)(2,1)S(1)}, bf16[1,1024,512]{2,1,0:T(8,128)(2,1)}, u32[]{:S(2)}) copy-start(bf16[1,1024,512]{2,1,0:T(8,128)(2,1)} %param.12) | copy-start | bytes 3145732
  7.2 18.2 %copy-start.2 = (bf16[1,512,1024]{2,1,0:T(8,128)(2,1)S(1)}, bf16[1,512,1024]{2,1,0:T(8,128)(2,1)}, u32[]{:S(2)}) copy-start(bf16[1,512,1024]{2,1,0:T(8,128)(2,1)} %param.13) | copy-start | bytes 3145732
  10.9 13.1 %all-to-all-start = ((bf16[4,64,1024]{2,1,0:T(8,128)(2,1)}), bf16[4,64,1024]{2,1,0:T(8,128)(2,1)S(1)}, u32[]{:S(2)}, u32[]{:S(2)}) async-start(bf16[4,64,1024]{2,1,0:T(8,128)(2,1)} %bitcast.5), calls=%async_computation | async-start | bytes 1048576 | tf_op jit(solution)/shard_map/all_to_all | solution.py:44
  15.1 57.2 %all-gather.3.cloned.1.call-start = ((), (), s32[]{:S(2)}) async-start(), calls=%async_computation.4 | async-start | bytes 2621440 | tf_op jit(solution)/shard_map/all_gather | solution.py:57
  25.2 131.6 %reduce-scatter.2.cloned.1.call-start = ((), (), s32[]{:S(2)}) async-start(), calls=%async_computation.5 | async-start | bytes 5242880 | tf_op jit(solution)/shard_map/reduce_scatter | solution.py:62
  25.3 3.3 %collective-permute-start = (bf16[1024,512]{1,0:T(8,128)(2,1)S(1)}, bf16[1024,512]{1,0:T(8,128)(2,1)S(1)}, u32[]{:S(2)}, u32[]{:S(2)}) collective-permute-start(bf16[1024,512]{1,0:T(8,128)(2,1)S(1)} %bitcast.43), channel_id=1, source_target_pairs={{0,4},{4,0},{8,12},{12,8},{1,5},{5,1},{9,13},{13,9},{2,6},{6,2},{1... | collective-permute-start | bytes 3145736 | tf_op jit(solution)/shard_map/ppermute | solution.py:11
  25.4 4.3 %collective-permute-start.1 = (bf16[512,1024]{1,0:T(8,128)(2,1)S(1)}, bf16[512,1024]{1,0:T(8,128)(2,1)}, u32[]{:S(2)}, u32[]{:S(2)}) collective-permute-start(bf16[512,1024]{1,0:T(8,128)(2,1)S(1)} %bitcast.41), channel_id=1, source_target_pairs={{0,4},{4,0},{8,12},{12,8},{1,5},{5,1},{9,13},{13,9},{2,6},{6,2},{1... | collective-permute-start | bytes 3145736 | tf_op jit(solution)/shard_map/ppermute | solution.py:11
  28.6 1.0 copy-start.4
  81.0 0.7 copy-start.1
  81.0 106.6 %copy-start.5 = (bf16[1024,128]{1,0:T(8,128)(2,1)S(1)}, bf16[1024,128]{1,0:T(8,128)(2,1)}, u32[]{:S(2)}) copy-start(bf16[1024,128]{1,0:T(8,128)(2,1)} %param.15) | copy-start | bytes 786436
  81.0 106.6 %copy-start.6 = (f32[1024]{0:T(1024)S(1)}, f32[1024]{0:T(1024)}, u32[]{:S(2)}) copy-start(f32[1024]{0:T(1024)} %param.14) | copy-start | bytes 12292
  158.9 12.3 %all-to-all-start.1 = ((bf16[4,64,1024]{2,1,0:T(8,128)(2,1)}), bf16[4,64,1024]{2,1,0:T(8,128)(2,1)S(1)}, u32[]{:S(2)}, u32[]{:S(2)}) async-start(bf16[4,64,1024]{2,1,0:T(8,128)(2,1)} %bitcast.10), calls=%async_computation.2 | async-start | bytes 1048576 | tf_op jit(solution)/shard_map/all_to_all | solution.py:69
  172.4 14.4 %all-to-all-start.2 = ((bf16[16,8,1024]{2,1,0:T(8,128)(2,1)}), bf16[16,8,1024]{2,1,0:T(8,128)(2,1)S(1)}, u32[]{:S(2)}, u32[]{:S(2)}) async-start(bf16[16,8,1024]{2,1,0:T(8,128)(2,1)} %fusion.25), calls=%async_computation.3 | async-start | bytes 524288 | tf_op jit(solution)/shard_map/all_to_all | solution.py:90
  187.6 1.0 copy-start.7
Sparse Core Ops, SparseCore 0:
  25.3 46.8 all-gather.2
  81.1 75.6 reduce-scatter.1

commit v4 on v3

--- a/solution.py
+++ b/solution.py
@@ -28,7 +28,6 @@
     rows_here = states.shape[0]
     feature_width = states.shape[1]
     pair_slots = rows_here // member_total
-    all_place = lax.all_gather(place, ("member", "tp"), axis=0, tiled=True)
     up_local = jnp.concatenate([w_up[0], from_partner(w_up[0], "member", 0)], axis=1)
     down_local = jnp.concatenate([w_down[0], from_partner(w_down[0], "member", 0)], axis=0)
     member = member_of[:, 0]
@@ -84,35 +83,29 @@
     )
     lane_index = learner * per_learner + running_rank(learner_hits)
     placer = jnp.arange(rows_here, dtype=jnp.int32)[:, None] == lane_index[None, :]
+    spot_index = place % rows_here
     packed = jnp.dot(
         placer.astype(jnp.bfloat16), own_rows, preferred_element_type=jnp.float32
     ).astype(jnp.bfloat16)
+    packed_spot = jnp.sum(placer.astype(jnp.int32) * spot_index[None, :], axis=1)
+    spot_lanes = jnp.where(
+        jnp.arange(128, dtype=jnp.int32)[None, :] == 0, packed_spot[:, None], 0
+    ).astype(jnp.bfloat16)
     arrivals = lax.all_to_all(
-        packed.reshape(n_dev, per_learner, feature_width),
+        jnp.concatenate([packed, spot_lanes], axis=1).reshape(n_dev, per_learner, feature_width + 128),
         ("member", "tp"),
         split_axis=0,
         concat_axis=0,
         tiled=True,
     )
-    arrivals = arrivals.reshape(n_dev * per_learner, feature_width)
-    me = lax.axis_index("member") * n_tp + lax.axis_index("tp")
-    source_place = all_place.reshape(n_dev, rows_here)
-    mine = (source_place // rows_here == me).astype(jnp.int32)
-    slot_of = (
-        jnp.arange(n_dev, dtype=jnp.int32)[:, None] * per_learner
-        + jnp.cumsum(mine, axis=1)
-        - mine
-    ).reshape(-1)
-    spot_of = (source_place % rows_here).reshape(-1)
-    mine = mine.reshape(-1)
-    spot_pick = (
-        (jnp.arange(rows_here, dtype=jnp.int32)[:, None] == spot_of[None, :]) & (mine[None, :] > 0)
-    ).astype(jnp.bfloat16)
-    slot_pick = (slot_of[:, None] == jnp.arange(n_dev * per_learner, dtype=jnp.int32)[None, :]).astype(
+    arrivals = arrivals.reshape(n_dev * per_learner, feature_width + 128)
+    arrival_spots = arrivals[:, feature_width].astype(jnp.int32)
+    settle = (jnp.arange(rows_here, dtype=jnp.int32)[:, None] == arrival_spots[None, :]).astype(
         jnp.bfloat16
     )
-    settle = jnp.dot(spot_pick, slot_pick, preferred_element_type=jnp.float32).astype(jnp.bfloat16)
-    imagined = jnp.dot(settle, arrivals, preferred_element_type=jnp.float32).astype(jnp.bfloat16)
+    imagined = jnp.dot(
+        settle, arrivals[:, :feature_width], preferred_element_type=jnp.float32
+    ).astype(jnp.bfloat16)
     policy_normed = rms_scale(imagined.astype(jnp.float32), policy_gain).astype(jnp.bfloat16)
     action = jnp.tanh(jnp.dot(policy_normed, w_policy, preferred_element_type=jnp.float32)).astype(
         jnp.bfloat16

time: 196 us -> 195 us (level)
  waiting for transfers between devices: 116 us -> 137 us
  blocking collectives: 30.9 us -> 14.9 us
  starting transfers between devices: 12.6 us -> 8.31 us
    all_gather x1 -> x0, blocking collectives: 30.9 us -> none  [local(): all_place = lax.all_gather(place, ('member', 'tp'), axis=0, tiled=True)]
    reduce_scatter x1, waiting for transfers between devices: 43.8 us -> 74.5 us  [local(): lax.psum_scatter(jnp.dot(hidden, down_local, preferred_element_type=jnp.f...]
    all_to_all x0 -> x1, blocking collectives: none -> 14.9 us  [local(): lax.all_to_all(jnp.concatenate([packed, spot_lanes], axis=1).reshape(n_de...]
    all_to_all x1 -> x0, waiting for transfers between devices: 9.68 us -> none  [local(): lax.all_to_all(packed.reshape(n_dev, per_learner, feature_width), ('membe...]
    all_to_all x1 -> x0, starting transfers between devices: 4.3 us -> none  [local(): lax.all_to_all(packed.reshape(n_dev, per_learner, feature_width), ('membe...]
  transfers between devices with their start and end apart: 7 -> 6, of which waited for: 6 -> 5; matrix products, arithmetic and copies ran while one was open for 1% -> 1% of each run, Pallas kernels for 0% -> 0%
where the time goes in v4:
time: 195 us
  waiting for transfers between devices  137 us (70%)
  blocking collectives  14.9 us (8%)
  between operations  14.2 us (7%)
  matrix products  11.4 us (6%)
  starting transfers between devices  8.31 us (4%)
  other arithmetic  6.69 us (3%)
  local copies, waits for them, and re-layouts  2.42 us (1%)
    reduce_scatter x1, waiting for transfers between devices, local(): lax.psum_scatter(jnp.dot(hidden, down_local, preferred_element_type=jnp.f...  74.5 us
    all_gather x1, waiting for transfers between devices, local(): lax.all_gather(normed, 'tp', axis=0, tiled=True)  42.6 us
    all_to_all x1, blocking collectives, local(): lax.all_to_all(jnp.concatenate([packed, spot_lanes], axis=1).reshape(n_de...  14.9 us
    dot_general x1, matrix products, local(): jnp.dot(hidden, down_local, preferred_element_type=jnp.float32)  8.7 us
    all_to_all x1, waiting for transfers between devices, local(): lax.all_to_all(predicted.reshape(n_member, pair_slots, feature_width), 'm...  8.59 us
    all_to_all x1, waiting for transfers between devices, local(): lax.all_to_all(outgoing.reshape(n_member, pair_slots, feature_width), 'me...  8.14 us
    all_to_all x1, starting transfers between devices, local(): lax.all_to_all(outgoing.reshape(n_member, pair_slots, feature_width), 'me...  4.24 us
  transfers between devices with their start and end apart: 6, of which 5 were waited for; matrix products, arithmetic and copies ran while one was open for 1% of the time, Pallas kernels for 0%

profile of v4, /device:TPU:0, one launch (start us, length us, event | category | flops | bytes accessed | tf_op | source)
XLA Modules:
  0.0 194.7 jit_solution(10290911222829956841)
XLA Ops:
  7.2 0.9 fusion.40
  8.1 0.2 reduce_window_sum.23
  8.3 0.8 select_reduce_fusion.1
  9.1 0.7 multiply_add_fusion
  9.8 1.1 convolution_convert_fusion
  10.9 4.2 %all-to-all-start = ((bf16[4,64,1024]{2,1,0:T(8,128)(2,1)}), bf16[4,64,1024]{2,1,0:T(8,128)(2,1)S(1)}, u32[]{:S(2)}, u32[]{:S(2)}) async-start(bf16[4,64,1024]{2,1,0:T(8,128)(2,1)} %bitcast.1), calls=%async_computation | async-start | bytes 1048576 | tf_op jit(solution)/shard_map/all_to_all | solution.py:43
  15.1 0.7 constant_dynamic-slice_fusion
  15.8 8.1 %all-to-all-done = bf16[4,64,1024]{2,1,0:T(8,128)(2,1)S(1)} async-done(((bf16[4,64,1024]{2,1,0:T(8,128)(2,1)}), bf16[4,64,1024]{2,1,0:T(8,128)(2,1)S(1)}, u32[]{:S(2)}, u32[]{:S(2)}) %all-to-all-start) | async-done | bytes 524320 | tf_op jit(solution)/shard_map/all_to_all | solution.py:43
  23.9 0.2 fusion.26
  24.2 1.0 fusion.28
  25.4 0.5 collective-permute-start.1
  25.9 2.8 %collective-permute-done = bf16[1024,512]{1,0:T(8,128)(2,1)S(1)} collective-permute-done((bf16[1024,512]{1,0:T(8,128)(2,1)S(1)}, bf16[1024,512]{1,0:T(8,128)(2,1)S(1)}, u32[]{:S(2)}, u32[]{:S(2)}) %collective-permute-start) | collective-permute-done | bytes 1048608 | tf_op jit(solution)/shard_map/ppermute | solution.py:11
  28.6 1.0 copy-done.3
  29.7 42.6 %all-gather.2.cloned.1.call-done = bf16[1024,1024]{1,0:T(8,128)(2,1)} async-done(((bf16[256,1024]{1,0:T(8,128)(2,1)}), bf16[1024,1024]{1,0:T(8,128)(2,1)}) %all-gather.2.cloned.1.call-update) | async-done | bytes 2097168 | tf_op jit(solution)/shard_map/all_gather | solution.py:56
  72.3 8.7 %fusion.8 = f32[1024,1024]{1,0:T(8,128)} fusion(bf16[512,1024]{1,0:T(8,128)(2,1)} %collective-permute-done.1, bf16[512,1024]{1,0:T(8,128)(2,1)S(1)} %bitcast.31, bf16[1024,1024]{1,0:T(8,128)(2,1)} %all-gather.2.cloned.1.call-done, bf16[1024,512]{1,0:T(8,128)(2,1)} %copy-done.3, bf16[1024,512]{1,0:T(8,128)(2,1)S(1)} %bitcast.33), kind=kOutput, calls=%fused_computation.9 | convolution fusion | flops 4312793088 | bytes 10485760 | tf_op jit(solution)/shard_map/dot_general | solution.py:62
  81.0 0.6 copy-done.6
  82.1 74.5 %reduce-scatter.2.cloned.1.call-done = f32[256,1024]{1,0:T(8,128)} async-done(((f32[1024,1024]{1,0:T(8,128)}), f32[256,1024]{1,0:T(8,128)}) %reduce-scatter.2.cloned.1.call-update) | async-done | bytes 1048592 | tf_op jit(solution)/shard_map/reduce_scatter | solution.py:61
  156.7 2.2 %fusion.29 = bf16[256,1024]{1,0:T(8,128)(2,1)} fusion(f32[256,1024]{1,0:T(8,128)} %reduce-scatter.2.cloned.1.call-done, bf16[4,64,1024]{2,1,0:T(8,128)(2,1)S(1)} %all-to-all-done), kind=kLoop, calls=%fused_computation.33 | loop fusion | flops 786432 | bytes 2097152 | tf_op jit(solution)/shard_map/convert_element_type | solution.py:67
  158.8 3.5 %all-to-all-start.1 = ((bf16[4,64,1024]{2,1,0:T(8,128)(2,1)}), bf16[4,64,1024]{2,1,0:T(8,128)(2,1)S(1)}, u32[]{:S(2)}, u32[]{:S(2)}) async-start(bf16[4,64,1024]{2,1,0:T(8,128)(2,1)} %bitcast.6), calls=%async_computation.2 | async-start | bytes 1048576 | tf_op jit(solution)/shard_map/all_to_all | solution.py:68
  162.5 8.6 %all-to-all-done.1 = bf16[4,64,1024]{2,1,0:T(8,128)(2,1)S(1)} async-done(((bf16[4,64,1024]{2,1,0:T(8,128)(2,1)}), bf16[4,64,1024]{2,1,0:T(8,128)(2,1)S(1)}, u32[]{:S(2)}, u32[]{:S(2)}) %all-to-all-start.1) | async-done | bytes 524320 | tf_op jit(solution)/shard_map/all_to_all | solution.py:68
  171.1 0.4 convolution_convert_fusion.2
  171.6 14.9 %all_to_all.15 = bf16[16,8,1152]{2,1,0:T(8,128)(2,1)S(1)} all-to-all(bf16[16,8,1152]{2,1,0:T(8,128)(2,1)S(1)} %maximum_bitcast_fusion), channel_id=1, replica_groups=mesh['rep'=2,'member'=4,'tp'=4] {'member','tp'}, dimensions={0} | all-to-all | bytes 589824 | tf_op jit(solution)/shard_map/all_to_all | solution.py:94
  186.6 0.3 fusion.30
  186.9 0.9 fusion.25
  (33 shorter events, 1.1 us)
Async XLA Ops:
  7.2 2.6 %copy-start = (bf16[128,1024]{1,0:T(8,128)(2,1)S(1)}, bf16[128,1024]{1,0:T(8,128)(2,1)}, u32[]{:S(2)}) copy-start(bf16[128,1024]{1,0:T(8,128)(2,1)} %param.8) | copy-start | bytes 786436
  7.2 18.1 %copy-start.2 = (bf16[1,1024,512]{2,1,0:T(8,128)(2,1)S(1)}, bf16[1,1024,512]{2,1,0:T(8,128)(2,1)}, u32[]{:S(2)}) copy-start(bf16[1,1024,512]{2,1,0:T(8,128)(2,1)} %param.12) | copy-start | bytes 3145732
  7.2 18.2 %copy-start.1 = (bf16[1,512,1024]{2,1,0:T(8,128)(2,1)S(1)}, bf16[1,512,1024]{2,1,0:T(8,128)(2,1)}, u32[]{:S(2)}) copy-start(bf16[1,512,1024]{2,1,0:T(8,128)(2,1)} %param.13) | copy-start | bytes 3145732
  10.9 13.1 %all-to-all-start = ((bf16[4,64,1024]{2,1,0:T(8,128)(2,1)}), bf16[4,64,1024]{2,1,0:T(8,128)(2,1)S(1)}, u32[]{:S(2)}, u32[]{:S(2)}) async-start(bf16[4,64,1024]{2,1,0:T(8,128)(2,1)} %bitcast.1), calls=%async_computation | async-start | bytes 1048576 | tf_op jit(solution)/shard_map/all_to_all | solution.py:43
  15.1 57.2 %all-gather.2.cloned.1.call-start = ((), (), s32[]{:S(2)}) async-start(), calls=%async_computation.4 | async-start | bytes 2621440 | tf_op jit(solution)/shard_map/all_gather | solution.py:56
  25.2 131.4 %reduce-scatter.2.cloned.1.call-start = ((), (), s32[]{:S(2)}) async-start(), calls=%async_computation.5 | async-start | bytes 5242880 | tf_op jit(solution)/shard_map/reduce_scatter | solution.py:61
  25.3 3.3 %collective-permute-start = (bf16[1024,512]{1,0:T(8,128)(2,1)S(1)}, bf16[1024,512]{1,0:T(8,128)(2,1)S(1)}, u32[]{:S(2)}, u32[]{:S(2)}) collective-permute-start(bf16[1024,512]{1,0:T(8,128)(2,1)S(1)} %bitcast.32), channel_id=1, source_target_pairs={{0,4},{4,0},{8,12},{12,8},{1,5},{5,1},{9,13},{13,9},{2,6},{6,2},{1... | collective-permute-start | bytes 3145736 | tf_op jit(solution)/shard_map/ppermute | solution.py:11
  25.4 4.3 %collective-permute-start.1 = (bf16[512,1024]{1,0:T(8,128)(2,1)S(1)}, bf16[512,1024]{1,0:T(8,128)(2,1)}, u32[]{:S(2)}, u32[]{:S(2)}) collective-permute-start(bf16[512,1024]{1,0:T(8,128)(2,1)S(1)} %bitcast.30), channel_id=1, source_target_pairs={{0,4},{4,0},{8,12},{12,8},{1,5},{5,1},{9,13},{13,9},{2,6},{6,2},{1... | collective-permute-start | bytes 3145736 | tf_op jit(solution)/shard_map/ppermute | solution.py:11
  28.6 1.0 copy-start.3
  81.0 0.7 copy-start.6
  81.0 105.9 %copy-start.4 = (bf16[1024,128]{1,0:T(8,128)(2,1)S(1)}, bf16[1024,128]{1,0:T(8,128)(2,1)}, u32[]{:S(2)}) copy-start(bf16[1024,128]{1,0:T(8,128)(2,1)} %param.15) | copy-start | bytes 786436
  81.0 105.9 %copy-start.5 = (f32[1024]{0:T(1024)S(1)}, f32[1024]{0:T(1024)}, u32[]{:S(2)}) copy-start(f32[1024]{0:T(1024)} %param.14) | copy-start | bytes 12292
  158.8 12.3 %all-to-all-start.1 = ((bf16[4,64,1024]{2,1,0:T(8,128)(2,1)}), bf16[4,64,1024]{2,1,0:T(8,128)(2,1)S(1)}, u32[]{:S(2)}, u32[]{:S(2)}) async-start(bf16[4,64,1024]{2,1,0:T(8,128)(2,1)} %bitcast.6), calls=%async_computation.2 | async-start | bytes 1048576 | tf_op jit(solution)/shard_map/all_to_all | solution.py:68
  186.9 1.0 copy-start.7
Sparse Core Ops, SparseCore 0:
  25.4 46.8 all-gather.1
  81.1 75.4 reduce-scatter.1

commit v5 on v4

--- a/solution.py
+++ b/solution.py
@@ -2,13 +2,17 @@
 import jax.numpy as jnp
 from jax import lax
 from jax.sharding import PartitionSpec as P
-
 
 PARTIAL_DTYPE = jnp.float32
 
 
 def from_partner(value, axis, distance):
     return lax.ppermute(value, axis, [(i, i ^ 1 << distance) for i in range(lax.axis_size(axis))])
+
+
+def from_chip_behind(value, axis, chips_back):
+    size = lax.axis_size(axis)
+    return lax.ppermute(value, axis, [(i, (i + 2 * chips_back) % size) for i in range(size)])
 
 
 def rms_scale(values, gain):
@@ -27,55 +31,42 @@
     member_total = n_member // 2
     rows_here = states.shape[0]
     feature_width = states.shape[1]
-    pair_slots = rows_here // member_total
-    up_local = jnp.concatenate([w_up[0], from_partner(w_up[0], "member", 0)], axis=1)
-    down_local = jnp.concatenate([w_down[0], from_partner(w_down[0], "member", 0)], axis=0)
+    own_member = lax.axis_index("member") // 2
+    blocks = []
+    for back in range(member_total):
+        if back == 0:
+            up_here, down_here = w_up[0], w_down[0]
+        else:
+            up_here = from_chip_behind(w_up[0], "member", back)
+            down_here = from_chip_behind(w_down[0], "member", back)
+        block_member = (own_member - back + member_total) % member_total
+        blocks.append((block_member, up_here, down_here))
+        blocks.append(
+            (block_member, from_partner(up_here, "member", 0), from_partner(down_here, "member", 0))
+        )
     member = member_of[:, 0]
-    member_hits = (member[:, None] == jnp.arange(member_total, dtype=jnp.int32)[None, :]).astype(
-        jnp.int32
+    gain_rows = jnp.take(norm_gain, member, axis=0)
+    normed = rms_scale(states.astype(jnp.float32), gain_rows).astype(jnp.bfloat16)
+    member_lanes = jnp.where(
+        jnp.arange(128, dtype=jnp.int32)[None, :] == 0, member[:, None], 0
+    ).astype(jnp.bfloat16)
+    gathered = lax.all_gather(
+        jnp.concatenate([normed, member_lanes], axis=1), "tp", axis=0, tiled=True
     )
-    earlier = running_rank(member_hits)
-    target = (2 * member + earlier % 2) * pair_slots + earlier // 2
-    picker = (jnp.arange(n_member * pair_slots, dtype=jnp.int32)[:, None] == target[None, :]).astype(
-        jnp.bfloat16
-    )
-    outgoing = jnp.dot(picker, states, preferred_element_type=jnp.float32).astype(jnp.bfloat16)
-    arrived = lax.all_to_all(
-        outgoing.reshape(n_member, pair_slots, feature_width),
-        "member",
-        split_axis=0,
-        concat_axis=0,
-        tiled=True,
-    )
-    arrived = arrived.reshape(n_member * pair_slots, feature_width)
-    own_member = lax.axis_index("member") // 2
-    gain_here = lax.dynamic_index_in_dim(norm_gain, own_member, 0, keepdims=False)
-    normed = rms_scale(arrived.astype(jnp.float32), gain_here).astype(jnp.bfloat16)
-    hidden = jax.nn.gelu(
-        jnp.dot(
-            lax.all_gather(normed, "tp", axis=0, tiled=True),
-            up_local,
-            preferred_element_type=jnp.float32,
-        )
-    ).astype(jnp.bfloat16)
+    gathered_rows = gathered[:, :feature_width]
+    gathered_member = gathered[:, feature_width].astype(jnp.int32)
+    partial = None
+    for block_member, up_here, down_here in blocks:
+        keep = (gathered_member == block_member).astype(jnp.bfloat16)[:, None]
+        hidden = jax.nn.gelu(
+            jnp.dot(gathered_rows, up_here, preferred_element_type=jnp.float32)
+        ).astype(jnp.bfloat16) * keep
+        term = jnp.dot(hidden, down_here, preferred_element_type=jnp.float32)
+        partial = term if partial is None else partial + term
     change = lax.psum_scatter(
-        jnp.dot(hidden, down_local, preferred_element_type=jnp.float32).astype(PARTIAL_DTYPE),
-        "tp",
-        scatter_dimension=0,
-        tiled=True,
+        partial.astype(PARTIAL_DTYPE), "tp", scatter_dimension=0, tiled=True
     ).astype(jnp.float32)
-    predicted = (arrived.astype(jnp.float32) + change).astype(jnp.bfloat16)
-    returned = lax.all_to_all(
-        predicted.reshape(n_member, pair_slots, feature_width),
-        "member",
-        split_axis=0,
-        concat_axis=0,
-        tiled=True,
-    )
-    returned = returned.reshape(n_member * pair_slots, feature_width)
-    own_rows = jnp.einsum("sr,sd->rd", picker, returned, preferred_element_type=jnp.float32).astype(
-        jnp.bfloat16
-    )
+    own_rows = (states.astype(jnp.float32) + change).astype(jnp.bfloat16)
     per_learner = rows_here // n_dev
     learner = place // rows_here
     learner_hits = (learner[:, None] == jnp.arange(n_dev, dtype=jnp.int32)[None, :]).astype(

time: 195 us -> 152 us (0.78)
  waiting for transfers between devices: 137 us -> 91 us
  matrix products: 11.4 us -> 21.2 us
  starting transfers between devices: 8.31 us -> 3.71 us
    ppermute x0 -> x2, waiting for transfers between devices: none -> 45.4 us  [from_chip_behind(): lax.ppermute(value, axis, [(i, (i + 2 * chips_back) % size) for i in rang...]
    all_gather x1, waiting for transfers between devices: 42.6 us -> 0.01 us  [local(): lax.all_gather(jnp.concatenate([normed, member_lanes], axis=1), 'tp', axi...]
    reduce_scatter x1, waiting for transfers between devices: 74.5 us -> 45.6 us  [local(): lax.psum_scatter(partial.astype(PARTIAL_DTYPE), 'tp', scatter_dimension=0...]
    all_to_all x2 -> x0, waiting for transfers between devices: 16.7 us -> none  [the longest x1 8.59 us: local(): lax.all_to_all(predicted.reshape(n_member, pair_slots, feature_width), 'm...]
    dot_general x2 -> x4, matrix products: 9.78 us -> 18.7 us  [local(): term = jnp.dot(hidden, down_here, preferred_element_type=jnp.float32)]
    all_to_all x2 -> x0, starting transfers between devices: 7.7 us -> none  [the longest x1 4.24 us: local(): lax.all_to_all(outgoing.reshape(n_member, pair_slots, feature_width), 'me...]
    convert_element_type x4 -> x2, other arithmetic: 4.14 us -> 0.25 us  [the longest x1 0.14 us: local(): rms_scale(states.astype(jnp.float32), gain_rows).astype(jnp.bfloat16)]
    ppermute x0 -> x2, starting transfers between devices: none -> 3.11 us  [from_chip_behind(): lax.ppermute(value, axis, [(i, (i + 2 * chips_back) % size) for i in rang...]
  transfers between devices with their start and end apart: 6 -> 8, of which waited for: 5 -> 3; matrix products, arithmetic and copies ran while one was open for 1% -> 9% of each run, Pallas kernels for 0% -> 0%
where the time goes in v5:
time: 152 us; the launch traced here: 151 us
  waiting for transfers between devices  91 us (60%)
  matrix products  21.2 us (14%)
  blocking collectives  14.6 us (10%)
  between operations  14.2 us (9%)
  other arithmetic  5.83 us (4%)
  starting transfers between devices  3.71 us (2%)
    reduce_scatter x1, waiting for transfers between devices, local(): lax.psum_scatter(partial.astype(PARTIAL_DTYPE), 'tp', scatter_dimension=0...  45.6 us
    ppermute x2, waiting for transfers between devices, from_chip_behind(): lax.ppermute(value, axis, [(i, (i + 2 * chips_back) % size) for i in rang...  45.4 us
    dot_general x4, matrix products, local(): term = jnp.dot(hidden, down_here, preferred_element_type=jnp.float32)  18.7 us
    all_to_all x1, blocking collectives, local(): lax.all_to_all(jnp.concatenate([packed, spot_lanes], axis=1).reshape(n_de...  14.6 us
    ppermute x2, starting transfers between devices, from_chip_behind(): lax.ppermute(value, axis, [(i, (i + 2 * chips_back) % size) for i in rang...  3.11 us
  transfers between devices with their start and end apart: 8, of which 3 were waited for; matrix products, arithmetic and copies ran while one was open for 9% of the time, Pallas kernels for 0%

profile of v5, /device:TPU:0, one launch (start us, length us, event | category | flops | bytes accessed | tf_op | source)
XLA Modules:
  0.0 151.4 jit_solution(2857680168190549668)
XLA Ops:
  7.2 0.7 and_bitcast_fusion
  7.9 0.7 fusion.130
  8.6 1.1 fusion.75
  9.7 0.7 and_select_fusion.1
  10.4 0.2 reduce_window_sum.11
  10.6 0.2 select_reduce_fusion.1
  10.8 0.1 select_reduce_fusion
  10.9 0.8 gather_fusion
  11.9 0.1 fusion.77
  12.0 0.7 pad_maximum_fusion
  12.8 3.0 %collective-permute-start.2 = (bf16[1024,512]{1,0:T(8,128)(2,1)}, bf16[1024,512]{1,0:T(8,128)(2,1)}, u32[]{:S(2)}, u32[]{:S(2)}) collective-permute-start(bf16[1024,512]{1,0:T(8,128)(2,1)} %bitcast.3), channel_id=1, source_target_pairs={{0,8},{4,12},{8,0},{12,4},{1,9},{5,13},{9,1},{13,5},{2,10},{6,14},... | collective-permute-start | bytes 3145736 | tf_op jit(solution)/shard_map/ppermute | solution.py:15
  16.0 0.5 collective-permute-start.1
  16.5 23.7 %collective-permute-done.2 = bf16[1024,512]{1,0:T(8,128)(2,1)} collective-permute-done((bf16[1024,512]{1,0:T(8,128)(2,1)}, bf16[1024,512]{1,0:T(8,128)(2,1)}, u32[]{:S(2)}, u32[]{:S(2)}) %collective-permute-start.2) | collective-permute-done | bytes 1048608 | tf_op jit(solution)/shard_map/ppermute | solution.py:15
  40.2 21.6 %collective-permute-done.3 = bf16[512,1024]{1,0:T(8,128)(2,1)} collective-permute-done((bf16[512,1024]{1,0:T(8,128)(2,1)}, bf16[512,1024]{1,0:T(8,128)(2,1)}, u32[]{:S(2)}, u32[]{:S(2)}) %collective-permute-start.3) | collective-permute-done | bytes 1048608 | tf_op jit(solution)/shard_map/ppermute | solution.py:15
  61.8 1.1 fusion.107
  62.9 3.3 %fusion.56 = f32[512,1024]{1,0:T(8,128)S(1)} fusion(bf16[512,1024]{1,0:T(8,128)(2,1)} %collective-permute-done.3, bf16[1024,512]{1,0:T(8,128)(2,1)} %collective-permute-done.2, bf16[512,1152]{1,0:T(8,128)(2,1)} %all-gather.2.cloned.1.call-done, bf16[512]{0:T(512)(128)(2,1)S(1)} %get-tuple-element.3), kind=kOutput, calls=%fused_computation.55 | convolution fusion | flops 1076363264 | bytes 5243904 | tf_op jit(solution)/shard_map/dot_general | solution.py:64
  66.3 4.6 %fusion.68 = f32[512,1024]{1,0:T(8,128)} fusion(bf16[512,1152]{1,0:T(8,128)(2,1)} %all-gather.2.cloned.1.call-done, bf16[512]{0:T(512)(128)(2,1)S(1)} %get-tuple-element.2, bf16[1,512,1024]{2,1,0:T(8,128)(2,1)} %param.13, bf16[1,1024,512]{2,1,0:T(8,128)(2,1)} %param.12), kind=kOutput, calls=%fused_computation.59 | convolution fusion | flops 1076363264 | bytes 5243904 | tf_op jit(solution)/shard_map/dot_general | solution.py:64
  70.9 4.7 %fusion.62 = f32[512,1024]{1,0:T(8,128)} fusion(bf16[512,1024]{1,0:T(8,128)(2,1)} %collective-permute-done.1, bf16[1024,512]{1,0:T(8,128)(2,1)} %collective-permute-done, bf16[512,1152]{1,0:T(8,128)(2,1)} %all-gather.2.cloned.1.call-done, bf16[512]{0:T(512)(128)(2,1)S(1)} %get-tuple-element.2), kind=kOutput, calls=%fused_computation.57 | convolution fusion | flops 1076363264 | bytes 5243904 | tf_op jit(solution)/shard_map/dot_general | solution.py:64
  75.6 6.0 %add_add_fusion = f32[512,1024]{1,0:T(8,128)} fusion(f32[512,1024]{1,0:T(8,128)S(1)} %fusion.56, f32[512,1024]{1,0:T(8,128)} %fusion.68, f32[512,1024]{1,0:T(8,128)} %fusion.62, bf16[512,1024]{1,0:T(8,128)(2,1)} %collective-permute-done.5, bf16[1024,512]{1,0:T(8,128)(2,1)} %collective-permute-done.4, bf16[512,1152]{1,0:T(8,128)(2,1)} %all-gather.2.cloned.1.call-done, ...), kind=kOutput, calls=%fused_computation.1 | convolution fusion | flops 1077936128 | bytes 11535360 | tf_op jit(solution)/shard_map/dot_general | solution.py:64
  81.6 45.6 %reduce-scatter.2.cloned.1.call-done = f32[128,1024]{1,0:T(8,128)} async-done(((f32[512,1024]{1,0:T(8,128)}), f32[128,1024]{1,0:T(8,128)}) %reduce-scatter.2.cloned.1.call-update) | async-done | bytes 524304 | tf_op jit(solution)/shard_map/reduce_scatter | solution.py:66
  127.3 1.3 convolution_convert_fusion.1
  128.6 14.6 %all_to_all.5 = bf16[16,8,1152]{2,1,0:T(8,128)(2,1)S(1)} all-to-all(bf16[16,8,1152]{2,1,0:T(8,128)(2,1)S(1)} %maximum_bitcast_fusion), channel_id=1, replica_groups=mesh['rep'=2,'member'=4,'tp'=4] {'member','tp'}, dimensions={0} | all-to-all | bytes 589824 | tf_op jit(solution)/shard_map/all_to_all | solution.py:85
  143.3 0.3 fusion.72
  143.6 0.9 fusion
  (34 shorter events, 0.6 us)
Async XLA Ops:
  7.2 136.4 %copy-start = (bf16[1024,128]{1,0:T(8,128)(2,1)S(1)}, bf16[1024,128]{1,0:T(8,128)(2,1)}, u32[]{:S(2)}) copy-start(bf16[1024,128]{1,0:T(8,128)(2,1)} %param.15) | copy-start | bytes 786436
  7.2 3.7 %copy-start.1 = (f32[2,1024]{1,0:T(2,128)S(1)}, f32[2,1024]{1,0:T(2,128)}, u32[]{:S(2)}) copy-start(f32[2,1024]{1,0:T(2,128)} %param.11) | copy-start | bytes 24580
  7.2 54.6 %all-gather.2.cloned.1.call-start = ((), (), s32[]{:S(2)}) async-start(), calls=%async_computation.2 | async-start | bytes 1474560 | tf_op jit(solution)/shard_map/all_gather | solution.py:53
  10.9 0.8 copy-start.3
  10.9 1.0 copy-start.2
  12.8 114.5 %reduce-scatter.2.cloned.1.call-start = ((), (), s32[]{:S(2)}) async-start(), calls=%async_computation.3 | async-start | bytes 2621440 | tf_op jit(solution)/shard_map/reduce_scatter | solution.py:66
  12.8 27.3 %collective-permute-start.2 = (bf16[1024,512]{1,0:T(8,128)(2,1)}, bf16[1024,512]{1,0:T(8,128)(2,1)}, u32[]{:S(2)}, u32[]{:S(2)}) collective-permute-start(bf16[1024,512]{1,0:T(8,128)(2,1)} %bitcast.3), channel_id=1, source_target_pairs={{0,8},{4,12},{8,0},{12,4},{1,9},{5,13},{9,1},{13,5},{2,10},{6,14},... | collective-permute-start | bytes 3145736 | tf_op jit(solution)/shard_map/ppermute | solution.py:15
  15.9 45.9 %collective-permute-start.3 = (bf16[512,1024]{1,0:T(8,128)(2,1)}, bf16[512,1024]{1,0:T(8,128)(2,1)}, u32[]{:S(2)}, u32[]{:S(2)}) collective-permute-start(bf16[512,1024]{1,0:T(8,128)(2,1)} %bitcast.4), channel_id=1, source_target_pairs={{0,8},{4,12},{8,0},{12,4},{1,9},{5,13},{9,1},{13,5},{2,10},{6,14},... | collective-permute-start | bytes 3145736 | tf_op jit(solution)/shard_map/ppermute | solution.py:15
  16.0 54.9 %collective-permute-start = (bf16[1024,512]{1,0:T(8,128)(2,1)}, bf16[1024,512]{1,0:T(8,128)(2,1)}, u32[]{:S(2)}, u32[]{:S(2)}) collective-permute-start(bf16[1024,512]{1,0:T(8,128)(2,1)} %bitcast.3), channel_id=1, source_target_pairs={{0,4},{4,0},{8,12},{12,8},{1,5},{5,1},{9,13},{13,9},{2,6},{6,2},{1... | collective-permute-start | bytes 3145736 | tf_op jit(solution)/shard_map/ppermute | solution.py:10
  16.0 54.9 %collective-permute-start.1 = (bf16[512,1024]{1,0:T(8,128)(2,1)}, bf16[512,1024]{1,0:T(8,128)(2,1)}, u32[]{:S(2)}, u32[]{:S(2)}) collective-permute-start(bf16[512,1024]{1,0:T(8,128)(2,1)} %bitcast.4), channel_id=1, source_target_pairs={{0,4},{4,0},{8,12},{12,8},{1,5},{5,1},{9,13},{13,9},{2,6},{6,2},{1... | collective-permute-start | bytes 3145736 | tf_op jit(solution)/shard_map/ppermute | solution.py:10
  40.2 35.4 %collective-permute-start.4 = (bf16[1024,512]{1,0:T(8,128)(2,1)}, bf16[1024,512]{1,0:T(8,128)(2,1)}, u32[]{:S(2)}, u32[]{:S(2)}) collective-permute-start(bf16[1024,512]{1,0:T(8,128)(2,1)} %collective-permute-done.2), channel_id=1, source_target_pairs={{0,4},{4,0},{8,12},{12,8},{1,5},{5,1},{9,13},{13,9},{2,6},{6,2},{1... | collective-permute-start | bytes 3145736 | tf_op jit(solution)/shard_map/ppermute | solution.py:10
  61.8 13.8 %collective-permute-start.5 = (bf16[512,1024]{1,0:T(8,128)(2,1)}, bf16[512,1024]{1,0:T(8,128)(2,1)}, u32[]{:S(2)}, u32[]{:S(2)}) collective-permute-start(bf16[512,1024]{1,0:T(8,128)(2,1)} %collective-permute-done.3), channel_id=1, source_target_pairs={{0,4},{4,0},{8,12},{12,8},{1,5},{5,1},{9,13},{13,9},{2,6},{6,2},{1... | collective-permute-start | bytes 3145736 | tf_op jit(solution)/shard_map/ppermute | solution.py:10
  81.6 62.0 %copy-start.4 = (f32[1024]{0:T(1024)S(1)}, f32[1024]{0:T(1024)}, u32[]{:S(2)}) copy-start(f32[1024]{0:T(1024)} %param.14) | copy-start | bytes 12292
  143.6 1.0 copy-start.5
Sparse Core Ops, SparseCore 0:
  12.9 33.1 all-gather.1
  81.7 45.4 reduce-scatter.1

commit v6 on v5

--- a/solution.py
+++ b/solution.py
@@ -32,18 +32,15 @@
     rows_here = states.shape[0]
     feature_width = states.shape[1]
     own_member = lax.axis_index("member") // 2
-    blocks = []
-    for back in range(member_total):
-        if back == 0:
-            up_here, down_here = w_up[0], w_down[0]
-        else:
-            up_here = from_chip_behind(w_up[0], "member", back)
-            down_here = from_chip_behind(w_down[0], "member", back)
-        block_member = (own_member - back + member_total) % member_total
-        blocks.append((block_member, up_here, down_here))
-        blocks.append(
-            (block_member, from_partner(up_here, "member", 0), from_partner(down_here, "member", 0))
+    own_block = (own_member, w_up[0], w_down[0])
+    fetched = [
+        (
+            (own_member - back + member_total) % member_total,
+            from_chip_behind(w_up[0], "member", back),
+            from_chip_behind(w_down[0], "member", back),
         )
+        for back in range(1, member_total)
+    ]
     member = member_of[:, 0]
     gain_rows = jnp.take(norm_gain, member, axis=0)
     normed = rms_scale(states.astype(jnp.float32), gain_rows).astype(jnp.bfloat16)
@@ -55,14 +52,23 @@
     )
     gathered_rows = gathered[:, :feature_width]
     gathered_member = gathered[:, feature_width].astype(jnp.int32)
-    partial = None
-    for block_member, up_here, down_here in blocks:
+
+    def apply_block(block_member, up_here, down_here):
         keep = (gathered_member == block_member).astype(jnp.bfloat16)[:, None]
         hidden = jax.nn.gelu(
             jnp.dot(gathered_rows, up_here, preferred_element_type=jnp.float32)
         ).astype(jnp.bfloat16) * keep
-        term = jnp.dot(hidden, down_here, preferred_element_type=jnp.float32)
-        partial = term if partial is None else partial + term
+        return jnp.dot(hidden, down_here, preferred_element_type=jnp.float32)
+
+    def apply_pair(block_member, up_here, down_here):
+        return apply_block(block_member, up_here, down_here) + apply_block(
+            block_member, from_partner(up_here, "member", 0), from_partner(down_here, "member", 0)
+        )
+
+    partial = apply_pair(*own_block)
+    for block_member, up_here, down_here in fetched:
+        partial, up_here, down_here = lax.optimization_barrier((partial, up_here, down_here))
+        partial = partial + apply_pair(block_member, up_here, down_here)
     change = lax.psum_scatter(
         partial.astype(PARTIAL_DTYPE), "tp", scatter_dimension=0, tiled=True
     ).astype(jnp.float32)

time: 152 us -> 147 us (0.967)
  waiting for transfers between devices: 91 us -> 80.9 us
  other arithmetic: 5.83 us -> 10.1 us
    ppermute x2, waiting for transfers between devices: 45.4 us -> 5.65 us  [from_chip_behind(): lax.ppermute(value, axis, [(i, (i + 2 * chips_back) % size) for i in rang...]
    all_gather x1, waiting for transfers between devices: 0.01 us -> 29.7 us  [local(): lax.all_gather(jnp.concatenate([normed, member_lanes], axis=1), 'tp', axi...]
    add x0 -> x1, other arithmetic: none -> 4.24 us  [local(): partial = partial + apply_pair(block_member, up_here, down_here)]
  transfers between devices with their start and end apart: 8 -> 8, of which waited for: 3 -> 3; matrix products, arithmetic and copies ran while one was open for 9% -> 10% of each run, Pallas kernels for 0% -> 0%
where the time goes in v6:
time: 147 us; the launch traced here: 146 us
  waiting for transfers between devices  80.9 us (55%)
  matrix products  20.5 us (14%)
  blocking collectives  14.6 us (10%)
  between operations  14.2 us (10%)
  other arithmetic  10.1 us (7%)
  starting transfers between devices  4.17 us (3%)
  local copies, waits for them, and re-layouts  1.85 us (1%)
    reduce_scatter x1, waiting for transfers between devices, local(): lax.psum_scatter(partial.astype(PARTIAL_DTYPE), 'tp', scatter_dimension=0...  45.5 us
    all_gather x1, waiting for transfers between devices, local(): lax.all_gather(jnp.concatenate([normed, member_lanes], axis=1), 'tp', axi...  29.7 us
    dot_general x4, matrix products, apply_block(): return jnp.dot(hidden, down_here, preferred_element_type=jnp.float32)  18.1 us
    all_to_all x1, blocking collectives, local(): lax.all_to_all(jnp.concatenate([packed, spot_lanes], axis=1).reshape(n_de...  14.6 us
    ppermute x2, waiting for transfers between devices, from_chip_behind(): lax.ppermute(value, axis, [(i, (i + 2 * chips_back) % size) for i in rang...  5.65 us
    add x1, other arithmetic, local(): partial = partial + apply_pair(block_member, up_here, down_here)  4.24 us
    ppermute x2, starting transfers between devices, from_chip_behind(): lax.ppermute(value, axis, [(i, (i + 2 * chips_back) % size) for i in rang...  2.98 us
  transfers between devices with their start and end apart: 8, of which 3 were waited for; matrix products, arithmetic and copies ran while one was open for 10% of the time, Pallas kernels for 0%

profile of v6, /device:TPU:0, one launch (start us, length us, event | category | flops | bytes accessed | tf_op | source)
XLA Modules:
  0.0 146.3 jit_solution(8545671103130344158)
XLA Ops:
  7.2 0.7 and_bitcast_fusion
  7.9 0.7 fusion.130
  8.6 1.1 fusion.75
  9.7 0.7 and_select_fusion.1
  10.4 0.2 reduce_window_sum.11
  10.9 0.8 gather_fusion
  12.0 0.7 pad_maximum_fusion
  12.8 0.5 collective-permute-start
  13.4 2.9 %collective-permute-start.2 = (bf16[1024,512]{1,0:T(8,128)(2,1)}, bf16[1024,512]{1,0:T(8,128)(2,1)}, u32[]{:S(2)}, u32[]{:S(2)}) collective-permute-start(bf16[1024,512]{1,0:T(8,128)(2,1)} %bitcast.3), channel_id=1, source_target_pairs={{0,8},{4,12},{8,0},{12,4},{1,9},{5,13},{9,1},{13,5},{2,10},{6,14},... | collective-permute-start | bytes 3145736 | tf_op jit(solution)/shard_map/ppermute | solution.py:15
  16.4 29.7 %all-gather.2.cloned.1.call-done = bf16[512,1152]{1,0:T(8,128)(2,1)} async-done(((bf16[128,1152]{1,0:T(8,128)(2,1)}), bf16[512,1152]{1,0:T(8,128)(2,1)}) %all-gather.2.cloned.1.call-update) | async-done | bytes 1179664 | tf_op jit(solution)/shard_map/all_gather | solution.py:50
  46.1 1.1 fusion.106
  47.2 4.7 %fusion.68 = f32[512,1024]{1,0:T(8,128)} fusion(bf16[512,1152]{1,0:T(8,128)(2,1)} %all-gather.2.cloned.1.call-done, bf16[512]{0:T(512)(128)(2,1)S(1)} %get-tuple-element.9, bf16[1,512,1024]{2,1,0:T(8,128)(2,1)} %param.13, bf16[1,1024,512]{2,1,0:T(8,128)(2,1)} %param.12), kind=kOutput, calls=%fused_computation.60 | convolution fusion | flops 1076363264 | bytes 5243904 | tf_op jit(solution)/shard_map/dot_general | solution.py:61
  51.9 1.0 copy-done.4
  52.9 4.0 %convolution_add_fusion = f32[512,1024]{1,0:T(8,128)S(1)} fusion(f32[512,1024]{1,0:T(8,128)} %fusion.68, bf16[512,1024]{1,0:T(8,128)(2,1)} %collective-permute-done.1, bf16[1024,512]{1,0:T(8,128)(2,1)} %copy-done.4, bf16[512,1152]{1,0:T(8,128)(2,1)} %all-gather.2.cloned.1.call-done, bf16[512]{0:T(512)(128)(2,1)S(1)} %get-tuple-element.9), kind=kOutput, calls=%fused_computation.2 | convolution fusion | flops 1076887552 | bytes 7341056 | tf_op jit(solution)/shard_map/dot_general | solution.py:61
  56.9 5.6 %collective-permute-done.3 = bf16[512,1024]{1,0:T(8,128)(2,1)} collective-permute-done((bf16[512,1024]{1,0:T(8,128)(2,1)}, bf16[512,1024]{1,0:T(8,128)(2,1)}, u32[]{:S(2)}, u32[]{:S(2)}) %collective-permute-start.3) | collective-permute-done | bytes 1048608 | tf_op jit(solution)/shard_map/ppermute | solution.py:15
  62.6 0.5 collective-permute-start.5
  63.1 4.7 %fusion.59 = f32[512,1024]{1,0:T(8,128)} fusion(bf16[512,1024]{1,0:T(8,128)(2,1)} %collective-permute-done.3, bf16[1024,512]{1,0:T(8,128)(2,1)} %collective-permute-done.2, bf16[512,1152]{1,0:T(8,128)(2,1)} %all-gather.2.cloned.1.call-done, bf16[512]{0:T(512)(128)(2,1)S(1)} %get-tuple-element.8), kind=kOutput, calls=%fused_computation.57 | convolution fusion | flops 1076363264 | bytes 5243904 | tf_op jit(solution)/shard_map/dot_general | solution.py:61
  67.8 4.6 %fusion.53 = f32[512,1024]{1,0:T(8,128)} fusion(bf16[512,1024]{1,0:T(8,128)(2,1)} %collective-permute-done.5, bf16[1024,512]{1,0:T(8,128)(2,1)} %collective-permute-done.4, bf16[512,1152]{1,0:T(8,128)(2,1)} %all-gather.2.cloned.1.call-done, bf16[512]{0:T(512)(128)(2,1)S(1)} %get-tuple-element.8), kind=kOutput, calls=%fused_computation.55 | convolution fusion | flops 1076363264 | bytes 5243904 | tf_op jit(solution)/shard_map/dot_general | solution.py:61
  72.4 4.2 %add_add_fusion = f32[512,1024]{1,0:T(8,128)} fusion(f32[512,1024]{1,0:T(8,128)S(1)} %convolution_add_fusion, f32[512,1024]{1,0:T(8,128)} %fusion.59, f32[512,1024]{1,0:T(8,128)} %fusion.53), kind=kLoop, calls=%fused_computation.1 | loop fusion | flops 1048576 | bytes 8388608 | tf_op jit(solution)/shard_map/add | solution.py:71
  76.7 45.5 %reduce-scatter.2.cloned.1.call-done = f32[128,1024]{1,0:T(8,128)} async-done(((f32[512,1024]{1,0:T(8,128)}), f32[128,1024]{1,0:T(8,128)}) %reduce-scatter.2.cloned.1.call-update) | async-done | bytes 524304 | tf_op jit(solution)/shard_map/reduce_scatter | solution.py:72
  122.2 1.3 convolution_convert_fusion.1
  123.5 14.6 %all_to_all.5 = bf16[16,8,1152]{2,1,0:T(8,128)(2,1)S(1)} all-to-all(bf16[16,8,1152]{2,1,0:T(8,128)(2,1)S(1)} %maximum_bitcast_fusion), channel_id=1, replica_groups=mesh['rep'=2,'member'=4,'tp'=4] {'member','tp'}, dimensions={0} | all-to-all | bytes 589824 | tf_op jit(solution)/shard_map/all_to_all | solution.py:91
  138.2 0.3 fusion.72
  138.5 0.9 fusion
  (37 shorter events, 1.1 us)
Async XLA Ops:
  7.2 131.3 %copy-start = (bf16[1024,128]{1,0:T(8,128)(2,1)S(1)}, bf16[1024,128]{1,0:T(8,128)(2,1)}, u32[]{:S(2)}) copy-start(bf16[1024,128]{1,0:T(8,128)(2,1)} %param.15) | copy-start | bytes 786436
  7.2 3.7 %copy-start.1 = (f32[2,1024]{1,0:T(2,128)S(1)}, f32[2,1024]{1,0:T(2,128)}, u32[]{:S(2)}) copy-start(f32[2,1024]{1,0:T(2,128)} %param.11) | copy-start | bytes 24580
  7.2 38.9 %all-gather.2.cloned.1.call-start = ((), (), s32[]{:S(2)}) async-start(), calls=%async_computation.2 | async-start | bytes 1474560 | tf_op jit(solution)/shard_map/all_gather | solution.py:50
  10.9 0.8 copy-start.3
  10.9 1.0 copy-start.2
  12.8 109.4 %reduce-scatter.2.cloned.1.call-start = ((), (), s32[]{:S(2)}) async-start(), calls=%async_computation.3 | async-start | bytes 2621440 | tf_op jit(solution)/shard_map/reduce_scatter | solution.py:72
  12.8 39.0 %collective-permute-start = (bf16[1024,512]{1,0:T(8,128)(2,1)}, bf16[1024,512]{1,0:T(8,128)(2,1)S(1)}, u32[]{:S(2)}, u32[]{:S(2)}) collective-permute-start(bf16[1024,512]{1,0:T(8,128)(2,1)} %bitcast.3), channel_id=1, source_target_pairs={{0,4},{4,0},{8,12},{12,8},{1,5},{5,1},{9,13},{13,9},{2,6},{6,2},{1... | collective-permute-start | bytes 3145736 | tf_op jit(solution)/shard_map/ppermute | solution.py:10
  13.4 39.5 %collective-permute-start.1 = (bf16[512,1024]{1,0:T(8,128)(2,1)}, bf16[512,1024]{1,0:T(8,128)(2,1)}, u32[]{:S(2)}, u32[]{:S(2)}) collective-permute-start(bf16[512,1024]{1,0:T(8,128)(2,1)} %bitcast.4), channel_id=1, source_target_pairs={{0,4},{4,0},{8,12},{12,8},{1,5},{5,1},{9,13},{13,9},{2,6},{6,2},{1... | collective-permute-start | bytes 3145736 | tf_op jit(solution)/shard_map/ppermute | solution.py:10
  13.4 43.5 %collective-permute-start.2 = (bf16[1024,512]{1,0:T(8,128)(2,1)}, bf16[1024,512]{1,0:T(8,128)(2,1)}, u32[]{:S(2)}, u32[]{:S(2)}) collective-permute-start(bf16[1024,512]{1,0:T(8,128)(2,1)} %bitcast.3), channel_id=1, source_target_pairs={{0,8},{4,12},{8,0},{12,4},{1,9},{5,13},{9,1},{13,5},{2,10},{6,14},... | collective-permute-start | bytes 3145736 | tf_op jit(solution)/shard_map/ppermute | solution.py:15
  16.4 46.2 %collective-permute-start.3 = (bf16[512,1024]{1,0:T(8,128)(2,1)}, bf16[512,1024]{1,0:T(8,128)(2,1)}, u32[]{:S(2)}, u32[]{:S(2)}) collective-permute-start(bf16[512,1024]{1,0:T(8,128)(2,1)} %bitcast.4), channel_id=1, source_target_pairs={{0,8},{4,12},{8,0},{12,4},{1,9},{5,13},{9,1},{13,5},{2,10},{6,14},... | collective-permute-start | bytes 3145736 | tf_op jit(solution)/shard_map/ppermute | solution.py:15
  51.9 1.0 copy-start.4
  62.6 5.2 %collective-permute-start.4 = (bf16[1024,512]{1,0:T(8,128)(2,1)}, bf16[1024,512]{1,0:T(8,128)(2,1)}, u32[]{:S(2)}, u32[]{:S(2)}) collective-permute-start(bf16[1024,512]{1,0:T(8,128)(2,1)} %collective-permute-done.2), channel_id=1, source_target_pairs={{0,4},{4,0},{8,12},{12,8},{1,5},{5,1},{9,13},{13,9},{2,6},{6,2},{1... | collective-permute-start | bytes 3145736 | tf_op jit(solution)/shard_map/ppermute | solution.py:10
  62.6 5.2 %collective-permute-start.5 = (bf16[512,1024]{1,0:T(8,128)(2,1)}, bf16[512,1024]{1,0:T(8,128)(2,1)}, u32[]{:S(2)}, u32[]{:S(2)}) collective-permute-start(bf16[512,1024]{1,0:T(8,128)(2,1)} %collective-permute-done.3), channel_id=1, source_target_pairs={{0,4},{4,0},{8,12},{12,8},{1,5},{5,1},{9,13},{13,9},{2,6},{6,2},{1... | collective-permute-start | bytes 3145736 | tf_op jit(solution)/shard_map/ppermute | solution.py:10
  76.7 61.9 %copy-start.5 = (f32[1024]{0:T(1024)S(1)}, f32[1024]{0:T(1024)}, u32[]{:S(2)}) copy-start(f32[1024]{0:T(1024)} %param.14) | copy-start | bytes 12292
  138.5 1.0 copy-start.6
Sparse Core Ops, SparseCore 0:
  12.9 33.1 all-gather.1
  76.8 45.3 reduce-scatter.1

commit v7 on v6

v7 whole, which is shorter than its diff:
```python
import jax
import jax.numpy as jnp
from jax import lax
from jax.sharding import PartitionSpec as P

PARTIAL_DTYPE = jnp.float32


def from_partner(value, axis, distance):
    return lax.ppermute(value, axis, [(i, i ^ 1 << distance) for i in range(lax.axis_size(axis))])


def from_chip_behind(value, axis, chips_back):
    size = lax.axis_size(axis)
    return lax.ppermute(value, axis, [(i, (i + 2 * chips_back) % size) for i in range(size)])


def rms_scale(values, gain):
    mean_square = jnp.mean(values * values, axis=-1, keepdims=True)
    return values * lax.rsqrt(mean_square + 1e-06) * gain


def running_rank(member_hits):
    return jnp.sum((jnp.cumsum(member_hits, axis=0) - member_hits) * member_hits, axis=1)


def lane_column(values):
    return jnp.where(jnp.arange(128, dtype=jnp.int32)[None, :] == 0, values[:, None], 0).astype(
        jnp.bfloat16
    )


def local(states, member_of, place, norm_gain, w_up, w_down, policy_gain, w_policy):
    n_member = lax.axis_size("member")
    n_tp = lax.axis_size("tp")
    n_dev = n_member * n_tp
    member_total = n_member // 2
    rows_here = states.shape[0]
    feature_width = states.shape[1]
    per_learner = rows_here // n_dev
    chunks = 2 if per_learner % 2 == 0 else 1
    per_chunk = per_learner // chunks
    chunk_rows = rows_here // chunks
    own_member = lax.axis_index("member") // 2
    own_block = (own_member, w_up[0], w_down[0])
    fetched = [
        (
            (own_member - back + member_total) % member_total,
            from_chip_behind(w_up[0], "member", back),
            from_chip_behind(w_down[0], "member", back),
        )
        for back in range(1, member_total)
    ]
    learner = place // rows_here
    learner_hits = (learner[:, None] == jnp.arange(n_dev, dtype=jnp.int32)[None, :]).astype(
        jnp.int32
    )
    rank = running_rank(learner_hits)
    slot = (rank // per_chunk) * chunk_rows + learner * per_chunk + rank % per_chunk
    slot_hits = jnp.arange(rows_here, dtype=jnp.int32)[:, None] == slot[None, :]
    sorted_states = jnp.dot(
        slot_hits.astype(jnp.bfloat16), states, preferred_element_type=jnp.float32
    ).astype(jnp.bfloat16)
    sorted_member = jnp.sum(slot_hits.astype(jnp.int32) * member_of[:, 0][None, :], axis=1)
    sorted_spot = jnp.sum(slot_hits.astype(jnp.int32) * (place % rows_here)[None, :], axis=1)
    gain_rows = jnp.take(norm_gain, sorted_member, axis=0)
    normed = rms_scale(sorted_states.astype(jnp.float32), gain_rows).astype(jnp.bfloat16)
    gathered = lax.all_gather(
        jnp.concatenate([normed, lane_column(sorted_member)], axis=1), "tp", axis=0, tiled=True
    ).reshape(n_tp, chunks, chunk_rows, feature_width + 128)

    def apply_block(chunk, block_member, up_here, down_here):
        rows = chunk[:, :feature_width]
        keep = (chunk[:, feature_width].astype(jnp.int32) == block_member).astype(jnp.bfloat16)
        hidden = jax.nn.gelu(
            jnp.dot(rows, up_here, preferred_element_type=jnp.float32)
        ).astype(jnp.bfloat16) * keep[:, None]
        return jnp.dot(hidden, down_here, preferred_element_type=jnp.float32)

    def apply_pair(chunk, block_member, up_here, down_here):
        return apply_block(chunk, block_member, up_here, down_here) + apply_block(
            chunk, block_member, from_partner(up_here, "member", 0), from_partner(down_here, "member", 0)
        )

    chunk_inputs = [
        gathered[:, c].reshape(n_tp * chunk_rows, feature_width + 128) for c in range(chunks)
    ]
    partials = [apply_pair(chunk, *own_block) for chunk in chunk_inputs]
    for block_member, up_here, down_here in fetched:
        partials, up_here, down_here = lax.optimization_barrier((partials, up_here, down_here))
        partials = [
            partial + apply_pair(chunk, block_member, up_here, down_here)
            for partial, chunk in zip(partials, chunk_inputs)
        ]
    changes = [
        lax.psum_scatter(partial.astype(PARTIAL_DTYPE), "tp", scatter_dimension=0, tiled=True)
        for partial in partials
    ]
    arrivals = []
    for c in range(chunks):
        change = changes[c].astype(jnp.float32)
        rows_out = sorted_states[c * chunk_rows:(c + 1) * chunk_rows]
        predicted = (rows_out.astype(jnp.float32) + change).astype(jnp.bfloat16)
        spots_out = lane_column(sorted_spot[c * chunk_rows:(c + 1) * chunk_rows])
        arrivals.append(
            lax.all_to_all(
                jnp.concatenate([predicted, spots_out], axis=1).reshape(
                    n_dev, per_chunk, feature_width + 128
                ),
                ("member", "tp"),
                split_axis=0,
                concat_axis=0,
                tiled=True,
            ).reshape(n_dev * per_chunk, feature_width + 128)
        )
        if c + 1 < chunks:
            arrivals[c], changes[c + 1] = lax.optimization_barrier((arrivals[c], changes[c + 1]))
    arrivals = jnp.concatenate(arrivals, axis=0)
    arrival_spots = arrivals[:, feature_width].astype(jnp.int32)
    settle = (jnp.arange(rows_here, dtype=jnp.int32)[:, None] == arrival_spots[None, :]).astype(
        jnp.bfloat16
    )
    imagined = jnp.dot(
        settle, arrivals[:, :feature_width], preferred_element_type=jnp.float32
    ).astype(jnp.bfloat16)
    policy_normed = rms_scale(imagined.astype(jnp.float32), policy_gain).astype(jnp.bfloat16)
    action = jnp.tanh(jnp.dot(policy_normed, w_policy, preferred_element_type=jnp.float32)).astype(
        jnp.bfloat16
    )
    return (imagined, action)


def solution(mesh):
    in_specs = (
        P(("rep", "member", "tp"), None),
        P(("rep", "member", "tp"), None),
        P(("rep", "member", "tp")),
        P(),
        P("member", None, "tp"),
        P("member", "tp", None),
        P(),
        P(),
    )
    out_specs = (P(("rep", "member", "tp"), None), P(("rep", "member", "tp"), None))
    return jax.shard_map(local, mesh=mesh, in_specs=in_specs, out_specs=out_specs, check_vma=False)
```

time: 147 us -> 154 us (1.048)
  matrix products: 20.5 us -> 27.8 us
  blocking collectives: 14.6 us -> 10.9 us
  starting transfers between devices: 4.17 us -> 7.69 us
    dot_general x4 -> x8, matrix products: 18.1 us -> 26.2 us  [apply_block(): return jnp.dot(hidden, down_here, preferred_element_type=jnp.float32)]
    reduce_scatter x1 -> x2, waiting for transfers between devices: 45.5 us -> 38 us  [local(): lax.psum_scatter(partial.astype(PARTIAL_DTYPE), 'tp', scatter_dimension=0...]
    all_to_all x0 -> x1, waiting for transfers between devices: none -> 7.42 us  [local(): lax.all_to_all(jnp.concatenate([predicted, spots_out], axis=1).reshape(n_...]
    ppermute x4, waiting for transfers between devices: 0.01 us -> 4 us  [from_partner(): lax.ppermute(value, axis, [(i, i ^ 1 << distance) for i in range(lax.axis...]
    all_to_all x1, blocking collectives: 14.6 us -> 10.9 us  [local(): lax.all_to_all(jnp.concatenate([predicted, spots_out], axis=1).reshape(n_...]
    all_to_all x0 -> x1, starting transfers between devices: none -> 3.52 us  [local(): lax.all_to_all(jnp.concatenate([predicted, spots_out], axis=1).reshape(n_...]
    ppermute x2, waiting for transfers between devices: 5.65 us -> 2.24 us  [from_chip_behind(): lax.ppermute(value, axis, [(i, (i + 2 * chips_back) % size) for i in rang...]
    convert_element_type x2 -> x5, other arithmetic: 0.24 us -> 2.28 us  [the longest x2 1.95 us: local(): predicted = (rows_out.astype(jnp.float32) + change).astype(jnp.bfloat16)]
  transfers between devices with their start and end apart: 8 -> 10, of which waited for: 3 -> 7; matrix products, arithmetic and copies ran while one was open for 10% -> 15% of each run, Pallas kernels for 0% -> 0%
where the time goes in v7:
time: 154 us
  waiting for transfers between devices  81.4 us (53%)
  matrix products  27.8 us (18%)
  between operations  14 us (9%)
  blocking collectives  10.9 us (7%)
  other arithmetic  8.74 us (6%)
  starting transfers between devices  7.69 us (5%)
  local copies, waits for them, and re-layouts  3.09 us (2%)
    reduce_scatter x2, waiting for transfers between devices, local(): lax.psum_scatter(partial.astype(PARTIAL_DTYPE), 'tp', scatter_dimension=0...  38 us
    all_gather x1, waiting for transfers between devices, local(): lax.all_gather(jnp.concatenate([normed, lane_column(sorted_member)], axis...  29.7 us
    dot_general x8, matrix products, apply_block(): return jnp.dot(hidden, down_here, preferred_element_type=jnp.float32)  26.2 us
    all_to_all x1, blocking collectives, local(): lax.all_to_all(jnp.concatenate([predicted, spots_out], axis=1).reshape(n_...  10.9 us
    all_to_all x1, waiting for transfers between devices, local(): lax.all_to_all(jnp.concatenate([predicted, spots_out], axis=1).reshape(n_...  7.42 us
    ppermute x4, waiting for transfers between devices, from_partner(): lax.ppermute(value, axis, [(i, i ^ 1 << distance) for i in range(lax.axis...  4 us
    all_to_all x1, starting transfers between devices, local(): lax.all_to_all(jnp.concatenate([predicted, spots_out], axis=1).reshape(n_...  3.52 us
    add x2, other arithmetic, local(): partial + apply_pair(chunk, block_member, up_here, down_here)  3.47 us
  transfers between devices with their start and end apart: 10, of which 7 were waited for; matrix products, arithmetic and copies ran while one was open for 15% of the time, Pallas kernels for 0%

profile of v7, /device:TPU:0, one launch (start us, length us, event | category | flops | bytes accessed | tf_op | source)
XLA Modules:
  0.0 153.6 jit_solution(4763051067200948439)
XLA Ops:
  11.9 2.6 %collective-permute-start.2 = (bf16[1024,512]{1,0:T(8,128)(2,1)}, bf16[1024,512]{1,0:T(8,128)(2,1)}, u32[]{:S(2)}, u32[]{:S(2)}) collective-permute-start(bf16[1024,512]{1,0:T(8,128)(2,1)} %bitcast.5), channel_id=1, source_target_pairs={{0,8},{4,12},{8,0},{12,4},{1,9},{5,13},{9,1},{13,5},{2,10},{6,14},... | collective-permute-start | bytes 3145736 | tf_op jit(solution)/shard_map/ppermute | solution.py:15
  15.0 29.7 %all-gather.2.cloned.1.call-done = bf16[512,1152]{1,0:T(8,128)(2,1)} async-done(((bf16[128,1152]{1,0:T(8,128)(2,1)}), bf16[512,1152]{1,0:T(8,128)(2,1)}) %all-gather.2.cloned.1.call-update) | async-done | bytes 1179664 | tf_op jit(solution)/shard_map/all_gather | solution.py:68
  44.7 1.3 fusion.242
  46.2 3.5 %fusion.104 = f32[256,1024]{1,0:T(8,128)} fusion(bf16[256,1152]{1,0:T(8,128)(2,1)S(1)} %bitcast.40, bf16[256]{0:T(256)(128)(2,1)S(1)} %get-tuple-element.15, bf16[1,512,1024]{2,1,0:T(8,128)(2,1)} %param.13, bf16[1,1024,512]{2,1,0:T(8,128)(2,1)} %param.12), kind=kOutput, calls=%fused_computation.103 | convolution fusion | flops 538181632 | bytes 3670528 | tf_op jit(solution)/shard_map/dot_general | solution.py:78
  49.6 3.5 %fusion.142 = f32[256,1024]{1,0:T(8,128)} fusion(bf16[256,1152]{1,0:T(8,128)(2,1)S(1)} %bitcast.45, bf16[256]{0:T(256)(128)(2,1)S(1)} %get-tuple-element.32, bf16[1,512,1024]{2,1,0:T(8,128)(2,1)} %param.13, bf16[1,1024,512]{2,1,0:T(8,128)(2,1)} %param.12), kind=kOutput, calls=%fused_computation.117 | convolution fusion | flops 538181632 | bytes 3670528 | tf_op jit(solution)/shard_map/dot_general | solution.py:78
  53.1 2.8 %convolution_add_fusion.2 = f32[256,1024]{1,0:T(8,128)S(1)} fusion(f32[256,1024]{1,0:T(8,128)} %fusion.104, bf16[512,1024]{1,0:T(8,128)(2,1)} %collective-permute-done.1, bf16[1024,512]{1,0:T(8,128)(2,1)} %collective-permute-done, bf16[256,1152]{1,0:T(8,128)(2,1)S(1)} %bitcast.41, bf16[256]{0:T(256)(128)(2,1)S(1)} %get-tuple-element.15), kind=kOutput, calls=%fused_computation.3 | convolution fusion | flops 538443776 | bytes 4719104 | tf_op jit(solution)/shard_map/dot_general | solution.py:78
  55.9 2.9 %convolution_add_fusion.3 = f32[256,1024]{1,0:T(8,128)S(1)} fusion(f32[256,1024]{1,0:T(8,128)} %fusion.142, bf16[512,1024]{1,0:T(8,128)(2,1)} %collective-permute-done.1, bf16[1024,512]{1,0:T(8,128)(2,1)} %collective-permute-done, bf16[256,1152]{1,0:T(8,128)(2,1)} %bitcast.46, bf16[256]{0:T(256)(128)(2,1)S(1)} %get-tuple-element.32), kind=kOutput, calls=%fused_computation.4 | convolution fusion | flops 538443776 | bytes 4719104 | tf_op jit(solution)/shard_map/dot_general | solution.py:78
  58.8 2.2 %collective-permute-done.3 = bf16[512,1024]{1,0:T(8,128)(2,1)} collective-permute-done((bf16[512,1024]{1,0:T(8,128)(2,1)}, bf16[512,1024]{1,0:T(8,128)(2,1)}, u32[]{:S(2)}, u32[]{:S(2)}) %collective-permute-start.3) | collective-permute-done | bytes 1048608 | tf_op jit(solution)/shard_map/ppermute | solution.py:15
  61.6 2.5 %collective-permute-done.4 = bf16[1024,512]{1,0:T(8,128)(2,1)} collective-permute-done((bf16[1024,512]{1,0:T(8,128)(2,1)}, bf16[1024,512]{1,0:T(8,128)(2,1)}, u32[]{:S(2)}, u32[]{:S(2)}) %collective-permute-start.4) | collective-permute-done | bytes 1048608 | tf_op jit(solution)/shard_map/ppermute | solution.py:10
  64.1 1.5 collective-permute-done.5
  65.6 3.6 %fusion.145 = f32[256,1024]{1,0:T(8,128)} fusion(bf16[512,1024]{1,0:T(8,128)(2,1)} %collective-permute-done.5, bf16[1024,512]{1,0:T(8,128)(2,1)} %collective-permute-done.4, bf16[256,1152]{1,0:T(8,128)(2,1)} %bitcast.47, bf16[256]{0:T(256)(128)(2,1)S(1)} %get-tuple-element.33), kind=kOutput, calls=%fused_computation.118 | convolution fusion | flops 538181632 | bytes 3670528 | tf_op jit(solution)/shard_map/dot_general | solution.py:78
  69.1 3.9 %convolution_add_fusion.1 = f32[256,1024]{1,0:T(8,128)} fusion(f32[256,1024]{1,0:T(8,128)} %fusion.145, bf16[512,1024]{1,0:T(8,128)(2,1)} %collective-permute-done.3, bf16[1024,512]{1,0:T(8,128)(2,1)} %collective-permute-done.2, bf16[256,1152]{1,0:T(8,128)(2,1)} %bitcast.48, bf16[256]{0:T(256)(128)(2,1)S(1)} %get-tuple-element.33), kind=kOutput, calls=%fused_computation.2 | convolution fusion | flops 538443776 | bytes 4719104 | tf_op jit(solution)/shard_map/dot_general | solution.py:78
  73.0 2.3 %add.164 = f32[256,1024]{1,0:T(8,128)} add(f32[256,1024]{1,0:T(8,128)S(1)} %convolution_add_fusion.3, f32[256,1024]{1,0:T(8,128)} %convolution_add_fusion.1) | non-fusion elementwise | flops 262144 | bytes 3145728 | tf_op jit(solution)/shard_map/add | solution.py:92
  75.5 3.4 %fusion.107 = f32[256,1024]{1,0:T(8,128)} fusion(bf16[512,1024]{1,0:T(8,128)(2,1)} %collective-permute-done.5, bf16[1024,512]{1,0:T(8,128)(2,1)} %collective-permute-done.4, bf16[256,1152]{1,0:T(8,128)(2,1)S(1)} %bitcast.42, bf16[256]{0:T(256)(128)(2,1)S(1)} %get-tuple-element.14), kind=kOutput, calls=%fused_computation.104 | convolution fusion | flops 538181632 | bytes 3670528 | tf_op jit(solution)/shard_map/dot_general | solution.py:78
  78.9 2.7 %convolution_add_fusion = f32[256,1024]{1,0:T(8,128)S(1)} fusion(f32[256,1024]{1,0:T(8,128)} %fusion.107, bf16[512,1024]{1,0:T(8,128)(2,1)} %collective-permute-done.3, bf16[1024,512]{1,0:T(8,128)(2,1)} %collective-permute-done.2, bf16[256,1152]{1,0:T(8,128)(2,1)S(1)} %bitcast.43, bf16[256]{0:T(256)(128)(2,1)S(1)} %get-tuple-element.14), kind=kOutput, calls=%fused_computation.1 | convolution fusion | flops 538443776 | bytes 4719104 | tf_op jit(solution)/shard_map/dot_general | solution.py:78
  81.6 1.1 add.172
  83.0 21.2 %reduce-scatter.3.cloned.1.call-done = f32[64,1024]{1,0:T(8,128)} async-done(((f32[256,1024]{1,0:T(8,128)}), f32[64,1024]{1,0:T(8,128)}) %reduce-scatter.3.cloned.1.call-update) | async-done | bytes 262160 | tf_op jit(solution)/shard_map/reduce_scatter | solution.py:96
  104.2 1.0 add_convert_fusion.1
  105.2 10.9 %all_to_all.10 = bf16[16,4,1152]{2,1,0:T(4,128)(2,1)S(1)} all-to-all(bf16[16,4,1152]{2,1,0:T(4,128)(2,1)S(1)} %reshape.74), channel_id=1, replica_groups=mesh['rep'=2,'member'=4,'tp'=4] {'member','tp'}, dimensions={0} | all-to-all | bytes 294912 | tf_op jit(solution)/shard_map/all_to_all | solution.py:106
  116.2 16.7 %reduce-scatter.5.cloned.1.call-done = f32[64,1024]{1,0:T(8,128)} async-done(((f32[256,1024]{1,0:T(8,128)}), f32[64,1024]{1,0:T(8,128)}) %reduce-scatter.5.cloned.1.call-update) | async-done | bytes 262160 | tf_op jit(solution)/shard_map/reduce_scatter | solution.py:96
  132.9 1.0 add_convert_fusion
  134.6 3.5 %all-to-all-start.1 = ((bf16[16,4,1152]{2,1,0:T(4,128)(2,1)}), bf16[16,4,1152]{2,1,0:T(4,128)(2,1)S(1)}, u32[]{:S(2)}, u32[]{:S(2)}) async-start(bf16[16,4,1152]{2,1,0:T(4,128)(2,1)} %reshape.76), calls=%async_computation.3 | async-start | bytes 294912 | tf_op jit(solution)/shard_map/all_to_all | solution.py:106
  138.2 7.4 %all-to-all-done.1 = bf16[16,4,1152]{2,1,0:T(4,128)(2,1)S(1)} async-done(((bf16[16,4,1152]{2,1,0:T(4,128)(2,1)}), bf16[16,4,1152]{2,1,0:T(4,128)(2,1)S(1)}, u32[]{:S(2)}, u32[]{:S(2)}) %all-to-all-start.1) | async-done | bytes 147488 | tf_op jit(solution)/shard_map/all_to_all | solution.py:106
  146.1 0.9 fusion
  (56 shorter events, 7.3 us)
Async XLA Ops:
  7.2 2.1 %copy-start = (bf16[128,1024]{1,0:T(8,128)(2,1)S(1)}, bf16[128,1024]{1,0:T(8,128)(2,1)}, u32[]{:S(2)}) copy-start(bf16[128,1024]{1,0:T(8,128)(2,1)} %param.8) | copy-start | bytes 786436
  7.2 2.5 %copy-start.1 = (f32[2,1024]{1,0:T(2,128)S(1)}, f32[2,1024]{1,0:T(2,128)}, u32[]{:S(2)}) copy-start(f32[2,1024]{1,0:T(2,128)} %param.11) | copy-start | bytes 24580
  7.2 37.5 %all-gather.2.cloned.1.call-start = ((), (), s32[]{:S(2)}) async-start(), calls=%async_computation.4 | async-start | bytes 1474560 | tf_op jit(solution)/shard_map/all_gather | solution.py:68
  11.4 92.8 %reduce-scatter.3.cloned.1.call-start = ((), (), s32[]{:S(2)}) async-start(), calls=%async_computation.5 | async-start | bytes 1310720 | tf_op jit(solution)/shard_map/reduce_scatter | solution.py:96
  11.4 41.7 %collective-permute-start = (bf16[1024,512]{1,0:T(8,128)(2,1)}, bf16[1024,512]{1,0:T(8,128)(2,1)}, u32[]{:S(2)}, u32[]{:S(2)}) collective-permute-start(bf16[1024,512]{1,0:T(8,128)(2,1)} %bitcast.5), channel_id=1, source_target_pairs={{0,4},{4,0},{8,12},{12,8},{1,5},{5,1},{9,13},{13,9},{2,6},{6,2},{1... | collective-permute-start | bytes 3145736 | tf_op jit(solution)/shard_map/ppermute | solution.py:10
  11.9 46.9 %collective-permute-start.2 = (bf16[1024,512]{1,0:T(8,128)(2,1)}, bf16[1024,512]{1,0:T(8,128)(2,1)}, u32[]{:S(2)}, u32[]{:S(2)}) collective-permute-start(bf16[1024,512]{1,0:T(8,128)(2,1)} %bitcast.5), channel_id=1, source_target_pairs={{0,8},{4,12},{8,0},{12,4},{1,9},{5,13},{9,1},{13,5},{2,10},{6,14},... | collective-permute-start | bytes 3145736 | tf_op jit(solution)/shard_map/ppermute | solution.py:15
  14.5 38.6 %collective-permute-start.1 = (bf16[512,1024]{1,0:T(8,128)(2,1)}, bf16[512,1024]{1,0:T(8,128)(2,1)}, u32[]{:S(2)}, u32[]{:S(2)}) collective-permute-start(bf16[512,1024]{1,0:T(8,128)(2,1)} %bitcast.6), channel_id=1, source_target_pairs={{0,4},{4,0},{8,12},{12,8},{1,5},{5,1},{9,13},{13,9},{2,6},{6,2},{1... | collective-permute-start | bytes 3145736 | tf_op jit(solution)/shard_map/ppermute | solution.py:10
  14.7 46.4 %collective-permute-start.3 = (bf16[512,1024]{1,0:T(8,128)(2,1)}, bf16[512,1024]{1,0:T(8,128)(2,1)}, u32[]{:S(2)}, u32[]{:S(2)}) collective-permute-start(bf16[512,1024]{1,0:T(8,128)(2,1)} %bitcast.6), channel_id=1, source_target_pairs={{0,8},{4,12},{8,0},{12,4},{1,9},{5,13},{9,1},{13,5},{2,10},{6,14},... | collective-permute-start | bytes 3145736 | tf_op jit(solution)/shard_map/ppermute | solution.py:15
  46.0 3.6 %copy-start.2 = (bf16[4,1,64,1152]{3,2,1,0:T(8,128)(2,1)}, bf16[4,1,64,1152]{3,2,1,0:T(8,128)(2,1)S(1)}, u32[]{:S(2)}) copy-start(bf16[4,1,64,1152]{3,2,1,0:T(8,128)(2,1)S(1)} %get-tuple-element.21) | copy-start | bytes 1769476
  61.1 3.0 %collective-permute-start.4 = (bf16[1024,512]{1,0:T(8,128)(2,1)}, bf16[1024,512]{1,0:T(8,128)(2,1)}, u32[]{:S(2)}, u32[]{:S(2)}) collective-permute-start(bf16[1024,512]{1,0:T(8,128)(2,1)} %collective-permute-done.2), channel_id=1, source_target_pairs={{0,4},{4,0},{8,12},{12,8},{1,5},{5,1},{9,13},{13,9},{2,6},{6,2},{1... | collective-permute-start | bytes 3145736 | tf_op jit(solution)/shard_map/ppermute | solution.py:10
  61.1 4.5 %collective-permute-start.5 = (bf16[512,1024]{1,0:T(8,128)(2,1)}, bf16[512,1024]{1,0:T(8,128)(2,1)}, u32[]{:S(2)}, u32[]{:S(2)}) collective-permute-start(bf16[512,1024]{1,0:T(8,128)(2,1)} %collective-permute-done.3), channel_id=1, source_target_pairs={{0,4},{4,0},{8,12},{12,8},{1,5},{5,1},{9,13},{13,9},{2,6},{6,2},{1... | collective-permute-start | bytes 3145736 | tf_op jit(solution)/shard_map/ppermute | solution.py:10
  75.4 57.5 %reduce-scatter.5.cloned.1.call-start = ((), (), s32[]{:S(2)}) async-start(), calls=%async_computation.6 | async-start | bytes 1310720 | tf_op jit(solution)/shard_map/reduce_scatter | solution.py:96
  133.9 12.2 %copy-start.3 = (bf16[1024,128]{1,0:T(8,128)(2,1)S(1)}, bf16[1024,128]{1,0:T(8,128)(2,1)}, u32[]{:S(2)}) copy-start(bf16[1024,128]{1,0:T(8,128)(2,1)} %param.15) | copy-start | bytes 786436
  133.9 12.2 %copy-start.4 = (f32[1024]{0:T(1024)S(1)}, f32[1024]{0:T(1024)}, u32[]{:S(2)}) copy-start(f32[1024]{0:T(1024)} %param.14) | copy-start | bytes 12292
  134.6 11.0 %all-to-all-start.1 = ((bf16[16,4,1152]{2,1,0:T(4,128)(2,1)}), bf16[16,4,1152]{2,1,0:T(4,128)(2,1)S(1)}, u32[]{:S(2)}, u32[]{:S(2)}) async-start(bf16[16,4,1152]{2,1,0:T(4,128)(2,1)} %reshape.76), calls=%async_computation.3 | async-start | bytes 294912 | tf_op jit(solution)/shard_map/all_to_all | solution.py:106
  146.1 1.0 copy-start.5
Sparse Core Ops, SparseCore 0:
  11.5 33.1 all-gather.1
  75.5 28.6 reduce-scatter.2
  106.6 26.2 reduce-scatter.4

commit v8 on v6

--- a/solution.py
+++ b/solution.py
@@ -33,14 +33,12 @@
     feature_width = states.shape[1]
     own_member = lax.axis_index("member") // 2
     own_block = (own_member, w_up[0], w_down[0])
-    fetched = [
-        (
-            (own_member - back + member_total) % member_total,
-            from_chip_behind(w_up[0], "member", back),
-            from_chip_behind(w_down[0], "member", back),
-        )
-        for back in range(1, member_total)
-    ]
+    fetched = []
+    for back in range(1, member_total):
+        up_here = from_chip_behind(w_up[0], "member", back)
+        up_here, down_source = lax.optimization_barrier((up_here, w_down[0]))
+        down_here = from_chip_behind(down_source, "member", back)
+        fetched.append(((own_member - back + member_total) % member_total, up_here, down_here))
     member = member_of[:, 0]
     gain_rows = jnp.take(norm_gain, member, axis=0)
     normed = rms_scale(states.astype(jnp.float32), gain_rows).astype(jnp.bfloat16)
@@ -53,22 +51,30 @@
     gathered_rows = gathered[:, :feature_width]
     gathered_member = gathered[:, feature_width].astype(jnp.int32)
 
-    def apply_block(block_member, up_here, down_here):
+    def hidden_of(block_member, up_here):
         keep = (gathered_member == block_member).astype(jnp.bfloat16)[:, None]
-        hidden = jax.nn.gelu(
+        return jax.nn.gelu(
             jnp.dot(gathered_rows, up_here, preferred_element_type=jnp.float32)
         ).astype(jnp.bfloat16) * keep
-        return jnp.dot(hidden, down_here, preferred_element_type=jnp.float32)
 
     def apply_pair(block_member, up_here, down_here):
-        return apply_block(block_member, up_here, down_here) + apply_block(
-            block_member, from_partner(up_here, "member", 0), from_partner(down_here, "member", 0)
+        first = hidden_of(block_member, up_here)
+        second = hidden_of(block_member, from_partner(up_here, "member", 0))
+        return jnp.dot(first, down_here, preferred_element_type=jnp.float32) + jnp.dot(
+            second, from_partner(down_here, "member", 0), preferred_element_type=jnp.float32
         )
 
     partial = apply_pair(*own_block)
     for block_member, up_here, down_here in fetched:
-        partial, up_here, down_here = lax.optimization_barrier((partial, up_here, down_here))
-        partial = partial + apply_pair(block_member, up_here, down_here)
+        partial, up_here = lax.optimization_barrier((partial, up_here))
+        first = hidden_of(block_member, up_here)
+        second = hidden_of(block_member, from_partner(up_here, "member", 0))
+        first, second, down_here = lax.optimization_barrier((first, second, down_here))
+        partial = (
+            partial
+            + jnp.dot(first, down_here, preferred_element_type=jnp.float32)
+            + jnp.dot(second, from_partner(down_here, "member", 0), preferred_element_type=jnp.float32)
+        )
     change = lax.psum_scatter(
         partial.astype(PARTIAL_DTYPE), "tp", scatter_dimension=0, tiled=True
     ).astype(jnp.float32)

time: 147 us -> 154 us (1.048)
  waiting for transfers between devices: 80.9 us -> 95.5 us
  other arithmetic: 10.1 us -> 5.82 us
  matrix products: 20.5 us -> 17.3 us
    ppermute x2, waiting for transfers between devices: 5.65 us -> 43.3 us  [from_chip_behind(): lax.ppermute(value, axis, [(i, (i + 2 * chips_back) % size) for i in rang...]
    all_gather x1, waiting for transfers between devices: 29.7 us -> 7.04 us  [local(): lax.all_gather(jnp.concatenate([normed, member_lanes], axis=1), 'tp', axi...]
    add x1 -> x0, other arithmetic: 4.24 us -> none  [local(): partial = partial + apply_pair(block_member, up_here, down_here)]
    dot_general x4 -> x6, matrix products: 18.1 us -> 14.8 us  [the longest x1 4.38 us: apply_pair(): jnp.dot(first, down_here, preferred_element_type=jnp.float32)]
    reduce_scatter x1, waiting for transfers between devices: 45.5 us -> 43.1 us  [local(): lax.psum_scatter(partial.astype(PARTIAL_DTYPE), 'tp', scatter_dimension=0...]
    ppermute x4, waiting for transfers between devices: 0.01 us -> 1.95 us  [from_partner(): lax.ppermute(value, axis, [(i, i ^ 1 << distance) for i in range(lax.axis...]
    ppermute x2, starting transfers between devices: 2.98 us -> 4.57 us  [from_chip_behind(): lax.ppermute(value, axis, [(i, (i + 2 * chips_back) % size) for i in rang...]
  transfers between devices with their start and end apart: 8 -> 8, of which waited for: 3 -> 5; matrix products, arithmetic and copies ran while one was open for 10% -> 6% of each run, Pallas kernels for 0% -> 0%
where the time goes in v8:
time: 154 us
  waiting for transfers between devices  95.5 us (62%)
  matrix products  17.3 us (11%)
  blocking collectives  14.6 us (9%)
  between operations  14.3 us (9%)
  other arithmetic  5.82 us (4%)
  starting transfers between devices  5.24 us (3%)
    ppermute x2, waiting for transfers between devices, from_chip_behind(): lax.ppermute(value, axis, [(i, (i + 2 * chips_back) % size) for i in rang...  43.3 us
    reduce_scatter x1, waiting for transfers between devices, local(): lax.psum_scatter(partial.astype(PARTIAL_DTYPE), 'tp', scatter_dimension=0...  43.1 us
    all_to_all x1, blocking collectives, local(): lax.all_to_all(jnp.concatenate([packed, spot_lanes], axis=1).reshape(n_de...  14.6 us
    all_gather x1, waiting for transfers between devices, local(): lax.all_gather(jnp.concatenate([normed, member_lanes], axis=1), 'tp', axi...  7.04 us
    ppermute x2, starting transfers between devices, from_chip_behind(): lax.ppermute(value, axis, [(i, (i + 2 * chips_back) % size) for i in rang...  4.57 us
    dot_general x1, matrix products, apply_pair(): jnp.dot(first, down_here, preferred_element_type=jnp.float32)  4.38 us
    dot_general x1, matrix products, apply_pair(): jnp.dot(second, from_partner(down_here, 'member', 0), preferred_element_t...  4.03 us
    dot_general x2, matrix products, hidden_of(): jnp.dot(gathered_rows, up_here, preferred_element_type=jnp.float32)  3.51 us
  transfers between devices with their start and end apart: 8, of which 5 were waited for; matrix products, arithmetic and copies ran while one was open for 6% of the time, Pallas kernels for 0%

profile of v8, /device:TPU:0, one launch (start us, length us, event | category | flops | bytes accessed | tf_op | source)
XLA Modules:
  0.0 153.6 jit_solution(12476810909386118748)
XLA Ops:
  7.2 0.7 fusion.106
  7.9 0.7 and_bitcast_fusion
  8.6 0.7 and_select_fusion.1
  9.7 1.1 fusion.69
  11.0 0.8 gather_fusion
  12.0 0.7 pad_maximum_fusion
  12.9 3.0 %collective-permute-start.2 = (bf16[1024,512]{1,0:T(8,128)(2,1)S(1)}, bf16[1024,512]{1,0:T(8,128)(2,1)S(1)}, u32[]{:S(2)}, u32[]{:S(2)}) collective-permute-start(bf16[1024,512]{1,0:T(8,128)(2,1)S(1)} %bitcast.27), channel_id=1, source_target_pairs={{0,8},{4,12},{8,0},{12,4},{1,9},{5,13},{9,1},{13,5},{2,10},{6,14},... | collective-permute-start | bytes 3145736 | tf_op jit(solution)/shard_map/ppermute | solution.py:15
  15.9 0.5 collective-permute-start
  16.4 22.6 %collective-permute-done.2 = bf16[1024,512]{1,0:T(8,128)(2,1)S(1)} collective-permute-done((bf16[1024,512]{1,0:T(8,128)(2,1)S(1)}, bf16[1024,512]{1,0:T(8,128)(2,1)S(1)}, u32[]{:S(2)}, u32[]{:S(2)}) %collective-permute-start.2) | collective-permute-done | bytes 1048608 | tf_op jit(solution)/shard_map/ppermute | solution.py:15
  39.0 7.0 %all-gather.2.cloned.1.call-done = bf16[512,1152]{1,0:T(8,128)(2,1)} async-done(((bf16[128,1152]{1,0:T(8,128)(2,1)}), bf16[512,1152]{1,0:T(8,128)(2,1)}) %all-gather.2.cloned.1.call-update) | async-done | bytes 1179664 | tf_op jit(solution)/shard_map/all_gather | solution.py:48
  46.1 1.1 fusion.90
  47.2 4.4 %fusion.62 = f32[512,1024]{1,0:T(8,128)} fusion(bf16[512,1152]{1,0:T(8,128)(2,1)} %all-gather.2.cloned.1.call-done, bf16[512]{0:T(512)(128)(2,1)S(1)} %get-tuple-element.17, bf16[1,512,1024]{2,1,0:T(8,128)(2,1)} %param.13, bf16[1,1024,512]{2,1,0:T(8,128)(2,1)S(1)} %copy-done.5), kind=kOutput, calls=%fused_computation.58 | convolution fusion | flops 1076363264 | bytes 5243904 | tf_op jit(solution)/shard_map/dot_general | solution.py:63
  51.6 4.0 %convolution_add_fusion = f32[512,1024]{1,0:T(8,128)S(1)} fusion(f32[512,1024]{1,0:T(8,128)} %fusion.62, bf16[512,1024]{1,0:T(8,128)(2,1)} %collective-permute-done.1, bf16[1024,512]{1,0:T(8,128)(2,1)} %collective-permute-done, bf16[512,1152]{1,0:T(8,128)(2,1)} %all-gather.2.cloned.1.call-done, bf16[512]{0:T(512)(128)(2,1)S(1)} %get-tuple-element.17), kind=kOutput, calls=%fused_computation.2 | convolution fusion | flops 1076887552 | bytes 7341056 | tf_op jit(solution)/shard_map/dot_general | solution.py:63
  55.7 1.5 %collective-permute-start.4 = (bf16[512,1024]{1,0:T(8,128)(2,1)}, bf16[512,1024]{1,0:T(8,128)(2,1)S(1)}, u32[]{:S(2)}, u32[]{:S(2)}) collective-permute-start(bf16[512,1024]{1,0:T(8,128)(2,1)} %bitcast.4), channel_id=1, source_target_pairs={{0,8},{4,12},{8,0},{12,4},{1,9},{5,13},{9,1},{13,5},{2,10},{6,14},... | collective-permute-start | bytes 3145736 | tf_op jit(solution)/shard_map/ppermute | solution.py:15
  57.2 2.6 %fusion.52 = bf16[512,512]{1,0:T(8,128)(2,1)S(1)} fusion(bf16[1024,512]{1,0:T(8,128)(2,1)} %copy-done.6, bf16[512,1152]{1,0:T(8,128)(2,1)} %all-gather.2.cloned.1.call-done, bf16[512]{0:T(512)(128)(2,1)S(1)} %get-tuple-element.16), kind=kOutput, calls=%fused_computation.55 | convolution fusion | flops 539492352 | bytes 2622464 | tf_op jit(solution)/shard_map/dot_general | solution.py:57
  59.8 0.9 fusion.49
  60.8 20.7 %collective-permute-done.4 = bf16[512,1024]{1,0:T(8,128)(2,1)S(1)} collective-permute-done((bf16[512,1024]{1,0:T(8,128)(2,1)}, bf16[512,1024]{1,0:T(8,128)(2,1)S(1)}, u32[]{:S(2)}, u32[]{:S(2)}) %collective-permute-start.4) | collective-permute-done | bytes 1048608 | tf_op jit(solution)/shard_map/ppermute | solution.py:15
  81.5 0.7 fusion.107
  82.2 1.9 %collective-permute-done.5 = bf16[512,1024]{1,0:T(8,128)(2,1)S(1)} collective-permute-done((bf16[512,1024]{1,0:T(8,128)(2,1)S(1)}, bf16[512,1024]{1,0:T(8,128)(2,1)S(1)}, u32[]{:S(2)}, u32[]{:S(2)}) %collective-permute-start.5) | collective-permute-done | bytes 1048608 | tf_op jit(solution)/shard_map/ppermute | solution.py:10
  84.1 2.1 %add_add_fusion = f32[512,1024]{1,0:T(8,128)} fusion(f32[512,1024]{1,0:T(8,128)S(1)} %convolution_add_fusion, f32[512,1024]{1,0:T(8,128)S(1)} %fusion.107, bf16[512,512]{1,0:T(8,128)(2,1)S(1)} %fusion.49, bf16[512,1024]{1,0:T(8,128)(2,1)S(1)} %collective-permute-done.5), kind=kOutput, calls=%fused_computation.1 | convolution fusion | flops 537919488 | bytes 7864320 | tf_op jit(solution)/shard_map/dot_general | solution.py:76
  86.3 43.1 %reduce-scatter.2.cloned.1.call-done = f32[128,1024]{1,0:T(8,128)} async-done(((f32[512,1024]{1,0:T(8,128)}), f32[128,1024]{1,0:T(8,128)}) %reduce-scatter.2.cloned.1.call-update) | async-done | bytes 524304 | tf_op jit(solution)/shard_map/reduce_scatter | solution.py:78
  129.4 1.3 convolution_convert_fusion.1
  130.7 14.6 %all_to_all.5 = bf16[16,8,1152]{2,1,0:T(8,128)(2,1)S(1)} all-to-all(bf16[16,8,1152]{2,1,0:T(8,128)(2,1)S(1)} %maximum_bitcast_fusion), channel_id=1, replica_groups=mesh['rep'=2,'member'=4,'tp'=4] {'member','tp'}, dimensions={0} | all-to-all | bytes 589824 | tf_op jit(solution)/shard_map/all_to_all | solution.py:97
  145.8 0.9 fusion
  (42 shorter events, 1.5 us)
Async XLA Ops:
  7.2 138.6 %copy-start = (bf16[1024,128]{1,0:T(8,128)(2,1)S(1)}, bf16[1024,128]{1,0:T(8,128)(2,1)}, u32[]{:S(2)}) copy-start(bf16[1024,128]{1,0:T(8,128)(2,1)} %param.15) | copy-start | bytes 786436
  7.2 3.7 %copy-start.1 = (f32[2,1024]{1,0:T(2,128)S(1)}, f32[2,1024]{1,0:T(2,128)}, u32[]{:S(2)}) copy-start(f32[2,1024]{1,0:T(2,128)} %param.11) | copy-start | bytes 24580
  7.2 38.9 %all-gather.2.cloned.1.call-start = ((), (), s32[]{:S(2)}) async-start(), calls=%async_computation.2 | async-start | bytes 1474560 | tf_op jit(solution)/shard_map/all_gather | solution.py:48
  10.9 0.8 copy-start.4
  10.9 1.0 copy-start.2
  10.9 1.9 %copy-start.5 = (bf16[1,1024,512]{2,1,0:T(8,128)(2,1)S(1)}, bf16[1,1024,512]{2,1,0:T(8,128)(2,1)}, u32[]{:S(2)}) copy-start(bf16[1,1024,512]{2,1,0:T(8,128)(2,1)} %param.12) | copy-start | bytes 3145732
  12.8 116.6 %reduce-scatter.2.cloned.1.call-start = ((), (), s32[]{:S(2)}) async-start(), calls=%async_computation.3 | async-start | bytes 2621440 | tf_op jit(solution)/shard_map/reduce_scatter | solution.py:78
  12.9 26.2 %collective-permute-start.2 = (bf16[1024,512]{1,0:T(8,128)(2,1)S(1)}, bf16[1024,512]{1,0:T(8,128)(2,1)S(1)}, u32[]{:S(2)}, u32[]{:S(2)}) collective-permute-start(bf16[1024,512]{1,0:T(8,128)(2,1)S(1)} %bitcast.27), channel_id=1, source_target_pairs={{0,8},{4,12},{8,0},{12,4},{1,9},{5,13},{9,1},{13,5},{2,10},{6,14},... | collective-permute-start | bytes 3145736 | tf_op jit(solution)/shard_map/ppermute | solution.py:15
  15.9 35.7 %collective-permute-start.1 = (bf16[512,1024]{1,0:T(8,128)(2,1)}, bf16[512,1024]{1,0:T(8,128)(2,1)}, u32[]{:S(2)}, u32[]{:S(2)}) collective-permute-start(bf16[512,1024]{1,0:T(8,128)(2,1)} %bitcast.4), channel_id=1, source_target_pairs={{0,4},{4,0},{8,12},{12,8},{1,5},{5,1},{9,13},{13,9},{2,6},{6,2},{1... | collective-permute-start | bytes 3145736 | tf_op jit(solution)/shard_map/ppermute | solution.py:10
  15.9 35.7 %collective-permute-start = (bf16[1024,512]{1,0:T(8,128)(2,1)S(1)}, bf16[1024,512]{1,0:T(8,128)(2,1)}, u32[]{:S(2)}, u32[]{:S(2)}) collective-permute-start(bf16[1024,512]{1,0:T(8,128)(2,1)S(1)} %bitcast.28), channel_id=1, source_target_pairs={{0,4},{4,0},{8,12},{12,8},{1,5},{5,1},{9,13},{13,9},{2,6},{6,2},{1... | collective-permute-start | bytes 3145736 | tf_op jit(solution)/shard_map/ppermute | solution.py:10
  39.0 12.5 %copy-start.6 = (bf16[1024,512]{1,0:T(8,128)(2,1)}, bf16[1024,512]{1,0:T(8,128)(2,1)S(1)}, u32[]{:S(2)}) copy-start(bf16[1024,512]{1,0:T(8,128)(2,1)S(1)} %collective-permute-done.2) | copy-start | bytes 3145732
  55.6 4.2 %collective-permute-start.3 = (bf16[1024,512]{1,0:T(8,128)(2,1)}, bf16[1024,512]{1,0:T(8,128)(2,1)S(1)}, u32[]{:S(2)}, u32[]{:S(2)}) collective-permute-start(bf16[1024,512]{1,0:T(8,128)(2,1)} %copy-done.6), channel_id=1, source_target_pairs={{0,4},{4,0},{8,12},{12,8},{1,5},{5,1},{9,13},{13,9},{2,6},{6,2},{1... | collective-permute-start | bytes 3145736 | tf_op jit(solution)/shard_map/ppermute | solution.py:10
  55.7 25.8 %collective-permute-start.4 = (bf16[512,1024]{1,0:T(8,128)(2,1)}, bf16[512,1024]{1,0:T(8,128)(2,1)S(1)}, u32[]{:S(2)}, u32[]{:S(2)}) collective-permute-start(bf16[512,1024]{1,0:T(8,128)(2,1)} %bitcast.4), channel_id=1, source_target_pairs={{0,8},{4,12},{8,0},{12,4},{1,9},{5,13},{9,1},{13,5},{2,10},{6,14},... | collective-permute-start | bytes 3145736 | tf_op jit(solution)/shard_map/ppermute | solution.py:15
  57.2 2.6 %copy-start.3 = (bf16[512,1152]{1,0:T(8,128)(2,1)S(1)}, bf16[512,1152]{1,0:T(8,128)(2,1)}, u32[]{:S(2)}) copy-start(bf16[512,1152]{1,0:T(8,128)(2,1)} %all-gather.2.cloned.1.call-done) | copy-start | bytes 3538948
  81.5 2.7 %collective-permute-start.5 = (bf16[512,1024]{1,0:T(8,128)(2,1)S(1)}, bf16[512,1024]{1,0:T(8,128)(2,1)S(1)}, u32[]{:S(2)}, u32[]{:S(2)}) collective-permute-start(bf16[512,1024]{1,0:T(8,128)(2,1)S(1)} %collective-permute-done.4), channel_id=1, source_target_pairs={{0,4},{4,0},{8,12},{12,8},{1,5},{5,1},{9,13},{13,9},{2,6},{6,2},{1... | collective-permute-start | bytes 3145736 | tf_op jit(solution)/shard_map/ppermute | solution.py:10
  86.3 59.5 %copy-start.7 = (f32[1024]{0:T(1024)S(1)}, f32[1024]{0:T(1024)}, u32[]{:S(2)}) copy-start(f32[1024]{0:T(1024)} %param.14) | copy-start | bytes 12292
  145.8 1.0 copy-start.8
Sparse Core Ops, SparseCore 0:
  12.9 33.1 all-gather.1
  86.4 42.9 reduce-scatter.1

commit v9 on v6

--- a/solution.py
+++ b/solution.py
@@ -3,7 +3,7 @@
 from jax import lax
 from jax.sharding import PartitionSpec as P
 
-PARTIAL_DTYPE = jnp.float32
+PARTIAL_DTYPE = jnp.bfloat16
 
 
 def from_partner(value, axis, distance):
@@ -69,9 +69,16 @@
     for block_member, up_here, down_here in fetched:
         partial, up_here, down_here = lax.optimization_barrier((partial, up_here, down_here))
         partial = partial + apply_pair(block_member, up_here, down_here)
-    change = lax.psum_scatter(
-        partial.astype(PARTIAL_DTYPE), "tp", scatter_dimension=0, tiled=True
-    ).astype(jnp.float32)
+    tp_here = lax.axis_index("tp")
+    by_target = partial.reshape(n_tp, rows_here, feature_width)
+    change = lax.dynamic_index_in_dim(by_target, tp_here, 0, keepdims=False)
+    for shift in range(1, n_tp):
+        outgoing = lax.dynamic_index_in_dim(by_target, (tp_here + shift) % n_tp, 0, keepdims=False)
+        change = change + lax.ppermute(
+            outgoing.astype(PARTIAL_DTYPE),
+            "tp",
+            [(i, (i + shift) % n_tp) for i in range(n_tp)],
+        ).astype(jnp.float32)
     own_rows = (states.astype(jnp.float32) + change).astype(jnp.bfloat16)
     per_learner = rows_here // n_dev
     learner = place // rows_here

time: 147 us -> 128 us (0.87)
  waiting for transfers between devices: 80.9 us -> 57.1 us
  starting transfers between devices: 4.17 us -> 8.95 us
    reduce_scatter x1 -> x0, waiting for transfers between devices: 45.5 us -> none  [local(): lax.psum_scatter(partial.astype(PARTIAL_DTYPE), 'tp', scatter_dimension=0...]
    ppermute x0 -> x3, waiting for transfers between devices: none -> 21.8 us  [local(): lax.ppermute(outgoing.astype(PARTIAL_DTYPE), 'tp', [(i, (i + shift) % n_t...]
    ppermute x0 -> x3, starting transfers between devices: none -> 4.83 us  [local(): lax.ppermute(outgoing.astype(PARTIAL_DTYPE), 'tp', [(i, (i + shift) % n_t...]
  transfers between devices with their start and end apart: 8 -> 10, of which waited for: 3 -> 4; matrix products, arithmetic and copies ran while one was open for 10% -> 12% of each run, Pallas kernels for 0% -> 0%
where the time goes in v9:
time: 128 us; the launch traced here: 127 us
  waiting for transfers between devices  57.1 us (45%)
  matrix products  20.5 us (16%)
  blocking collectives  15.5 us (12%)
  between operations  14.2 us (11%)
  other arithmetic  9.35 us (7%)
  starting transfers between devices  8.95 us (7%)
  local copies, waits for them, and re-layouts  1.69 us (1%)
    all_gather x1, waiting for transfers between devices, local(): lax.all_gather(jnp.concatenate([normed, member_lanes], axis=1), 'tp', axi...  29.7 us
    ppermute x3, waiting for transfers between devices, local(): lax.ppermute(outgoing.astype(PARTIAL_DTYPE), 'tp', [(i, (i + shift) % n_t...  21.8 us
    dot_general x4, matrix products, apply_block(): return jnp.dot(hidden, down_here, preferred_element_type=jnp.float32)  17.9 us
    all_to_all x1, blocking collectives, local(): lax.all_to_all(jnp.concatenate([packed, spot_lanes], axis=1).reshape(n_de...  15.5 us
    ppermute x2, waiting for transfers between devices, from_chip_behind(): lax.ppermute(value, axis, [(i, (i + 2 * chips_back) % size) for i in rang...  5.59 us
    ppermute x3, starting transfers between devices, local(): lax.ppermute(outgoing.astype(PARTIAL_DTYPE), 'tp', [(i, (i + shift) % n_t...  4.83 us
    add x1, other arithmetic, local(): partial = partial + apply_pair(block_member, up_here, down_here)  3.53 us
    ppermute x2, starting transfers between devices, from_chip_behind(): lax.ppermute(value, axis, [(i, (i + 2 * chips_back) % size) for i in rang...  2.97 us
  transfers between devices with their start and end apart: 10, of which 4 were waited for; matrix products, arithmetic and copies ran while one was open for 12% of the time, Pallas kernels for 0%

profile of v9, /device:TPU:0, one launch (start us, length us, event | category | flops | bytes accessed | tf_op | source)
XLA Modules:
  0.0 127.3 jit_solution(5106312000277789761)
XLA Ops:
  7.2 0.7 fusion.136
  7.9 0.7 and_bitcast_fusion
  8.6 0.7 and_select_fusion.1
  9.7 1.1 fusion.75
  11.0 0.8 gather_fusion
  12.0 0.7 pad_maximum_fusion
  12.8 0.5 collective-permute-start.1
  13.4 2.9 %collective-permute-start.2 = (bf16[1024,512]{1,0:T(8,128)(2,1)S(1)}, bf16[1024,512]{1,0:T(8,128)(2,1)}, u32[]{:S(2)}, u32[]{:S(2)}) collective-permute-start(bf16[1024,512]{1,0:T(8,128)(2,1)S(1)} %bitcast.44), channel_id=1, source_target_pairs={{0,8},{4,12},{8,0},{12,4},{1,9},{5,13},{9,1},{13,5},{2,10},{6,14},... | collective-permute-start | bytes 3145736 | tf_op jit(solution)/shard_map/ppermute | solution.py:15
  16.4 29.7 %all-gather.2.cloned.1.call-done = bf16[512,1152]{1,0:T(8,128)(2,1)} async-done(((bf16[128,1152]{1,0:T(8,128)(2,1)}), bf16[512,1152]{1,0:T(8,128)(2,1)}) %all-gather.2.cloned.1.call-update) | async-done | bytes 1179664 | tf_op jit(solution)/shard_map/all_gather | solution.py:50
  46.1 1.1 fusion.111
  47.2 4.5 %fusion.68 = f32[512,1024]{1,0:T(8,128)} fusion(bf16[512,1152]{1,0:T(8,128)(2,1)} %all-gather.2.cloned.1.call-done, bf16[512]{0:T(512)(128)(2,1)S(1)} %get-tuple-element.9, bf16[1,512,1024]{2,1,0:T(8,128)(2,1)} %param.13, bf16[1,1024,512]{2,1,0:T(8,128)(2,1)S(1)} %copy-done.5), kind=kOutput, calls=%fused_computation.60 | convolution fusion | flops 1076363264 | bytes 5243904 | tf_op jit(solution)/shard_map/dot_general | solution.py:61
  51.7 5.1 %convolution_add_fusion = f32[512,1024]{1,0:T(8,128)} fusion(f32[512,1024]{1,0:T(8,128)} %fusion.68, bf16[512,1024]{1,0:T(8,128)(2,1)} %collective-permute-done.1, bf16[1024,512]{1,0:T(8,128)(2,1)} %collective-permute-done, bf16[512,1152]{1,0:T(8,128)(2,1)S(1)} %copy-done.3, bf16[512]{0:T(512)(128)(2,1)S(1)} %get-tuple-element.9), kind=kOutput, calls=%fused_computation.2 | convolution fusion | flops 1076887552 | bytes 7341056 | tf_op jit(solution)/shard_map/dot_general | solution.py:61
  56.7 5.6 %collective-permute-done.3 = bf16[512,1024]{1,0:T(8,128)(2,1)} collective-permute-done((bf16[512,1024]{1,0:T(8,128)(2,1)}, bf16[512,1024]{1,0:T(8,128)(2,1)}, u32[]{:S(2)}, u32[]{:S(2)}) %collective-permute-start.3) | collective-permute-done | bytes 1048608 | tf_op jit(solution)/shard_map/ppermute | solution.py:15
  62.8 4.3 %fusion.59 = f32[512,1024]{1,0:T(8,128)} fusion(bf16[512,1024]{1,0:T(8,128)(2,1)} %collective-permute-done.3, bf16[1024,512]{1,0:T(8,128)(2,1)} %collective-permute-done.2, bf16[512,1152]{1,0:T(8,128)(2,1)S(1)} %copy-done.3, bf16[512]{0:T(512)(128)(2,1)S(1)} %get-tuple-element.8), kind=kOutput, calls=%fused_computation.57 | convolution fusion | flops 1076363264 | bytes 5243904 | tf_op jit(solution)/shard_map/dot_general | solution.py:61
  67.2 4.0 %fusion.53 = f32[512,1024]{1,0:T(8,128)} fusion(bf16[512,1024]{1,0:T(8,128)(2,1)S(1)} %collective-permute-done.5, bf16[1024,512]{1,0:T(8,128)(2,1)} %collective-permute-done.4, bf16[512,1152]{1,0:T(8,128)(2,1)S(1)} %copy-done.3, bf16[512]{0:T(512)(128)(2,1)S(1)} %get-tuple-element.8), kind=kOutput, calls=%fused_computation.55 | convolution fusion | flops 1076363264 | bytes 5243904 | tf_op jit(solution)/shard_map/dot_general | solution.py:61
  71.2 3.5 %add_add_fusion = f32[512,1024]{1,0:T(8,128)S(1)} fusion(f32[512,1024]{1,0:T(8,128)} %convolution_add_fusion, f32[512,1024]{1,0:T(8,128)} %fusion.59, f32[512,1024]{1,0:T(8,128)} %fusion.53), kind=kLoop, calls=%fused_computation.1 | loop fusion | flops 1048576 | bytes 8388608 | tf_op jit(solution)/shard_map/add | solution.py:71
  74.7 0.8 fusion.97
  75.6 3.8 %collective-permute-start.8 = (bf16[128,1024]{1,0:T(8,128)(2,1)}, bf16[128,1024]{1,0:T(8,128)(2,1)S(1)}, u32[]{:S(2)}, u32[]{:S(2)}) collective-permute-start(bf16[128,1024]{1,0:T(8,128)(2,1)} %get-tuple-element.11), channel_id=1, source_target_pairs={{0,3},{1,0},{2,1},{3,2},{4,7},{5,4},{6,5},{7,6},{8,11},{9,8},{10,9... | collective-permute-start | bytes 786440 | tf_op jit(solution)/shard_map/ppermute | solution.py:77
  79.4 1.0 collective-permute-start.6
  80.4 6.1 %collective-permute-done.8 = bf16[128,1024]{1,0:T(8,128)(2,1)S(1)} collective-permute-done((bf16[128,1024]{1,0:T(8,128)(2,1)}, bf16[128,1024]{1,0:T(8,128)(2,1)S(1)}, u32[]{:S(2)}, u32[]{:S(2)}) %collective-permute-start.8) | collective-permute-done | bytes 262176 | tf_op jit(solution)/shard_map/ppermute | solution.py:77
  86.5 15.7 %collective-permute-done.7 = bf16[128,1024]{1,0:T(8,128)(2,1)} collective-permute-done((bf16[128,1024]{1,0:T(8,128)(2,1)S(1)}, bf16[128,1024]{1,0:T(8,128)(2,1)}, u32[]{:S(2)}, u32[]{:S(2)}) %collective-permute-start.7) | collective-permute-done | bytes 262176 | tf_op jit(solution)/shard_map/ppermute | solution.py:77
  102.2 1.3 %convolution_convert_fusion.1 = bf16[128,1024]{1,0:T(8,128)(2,1)S(1)} fusion(bf16[128,1024]{1,0:T(8,128)(2,1)S(1)} %copy-done.2, bf16[128,1024]{1,0:T(8,128)(2,1)S(1)} %collective-permute-done.8, bf16[128,1024]{1,0:T(8,128)(2,1)} %collective-permute-done.7, bf16[128,1024]{1,0:T(8,128)(2,1)} %collective-permute-done.6, f32[4,128,1024]{2,1,0:T(8,128)S(1)} %bitcast.39, ...), kind=kOutput, calls=%fused_computation.8 | convolution fusion | flops 34881536 | bytes 1835524 | tf_op jit(solution)/shard_map/dot_general | solution.py:91
  103.6 15.5 %all_to_all.5 = bf16[16,8,1152]{2,1,0:T(8,128)(2,1)S(1)} all-to-all(bf16[16,8,1152]{2,1,0:T(8,128)(2,1)S(1)} %maximum_bitcast_fusion), channel_id=1, replica_groups=mesh['rep'=2,'member'=4,'tp'=4] {'member','tp'}, dimensions={0} | all-to-all | bytes 589824 | tf_op jit(solution)/shard_map/all_to_all | solution.py:98
  119.5 0.9 fusion
  (43 shorter events, 2.0 us)
Async XLA Ops:
  7.2 112.4 %copy-start = (bf16[1024,128]{1,0:T(8,128)(2,1)S(1)}, bf16[1024,128]{1,0:T(8,128)(2,1)}, u32[]{:S(2)}) copy-start(bf16[1024,128]{1,0:T(8,128)(2,1)} %param.15) | copy-start | bytes 786436
  7.2 3.7 %copy-start.1 = (f32[2,1024]{1,0:T(2,128)S(1)}, f32[2,1024]{1,0:T(2,128)}, u32[]{:S(2)}) copy-start(f32[2,1024]{1,0:T(2,128)} %param.11) | copy-start | bytes 24580
  7.2 38.9 %all-gather.2.cloned.1.call-start = ((), (), s32[]{:S(2)}) async-start(), calls=%async_computation.1 | async-start | bytes 1474560 | tf_op jit(solution)/shard_map/all_gather | solution.py:50
  10.9 0.8 copy-start.4
  10.9 1.0 copy-start.2
  10.9 2.4 %copy-start.5 = (bf16[1,1024,512]{2,1,0:T(8,128)(2,1)S(1)}, bf16[1,1024,512]{2,1,0:T(8,128)(2,1)}, u32[]{:S(2)}) copy-start(bf16[1,1024,512]{2,1,0:T(8,128)(2,1)} %param.12) | copy-start | bytes 3145732
  12.8 38.9 %collective-permute-start.1 = (bf16[512,1024]{1,0:T(8,128)(2,1)}, bf16[512,1024]{1,0:T(8,128)(2,1)}, u32[]{:S(2)}, u32[]{:S(2)}) collective-permute-start(bf16[512,1024]{1,0:T(8,128)(2,1)} %bitcast.45), channel_id=1, source_target_pairs={{0,4},{4,0},{8,12},{12,8},{1,5},{5,1},{9,13},{13,9},{2,6},{6,2},{1... | collective-permute-start | bytes 3145736 | tf_op jit(solution)/shard_map/ppermute | solution.py:10
  13.3 38.3 %collective-permute-start = (bf16[1024,512]{1,0:T(8,128)(2,1)S(1)}, bf16[1024,512]{1,0:T(8,128)(2,1)}, u32[]{:S(2)}, u32[]{:S(2)}) collective-permute-start(bf16[1024,512]{1,0:T(8,128)(2,1)S(1)} %bitcast.43), channel_id=1, source_target_pairs={{0,4},{4,0},{8,12},{12,8},{1,5},{5,1},{9,13},{13,9},{2,6},{6,2},{1... | collective-permute-start | bytes 3145736 | tf_op jit(solution)/shard_map/ppermute | solution.py:10
  13.4 43.3 %collective-permute-start.2 = (bf16[1024,512]{1,0:T(8,128)(2,1)S(1)}, bf16[1024,512]{1,0:T(8,128)(2,1)}, u32[]{:S(2)}, u32[]{:S(2)}) collective-permute-start(bf16[1024,512]{1,0:T(8,128)(2,1)S(1)} %bitcast.44), channel_id=1, source_target_pairs={{0,8},{4,12},{8,0},{12,4},{1,9},{5,13},{9,1},{13,5},{2,10},{6,14},... | collective-permute-start | bytes 3145736 | tf_op jit(solution)/shard_map/ppermute | solution.py:15
  16.3 46.0 %collective-permute-start.3 = (bf16[512,1024]{1,0:T(8,128)(2,1)}, bf16[512,1024]{1,0:T(8,128)(2,1)}, u32[]{:S(2)}, u32[]{:S(2)}) collective-permute-start(bf16[512,1024]{1,0:T(8,128)(2,1)} %bitcast.46), channel_id=1, source_target_pairs={{0,8},{4,12},{8,0},{12,4},{1,9},{5,13},{9,1},{13,5},{2,10},{6,14},... | collective-permute-start | bytes 3145736 | tf_op jit(solution)/shard_map/ppermute | solution.py:15
  47.2 4.5 %copy-start.3 = (bf16[512,1152]{1,0:T(8,128)(2,1)S(1)}, bf16[512,1152]{1,0:T(8,128)(2,1)}, u32[]{:S(2)}) copy-start(bf16[512,1152]{1,0:T(8,128)(2,1)} %all-gather.2.cloned.1.call-done) | copy-start | bytes 3538948
  62.3 4.9 %collective-permute-start.5 = (bf16[512,1024]{1,0:T(8,128)(2,1)}, bf16[512,1024]{1,0:T(8,128)(2,1)S(1)}, u32[]{:S(2)}, u32[]{:S(2)}) collective-permute-start(bf16[512,1024]{1,0:T(8,128)(2,1)} %collective-permute-done.3), channel_id=1, source_target_pairs={{0,4},{4,0},{8,12},{12,8},{1,5},{5,1},{9,13},{13,9},{2,6},{6,2},{1... | collective-permute-start | bytes 3145736 | tf_op jit(solution)/shard_map/ppermute | solution.py:10
  62.3 4.9 %collective-permute-start.4 = (bf16[1024,512]{1,0:T(8,128)(2,1)}, bf16[1024,512]{1,0:T(8,128)(2,1)}, u32[]{:S(2)}, u32[]{:S(2)}) collective-permute-start(bf16[1024,512]{1,0:T(8,128)(2,1)} %collective-permute-done.2), channel_id=1, source_target_pairs={{0,4},{4,0},{8,12},{12,8},{1,5},{5,1},{9,13},{13,9},{2,6},{6,2},{1... | collective-permute-start | bytes 3145736 | tf_op jit(solution)/shard_map/ppermute | solution.py:10
  75.6 43.9 %copy-start.6 = (f32[1024]{0:T(1024)S(1)}, f32[1024]{0:T(1024)}, u32[]{:S(2)}) copy-start(f32[1024]{0:T(1024)} %param.14) | copy-start | bytes 12292
  75.6 10.9 %collective-permute-start.8 = (bf16[128,1024]{1,0:T(8,128)(2,1)}, bf16[128,1024]{1,0:T(8,128)(2,1)S(1)}, u32[]{:S(2)}, u32[]{:S(2)}) collective-permute-start(bf16[128,1024]{1,0:T(8,128)(2,1)} %get-tuple-element.11), channel_id=1, source_target_pairs={{0,3},{1,0},{2,1},{3,2},{4,7},{5,4},{6,5},{7,6},{8,11},{9,8},{10,9... | collective-permute-start | bytes 786440 | tf_op jit(solution)/shard_map/ppermute | solution.py:77
  79.4 22.8 %collective-permute-start.7 = (bf16[128,1024]{1,0:T(8,128)(2,1)S(1)}, bf16[128,1024]{1,0:T(8,128)(2,1)}, u32[]{:S(2)}, u32[]{:S(2)}) collective-permute-start(bf16[128,1024]{1,0:T(8,128)(2,1)S(1)} %get-tuple-element.12), channel_id=1, source_target_pairs={{0,2},{1,3},{2,0},{3,1},{4,6},{5,7},{6,4},{7,5},{8,10},{9,11},{10,... | collective-permute-start | bytes 786440 | tf_op jit(solution)/shard_map/ppermute | solution.py:77
  79.4 22.8 %collective-permute-start.6 = (bf16[128,1024]{1,0:T(8,128)(2,1)S(1)}, bf16[128,1024]{1,0:T(8,128)(2,1)}, u32[]{:S(2)}, u32[]{:S(2)}) collective-permute-start(bf16[128,1024]{1,0:T(8,128)(2,1)S(1)} %get-tuple-element.10), channel_id=1, source_target_pairs={{0,1},{1,2},{2,3},{3,0},{4,5},{5,6},{6,7},{7,4},{8,9},{9,10},{10,1... | collective-permute-start | bytes 786440 | tf_op jit(solution)/shard_map/ppermute | solution.py:77
  119.5 1.0 copy-start.7
Sparse Core Ops, SparseCore 0:
  12.9 33.1 all-gather.1

commit v10 on v9

--- a/solution.py
+++ b/solution.py
@@ -61,9 +61,9 @@
         return jnp.dot(hidden, down_here, preferred_element_type=jnp.float32)
 
     def apply_pair(block_member, up_here, down_here):
-        return apply_block(block_member, up_here, down_here) + apply_block(
-            block_member, from_partner(up_here, "member", 0), from_partner(down_here, "member", 0)
-        )
+        both_up = jnp.concatenate([up_here, from_partner(up_here, "member", 0)], axis=1)
+        both_down = jnp.concatenate([down_here, from_partner(down_here, "member", 0)], axis=0)
+        return apply_block(block_member, both_up, both_down)
 
     partial = apply_pair(*own_block)
     for block_member, up_here, down_here in fetched:

time: 128 us -> 128 us (level)
  waiting for transfers between devices: 57.1 us -> 63.8 us
  matrix products: 20.5 us -> 14.3 us
    dot_general x4 -> x2, matrix products: 17.9 us -> 11.7 us  [apply_block(): return jnp.dot(hidden, down_here, preferred_element_type=jnp.float32)]
    ppermute x4, waiting for transfers between devices: 0.01 us -> 4 us  [from_partner(): lax.ppermute(value, axis, [(i, i ^ 1 << distance) for i in range(lax.axis...]
    ppermute x2, waiting for transfers between devices: 5.59 us -> 8.12 us  [from_chip_behind(): lax.ppermute(value, axis, [(i, (i + 2 * chips_back) % size) for i in rang...]
  transfers between devices with their start and end apart: 10 -> 10, of which waited for: 4 -> 6; matrix products, arithmetic and copies ran while one was open for 12% -> 6% of each run, Pallas kernels for 0% -> 0%
where the time goes in v10:
time: 128 us
  waiting for transfers between devices  63.8 us (50%)
  blocking collectives  15.5 us (12%)
  matrix products  14.3 us (11%)
  between operations  14.2 us (11%)
  starting transfers between devices  8.96 us (7%)
  other arithmetic  8.45 us (7%)
  local copies, waits for them, and re-layouts  2.66 us (2%)
    all_gather x1, waiting for transfers between devices, local(): lax.all_gather(jnp.concatenate([normed, member_lanes], axis=1), 'tp', axi...  29.7 us
    ppermute x3, waiting for transfers between devices, local(): lax.ppermute(outgoing.astype(PARTIAL_DTYPE), 'tp', [(i, (i + shift) % n_t...  21.9 us
    all_to_all x1, blocking collectives, local(): lax.all_to_all(jnp.concatenate([packed, spot_lanes], axis=1).reshape(n_de...  15.5 us
    dot_general x2, matrix products, apply_block(): return jnp.dot(hidden, down_here, preferred_element_type=jnp.float32)  11.7 us
    ppermute x2, waiting for transfers between devices, from_chip_behind(): lax.ppermute(value, axis, [(i, (i + 2 * chips_back) % size) for i in rang...  8.12 us
    ppermute x3, starting transfers between devices, local(): lax.ppermute(outgoing.astype(PARTIAL_DTYPE), 'tp', [(i, (i + shift) % n_t...  4.84 us
    ppermute x4, waiting for transfers between devices, from_partner(): lax.ppermute(value, axis, [(i, i ^ 1 << distance) for i in range(lax.axis...  4 us
    ppermute x2, starting transfers between devices, from_chip_behind(): lax.ppermute(value, axis, [(i, (i + 2 * chips_back) % size) for i in rang...  2.97 us
  transfers between devices with their start and end apart: 10, of which 6 were waited for; matrix products, arithmetic and copies ran while one was open for 6% of the time, Pallas kernels for 0%

profile of v10, /device:TPU:0, one launch (start us, length us, event | category | flops | bytes accessed | tf_op | source)
XLA Modules:
  0.0 127.8 jit_solution(15291353027599017493)
XLA Ops:
  7.2 0.7 fusion.92
  7.9 0.7 and_bitcast_fusion
  8.6 0.7 and_select_fusion.1
  9.7 1.1 fusion.56
  11.0 0.8 gather_fusion
  12.0 0.7 pad_maximum_fusion
  12.8 0.5 collective-permute-start.1
  13.4 2.9 %collective-permute-start.2 = (bf16[1024,512]{1,0:T(8,128)(2,1)S(1)}, bf16[1024,512]{1,0:T(8,128)(2,1)}, u32[]{:S(2)}, u32[]{:S(2)}) collective-permute-start(bf16[1024,512]{1,0:T(8,128)(2,1)S(1)} %bitcast.33), channel_id=1, source_target_pairs={{0,8},{4,12},{8,0},{12,4},{1,9},{5,13},{9,1},{13,5},{2,10},{6,14},... | collective-permute-start | bytes 3145736 | tf_op jit(solution)/shard_map/ppermute | solution.py:15
  16.4 29.7 %all-gather.2.cloned.1.call-done = bf16[512,1152]{1,0:T(8,128)(2,1)} async-done(((bf16[128,1152]{1,0:T(8,128)(2,1)}), bf16[512,1152]{1,0:T(8,128)(2,1)}) %all-gather.2.cloned.1.call-update) | async-done | bytes 1179664 | tf_op jit(solution)/shard_map/all_gather | solution.py:50
  46.1 1.1 fusion.74
  47.2 1.0 copy-done.6
  48.2 6.0 %fusion.20 = f32[512,1024]{1,0:T(8,128)} fusion(bf16[512,1024]{1,0:T(8,128)(2,1)} %copy-done.6, bf16[512,1024]{1,0:T(8,128)(2,1)} %bitcast.4, bf16[1024,512]{1,0:T(8,128)(2,1)} %collective-permute-done, bf16[1024,512]{1,0:T(8,128)(2,1)S(1)} %bitcast.34, bf16[512,1152]{1,0:T(8,128)(2,1)} %all-gather.2.cloned.1.call-done, bf16[512]{0:T(512)(128)(2,1)S(1)} %get-tuple-element.9), kind=kOutput, calls=%fused_computation.23 | convolution fusion | flops 2161115136 | bytes 7341056 | tf_op jit(solution)/shard_map/dot_general | solution.py:61
  54.2 8.1 %collective-permute-done.3 = bf16[512,1024]{1,0:T(8,128)(2,1)} collective-permute-done((bf16[512,1024]{1,0:T(8,128)(2,1)}, bf16[512,1024]{1,0:T(8,128)(2,1)}, u32[]{:S(2)}, u32[]{:S(2)}) %collective-permute-start.3) | collective-permute-done | bytes 1048608 | tf_op jit(solution)/shard_map/ppermute | solution.py:15
  62.8 3.8 %collective-permute-done.5 = bf16[512,1024]{1,0:T(8,128)(2,1)S(1)} collective-permute-done((bf16[512,1024]{1,0:T(8,128)(2,1)}, bf16[512,1024]{1,0:T(8,128)(2,1)S(1)}, u32[]{:S(2)}, u32[]{:S(2)}) %collective-permute-start.5) | collective-permute-done | bytes 1048608 | tf_op jit(solution)/shard_map/ppermute | solution.py:10
  66.8 5.7 %fusion.28 = f32[512,1024]{1,0:T(8,128)} fusion(bf16[512,1024]{1,0:T(8,128)(2,1)S(1)} %collective-permute-done.5, bf16[512,1024]{1,0:T(8,128)(2,1)} %collective-permute-done.3, bf16[1024,512]{1,0:T(8,128)(2,1)} %collective-permute-done.4, bf16[1024,512]{1,0:T(8,128)(2,1)} %collective-permute-done.2, bf16[512,1152]{1,0:T(8,128)(2,1)S(1)} %copy-done.3, ...), kind=kOutput, calls=%fused_computation.31 | convolution fusion | flops 2161115136 | bytes 7341056 | tf_op jit(solution)/shard_map/dot_general | solution.py:61
  72.5 2.6 %add.115 = f32[512,1024]{1,0:T(8,128)S(1)} add(f32[512,1024]{1,0:T(8,128)} %fusion.20, f32[512,1024]{1,0:T(8,128)} %fusion.28) | non-fusion elementwise | flops 524288 | bytes 6291456 | tf_op jit(solution)/shard_map/add | solution.py:71
  75.1 0.8 fusion.64
  75.9 3.8 %collective-permute-start.8 = (bf16[128,1024]{1,0:T(8,128)(2,1)}, bf16[128,1024]{1,0:T(8,128)(2,1)S(1)}, u32[]{:S(2)}, u32[]{:S(2)}) collective-permute-start(bf16[128,1024]{1,0:T(8,128)(2,1)} %get-tuple-element.11), channel_id=1, source_target_pairs={{0,3},{1,0},{2,1},{3,2},{4,7},{5,4},{6,5},{7,6},{8,11},{9,8},{10,9... | collective-permute-start | bytes 786440 | tf_op jit(solution)/shard_map/ppermute | solution.py:77
  79.8 1.0 collective-permute-start.6
  80.8 6.1 %collective-permute-done.8 = bf16[128,1024]{1,0:T(8,128)(2,1)S(1)} collective-permute-done((bf16[128,1024]{1,0:T(8,128)(2,1)}, bf16[128,1024]{1,0:T(8,128)(2,1)S(1)}, u32[]{:S(2)}, u32[]{:S(2)}) %collective-permute-start.8) | collective-permute-done | bytes 262176 | tf_op jit(solution)/shard_map/ppermute | solution.py:77
  86.8 15.9 %collective-permute-done.7 = bf16[128,1024]{1,0:T(8,128)(2,1)} collective-permute-done((bf16[128,1024]{1,0:T(8,128)(2,1)S(1)}, bf16[128,1024]{1,0:T(8,128)(2,1)}, u32[]{:S(2)}, u32[]{:S(2)}) %collective-permute-start.7) | collective-permute-done | bytes 262176 | tf_op jit(solution)/shard_map/ppermute | solution.py:77
  102.7 1.4 %convolution_convert_fusion.1 = bf16[128,1024]{1,0:T(8,128)(2,1)S(1)} fusion(bf16[128,1024]{1,0:T(8,128)(2,1)S(1)} %copy-done.2, bf16[128,1024]{1,0:T(8,128)(2,1)S(1)} %collective-permute-done.8, bf16[128,1024]{1,0:T(8,128)(2,1)} %collective-permute-done.7, bf16[128,1024]{1,0:T(8,128)(2,1)} %collective-permute-done.6, f32[4,128,1024]{2,1,0:T(8,128)S(1)} %bitcast.28, ...), kind=kOutput, calls=%fused_computation.36 | convolution fusion | flops 34881536 | bytes 1835524 | tf_op jit(solution)/shard_map/dot_general | solution.py:91
  104.1 15.5 %all_to_all.5 = bf16[16,8,1152]{2,1,0:T(8,128)(2,1)S(1)} all-to-all(bf16[16,8,1152]{2,1,0:T(8,128)(2,1)S(1)} %maximum_bitcast_fusion), channel_id=1, replica_groups=mesh['rep'=2,'member'=4,'tp'=4] {'member','tp'}, dimensions={0} | all-to-all | bytes 589824 | tf_op jit(solution)/shard_map/all_to_all | solution.py:98
  120.1 0.9 fusion.32
  (43 shorter events, 2.2 us)
Async XLA Ops:
  7.2 112.9 %copy-start = (bf16[1024,128]{1,0:T(8,128)(2,1)S(1)}, bf16[1024,128]{1,0:T(8,128)(2,1)}, u32[]{:S(2)}) copy-start(bf16[1024,128]{1,0:T(8,128)(2,1)} %param.15) | copy-start | bytes 786436
  7.2 3.7 %copy-start.1 = (f32[2,1024]{1,0:T(2,128)S(1)}, f32[2,1024]{1,0:T(2,128)}, u32[]{:S(2)}) copy-start(f32[2,1024]{1,0:T(2,128)} %param.11) | copy-start | bytes 24580
  7.2 38.9 %all-gather.2.cloned.1.call-start = ((), (), s32[]{:S(2)}) async-start(), calls=%async_computation.1 | async-start | bytes 1474560 | tf_op jit(solution)/shard_map/all_gather | solution.py:50
  10.9 0.8 copy-start.4
  10.9 1.0 copy-start.2
  10.9 2.4 %copy-start.5 = (bf16[1,1024,512]{2,1,0:T(8,128)(2,1)S(1)}, bf16[1,1024,512]{2,1,0:T(8,128)(2,1)}, u32[]{:S(2)}) copy-start(bf16[1,1024,512]{2,1,0:T(8,128)(2,1)} %param.12) | copy-start | bytes 3145732
  12.8 34.4 %collective-permute-start.1 = (bf16[512,1024]{1,0:T(8,128)(2,1)}, bf16[512,1024]{1,0:T(8,128)(2,1)S(1)}, u32[]{:S(2)}, u32[]{:S(2)}) collective-permute-start(bf16[512,1024]{1,0:T(8,128)(2,1)} %bitcast.4), channel_id=1, source_target_pairs={{0,4},{4,0},{8,12},{12,8},{1,5},{5,1},{9,13},{13,9},{2,6},{6,2},{1... | collective-permute-start | bytes 3145736 | tf_op jit(solution)/shard_map/ppermute | solution.py:10
  13.3 33.9 %collective-permute-start = (bf16[1024,512]{1,0:T(8,128)(2,1)S(1)}, bf16[1024,512]{1,0:T(8,128)(2,1)}, u32[]{:S(2)}, u32[]{:S(2)}) collective-permute-start(bf16[1024,512]{1,0:T(8,128)(2,1)S(1)} %bitcast.32), channel_id=1, source_target_pairs={{0,4},{4,0},{8,12},{12,8},{1,5},{5,1},{9,13},{13,9},{2,6},{6,2},{1... | collective-permute-start | bytes 3145736 | tf_op jit(solution)/shard_map/ppermute | solution.py:10
  13.4 40.8 %collective-permute-start.2 = (bf16[1024,512]{1,0:T(8,128)(2,1)S(1)}, bf16[1024,512]{1,0:T(8,128)(2,1)}, u32[]{:S(2)}, u32[]{:S(2)}) collective-permute-start(bf16[1024,512]{1,0:T(8,128)(2,1)S(1)} %bitcast.33), channel_id=1, source_target_pairs={{0,8},{4,12},{8,0},{12,4},{1,9},{5,13},{9,1},{13,5},{2,10},{6,14},... | collective-permute-start | bytes 3145736 | tf_op jit(solution)/shard_map/ppermute | solution.py:15
  16.3 46.0 %collective-permute-start.3 = (bf16[512,1024]{1,0:T(8,128)(2,1)}, bf16[512,1024]{1,0:T(8,128)(2,1)}, u32[]{:S(2)}, u32[]{:S(2)}) collective-permute-start(bf16[512,1024]{1,0:T(8,128)(2,1)} %bitcast.4), channel_id=1, source_target_pairs={{0,8},{4,12},{8,0},{12,4},{1,9},{5,13},{9,1},{13,5},{2,10},{6,14},... | collective-permute-start | bytes 3145736 | tf_op jit(solution)/shard_map/ppermute | solution.py:15
  47.2 1.0 copy-start.6
  48.2 18.7 %copy-start.3 = (bf16[512,1152]{1,0:T(8,128)(2,1)S(1)}, bf16[512,1152]{1,0:T(8,128)(2,1)}, u32[]{:S(2)}) copy-start(bf16[512,1152]{1,0:T(8,128)(2,1)} %all-gather.2.cloned.1.call-done) | copy-start | bytes 3538948
  62.3 4.3 %collective-permute-start.5 = (bf16[512,1024]{1,0:T(8,128)(2,1)}, bf16[512,1024]{1,0:T(8,128)(2,1)S(1)}, u32[]{:S(2)}, u32[]{:S(2)}) collective-permute-start(bf16[512,1024]{1,0:T(8,128)(2,1)} %collective-permute-done.3), channel_id=1, source_target_pairs={{0,4},{4,0},{8,12},{12,8},{1,5},{5,1},{9,13},{13,9},{2,6},{6,2},{1... | collective-permute-start | bytes 3145736 | tf_op jit(solution)/shard_map/ppermute | solution.py:10
  62.3 4.5 %collective-permute-start.4 = (bf16[1024,512]{1,0:T(8,128)(2,1)}, bf16[1024,512]{1,0:T(8,128)(2,1)}, u32[]{:S(2)}, u32[]{:S(2)}) collective-permute-start(bf16[1024,512]{1,0:T(8,128)(2,1)} %collective-permute-done.2), channel_id=1, source_target_pairs={{0,4},{4,0},{8,12},{12,8},{1,5},{5,1},{9,13},{13,9},{2,6},{6,2},{1... | collective-permute-start | bytes 3145736 | tf_op jit(solution)/shard_map/ppermute | solution.py:10
  75.9 44.1 %copy-start.7 = (f32[1024]{0:T(1024)S(1)}, f32[1024]{0:T(1024)}, u32[]{:S(2)}) copy-start(f32[1024]{0:T(1024)} %param.14) | copy-start | bytes 12292
  75.9 10.9 %collective-permute-start.8 = (bf16[128,1024]{1,0:T(8,128)(2,1)}, bf16[128,1024]{1,0:T(8,128)(2,1)S(1)}, u32[]{:S(2)}, u32[]{:S(2)}) collective-permute-start(bf16[128,1024]{1,0:T(8,128)(2,1)} %get-tuple-element.11), channel_id=1, source_target_pairs={{0,3},{1,0},{2,1},{3,2},{4,7},{5,4},{6,5},{7,6},{8,11},{9,8},{10,9... | collective-permute-start | bytes 786440 | tf_op jit(solution)/shard_map/ppermute | solution.py:77
  79.8 22.9 %collective-permute-start.7 = (bf16[128,1024]{1,0:T(8,128)(2,1)S(1)}, bf16[128,1024]{1,0:T(8,128)(2,1)}, u32[]{:S(2)}, u32[]{:S(2)}) collective-permute-start(bf16[128,1024]{1,0:T(8,128)(2,1)S(1)} %get-tuple-element.12), channel_id=1, source_target_pairs={{0,2},{1,3},{2,0},{3,1},{4,6},{5,7},{6,4},{7,5},{8,10},{9,11},{10,... | collective-permute-start | bytes 786440 | tf_op jit(solution)/shard_map/ppermute | solution.py:77
  79.8 22.9 %collective-permute-start.6 = (bf16[128,1024]{1,0:T(8,128)(2,1)S(1)}, bf16[128,1024]{1,0:T(8,128)(2,1)}, u32[]{:S(2)}, u32[]{:S(2)}) collective-permute-start(bf16[128,1024]{1,0:T(8,128)(2,1)S(1)} %get-tuple-element.10), channel_id=1, source_target_pairs={{0,1},{1,2},{2,3},{3,0},{4,5},{5,6},{6,7},{7,4},{8,9},{9,10},{10,1... | collective-permute-start | bytes 786440 | tf_op jit(solution)/shard_map/ppermute | solution.py:77
  120.0 1.0 copy-start.8
Sparse Core Ops, SparseCore 0:
  12.9 33.1 all-gather.1

commit v11 on v9

--- a/solution.py
+++ b/solution.py
@@ -13,6 +13,29 @@
 def from_chip_behind(value, axis, chips_back):
     size = lax.axis_size(axis)
     return lax.ppermute(value, axis, [(i, (i + 2 * chips_back) % size) for i in range(size)])
+
+
+def swap_parts(value):
+    n_rep = lax.axis_size("rep")
+    return [value] + [
+        lax.ppermute(value, "rep", [(i, (i + step) % n_rep) for i in range(n_rep)])
+        for step in range(1, n_rep)
+    ]
+
+
+def fetch_shared(up, down, chips_back):
+    n_rep = lax.axis_size("rep")
+    share = up.shape[1] // n_rep
+    rep_here = lax.axis_index("rep")
+    got_up = from_chip_behind(
+        lax.dynamic_slice_in_dim(up, rep_here * share, share, axis=1), "member", chips_back
+    )
+    got_up, down = lax.optimization_barrier((got_up, down))
+    got_down = from_chip_behind(
+        lax.dynamic_slice_in_dim(down, rep_here * share, share, axis=0), "member", chips_back
+    )
+    up_parts = swap_parts(got_up)
+    return jnp.concatenate(up_parts, axis=1), jnp.concatenate(swap_parts(got_down), axis=0)
 
 
 def rms_scale(values, gain):
@@ -36,8 +59,7 @@
     fetched = [
         (
             (own_member - back + member_total) % member_total,
-            from_chip_behind(w_up[0], "member", back),
-            from_chip_behind(w_down[0], "member", back),
+            *fetch_shared(w_up[0], w_down[0], back),
         )
         for back in range(1, member_total)
     ]

time: 128 us -> 126 us (0.984)
  waiting for transfers between devices: 57.1 us -> 47.5 us
  starting transfers between devices: 8.95 us -> 13.4 us
  other arithmetic: 9.35 us -> 11.6 us
    all_gather x1, waiting for transfers between devices: 29.7 us -> 0.02 us  [local(): lax.all_gather(jnp.concatenate([normed, member_lanes], axis=1), 'tp', axi...]
    ppermute x2, waiting for transfers between devices: 5.59 us -> 16.2 us  [from_chip_behind(): lax.ppermute(value, axis, [(i, (i + 2 * chips_back) % size) for i in rang...]
    ppermute x0 -> x2, waiting for transfers between devices: none -> 9.46 us  [swap_parts(): lax.ppermute(value, 'rep', [(i, (i + step) % n_rep) for i in range(n_rep)])]
    ppermute x0 -> x2, starting transfers between devices: none -> 2.88 us  [swap_parts(): lax.ppermute(value, 'rep', [(i, (i + step) % n_rep) for i in range(n_rep)])]
    concatenate x0 -> x2, other arithmetic: none -> 2.22 us  [the longest x1 1.11 us: fetch_shared(): jnp.concatenate(up_parts, axis=1)]
    ppermute x2, starting transfers between devices: 2.97 us -> 4.84 us  [from_chip_behind(): lax.ppermute(value, axis, [(i, (i + 2 * chips_back) % size) for i in rang...]
  transfers between devices with their start and end apart: 10 -> 12, of which waited for: 4 -> 5; matrix products, arithmetic and copies ran while one was open for 12% -> 14% of each run, Pallas kernels for 0% -> 0%
where the time goes in v11:
time: 126 us
  waiting for transfers between devices  47.5 us (38%)
  matrix products  21.3 us (17%)
  blocking collectives  15 us (12%)
  between operations  14.2 us (11%)
  starting transfers between devices  13.4 us (11%)
  other arithmetic  11.6 us (9%)
  local copies, waits for them, and re-layouts  2.8 us (2%)
    ppermute x3, waiting for transfers between devices, local(): lax.ppermute(outgoing.astype(PARTIAL_DTYPE), 'tp', [(i, (i + shift) % n_t...  21.8 us
    dot_general x4, matrix products, apply_block(): return jnp.dot(hidden, down_here, preferred_element_type=jnp.float32)  18.7 us
    ppermute x2, waiting for transfers between devices, from_chip_behind(): lax.ppermute(value, axis, [(i, (i + 2 * chips_back) % size) for i in rang...  16.2 us
    all_to_all x1, blocking collectives, local(): lax.all_to_all(jnp.concatenate([packed, spot_lanes], axis=1).reshape(n_de...  15 us
    ppermute x2, waiting for transfers between devices, swap_parts(): lax.ppermute(value, 'rep', [(i, (i + step) % n_rep) for i in range(n_rep)])  9.46 us
    ppermute x2, starting transfers between devices, from_chip_behind(): lax.ppermute(value, axis, [(i, (i + 2 * chips_back) % size) for i in rang...  4.84 us
    ppermute x3, starting transfers between devices, local(): lax.ppermute(outgoing.astype(PARTIAL_DTYPE), 'tp', [(i, (i + shift) % n_t...  4.62 us
    add x1, other arithmetic, local(): partial = partial + apply_pair(block_member, up_here, down_here)  3.53 us
  transfers between devices with their start and end apart: 12, of which 5 were waited for; matrix products, arithmetic and copies ran while one was open for 14% of the time, Pallas kernels for 0%

profile of v11, /device:TPU:0, one launch (start us, length us, event | category | flops | bytes accessed | tf_op | source)
XLA Modules:
  0.0 125.8 jit_solution(13365706213395912320)
XLA Ops:
  7.2 1.1 dynamic-slice_bitcast_fusion
  8.3 3.0 %collective-permute-start.2 = (bf16[1024,256]{1,0:T(8,128)(2,1)S(1)}, bf16[1024,256]{1,0:T(8,128)(2,1)S(1)}, u32[]{:S(2)}, u32[]{:S(2)}) collective-permute-start(bf16[1024,256]{1,0:T(8,128)(2,1)S(1)} %dynamic-slice_bitcast_fusion), channel_id=1, source_target_pairs={{0,8},{4,12},{8,0},{12,4},{1,9},{5,13},{9,1},{13,5},{2,10},{6,14},... | collective-permute-start | bytes 1572872 | tf_op jit(solution)/shard_map/ppermute | solution.py:15
  13.8 1.1 fusion.75
  16.9 6.4 %collective-permute-done.2 = bf16[1024,256]{1,0:T(8,128)(2,1)S(1)} collective-permute-done((bf16[1024,256]{1,0:T(8,128)(2,1)S(1)}, bf16[1024,256]{1,0:T(8,128)(2,1)S(1)}, u32[]{:S(2)}, u32[]{:S(2)}) %collective-permute-start.2) | collective-permute-done | bytes 524320 | tf_op jit(solution)/shard_map/ppermute | solution.py:15
  23.3 1.8 %collective-permute-start.4 = (bf16[256,1024]{1,0:T(8,128)(2,1)S(1)}, bf16[256,1024]{1,0:T(8,128)(2,1)S(1)}, u32[]{:S(2)}, u32[]{:S(2)}) collective-permute-start(bf16[256,1024]{1,0:T(8,128)(2,1)S(1)} %constant_dynamic-slice_fusion), channel_id=1, source_target_pairs={{0,8},{4,12},{8,0},{12,4},{1,9},{5,13},{9,1},{13,5},{2,10},{6,14},... | collective-permute-start | bytes 1572872 | tf_op jit(solution)/shard_map/ppermute | solution.py:15
  25.1 1.5 %collective-permute-start.3 = (bf16[1024,256]{1,0:T(8,128)(2,1)S(1)}, bf16[1024,256]{1,0:T(8,128)(2,1)}, u32[]{:S(2)}, u32[]{:S(2)}) collective-permute-start(bf16[1024,256]{1,0:T(8,128)(2,1)S(1)} %collective-permute-done.2), channel_id=1, source_target_pairs={{0,16},{16,0},{1,17},{17,1},{2,18},{18,2},{3,19},{19,3},{4,20},{20... | collective-permute-start | bytes 1572872 | tf_op jit(solution)/shard_map/ppermute | solution.py:21
  26.6 9.9 %collective-permute-done.4 = bf16[256,1024]{1,0:T(8,128)(2,1)S(1)} collective-permute-done((bf16[256,1024]{1,0:T(8,128)(2,1)S(1)}, bf16[256,1024]{1,0:T(8,128)(2,1)S(1)}, u32[]{:S(2)}, u32[]{:S(2)}) %collective-permute-start.4) | collective-permute-done | bytes 524320 | tf_op jit(solution)/shard_map/ppermute | solution.py:15
  36.5 1.4 %collective-permute-start.5 = (bf16[256,1024]{1,0:T(8,128)(2,1)S(1)}, bf16[256,1024]{1,0:T(8,128)(2,1)}, u32[]{:S(2)}, u32[]{:S(2)}) collective-permute-start(bf16[256,1024]{1,0:T(8,128)(2,1)S(1)} %collective-permute-done.4), channel_id=1, source_target_pairs={{0,16},{16,0},{1,17},{17,1},{2,18},{18,2},{3,19},{19,3},{4,20},{20... | collective-permute-start | bytes 1572872 | tf_op jit(solution)/shard_map/ppermute | solution.py:21
  38.4 1.1 pad_maximum_fusion
  39.5 9.5 %collective-permute-done.5 = bf16[256,1024]{1,0:T(8,128)(2,1)} collective-permute-done((bf16[256,1024]{1,0:T(8,128)(2,1)S(1)}, bf16[256,1024]{1,0:T(8,128)(2,1)}, u32[]{:S(2)}, u32[]{:S(2)}) %collective-permute-start.5) | collective-permute-done | bytes 524320 | tf_op jit(solution)/shard_map/ppermute | solution.py:21
  49.0 1.1 pad_maximum_fusion.1
  50.1 1.1 fusion.111
  51.2 4.7 %fusion.68 = f32[512,1024]{1,0:T(8,128)} fusion(bf16[512,1152]{1,0:T(8,128)(2,1)} %all-gather.2.cloned.1.call-done, bf16[512]{0:T(512)(128)(2,1)S(1)} %get-tuple-element.13, bf16[1,512,1024]{2,1,0:T(8,128)(2,1)} %param.13, bf16[1,1024,512]{2,1,0:T(8,128)(2,1)} %param.12), kind=kOutput, calls=%fused_computation.62 | convolution fusion | flops 1076363264 | bytes 5243904 | tf_op jit(solution)/shard_map/dot_general | solution.py:83
  55.9 5.4 %convolution_add_fusion = f32[512,1024]{1,0:T(8,128)} fusion(f32[512,1024]{1,0:T(8,128)} %fusion.68, bf16[512,1024]{1,0:T(8,128)(2,1)} %collective-permute-done.1, bf16[1024,512]{1,0:T(8,128)(2,1)} %collective-permute-done, bf16[512,1152]{1,0:T(8,128)(2,1)} %all-gather.2.cloned.1.call-done, bf16[512]{0:T(512)(128)(2,1)S(1)} %get-tuple-element.13), kind=kOutput, calls=%fused_computation.2 | convolution fusion | flops 1076887552 | bytes 7341056 | tf_op jit(solution)/shard_map/dot_general | solution.py:83
  61.8 4.0 %fusion.59 = f32[512,1024]{1,0:T(8,128)} fusion(bf16[512,1024]{1,0:T(8,128)(2,1)S(1)} %pad_maximum_fusion.1, bf16[1024,512]{1,0:T(8,128)(2,1)S(1)} %pad_maximum_fusion, bf16[512,1152]{1,0:T(8,128)(2,1)} %all-gather.2.cloned.1.call-done, bf16[512]{0:T(512)(128)(2,1)S(1)} %get-tuple-element.12), kind=kOutput, calls=%fused_computation.59 | convolution fusion | flops 1076363264 | bytes 5243904 | tf_op jit(solution)/shard_map/dot_general | solution.py:83
  65.8 4.6 %fusion.53 = f32[512,1024]{1,0:T(8,128)} fusion(bf16[512,1024]{1,0:T(8,128)(2,1)} %collective-permute-done.7, bf16[1024,512]{1,0:T(8,128)(2,1)} %collective-permute-done.6, bf16[512,1152]{1,0:T(8,128)(2,1)} %all-gather.2.cloned.1.call-done, bf16[512]{0:T(512)(128)(2,1)S(1)} %get-tuple-element.12), kind=kOutput, calls=%fused_computation.57 | convolution fusion | flops 1076363264 | bytes 5243904 | tf_op jit(solution)/shard_map/dot_general | solution.py:83
  70.4 3.5 %add_add_fusion = f32[512,1024]{1,0:T(8,128)S(1)} fusion(f32[512,1024]{1,0:T(8,128)} %convolution_add_fusion, f32[512,1024]{1,0:T(8,128)} %fusion.59, f32[512,1024]{1,0:T(8,128)} %fusion.53), kind=kLoop, calls=%fused_computation.1 | loop fusion | flops 1048576 | bytes 8388608 | tf_op jit(solution)/shard_map/add | solution.py:93
  74.8 3.6 %collective-permute-start.10 = (bf16[128,1024]{1,0:T(8,128)(2,1)}, bf16[128,1024]{1,0:T(8,128)(2,1)S(1)}, u32[]{:S(2)}, u32[]{:S(2)}) collective-permute-start(bf16[128,1024]{1,0:T(8,128)(2,1)} %get-tuple-element.15), channel_id=1, source_target_pairs={{0,3},{1,0},{2,1},{3,2},{4,7},{5,4},{6,5},{7,6},{8,11},{9,8},{10,9... | collective-permute-start | bytes 786440 | tf_op jit(solution)/shard_map/ppermute | solution.py:99
  78.4 1.0 collective-permute-start.8
  79.4 6.1 %collective-permute-done.10 = bf16[128,1024]{1,0:T(8,128)(2,1)S(1)} collective-permute-done((bf16[128,1024]{1,0:T(8,128)(2,1)}, bf16[128,1024]{1,0:T(8,128)(2,1)S(1)}, u32[]{:S(2)}, u32[]{:S(2)}) %collective-permute-start.10) | collective-permute-done | bytes 262176 | tf_op jit(solution)/shard_map/ppermute | solution.py:99
  85.5 15.7 %collective-permute-done.9 = bf16[128,1024]{1,0:T(8,128)(2,1)} collective-permute-done((bf16[128,1024]{1,0:T(8,128)(2,1)S(1)}, bf16[128,1024]{1,0:T(8,128)(2,1)}, u32[]{:S(2)}, u32[]{:S(2)}) %collective-permute-start.9) | collective-permute-done | bytes 262176 | tf_op jit(solution)/shard_map/ppermute | solution.py:99
  101.2 1.3 %convolution_convert_fusion.1 = bf16[128,1024]{1,0:T(8,128)(2,1)S(1)} fusion(bf16[128,1024]{1,0:T(8,128)(2,1)S(1)} %copy-done.2, bf16[128,1024]{1,0:T(8,128)(2,1)S(1)} %collective-permute-done.10, bf16[128,1024]{1,0:T(8,128)(2,1)} %collective-permute-done.9, bf16[128,1024]{1,0:T(8,128)(2,1)} %collective-permute-done.8, f32[4,128,1024]{2,1,0:T(8,128)S(1)} %bitcast.41, ...), kind=kOutput, calls=%fused_computation.8 | convolution fusion | flops 34881536 | bytes 1835524 | tf_op jit(solution)/shard_map/dot_general | solution.py:113
  102.6 15.0 %all_to_all.5 = bf16[16,8,1152]{2,1,0:T(8,128)(2,1)S(1)} all-to-all(bf16[16,8,1152]{2,1,0:T(8,128)(2,1)S(1)} %maximum_bitcast_fusion), channel_id=1, replica_groups=mesh['rep'=2,'member'=4,'tp'=4] {'member','tp'}, dimensions={0} | all-to-all | bytes 589824 | tf_op jit(solution)/shard_map/all_to_all | solution.py:120
  118.1 0.9 fusion
  (49 shorter events, 6.8 us)
Async XLA Ops:
  7.2 110.9 %copy-start = (bf16[1024,128]{1,0:T(8,128)(2,1)S(1)}, bf16[1024,128]{1,0:T(8,128)(2,1)}, u32[]{:S(2)}) copy-start(bf16[1024,128]{1,0:T(8,128)(2,1)} %param.15) | copy-start | bytes 786436
  7.2 7.8 %copy-start.1 = (f32[2,1024]{1,0:T(2,128)S(1)}, f32[2,1024]{1,0:T(2,128)}, u32[]{:S(2)}) copy-start(f32[2,1024]{1,0:T(2,128)} %param.11) | copy-start | bytes 24580
  7.2 42.9 %all-gather.2.cloned.1.call-start = ((), (), s32[]{:S(2)}) async-start(), calls=%async_computation.1 | async-start | bytes 1474560 | tf_op jit(solution)/shard_map/all_gather | solution.py:72
  8.3 15.0 %collective-permute-start.2 = (bf16[1024,256]{1,0:T(8,128)(2,1)S(1)}, bf16[1024,256]{1,0:T(8,128)(2,1)S(1)}, u32[]{:S(2)}, u32[]{:S(2)}) collective-permute-start(bf16[1024,256]{1,0:T(8,128)(2,1)S(1)} %dynamic-slice_bitcast_fusion), channel_id=1, source_target_pairs={{0,8},{4,12},{8,0},{12,4},{1,9},{5,13},{9,1},{13,5},{2,10},{6,14},... | collective-permute-start | bytes 1572872 | tf_op jit(solution)/shard_map/ppermute | solution.py:15
  15.0 0.8 copy-start.4
  15.0 1.0 copy-start.2
  15.8 7.4 %copy-start.3 = (bf16[1,512,1024]{2,1,0:T(8,128)(2,1)S(1)}, bf16[1,512,1024]{2,1,0:T(8,128)(2,1)}, u32[]{:S(2)}) copy-start(bf16[1,512,1024]{2,1,0:T(8,128)(2,1)} %param.13) | copy-start | bytes 3145732
  23.3 13.2 %collective-permute-start.4 = (bf16[256,1024]{1,0:T(8,128)(2,1)S(1)}, bf16[256,1024]{1,0:T(8,128)(2,1)S(1)}, u32[]{:S(2)}, u32[]{:S(2)}) collective-permute-start(bf16[256,1024]{1,0:T(8,128)(2,1)S(1)} %constant_dynamic-slice_fusion), channel_id=1, source_target_pairs={{0,8},{4,12},{8,0},{12,4},{1,9},{5,13},{9,1},{13,5},{2,10},{6,14},... | collective-permute-start | bytes 1572872 | tf_op jit(solution)/shard_map/ppermute | solution.py:15
  25.1 13.3 %collective-permute-start.3 = (bf16[1024,256]{1,0:T(8,128)(2,1)S(1)}, bf16[1024,256]{1,0:T(8,128)(2,1)}, u32[]{:S(2)}, u32[]{:S(2)}) collective-permute-start(bf16[1024,256]{1,0:T(8,128)(2,1)S(1)} %collective-permute-done.2), channel_id=1, source_target_pairs={{0,16},{16,0},{1,17},{17,1},{2,18},{18,2},{3,19},{19,3},{4,20},{20... | collective-permute-start | bytes 1572872 | tf_op jit(solution)/shard_map/ppermute | solution.py:21
  36.5 12.5 %collective-permute-start.5 = (bf16[256,1024]{1,0:T(8,128)(2,1)S(1)}, bf16[256,1024]{1,0:T(8,128)(2,1)}, u32[]{:S(2)}, u32[]{:S(2)}) collective-permute-start(bf16[256,1024]{1,0:T(8,128)(2,1)S(1)} %collective-permute-done.4), channel_id=1, source_target_pairs={{0,16},{16,0},{1,17},{17,1},{2,18},{18,2},{3,19},{19,3},{4,20},{20... | collective-permute-start | bytes 1572872 | tf_op jit(solution)/shard_map/ppermute | solution.py:21
  37.9 18.0 %collective-permute-start.1 = (bf16[512,1024]{1,0:T(8,128)(2,1)}, bf16[512,1024]{1,0:T(8,128)(2,1)}, u32[]{:S(2)}, u32[]{:S(2)}) collective-permute-start(bf16[512,1024]{1,0:T(8,128)(2,1)} %bitcast.44), channel_id=1, source_target_pairs={{0,4},{4,0},{8,12},{12,8},{1,5},{5,1},{9,13},{13,9},{2,6},{6,2},{1... | collective-permute-start | bytes 3145736 | tf_op jit(solution)/shard_map/ppermute | solution.py:10
  37.9 18.0 %collective-permute-start = (bf16[1024,512]{1,0:T(8,128)(2,1)}, bf16[1024,512]{1,0:T(8,128)(2,1)}, u32[]{:S(2)}, u32[]{:S(2)}) collective-permute-start(bf16[1024,512]{1,0:T(8,128)(2,1)} %bitcast.46), channel_id=1, source_target_pairs={{0,4},{4,0},{8,12},{12,8},{1,5},{5,1},{9,13},{13,9},{2,6},{6,2},{1... | collective-permute-start | bytes 3145736 | tf_op jit(solution)/shard_map/ppermute | solution.py:10
  61.2 4.6 %collective-permute-start.7 = (bf16[512,1024]{1,0:T(8,128)(2,1)S(1)}, bf16[512,1024]{1,0:T(8,128)(2,1)}, u32[]{:S(2)}, u32[]{:S(2)}) collective-permute-start(bf16[512,1024]{1,0:T(8,128)(2,1)S(1)} %pad_maximum_fusion.1), channel_id=1, source_target_pairs={{0,4},{4,0},{8,12},{12,8},{1,5},{5,1},{9,13},{13,9},{2,6},{6,2},{1... | collective-permute-start | bytes 3145736 | tf_op jit(solution)/shard_map/ppermute | solution.py:10
  61.2 4.6 %collective-permute-start.6 = (bf16[1024,512]{1,0:T(8,128)(2,1)S(1)}, bf16[1024,512]{1,0:T(8,128)(2,1)}, u32[]{:S(2)}, u32[]{:S(2)}) collective-permute-start(bf16[1024,512]{1,0:T(8,128)(2,1)S(1)} %pad_maximum_fusion), channel_id=1, source_target_pairs={{0,4},{4,0},{8,12},{12,8},{1,5},{5,1},{9,13},{13,9},{2,6},{6,2},{1... | collective-permute-start | bytes 3145736 | tf_op jit(solution)/shard_map/ppermute | solution.py:10
  74.8 43.2 %copy-start.5 = (f32[1024]{0:T(1024)S(1)}, f32[1024]{0:T(1024)}, u32[]{:S(2)}) copy-start(f32[1024]{0:T(1024)} %param.14) | copy-start | bytes 12292
  74.8 10.7 %collective-permute-start.10 = (bf16[128,1024]{1,0:T(8,128)(2,1)}, bf16[128,1024]{1,0:T(8,128)(2,1)S(1)}, u32[]{:S(2)}, u32[]{:S(2)}) collective-permute-start(bf16[128,1024]{1,0:T(8,128)(2,1)} %get-tuple-element.15), channel_id=1, source_target_pairs={{0,3},{1,0},{2,1},{3,2},{4,7},{5,4},{6,5},{7,6},{8,11},{9,8},{10,9... | collective-permute-start | bytes 786440 | tf_op jit(solution)/shard_map/ppermute | solution.py:99
  78.4 22.8 %collective-permute-start.9 = (bf16[128,1024]{1,0:T(8,128)(2,1)S(1)}, bf16[128,1024]{1,0:T(8,128)(2,1)}, u32[]{:S(2)}, u32[]{:S(2)}) collective-permute-start(bf16[128,1024]{1,0:T(8,128)(2,1)S(1)} %get-tuple-element.16), channel_id=1, source_target_pairs={{0,2},{1,3},{2,0},{3,1},{4,6},{5,7},{6,4},{7,5},{8,10},{9,11},{10,... | collective-permute-start | bytes 786440 | tf_op jit(solution)/shard_map/ppermute | solution.py:99
  78.4 22.8 %collective-permute-start.8 = (bf16[128,1024]{1,0:T(8,128)(2,1)S(1)}, bf16[128,1024]{1,0:T(8,128)(2,1)}, u32[]{:S(2)}, u32[]{:S(2)}) collective-permute-start(bf16[128,1024]{1,0:T(8,128)(2,1)S(1)} %get-tuple-element.14), channel_id=1, source_target_pairs={{0,1},{1,2},{2,3},{3,0},{4,5},{5,6},{6,7},{7,4},{8,9},{9,10},{10,1... | collective-permute-start | bytes 786440 | tf_op jit(solution)/shard_map/ppermute | solution.py:99
  118.0 1.0 copy-start.6
Sparse Core Ops, SparseCore 0:
  17.0 30.7 all-gather.1

commit v12 on v11

--- a/solution.py
+++ b/solution.py
@@ -75,22 +75,16 @@
     gathered_rows = gathered[:, :feature_width]
     gathered_member = gathered[:, feature_width].astype(jnp.int32)
 
-    def apply_block(block_member, up_here, down_here):
+    ups, downs, keeps = [], [], []
+    for block_member, up_here, down_here in [own_block] + fetched:
         keep = (gathered_member == block_member).astype(jnp.bfloat16)[:, None]
-        hidden = jax.nn.gelu(
-            jnp.dot(gathered_rows, up_here, preferred_element_type=jnp.float32)
-        ).astype(jnp.bfloat16) * keep
-        return jnp.dot(hidden, down_here, preferred_element_type=jnp.float32)
-
-    def apply_pair(block_member, up_here, down_here):
-        return apply_block(block_member, up_here, down_here) + apply_block(
-            block_member, from_partner(up_here, "member", 0), from_partner(down_here, "member", 0)
-        )
-
-    partial = apply_pair(*own_block)
-    for block_member, up_here, down_here in fetched:
-        partial, up_here, down_here = lax.optimization_barrier((partial, up_here, down_here))
-        partial = partial + apply_pair(block_member, up_here, down_here)
+        ups += [up_here, from_partner(up_here, "member", 0)]
+        downs += [down_here, from_partner(down_here, "member", 0)]
+        keeps += [jnp.broadcast_to(keep, (keep.shape[0], 2 * up_here.shape[1]))]
+    hidden = jax.nn.gelu(
+        jnp.dot(gathered_rows, jnp.concatenate(ups, axis=1), preferred_element_type=jnp.float32)
+    ).astype(jnp.bfloat16) * jnp.concatenate(keeps, axis=1)
+    partial = jnp.dot(hidden, jnp.concatenate(downs, axis=0), preferred_element_type=jnp.float32)
     tp_here = lax.axis_index("tp")
     by_target = partial.reshape(n_tp, rows_here, feature_width)
     change = lax.dynamic_index_in_dim(by_target, tp_here, 0, keepdims=False)

time: 126 us -> 135 us (1.071)
  local copies, waits for them, and re-layouts: 2.8 us -> 24 us
  matrix products: 21.3 us -> 12.3 us
  waiting for transfers between devices: 47.5 us -> 45.9 us
    unnamed x14 -> x32, local copies, waits for them, and re-layouts: 0.06 us -> 14 us
    dot_general x4 -> x1, matrix products: 18.7 us -> 9.73 us  [local(): jnp.dot(hidden, jnp.concatenate(downs, axis=0), preferred_element_type=jn...]
    concatenate x0 -> x2, local copies, waits for them, and re-layouts: none -> 4.6 us  [the longest x1 2.32 us: local(): jnp.concatenate(ups, axis=1)]
    add x1 -> x0, other arithmetic: 3.53 us -> none  [local(): partial = partial + apply_pair(block_member, up_here, down_here)]
    ppermute x2, waiting for transfers between devices: 9.46 us -> 7.17 us  [swap_parts(): lax.ppermute(value, 'rep', [(i, (i + step) % n_rep) for i in range(n_rep)])]
  transfers between devices with their start and end apart: 12 -> 12, of which waited for: 5 -> 5; matrix products, arithmetic and copies ran while one was open for 14% -> 20% of each run, Pallas kernels for 0% -> 0%
where the time goes in v12:
time: 135 us
  waiting for transfers between devices  45.9 us (34%)
  local copies, waits for them, and re-layouts  24 us (18%)
  blocking collectives  15.2 us (11%)
  between operations  14.3 us (11%)
  starting transfers between devices  12.9 us (10%)
  matrix products  12.3 us (9%)
  other arithmetic  10.3 us (8%)
    ppermute x3, waiting for transfers between devices, local(): lax.ppermute(outgoing.astype(PARTIAL_DTYPE), 'tp', [(i, (i + shift) % n_t...  22 us
    ppermute x2, waiting for transfers between devices, from_chip_behind(): lax.ppermute(value, axis, [(i, (i + 2 * chips_back) % size) for i in rang...  16.7 us
    all_to_all x1, blocking collectives, local(): lax.all_to_all(jnp.concatenate([packed, spot_lanes], axis=1).reshape(n_de...  15.2 us
    unnamed x32, local copies, waits for them, and re-layouts  14 us
    dot_general x1, matrix products, local(): jnp.dot(hidden, jnp.concatenate(downs, axis=0), preferred_element_type=jn...  9.73 us
    ppermute x2, waiting for transfers between devices, swap_parts(): lax.ppermute(value, 'rep', [(i, (i + step) % n_rep) for i in range(n_rep)])  7.17 us
    ppermute x2, starting transfers between devices, from_chip_behind(): lax.ppermute(value, axis, [(i, (i + 2 * chips_back) % size) for i in rang...  4.71 us
    ppermute x3, starting transfers between devices, local(): lax.ppermute(outgoing.astype(PARTIAL_DTYPE), 'tp', [(i, (i + shift) % n_t...  4.66 us
  transfers between devices with their start and end apart: 12, of which 5 were waited for; matrix products, arithmetic and copies ran while one was open for 20% of the time, Pallas kernels for 0%

profile of v12, /device:TPU:0, one launch (start us, length us, event | category | flops | bytes accessed | tf_op | source)
XLA Modules:
  0.0 134.8 jit_solution(10302358856912758778)
XLA Ops:
  7.3 2.0 %dynamic-slice_bitcast_fusion = bf16[1024,256]{1,0:T(8,128)(2,1)} fusion(bf16[1,1024,512]{2,1,0:T(8,128)(2,1)} %param.12, s32[]{:T(128)S(6)} %select_n.72), kind=kLoop, calls=%fused_computation.38 | loop fusion | bytes 1048580 | tf_op jit(solution)/shard_map/dynamic_slice | solution.py:31
  9.3 3.0 %collective-permute-start.1 = (bf16[1024,256]{1,0:T(8,128)(2,1)}, bf16[1024,256]{1,0:T(8,128)(2,1)S(1)}, u32[]{:S(2)}, u32[]{:S(2)}) collective-permute-start(bf16[1024,256]{1,0:T(8,128)(2,1)} %dynamic-slice_bitcast_fusion), channel_id=1, source_target_pairs={{0,8},{4,12},{8,0},{12,4},{1,9},{5,13},{9,1},{13,5},{2,10},{6,14},... | collective-permute-start | bytes 1572872 | tf_op jit(solution)/shard_map/ppermute | solution.py:15
  16.9 7.5 %collective-permute-done.1 = bf16[1024,256]{1,0:T(8,128)(2,1)S(1)} collective-permute-done((bf16[1024,256]{1,0:T(8,128)(2,1)}, bf16[1024,256]{1,0:T(8,128)(2,1)S(1)}, u32[]{:S(2)}, u32[]{:S(2)}) %collective-permute-start.1) | collective-permute-done | bytes 524320 | tf_op jit(solution)/shard_map/ppermute | solution.py:15
  26.0 1.7 %collective-permute-start.5 = (bf16[256,1024]{1,0:T(8,128)(2,1)}, bf16[256,1024]{1,0:T(8,128)(2,1)}, u32[]{:S(2)}, u32[]{:S(2)}) collective-permute-start(bf16[256,1024]{1,0:T(8,128)(2,1)} %constant_dynamic-slice_fusion), channel_id=1, source_target_pairs={{0,8},{4,12},{8,0},{12,4},{1,9},{5,13},{9,1},{13,5},{2,10},{6,14},... | collective-permute-start | bytes 1572872 | tf_op jit(solution)/shard_map/ppermute | solution.py:15
  27.9 1.6 %collective-permute-start.2 = (bf16[1024,256]{1,0:T(8,128)(2,1)}, bf16[1024,256]{1,0:T(8,128)(2,1)}, u32[]{:S(2)}, u32[]{:S(2)}) collective-permute-start(bf16[1024,256]{1,0:T(8,128)(2,1)} %copy-done.5), channel_id=1, source_target_pairs={{0,16},{16,0},{1,17},{17,1},{2,18},{18,2},{3,19},{19,3},{4,20},{20... | collective-permute-start | bytes 1572872 | tf_op jit(solution)/shard_map/ppermute | solution.py:21
  30.3 9.2 %collective-permute-done.5 = bf16[256,1024]{1,0:T(8,128)(2,1)} collective-permute-done((bf16[256,1024]{1,0:T(8,128)(2,1)}, bf16[256,1024]{1,0:T(8,128)(2,1)}, u32[]{:S(2)}, u32[]{:S(2)}) %collective-permute-start.5) | collective-permute-done | bytes 524320 | tf_op jit(solution)/shard_map/ppermute | solution.py:15
  39.5 1.4 %collective-permute-start.6 = (bf16[256,1024]{1,0:T(8,128)(2,1)}, bf16[256,1024]{1,0:T(8,128)(2,1)S(1)}, u32[]{:S(2)}, u32[]{:S(2)}) collective-permute-start(bf16[256,1024]{1,0:T(8,128)(2,1)} %collective-permute-done.5), channel_id=1, source_target_pairs={{0,16},{16,0},{1,17},{17,1},{2,18},{18,2},{3,19},{19,3},{4,20},{20... | collective-permute-start | bytes 1572872 | tf_op jit(solution)/shard_map/ppermute | solution.py:21
  41.9 2.4 %pad_maximum_fusion = bf16[1024,512]{1,0:T(8,128)(2,1)} fusion(bf16[1024,256]{1,0:T(8,128)(2,1)} %collective-permute-done.2, bf16[1024,256]{1,0:T(8,128)(2,1)} %copy-done.5), kind=kLoop, calls=%fused_computation.18 | loop fusion | flops 2097152 | bytes 2097152 | tf_op jit(solution)/shard_map/concatenate | solution.py:38
  44.8 7.2 %collective-permute-done.6 = bf16[256,1024]{1,0:T(8,128)(2,1)S(1)} collective-permute-done((bf16[256,1024]{1,0:T(8,128)(2,1)}, bf16[256,1024]{1,0:T(8,128)(2,1)S(1)}, u32[]{:S(2)}, u32[]{:S(2)}) %collective-permute-start.6) | collective-permute-done | bytes 524320 | tf_op jit(solution)/shard_map/ppermute | solution.py:21
  52.7 2.1 %pad_maximum_fusion.1 = bf16[512,1024]{1,0:T(8,128)(2,1)} fusion(bf16[256,1024]{1,0:T(8,128)(2,1)S(1)} %collective-permute-done.6, bf16[256,1024]{1,0:T(8,128)(2,1)} %collective-permute-done.5), kind=kLoop, calls=%fused_computation.19 | loop fusion | flops 2097152 | bytes 2097152 | tf_op jit(solution)/shard_map/concatenate | solution.py:38
  54.8 1.1 constant_dynamic-update-slice_fusion.4
  55.9 2.4 %constant_dynamic-update-slice_fusion.3 = bf16[1024,2048]{1,0:T(8,128)(2,1)} fusion(bf16[1024,2048]{1,0:T(8,128)(2,1)} %constant_dynamic-update-slice_fusion.4, bf16[1024,512]{1,0:T(8,128)(2,1)} %collective-permute-done), kind=kLoop, calls=%fused_computation.67 | loop fusion | bytes 2097152
  59.2 2.3 %constant_dynamic-update-slice_fusion.8 = bf16[2048,1024]{1,0:T(8,128)(2,1)} fusion(bf16[2048,1024]{1,0:T(8,128)(2,1)} %constant_dynamic-update-slice_fusion.9, bf16[512,1024]{1,0:T(8,128)(2,1)} %collective-permute-done.4), kind=kLoop, calls=%fused_computation.72 | loop fusion | bytes 2097152
  61.5 1.9 %constant_dynamic-update-slice_fusion.7 = bf16[2048,1024]{1,0:T(8,128)(2,1)} fusion(bf16[2048,1024]{1,0:T(8,128)(2,1)} %constant_dynamic-update-slice_fusion.8, bf16[256,1024]{1,0:T(8,128)(2,1)} %collective-permute-done.5), kind=kLoop, calls=%fused_computation.71 | loop fusion | bytes 1048576
  63.4 1.9 %constant_dynamic-update-slice_fusion.1 = bf16[1024,2048]{1,0:T(8,128)(2,1)} fusion(bf16[1024,2048]{1,0:T(8,128)(2,1)} %constant_dynamic-update-slice_fusion.2, bf16[1024,256]{1,0:T(8,128)(2,1)} %collective-permute-done.2), kind=kLoop, calls=%fused_computation.65 | loop fusion | bytes 1048576
  67.3 2.3 %constant_dynamic-update-slice_fusion = bf16[1024,2048]{1,0:T(8,128)(2,1)} fusion(bf16[1024,2048]{1,0:T(8,128)(2,1)} %constant_dynamic-update-slice_fusion.1, bf16[1024,512]{1,0:T(8,128)(2,1)} %collective-permute-done.3), kind=kLoop, calls=%fused_computation.64 | loop fusion | bytes 2097152 | tf_op jit(solution)/shard_map/concatenate | solution.py:85
  69.6 2.3 %constant_dynamic-update-slice_fusion.5 = bf16[2048,1024]{1,0:T(8,128)(2,1)} fusion(bf16[2048,1024]{1,0:T(8,128)(2,1)} %constant_dynamic-update-slice_fusion.6, bf16[512,1024]{1,0:T(8,128)(2,1)} %collective-permute-done.7), kind=kLoop, calls=%fused_computation.69 | loop fusion | bytes 2097152 | tf_op jit(solution)/shard_map/concatenate | solution.py:87
  72.2 9.7 %fusion.9 = f32[512,1024]{1,0:T(8,128)} fusion(bf16[2048,1024]{1,0:T(8,128)(2,1)} %constant_dynamic-update-slice_fusion.5, bf16[512,1024]{1,0:T(8,128)(2,1)S(1)} %broadcast_in_dim.89, bf16[512,1024]{1,0:T(8,128)(2,1)S(1)} %broadcast_in_dim.86, bf16[1024,2048]{1,0:T(8,128)(2,1)} %constant_dynamic-update-slice_fusion, ...), kind=kOutput, calls=%fused_computation.11 | convolution fusion | flops 4310695936 | bytes 13631488 | tf_op jit(solution)/shard_map/dot_general | solution.py:87
  81.9 1.5 %fusion.27 = (bf16[128,1024]{1,0:T(8,128)(2,1)S(1)}, bf16[128,1024]{1,0:T(8,128)(2,1)S(1)}, bf16[128,1024]{1,0:T(8,128)(2,1)S(1)}) fusion(f32[4,128,1024]{2,1,0:T(8,128)} %bitcast.36, s32[]{:T(128)S(6)} %select_n.77, s32[]{:T(128)S(6)} %select_n.81, s32[]{:T(128)S(6)} %select_n.79), kind=kLoop, calls=%fused_computation.43 | loop fusion | bytes 1572876 | tf_op jit(solution)/shard_map/convert_element_type | solution.py:94
  83.4 3.6 %collective-permute-start.10 = (bf16[128,1024]{1,0:T(8,128)(2,1)S(1)}, bf16[128,1024]{1,0:T(8,128)(2,1)S(1)}, u32[]{:S(2)}, u32[]{:S(2)}) collective-permute-start(bf16[128,1024]{1,0:T(8,128)(2,1)S(1)} %get-tuple-element.9), channel_id=1, source_target_pairs={{0,3},{1,0},{2,1},{3,2},{4,7},{5,4},{6,5},{7,6},{8,11},{9,8},{10,9... | collective-permute-start | bytes 786440 | tf_op jit(solution)/shard_map/ppermute | solution.py:93
  88.1 5.7 %collective-permute-done.10 = bf16[128,1024]{1,0:T(8,128)(2,1)S(1)} collective-permute-done((bf16[128,1024]{1,0:T(8,128)(2,1)S(1)}, bf16[128,1024]{1,0:T(8,128)(2,1)S(1)}, u32[]{:S(2)}, u32[]{:S(2)}) %collective-permute-start.10) | collective-permute-done | bytes 262176 | tf_op jit(solution)/shard_map/ppermute | solution.py:93
  93.7 16.3 %collective-permute-done.9 = bf16[128,1024]{1,0:T(8,128)(2,1)S(1)} collective-permute-done((bf16[128,1024]{1,0:T(8,128)(2,1)S(1)}, bf16[128,1024]{1,0:T(8,128)(2,1)S(1)}, u32[]{:S(2)}, u32[]{:S(2)}) %collective-permute-start.9) | collective-permute-done | bytes 262176 | tf_op jit(solution)/shard_map/ppermute | solution.py:93
  110.0 1.4 %convolution_convert_fusion.1 = bf16[128,1024]{1,0:T(8,128)(2,1)S(1)} fusion(bf16[128,1024]{1,0:T(8,128)(2,1)S(1)} %copy-done.2, bf16[128,1024]{1,0:T(8,128)(2,1)S(1)} %collective-permute-done.10, bf16[128,1024]{1,0:T(8,128)(2,1)S(1)} %collective-permute-done.9, bf16[128,1024]{1,0:T(8,128)(2,1)S(1)} %collective-permute-done.8, ...), kind=kOutput, calls=%fused_computation.13 | convolution fusion | flops 34881536 | bytes 1835524 | tf_op jit(solution)/shard_map/dot_general | solution.py:107
  111.4 15.2 %all_to_all.5 = bf16[16,8,1152]{2,1,0:T(8,128)(2,1)S(1)} all-to-all(bf16[16,8,1152]{2,1,0:T(8,128)(2,1)S(1)} %maximum_bitcast_fusion), channel_id=1, replica_groups=mesh['rep'=2,'member'=4,'tp'=4] {'member','tp'}, dimensions={0} | all-to-all | bytes 589824 | tf_op jit(solution)/shard_map/all_to_all | solution.py:114
  (67 shorter events, 14.9 us)
Async XLA Ops:
  7.2 119.9 %copy-start = (bf16[1024,128]{1,0:T(8,128)(2,1)S(1)}, bf16[1024,128]{1,0:T(8,128)(2,1)}, u32[]{:S(2)}) copy-start(bf16[1024,128]{1,0:T(8,128)(2,1)} %param.15) | copy-start | bytes 786436
  7.2 9.6 %copy-start.9 = (s32[128,1]{0,1:T(1,128)S(1)}, s32[128,1]{0,1:T(1,128)}, u32[]{:S(2)}) copy-start(s32[128,1]{0,1:T(1,128)} %param.9) | copy-start | bytes 1540
  7.2 20.6 %copy-start.2 = (bf16[128,1024]{1,0:T(8,128)(2,1)S(1)}, bf16[128,1024]{1,0:T(8,128)(2,1)}, u32[]{:S(2)}) copy-start(bf16[128,1024]{1,0:T(8,128)(2,1)} %param.8) | copy-start | bytes 786436
  7.2 8.7 %copy-start.1 = (f32[2,1024]{1,0:T(2,128)S(1)}, f32[2,1024]{1,0:T(2,128)}, u32[]{:S(2)}) copy-start(f32[2,1024]{1,0:T(2,128)} %param.11) | copy-start | bytes 24580
  7.2 18.0 %copy-start.4 = (bf16[1,512,1024]{2,1,0:T(8,128)(2,1)S(1)}, bf16[1,512,1024]{2,1,0:T(8,128)(2,1)}, u32[]{:S(2)}) copy-start(bf16[1,512,1024]{2,1,0:T(8,128)(2,1)} %param.13) | copy-start | bytes 3145732
  7.2 59.0 %all-gather.2.cloned.1.call-start = ((), (), s32[]{:S(2)}) async-start(), calls=%async_computation.1 | async-start | bytes 1474560 | tf_op jit(solution)/shard_map/all_gather | solution.py:72
  9.3 15.1 %collective-permute-start.1 = (bf16[1024,256]{1,0:T(8,128)(2,1)}, bf16[1024,256]{1,0:T(8,128)(2,1)S(1)}, u32[]{:S(2)}, u32[]{:S(2)}) collective-permute-start(bf16[1024,256]{1,0:T(8,128)(2,1)} %dynamic-slice_bitcast_fusion), channel_id=1, source_target_pairs={{0,8},{4,12},{8,0},{12,4},{1,9},{5,13},{9,1},{13,5},{2,10},{6,14},... | collective-permute-start | bytes 1572872 | tf_op jit(solution)/shard_map/ppermute | solution.py:15
  12.3 43.7 %collective-permute-start = (bf16[1024,512]{1,0:T(8,128)(2,1)}, bf16[1024,512]{1,0:T(8,128)(2,1)}, u32[]{:S(2)}, u32[]{:S(2)}) collective-permute-start(bf16[1024,512]{1,0:T(8,128)(2,1)} %bitcast.33), channel_id=1, source_target_pairs={{0,4},{4,0},{8,12},{12,8},{1,5},{5,1},{9,13},{13,9},{2,6},{6,2},{1... | collective-permute-start | bytes 3145736 | tf_op jit(solution)/shard_map/ppermute | solution.py:10
  24.4 0.8 copy-start.5
  26.0 28.8 %copy-start.3 = (bf16[1,1024,512]{2,1,0:T(8,128)(2,1)S(1)}, bf16[1,1024,512]{2,1,0:T(8,128)(2,1)}, u32[]{:S(2)}) copy-start(bf16[1,1024,512]{2,1,0:T(8,128)(2,1)} %param.12) | copy-start | bytes 3145732
  26.0 13.4 %collective-permute-start.5 = (bf16[256,1024]{1,0:T(8,128)(2,1)}, bf16[256,1024]{1,0:T(8,128)(2,1)}, u32[]{:S(2)}, u32[]{:S(2)}) collective-permute-start(bf16[256,1024]{1,0:T(8,128)(2,1)} %constant_dynamic-slice_fusion), channel_id=1, source_target_pairs={{0,8},{4,12},{8,0},{12,4},{1,9},{5,13},{9,1},{13,5},{2,10},{6,14},... | collective-permute-start | bytes 1572872 | tf_op jit(solution)/shard_map/ppermute | solution.py:15
  27.9 14.0 %collective-permute-start.2 = (bf16[1024,256]{1,0:T(8,128)(2,1)}, bf16[1024,256]{1,0:T(8,128)(2,1)}, u32[]{:S(2)}, u32[]{:S(2)}) collective-permute-start(bf16[1024,256]{1,0:T(8,128)(2,1)} %copy-done.5), channel_id=1, source_target_pairs={{0,16},{16,0},{1,17},{17,1},{2,18},{18,2},{3,19},{19,3},{4,20},{20... | collective-permute-start | bytes 1572872 | tf_op jit(solution)/shard_map/ppermute | solution.py:21
  39.5 12.5 %collective-permute-start.6 = (bf16[256,1024]{1,0:T(8,128)(2,1)}, bf16[256,1024]{1,0:T(8,128)(2,1)S(1)}, u32[]{:S(2)}, u32[]{:S(2)}) collective-permute-start(bf16[256,1024]{1,0:T(8,128)(2,1)} %collective-permute-done.5), channel_id=1, source_target_pairs={{0,16},{16,0},{1,17},{17,1},{2,18},{18,2},{3,19},{19,3},{4,20},{20... | collective-permute-start | bytes 1572872 | tf_op jit(solution)/shard_map/ppermute | solution.py:21
  40.8 18.4 %collective-permute-start.4 = (bf16[512,1024]{1,0:T(8,128)(2,1)S(1)}, bf16[512,1024]{1,0:T(8,128)(2,1)}, u32[]{:S(2)}, u32[]{:S(2)}) collective-permute-start(bf16[512,1024]{1,0:T(8,128)(2,1)S(1)} %bitcast.35), channel_id=1, source_target_pairs={{0,4},{4,0},{8,12},{12,8},{1,5},{5,1},{9,13},{13,9},{2,6},{6,2},{1... | collective-permute-start | bytes 3145736 | tf_op jit(solution)/shard_map/ppermute | solution.py:10
  41.9 16.4 %copy-start.6 = (bf16[1024,256]{1,0:T(8,128)(2,1)S(1)}, bf16[1024,256]{1,0:T(8,128)(2,1)}, u32[]{:S(2)}) copy-start(bf16[1024,256]{1,0:T(8,128)(2,1)} %copy-done.5) | copy-start | bytes 1572868
  44.3 23.0 %collective-permute-start.3 = (bf16[1024,512]{1,0:T(8,128)(2,1)}, bf16[1024,512]{1,0:T(8,128)(2,1)}, u32[]{:S(2)}, u32[]{:S(2)}) collective-permute-start(bf16[1024,512]{1,0:T(8,128)(2,1)} %pad_maximum_fusion), channel_id=1, source_target_pairs={{0,4},{4,0},{8,12},{12,8},{1,5},{5,1},{9,13},{13,9},{2,6},{6,2},{1... | collective-permute-start | bytes 3145736 | tf_op jit(solution)/shard_map/ppermute | solution.py:10
  51.9 0.8 copy-start.7
  54.8 14.8 %collective-permute-start.7 = (bf16[512,1024]{1,0:T(8,128)(2,1)}, bf16[512,1024]{1,0:T(8,128)(2,1)}, u32[]{:S(2)}, u32[]{:S(2)}) collective-permute-start(bf16[512,1024]{1,0:T(8,128)(2,1)} %pad_maximum_fusion.1), channel_id=1, source_target_pairs={{0,4},{4,0},{8,12},{12,8},{1,5},{5,1},{9,13},{13,9},{2,6},{6,2},{1... | collective-permute-start | bytes 3145736 | tf_op jit(solution)/shard_map/ppermute | solution.py:10
  55.9 9.4 %copy-start.8 = (bf16[256,1024]{1,0:T(8,128)(2,1)S(1)}, bf16[256,1024]{1,0:T(8,128)(2,1)}, u32[]{:S(2)}) copy-start(bf16[256,1024]{1,0:T(8,128)(2,1)} %copy-done.7) | copy-start | bytes 1572868
  81.9 45.2 %copy-start.10 = (f32[1024]{0:T(1024)S(1)}, f32[1024]{0:T(1024)}, u32[]{:S(2)}) copy-start(f32[1024]{0:T(1024)} %param.14) | copy-start | bytes 12292
  83.4 10.4 %collective-permute-start.10 = (bf16[128,1024]{1,0:T(8,128)(2,1)S(1)}, bf16[128,1024]{1,0:T(8,128)(2,1)S(1)}, u32[]{:S(2)}, u32[]{:S(2)}) collective-permute-start(bf16[128,1024]{1,0:T(8,128)(2,1)S(1)} %get-tuple-element.9), channel_id=1, source_target_pairs={{0,3},{1,0},{2,1},{3,2},{4,7},{5,4},{6,5},{7,6},{8,11},{9,8},{10,9... | collective-permute-start | bytes 786440 | tf_op jit(solution)/shard_map/ppermute | solution.py:93
  87.0 23.0 %collective-permute-start.9 = (bf16[128,1024]{1,0:T(8,128)(2,1)S(1)}, bf16[128,1024]{1,0:T(8,128)(2,1)S(1)}, u32[]{:S(2)}, u32[]{:S(2)}) collective-permute-start(bf16[128,1024]{1,0:T(8,128)(2,1)S(1)} %get-tuple-element.10), channel_id=1, source_target_pairs={{0,2},{1,3},{2,0},{3,1},{4,6},{5,7},{6,4},{7,5},{8,10},{9,11},{10,... | collective-permute-start | bytes 786440 | tf_op jit(solution)/shard_map/ppermute | solution.py:93
  87.0 23.0 %collective-permute-start.8 = (bf16[128,1024]{1,0:T(8,128)(2,1)S(1)}, bf16[128,1024]{1,0:T(8,128)(2,1)S(1)}, u32[]{:S(2)}, u32[]{:S(2)}) collective-permute-start(bf16[128,1024]{1,0:T(8,128)(2,1)S(1)} %get-tuple-element.8), channel_id=1, source_target_pairs={{0,1},{1,2},{2,3},{3,0},{4,5},{5,6},{6,7},{7,4},{8,9},{9,10},{10,1... | collective-permute-start | bytes 786440 | tf_op jit(solution)/shard_map/ppermute | solution.py:93
  127.0 1.0 copy-start.11
Sparse Core Ops, SparseCore 0:
  30.4 29.8 all-gather.1

commit v13 on v11

--- a/solution.py
+++ b/solution.py
@@ -83,9 +83,9 @@
         return jnp.dot(hidden, down_here, preferred_element_type=jnp.float32)
 
     def apply_pair(block_member, up_here, down_here):
-        return apply_block(block_member, up_here, down_here) + apply_block(
-            block_member, from_partner(up_here, "member", 0), from_partner(down_here, "member", 0)
-        )
+        both_up = jnp.concatenate([up_here, from_partner(up_here, "member", 0)], axis=1)
+        both_down = jnp.concatenate([down_here, from_partner(down_here, "member", 0)], axis=0)
+        return apply_block(block_member, both_up, both_down)
 
     partial = apply_pair(*own_block)
     for block_member, up_here, down_here in fetched:

time: 126 us -> 124 us (0.984)
  matrix products: 21.3 us -> 14.4 us
  waiting for transfers between devices: 47.5 us -> 53.3 us
    dot_general x4 -> x2, matrix products: 18.7 us -> 11.9 us  [apply_block(): return jnp.dot(hidden, down_here, preferred_element_type=jnp.float32)]
    ppermute x4, waiting for transfers between devices: 0.01 us -> 3.79 us  [from_partner(): lax.ppermute(value, axis, [(i, i ^ 1 << distance) for i in range(lax.axis...]
    ppermute x2, waiting for transfers between devices: 9.46 us -> 11.8 us  [swap_parts(): lax.ppermute(value, 'rep', [(i, (i + step) % n_rep) for i in range(n_rep)])]
  transfers between devices with their start and end apart: 12 -> 12, of which waited for: 5 -> 8; matrix products, arithmetic and copies ran while one was open for 14% -> 7% of each run, Pallas kernels for 0% -> 0%
where the time goes in v13:
time: 124 us; the launch traced here: 123 us
  waiting for transfers between devices  53.3 us (43%)
  blocking collectives  14.5 us (12%)
  matrix products  14.4 us (12%)
  between operations  14.3 us (12%)
  starting transfers between devices  13.4 us (11%)
  other arithmetic  10.7 us (9%)
  local copies, waits for them, and re-layouts  2.8 us (2%)
    ppermute x3, waiting for transfers between devices, local(): lax.ppermute(outgoing.astype(PARTIAL_DTYPE), 'tp', [(i, (i + shift) % n_t...  21.9 us
    ppermute x2, waiting for transfers between devices, from_chip_behind(): lax.ppermute(value, axis, [(i, (i + 2 * chips_back) % size) for i in rang...  15.7 us
    all_to_all x1, blocking collectives, local(): lax.all_to_all(jnp.concatenate([packed, spot_lanes], axis=1).reshape(n_de...  14.5 us
    dot_general x2, matrix products, apply_block(): return jnp.dot(hidden, down_here, preferred_element_type=jnp.float32)  11.9 us
    ppermute x2, waiting for transfers between devices, swap_parts(): lax.ppermute(value, 'rep', [(i, (i + step) % n_rep) for i in range(n_rep)])  11.8 us
    ppermute x2, starting transfers between devices, from_chip_behind(): lax.ppermute(value, axis, [(i, (i + 2 * chips_back) % size) for i in rang...  4.84 us
    ppermute x3, starting transfers between devices, local(): lax.ppermute(outgoing.astype(PARTIAL_DTYPE), 'tp', [(i, (i + shift) % n_t...  4.59 us
    ppermute x4, waiting for transfers between devices, from_partner(): lax.ppermute(value, axis, [(i, i ^ 1 << distance) for i in range(lax.axis...  3.79 us
  transfers between devices with their start and end apart: 12, of which 8 were waited for; matrix products, arithmetic and copies ran while one was open for 7% of the time, Pallas kernels for 0%

profile of v13, /device:TPU:0, one launch (start us, length us, event | category | flops | bytes accessed | tf_op | source)
XLA Modules:
  0.0 123.3 jit_solution(11827169600363252629)
XLA Ops:
  7.2 1.1 dynamic-slice_bitcast_fusion
  8.3 3.0 %collective-permute-start.2 = (bf16[1024,256]{1,0:T(8,128)(2,1)S(1)}, bf16[1024,256]{1,0:T(8,128)(2,1)S(1)}, u32[]{:S(2)}, u32[]{:S(2)}) collective-permute-start(bf16[1024,256]{1,0:T(8,128)(2,1)S(1)} %dynamic-slice_bitcast_fusion), channel_id=1, source_target_pairs={{0,8},{4,12},{8,0},{12,4},{1,9},{5,13},{9,1},{13,5},{2,10},{6,14},... | collective-permute-start | bytes 1572872 | tf_op jit(solution)/shard_map/ppermute | solution.py:15
  13.8 1.1 fusion.56
  16.9 6.4 %collective-permute-done.2 = bf16[1024,256]{1,0:T(8,128)(2,1)S(1)} collective-permute-done((bf16[1024,256]{1,0:T(8,128)(2,1)S(1)}, bf16[1024,256]{1,0:T(8,128)(2,1)S(1)}, u32[]{:S(2)}, u32[]{:S(2)}) %collective-permute-start.2) | collective-permute-done | bytes 524320 | tf_op jit(solution)/shard_map/ppermute | solution.py:15
  23.3 1.8 %collective-permute-start.4 = (bf16[256,1024]{1,0:T(8,128)(2,1)S(1)}, bf16[256,1024]{1,0:T(8,128)(2,1)S(1)}, u32[]{:S(2)}, u32[]{:S(2)}) collective-permute-start(bf16[256,1024]{1,0:T(8,128)(2,1)S(1)} %constant_dynamic-slice_fusion), channel_id=1, source_target_pairs={{0,8},{4,12},{8,0},{12,4},{1,9},{5,13},{9,1},{13,5},{2,10},{6,14},... | collective-permute-start | bytes 1572872 | tf_op jit(solution)/shard_map/ppermute | solution.py:15
  25.6 1.5 %collective-permute-start.3 = (bf16[1024,256]{1,0:T(8,128)(2,1)S(1)}, bf16[1024,256]{1,0:T(8,128)(2,1)}, u32[]{:S(2)}, u32[]{:S(2)}) collective-permute-start(bf16[1024,256]{1,0:T(8,128)(2,1)S(1)} %collective-permute-done.2), channel_id=1, source_target_pairs={{0,16},{16,0},{1,17},{17,1},{2,18},{18,2},{3,19},{19,3},{4,20},{20... | collective-permute-start | bytes 1572872 | tf_op jit(solution)/shard_map/ppermute | solution.py:21
  27.1 9.4 %collective-permute-done.4 = bf16[256,1024]{1,0:T(8,128)(2,1)S(1)} collective-permute-done((bf16[256,1024]{1,0:T(8,128)(2,1)S(1)}, bf16[256,1024]{1,0:T(8,128)(2,1)S(1)}, u32[]{:S(2)}, u32[]{:S(2)}) %collective-permute-start.4) | collective-permute-done | bytes 524320 | tf_op jit(solution)/shard_map/ppermute | solution.py:15
  36.5 1.4 %collective-permute-start.5 = (bf16[256,1024]{1,0:T(8,128)(2,1)S(1)}, bf16[256,1024]{1,0:T(8,128)(2,1)}, u32[]{:S(2)}, u32[]{:S(2)}) collective-permute-start(bf16[256,1024]{1,0:T(8,128)(2,1)S(1)} %collective-permute-done.4), channel_id=1, source_target_pairs={{0,16},{16,0},{1,17},{17,1},{2,18},{18,2},{3,19},{19,3},{4,20},{20... | collective-permute-start | bytes 1572872 | tf_op jit(solution)/shard_map/ppermute | solution.py:21
  37.9 2.6 %collective-permute-done.3 = bf16[1024,256]{1,0:T(8,128)(2,1)} collective-permute-done((bf16[1024,256]{1,0:T(8,128)(2,1)S(1)}, bf16[1024,256]{1,0:T(8,128)(2,1)}, u32[]{:S(2)}, u32[]{:S(2)}) %collective-permute-start.3) | collective-permute-done | bytes 524320 | tf_op jit(solution)/shard_map/ppermute | solution.py:21
  40.5 1.1 pad_maximum_fusion
  41.7 9.1 %collective-permute-done.5 = bf16[256,1024]{1,0:T(8,128)(2,1)} collective-permute-done((bf16[256,1024]{1,0:T(8,128)(2,1)S(1)}, bf16[256,1024]{1,0:T(8,128)(2,1)}, u32[]{:S(2)}, u32[]{:S(2)}) %collective-permute-start.5) | collective-permute-done | bytes 524320 | tf_op jit(solution)/shard_map/ppermute | solution.py:21
  50.8 1.1 pad_maximum_fusion.1
  52.0 1.1 fusion.74
  53.1 6.3 %fusion.20 = f32[512,1024]{1,0:T(8,128)} fusion(bf16[512,1024]{1,0:T(8,128)(2,1)} %collective-permute-done.1, bf16[512,1024]{1,0:T(8,128)(2,1)} %bitcast.34, bf16[1024,512]{1,0:T(8,128)(2,1)} %collective-permute-done, bf16[1024,512]{1,0:T(8,128)(2,1)} %bitcast.37, bf16[512,1152]{1,0:T(8,128)(2,1)} %all-gather.2.cloned.1.call-done, ...), kind=kOutput, calls=%fused_computation.23 | convolution fusion | flops 2161115136 | bytes 7341056 | tf_op jit(solution)/shard_map/dot_general | solution.py:83
  59.8 2.3 %collective-permute-done.7 = bf16[512,1024]{1,0:T(8,128)(2,1)} collective-permute-done((bf16[512,1024]{1,0:T(8,128)(2,1)S(1)}, bf16[512,1024]{1,0:T(8,128)(2,1)}, u32[]{:S(2)}, u32[]{:S(2)}) %collective-permute-start.7) | collective-permute-done | bytes 1048608 | tf_op jit(solution)/shard_map/ppermute | solution.py:10
  62.1 1.5 %collective-permute-done.6 = bf16[1024,512]{1,0:T(8,128)(2,1)} collective-permute-done((bf16[1024,512]{1,0:T(8,128)(2,1)S(1)}, bf16[1024,512]{1,0:T(8,128)(2,1)}, u32[]{:S(2)}, u32[]{:S(2)}) %collective-permute-start.6) | collective-permute-done | bytes 1048608 | tf_op jit(solution)/shard_map/ppermute | solution.py:10
  63.6 5.6 %fusion.28 = f32[512,1024]{1,0:T(8,128)} fusion(bf16[512,1024]{1,0:T(8,128)(2,1)} %collective-permute-done.7, bf16[512,1024]{1,0:T(8,128)(2,1)S(1)} %pad_maximum_fusion.1, bf16[1024,512]{1,0:T(8,128)(2,1)} %collective-permute-done.6, bf16[1024,512]{1,0:T(8,128)(2,1)S(1)} %pad_maximum_fusion, bf16[512,1152]{1,0:T(8,128)(2,1)} %all-gather.2.cloned.1.call-done, ...), kind=kOutput, calls=%fused_computation.31 | convolution fusion | flops 2161115136 | bytes 7341056 | tf_op jit(solution)/shard_map/dot_general | solution.py:83
  69.2 2.6 %add.120 = f32[512,1024]{1,0:T(8,128)S(1)} add(f32[512,1024]{1,0:T(8,128)} %fusion.20, f32[512,1024]{1,0:T(8,128)} %fusion.28) | non-fusion elementwise | flops 524288 | bytes 6291456 | tf_op jit(solution)/shard_map/add | solution.py:93
  72.7 3.6 %collective-permute-start.10 = (bf16[128,1024]{1,0:T(8,128)(2,1)}, bf16[128,1024]{1,0:T(8,128)(2,1)S(1)}, u32[]{:S(2)}, u32[]{:S(2)}) collective-permute-start(bf16[128,1024]{1,0:T(8,128)(2,1)} %get-tuple-element.15), channel_id=1, source_target_pairs={{0,3},{1,0},{2,1},{3,2},{4,7},{5,4},{6,5},{7,6},{8,11},{9,8},{10,9... | collective-permute-start | bytes 786440 | tf_op jit(solution)/shard_map/ppermute | solution.py:99
  76.3 1.0 collective-permute-start.8
  77.3 6.1 %collective-permute-done.10 = bf16[128,1024]{1,0:T(8,128)(2,1)S(1)} collective-permute-done((bf16[128,1024]{1,0:T(8,128)(2,1)}, bf16[128,1024]{1,0:T(8,128)(2,1)S(1)}, u32[]{:S(2)}, u32[]{:S(2)}) %collective-permute-start.10) | collective-permute-done | bytes 262176 | tf_op jit(solution)/shard_map/ppermute | solution.py:99
  83.3 15.8 %collective-permute-done.9 = bf16[128,1024]{1,0:T(8,128)(2,1)} collective-permute-done((bf16[128,1024]{1,0:T(8,128)(2,1)S(1)}, bf16[128,1024]{1,0:T(8,128)(2,1)}, u32[]{:S(2)}, u32[]{:S(2)}) %collective-permute-start.9) | collective-permute-done | bytes 262176 | tf_op jit(solution)/shard_map/ppermute | solution.py:99
  99.2 1.3 %convolution_convert_fusion.1 = bf16[128,1024]{1,0:T(8,128)(2,1)S(1)} fusion(bf16[128,1024]{1,0:T(8,128)(2,1)S(1)} %copy-done.2, bf16[128,1024]{1,0:T(8,128)(2,1)S(1)} %collective-permute-done.10, bf16[128,1024]{1,0:T(8,128)(2,1)} %collective-permute-done.9, bf16[128,1024]{1,0:T(8,128)(2,1)} %collective-permute-done.8, f32[4,128,1024]{2,1,0:T(8,128)S(1)} %bitcast.30, ...), kind=kOutput, calls=%fused_computation.36 | convolution fusion | flops 34881536 | bytes 1835524 | tf_op jit(solution)/shard_map/dot_general | solution.py:113
  100.6 14.5 %all_to_all.5 = bf16[16,8,1152]{2,1,0:T(8,128)(2,1)S(1)} all-to-all(bf16[16,8,1152]{2,1,0:T(8,128)(2,1)S(1)} %maximum_bitcast_fusion), channel_id=1, replica_groups=mesh['rep'=2,'member'=4,'tp'=4] {'member','tp'}, dimensions={0} | all-to-all | bytes 589824 | tf_op jit(solution)/shard_map/all_to_all | solution.py:120
  (47 shorter events, 7.7 us)
Async XLA Ops:
  7.2 108.4 %copy-start = (bf16[1024,128]{1,0:T(8,128)(2,1)S(1)}, bf16[1024,128]{1,0:T(8,128)(2,1)}, u32[]{:S(2)}) copy-start(bf16[1024,128]{1,0:T(8,128)(2,1)} %param.15) | copy-start | bytes 786436
  7.2 7.8 %copy-start.1 = (f32[2,1024]{1,0:T(2,128)S(1)}, f32[2,1024]{1,0:T(2,128)}, u32[]{:S(2)}) copy-start(f32[2,1024]{1,0:T(2,128)} %param.11) | copy-start | bytes 24580
  7.2 44.8 %all-gather.2.cloned.1.call-start = ((), (), s32[]{:S(2)}) async-start(), calls=%async_computation.1 | async-start | bytes 1474560 | tf_op jit(solution)/shard_map/all_gather | solution.py:72
  8.3 15.0 %collective-permute-start.2 = (bf16[1024,256]{1,0:T(8,128)(2,1)S(1)}, bf16[1024,256]{1,0:T(8,128)(2,1)S(1)}, u32[]{:S(2)}, u32[]{:S(2)}) collective-permute-start(bf16[1024,256]{1,0:T(8,128)(2,1)S(1)} %dynamic-slice_bitcast_fusion), channel_id=1, source_target_pairs={{0,8},{4,12},{8,0},{12,4},{1,9},{5,13},{9,1},{13,5},{2,10},{6,14},... | collective-permute-start | bytes 1572872 | tf_op jit(solution)/shard_map/ppermute | solution.py:15
  15.0 0.8 copy-start.4
  15.0 1.0 copy-start.2
  15.8 7.4 %copy-start.3 = (bf16[1,512,1024]{2,1,0:T(8,128)(2,1)S(1)}, bf16[1,512,1024]{2,1,0:T(8,128)(2,1)}, u32[]{:S(2)}) copy-start(bf16[1,512,1024]{2,1,0:T(8,128)(2,1)} %param.13) | copy-start | bytes 3145732
  23.3 13.2 %collective-permute-start.4 = (bf16[256,1024]{1,0:T(8,128)(2,1)S(1)}, bf16[256,1024]{1,0:T(8,128)(2,1)S(1)}, u32[]{:S(2)}, u32[]{:S(2)}) collective-permute-start(bf16[256,1024]{1,0:T(8,128)(2,1)S(1)} %constant_dynamic-slice_fusion), channel_id=1, source_target_pairs={{0,8},{4,12},{8,0},{12,4},{1,9},{5,13},{9,1},{13,5},{2,10},{6,14},... | collective-permute-start | bytes 1572872 | tf_op jit(solution)/shard_map/ppermute | solution.py:15
  25.1 27.9 %collective-permute-start.1 = (bf16[512,1024]{1,0:T(8,128)(2,1)}, bf16[512,1024]{1,0:T(8,128)(2,1)}, u32[]{:S(2)}, u32[]{:S(2)}) collective-permute-start(bf16[512,1024]{1,0:T(8,128)(2,1)} %bitcast.33), channel_id=1, source_target_pairs={{0,4},{4,0},{8,12},{12,8},{1,5},{5,1},{9,13},{13,9},{2,6},{6,2},{1... | collective-permute-start | bytes 3145736 | tf_op jit(solution)/shard_map/ppermute | solution.py:10
  25.1 27.9 %collective-permute-start = (bf16[1024,512]{1,0:T(8,128)(2,1)}, bf16[1024,512]{1,0:T(8,128)(2,1)}, u32[]{:S(2)}, u32[]{:S(2)}) collective-permute-start(bf16[1024,512]{1,0:T(8,128)(2,1)} %bitcast.36), channel_id=1, source_target_pairs={{0,4},{4,0},{8,12},{12,8},{1,5},{5,1},{9,13},{13,9},{2,6},{6,2},{1... | collective-permute-start | bytes 3145736 | tf_op jit(solution)/shard_map/ppermute | solution.py:10
  25.6 14.9 %collective-permute-start.3 = (bf16[1024,256]{1,0:T(8,128)(2,1)S(1)}, bf16[1024,256]{1,0:T(8,128)(2,1)}, u32[]{:S(2)}, u32[]{:S(2)}) collective-permute-start(bf16[1024,256]{1,0:T(8,128)(2,1)S(1)} %collective-permute-done.2), channel_id=1, source_target_pairs={{0,16},{16,0},{1,17},{17,1},{2,18},{18,2},{3,19},{19,3},{4,20},{20... | collective-permute-start | bytes 1572872 | tf_op jit(solution)/shard_map/ppermute | solution.py:21
  36.5 14.3 %collective-permute-start.5 = (bf16[256,1024]{1,0:T(8,128)(2,1)S(1)}, bf16[256,1024]{1,0:T(8,128)(2,1)}, u32[]{:S(2)}, u32[]{:S(2)}) collective-permute-start(bf16[256,1024]{1,0:T(8,128)(2,1)S(1)} %collective-permute-done.4), channel_id=1, source_target_pairs={{0,16},{16,0},{1,17},{17,1},{2,18},{18,2},{3,19},{19,3},{4,20},{20... | collective-permute-start | bytes 1572872 | tf_op jit(solution)/shard_map/ppermute | solution.py:21
  59.3 2.8 %collective-permute-start.7 = (bf16[512,1024]{1,0:T(8,128)(2,1)S(1)}, bf16[512,1024]{1,0:T(8,128)(2,1)}, u32[]{:S(2)}, u32[]{:S(2)}) collective-permute-start(bf16[512,1024]{1,0:T(8,128)(2,1)S(1)} %pad_maximum_fusion.1), channel_id=1, source_target_pairs={{0,4},{4,0},{8,12},{12,8},{1,5},{5,1},{9,13},{13,9},{2,6},{6,2},{1... | collective-permute-start | bytes 3145736 | tf_op jit(solution)/shard_map/ppermute | solution.py:10
  59.3 4.3 %collective-permute-start.6 = (bf16[1024,512]{1,0:T(8,128)(2,1)S(1)}, bf16[1024,512]{1,0:T(8,128)(2,1)}, u32[]{:S(2)}, u32[]{:S(2)}) collective-permute-start(bf16[1024,512]{1,0:T(8,128)(2,1)S(1)} %pad_maximum_fusion), channel_id=1, source_target_pairs={{0,4},{4,0},{8,12},{12,8},{1,5},{5,1},{9,13},{13,9},{2,6},{6,2},{1... | collective-permute-start | bytes 3145736 | tf_op jit(solution)/shard_map/ppermute | solution.py:10
  72.7 42.9 %copy-start.5 = (f32[1024]{0:T(1024)S(1)}, f32[1024]{0:T(1024)}, u32[]{:S(2)}) copy-start(f32[1024]{0:T(1024)} %param.14) | copy-start | bytes 12292
  72.7 10.7 %collective-permute-start.10 = (bf16[128,1024]{1,0:T(8,128)(2,1)}, bf16[128,1024]{1,0:T(8,128)(2,1)S(1)}, u32[]{:S(2)}, u32[]{:S(2)}) collective-permute-start(bf16[128,1024]{1,0:T(8,128)(2,1)} %get-tuple-element.15), channel_id=1, source_target_pairs={{0,3},{1,0},{2,1},{3,2},{4,7},{5,4},{6,5},{7,6},{8,11},{9,8},{10,9... | collective-permute-start | bytes 786440 | tf_op jit(solution)/shard_map/ppermute | solution.py:99
  76.3 22.9 %collective-permute-start.9 = (bf16[128,1024]{1,0:T(8,128)(2,1)S(1)}, bf16[128,1024]{1,0:T(8,128)(2,1)}, u32[]{:S(2)}, u32[]{:S(2)}) collective-permute-start(bf16[128,1024]{1,0:T(8,128)(2,1)S(1)} %get-tuple-element.16), channel_id=1, source_target_pairs={{0,2},{1,3},{2,0},{3,1},{4,6},{5,7},{6,4},{7,5},{8,10},{9,11},{10,... | collective-permute-start | bytes 786440 | tf_op jit(solution)/shard_map/ppermute | solution.py:99
  76.3 22.9 %collective-permute-start.8 = (bf16[128,1024]{1,0:T(8,128)(2,1)S(1)}, bf16[128,1024]{1,0:T(8,128)(2,1)}, u32[]{:S(2)}, u32[]{:S(2)}) collective-permute-start(bf16[128,1024]{1,0:T(8,128)(2,1)S(1)} %get-tuple-element.14), channel_id=1, source_target_pairs={{0,1},{1,2},{2,3},{3,0},{4,5},{5,6},{6,7},{7,4},{8,9},{9,10},{10,1... | collective-permute-start | bytes 786440 | tf_op jit(solution)/shard_map/ppermute | solution.py:99
  115.5 1.0 copy-start.6
Sparse Core Ops, SparseCore 0:
  17.0 30.7 all-gather.1

commit v14 on v13

--- a/solution.py
+++ b/solution.py
@@ -87,17 +87,24 @@
         both_down = jnp.concatenate([down_here, from_partner(down_here, "member", 0)], axis=0)
         return apply_block(block_member, both_up, both_down)
 
-    partial = apply_pair(*own_block)
+    terms = [apply_pair(*own_block)]
     for block_member, up_here, down_here in fetched:
-        partial, up_here, down_here = lax.optimization_barrier((partial, up_here, down_here))
-        partial = partial + apply_pair(block_member, up_here, down_here)
+        terms, up_here, down_here = lax.optimization_barrier((terms, up_here, down_here))
+        terms = terms + [apply_pair(block_member, up_here, down_here)]
     tp_here = lax.axis_index("tp")
-    by_target = partial.reshape(n_tp, rows_here, feature_width)
-    change = lax.dynamic_index_in_dim(by_target, tp_here, 0, keepdims=False)
+    by_target = [term.reshape(n_tp, rows_here, feature_width) for term in terms]
+
+    def slice_for(target):
+        pieces = [lax.dynamic_index_in_dim(term, target, 0, keepdims=False) for term in by_target]
+        total = pieces[0]
+        for piece in pieces[1:]:
+            total = total + piece
+        return total
+
+    change = slice_for(tp_here)
     for shift in range(1, n_tp):
-        outgoing = lax.dynamic_index_in_dim(by_target, (tp_here + shift) % n_tp, 0, keepdims=False)
         change = change + lax.ppermute(
-            outgoing.astype(PARTIAL_DTYPE),
+            slice_for((tp_here + shift) % n_tp).astype(PARTIAL_DTYPE),
             "tp",
             [(i, (i + shift) % n_tp) for i in range(n_tp)],
         ).astype(jnp.float32)

time: 124 us -> 123 us (level)
    add x1 -> x0, other arithmetic: 2.61 us -> none  [local(): partial = partial + apply_pair(block_member, up_here, down_here)]
    convert_element_type x0 -> x1, other arithmetic: none -> 2.35 us  [local(): slice_for((tp_here + shift) % n_tp).astype(PARTIAL_DTYPE)]
  transfers between devices with their start and end apart: 12 -> 12, of which waited for: 8 -> 8; matrix products, arithmetic and copies ran while one was open for 7% -> 8% of each run, Pallas kernels for 0% -> 0%
where the time goes in v14:
time: 123 us
  waiting for transfers between devices  53.3 us (43%)
  blocking collectives  14.9 us (12%)
  between operations  14.2 us (12%)
  matrix products  13.8 us (11%)
  starting transfers between devices  13.5 us (11%)
  other arithmetic  10.3 us (8%)
  local copies, waits for them, and re-layouts  3.03 us (2%)
    ppermute x3, waiting for transfers between devices, local(): lax.ppermute(slice_for((tp_here + shift) % n_tp).astype(PARTIAL_DTYPE), '...  21.8 us
    ppermute x2, waiting for transfers between devices, from_chip_behind(): lax.ppermute(value, axis, [(i, (i + 2 * chips_back) % size) for i in rang...  15.7 us
    all_to_all x1, blocking collectives, local(): lax.all_to_all(jnp.concatenate([packed, spot_lanes], axis=1).reshape(n_de...  14.9 us
    ppermute x2, waiting for transfers between devices, swap_parts(): lax.ppermute(value, 'rep', [(i, (i + step) % n_rep) for i in range(n_rep)])  11.8 us
    dot_general x2, matrix products, apply_block(): return jnp.dot(hidden, down_here, preferred_element_type=jnp.float32)  11.2 us
    ppermute x2, starting transfers between devices, from_chip_behind(): lax.ppermute(value, axis, [(i, (i + 2 * chips_back) % size) for i in rang...  4.84 us
    ppermute x3, starting transfers between devices, local(): lax.ppermute(slice_for((tp_here + shift) % n_tp).astype(PARTIAL_DTYPE), '...  4.62 us
    ppermute x4, waiting for transfers between devices, from_partner(): lax.ppermute(value, axis, [(i, i ^ 1 << distance) for i in range(lax.axis...  4 us
  transfers between devices with their start and end apart: 12, of which 8 were waited for; matrix products, arithmetic and copies ran while one was open for 8% of the time, Pallas kernels for 0%

profile of v14, /device:TPU:0, one launch (start us, length us, event | category | flops | bytes accessed | tf_op | source)
XLA Modules:
  0.0 123.0 jit_solution(17219872241214281731)
XLA Ops:
  7.2 1.1 dynamic-slice_bitcast_fusion
  8.3 3.0 %collective-permute-start.2 = (bf16[1024,256]{1,0:T(8,128)(2,1)S(1)}, bf16[1024,256]{1,0:T(8,128)(2,1)S(1)}, u32[]{:S(2)}, u32[]{:S(2)}) collective-permute-start(bf16[1024,256]{1,0:T(8,128)(2,1)S(1)} %dynamic-slice_bitcast_fusion), channel_id=1, source_target_pairs={{0,8},{4,12},{8,0},{12,4},{1,9},{5,13},{9,1},{13,5},{2,10},{6,14},... | collective-permute-start | bytes 1572872 | tf_op jit(solution)/shard_map/ppermute | solution.py:15
  13.8 1.1 fusion.56
  16.9 6.4 %collective-permute-done.2 = bf16[1024,256]{1,0:T(8,128)(2,1)S(1)} collective-permute-done((bf16[1024,256]{1,0:T(8,128)(2,1)S(1)}, bf16[1024,256]{1,0:T(8,128)(2,1)S(1)}, u32[]{:S(2)}, u32[]{:S(2)}) %collective-permute-start.2) | collective-permute-done | bytes 524320 | tf_op jit(solution)/shard_map/ppermute | solution.py:15
  23.3 1.1 constant_dynamic-slice_fusion
  24.4 1.8 %collective-permute-start.4 = (bf16[256,1024]{1,0:T(8,128)(2,1)S(1)}, bf16[256,1024]{1,0:T(8,128)(2,1)S(1)}, u32[]{:S(2)}, u32[]{:S(2)}) collective-permute-start(bf16[256,1024]{1,0:T(8,128)(2,1)S(1)} %constant_dynamic-slice_fusion), channel_id=1, source_target_pairs={{0,8},{4,12},{8,0},{12,4},{1,9},{5,13},{9,1},{13,5},{2,10},{6,14},... | collective-permute-start | bytes 1572872 | tf_op jit(solution)/shard_map/ppermute | solution.py:15
  26.7 1.5 %collective-permute-start.3 = (bf16[1024,256]{1,0:T(8,128)(2,1)S(1)}, bf16[1024,256]{1,0:T(8,128)(2,1)S(1)}, u32[]{:S(2)}, u32[]{:S(2)}) collective-permute-start(bf16[1024,256]{1,0:T(8,128)(2,1)S(1)} %collective-permute-done.2), channel_id=1, source_target_pairs={{0,16},{16,0},{1,17},{17,1},{2,18},{18,2},{3,19},{19,3},{4,20},{20... | collective-permute-start | bytes 1572872 | tf_op jit(solution)/shard_map/ppermute | solution.py:21
  28.2 9.3 %collective-permute-done.4 = bf16[256,1024]{1,0:T(8,128)(2,1)S(1)} collective-permute-done((bf16[256,1024]{1,0:T(8,128)(2,1)S(1)}, bf16[256,1024]{1,0:T(8,128)(2,1)S(1)}, u32[]{:S(2)}, u32[]{:S(2)}) %collective-permute-start.4) | collective-permute-done | bytes 524320 | tf_op jit(solution)/shard_map/ppermute | solution.py:15
  37.5 1.4 %collective-permute-start.5 = (bf16[256,1024]{1,0:T(8,128)(2,1)S(1)}, bf16[256,1024]{1,0:T(8,128)(2,1)S(1)}, u32[]{:S(2)}, u32[]{:S(2)}) collective-permute-start(bf16[256,1024]{1,0:T(8,128)(2,1)S(1)} %collective-permute-done.4), channel_id=1, source_target_pairs={{0,16},{16,0},{1,17},{17,1},{2,18},{18,2},{3,19},{19,3},{4,20},{20... | collective-permute-start | bytes 1572872 | tf_op jit(solution)/shard_map/ppermute | solution.py:21
  38.9 2.6 %collective-permute-done.3 = bf16[1024,256]{1,0:T(8,128)(2,1)S(1)} collective-permute-done((bf16[1024,256]{1,0:T(8,128)(2,1)S(1)}, bf16[1024,256]{1,0:T(8,128)(2,1)S(1)}, u32[]{:S(2)}, u32[]{:S(2)}) %collective-permute-start.3) | collective-permute-done | bytes 524320 | tf_op jit(solution)/shard_map/ppermute | solution.py:21
  41.5 1.0 pad_maximum_fusion
  42.5 9.2 %collective-permute-done.5 = bf16[256,1024]{1,0:T(8,128)(2,1)S(1)} collective-permute-done((bf16[256,1024]{1,0:T(8,128)(2,1)S(1)}, bf16[256,1024]{1,0:T(8,128)(2,1)S(1)}, u32[]{:S(2)}, u32[]{:S(2)}) %collective-permute-start.5) | collective-permute-done | bytes 524320 | tf_op jit(solution)/shard_map/ppermute | solution.py:21
  51.8 1.1 pad_maximum_fusion.1
  52.8 1.1 fusion.74
  53.9 4.9 %fusion.20 = f32[512,1024]{1,0:T(8,128)S(1)} fusion(bf16[512,1024]{1,0:T(8,128)(2,1)} %collective-permute-done.1, bf16[512,1024]{1,0:T(8,128)(2,1)} %bitcast.4, bf16[1024,512]{1,0:T(8,128)(2,1)} %collective-permute-done, bf16[1024,512]{1,0:T(8,128)(2,1)} %bitcast.3, bf16[512,1152]{1,0:T(8,128)(2,1)} %all-gather.2.cloned.1.call-done, ...), kind=kOutput, calls=%fused_computation.23 | convolution fusion | flops 2161115136 | bytes 7341056 | tf_op jit(solution)/shard_map/dot_general | solution.py:83
  59.4 2.5 %collective-permute-done.7 = bf16[512,1024]{1,0:T(8,128)(2,1)} collective-permute-done((bf16[512,1024]{1,0:T(8,128)(2,1)}, bf16[512,1024]{1,0:T(8,128)(2,1)}, u32[]{:S(2)}, u32[]{:S(2)}) %collective-permute-start.7) | collective-permute-done | bytes 1048608 | tf_op jit(solution)/shard_map/ppermute | solution.py:10
  61.9 1.5 %collective-permute-done.6 = bf16[1024,512]{1,0:T(8,128)(2,1)} collective-permute-done((bf16[1024,512]{1,0:T(8,128)(2,1)}, bf16[1024,512]{1,0:T(8,128)(2,1)}, u32[]{:S(2)}, u32[]{:S(2)}) %collective-permute-start.6) | collective-permute-done | bytes 1048608 | tf_op jit(solution)/shard_map/ppermute | solution.py:10
  63.4 6.3 %fusion.28 = f32[512,1024]{1,0:T(8,128)} fusion(bf16[512,1024]{1,0:T(8,128)(2,1)} %collective-permute-done.7, bf16[512,1024]{1,0:T(8,128)(2,1)} %pad_maximum_fusion.1, bf16[1024,512]{1,0:T(8,128)(2,1)} %collective-permute-done.6, bf16[1024,512]{1,0:T(8,128)(2,1)} %pad_maximum_fusion, bf16[512,1152]{1,0:T(8,128)(2,1)} %all-gather.2.cloned.1.call-done, ...), kind=kOutput, calls=%fused_computation.31 | convolution fusion | flops 2161115136 | bytes 7341056 | tf_op jit(solution)/shard_map/dot_general | solution.py:83
  69.7 2.4 %fusion.64 = (bf16[128,1024]{1,0:T(8,128)(2,1)S(1)}, bf16[128,1024]{1,0:T(8,128)(2,1)}, bf16[128,1024]{1,0:T(8,128)(2,1)}) fusion(f32[4,128,1024]{2,1,0:T(8,128)} %bitcast.32, s32[]{:T(128)S(6)} %select_n.81, f32[4,128,1024]{2,1,0:T(8,128)S(1)} %bitcast.30, s32[]{:T(128)S(6)} %select_n.85, s32[]{:T(128)S(6)} %select_n.83), kind=kLoop, calls=%fused_computation.70 | loop fusion | flops 786432 | bytes 3932172 | tf_op jit(solution)/shard_map/convert_element_type | solution.py:107
  72.0 3.6 %collective-permute-start.10 = (bf16[128,1024]{1,0:T(8,128)(2,1)}, bf16[128,1024]{1,0:T(8,128)(2,1)S(1)}, u32[]{:S(2)}, u32[]{:S(2)}) collective-permute-start(bf16[128,1024]{1,0:T(8,128)(2,1)} %get-tuple-element.15), channel_id=1, source_target_pairs={{0,3},{1,0},{2,1},{3,2},{4,7},{5,4},{6,5},{7,6},{8,11},{9,8},{10,9... | collective-permute-start | bytes 786440 | tf_op jit(solution)/shard_map/ppermute | solution.py:106
  76.6 6.1 %collective-permute-done.10 = bf16[128,1024]{1,0:T(8,128)(2,1)S(1)} collective-permute-done((bf16[128,1024]{1,0:T(8,128)(2,1)}, bf16[128,1024]{1,0:T(8,128)(2,1)S(1)}, u32[]{:S(2)}, u32[]{:S(2)}) %collective-permute-start.10) | collective-permute-done | bytes 262176 | tf_op jit(solution)/shard_map/ppermute | solution.py:106
  82.7 15.7 %collective-permute-done.9 = bf16[128,1024]{1,0:T(8,128)(2,1)S(1)} collective-permute-done((bf16[128,1024]{1,0:T(8,128)(2,1)}, bf16[128,1024]{1,0:T(8,128)(2,1)S(1)}, u32[]{:S(2)}, u32[]{:S(2)}) %collective-permute-start.9) | collective-permute-done | bytes 262176 | tf_op jit(solution)/shard_map/ppermute | solution.py:106
  98.4 1.5 %convolution_convert_fusion.1 = bf16[128,1024]{1,0:T(8,128)(2,1)S(1)} fusion(bf16[128,1024]{1,0:T(8,128)(2,1)S(1)} %copy-done.2, bf16[128,1024]{1,0:T(8,128)(2,1)S(1)} %collective-permute-done.10, bf16[128,1024]{1,0:T(8,128)(2,1)S(1)} %collective-permute-done.9, bf16[128,1024]{1,0:T(8,128)(2,1)} %collective-permute-done.8, f32[4,128,1024]{2,1,0:T(8,128)} %bitcast.33, ...), kind=kOutput, calls=%fused_computation.36 | convolution fusion | flops 35012608 | bytes 2359812 | tf_op jit(solution)/shard_map/dot_general | solution.py:120
  99.9 14.9 %all_to_all.5 = bf16[16,8,1152]{2,1,0:T(8,128)(2,1)S(1)} all-to-all(bf16[16,8,1152]{2,1,0:T(8,128)(2,1)S(1)} %maximum_bitcast_fusion), channel_id=1, replica_groups=mesh['rep'=2,'member'=4,'tp'=4] {'member','tp'}, dimensions={0} | all-to-all | bytes 589824 | tf_op jit(solution)/shard_map/all_to_all | solution.py:127
  (44 shorter events, 7.9 us)
Async XLA Ops:
  7.2 108.1 %copy-start = (bf16[1024,128]{1,0:T(8,128)(2,1)S(1)}, bf16[1024,128]{1,0:T(8,128)(2,1)}, u32[]{:S(2)}) copy-start(bf16[1024,128]{1,0:T(8,128)(2,1)} %param.15) | copy-start | bytes 786436
  7.2 7.8 %copy-start.1 = (f32[2,1024]{1,0:T(2,128)S(1)}, f32[2,1024]{1,0:T(2,128)}, u32[]{:S(2)}) copy-start(f32[2,1024]{1,0:T(2,128)} %param.11) | copy-start | bytes 24580
  7.2 45.6 %all-gather.2.cloned.1.call-start = ((), (), s32[]{:S(2)}) async-start(), calls=%async_computation.1 | async-start | bytes 1474560 | tf_op jit(solution)/shard_map/all_gather | solution.py:72
  8.3 15.0 %collective-permute-start.2 = (bf16[1024,256]{1,0:T(8,128)(2,1)S(1)}, bf16[1024,256]{1,0:T(8,128)(2,1)S(1)}, u32[]{:S(2)}, u32[]{:S(2)}) collective-permute-start(bf16[1024,256]{1,0:T(8,128)(2,1)S(1)} %dynamic-slice_bitcast_fusion), channel_id=1, source_target_pairs={{0,8},{4,12},{8,0},{12,4},{1,9},{5,13},{9,1},{13,5},{2,10},{6,14},... | collective-permute-start | bytes 1572872 | tf_op jit(solution)/shard_map/ppermute | solution.py:15
  15.0 0.8 copy-start.3
  15.0 1.0 copy-start.2
  24.4 13.2 %collective-permute-start.4 = (bf16[256,1024]{1,0:T(8,128)(2,1)S(1)}, bf16[256,1024]{1,0:T(8,128)(2,1)S(1)}, u32[]{:S(2)}, u32[]{:S(2)}) collective-permute-start(bf16[256,1024]{1,0:T(8,128)(2,1)S(1)} %constant_dynamic-slice_fusion), channel_id=1, source_target_pairs={{0,8},{4,12},{8,0},{12,4},{1,9},{5,13},{9,1},{13,5},{2,10},{6,14},... | collective-permute-start | bytes 1572872 | tf_op jit(solution)/shard_map/ppermute | solution.py:15
  26.2 27.7 %collective-permute-start.1 = (bf16[512,1024]{1,0:T(8,128)(2,1)}, bf16[512,1024]{1,0:T(8,128)(2,1)}, u32[]{:S(2)}, u32[]{:S(2)}) collective-permute-start(bf16[512,1024]{1,0:T(8,128)(2,1)} %bitcast.4), channel_id=1, source_target_pairs={{0,4},{4,0},{8,12},{12,8},{1,5},{5,1},{9,13},{13,9},{2,6},{6,2},{1... | collective-permute-start | bytes 3145736 | tf_op jit(solution)/shard_map/ppermute | solution.py:10
  26.2 27.7 %collective-permute-start = (bf16[1024,512]{1,0:T(8,128)(2,1)}, bf16[1024,512]{1,0:T(8,128)(2,1)}, u32[]{:S(2)}, u32[]{:S(2)}) collective-permute-start(bf16[1024,512]{1,0:T(8,128)(2,1)} %bitcast.3), channel_id=1, source_target_pairs={{0,4},{4,0},{8,12},{12,8},{1,5},{5,1},{9,13},{13,9},{2,6},{6,2},{1... | collective-permute-start | bytes 3145736 | tf_op jit(solution)/shard_map/ppermute | solution.py:10
  26.7 14.8 %collective-permute-start.3 = (bf16[1024,256]{1,0:T(8,128)(2,1)S(1)}, bf16[1024,256]{1,0:T(8,128)(2,1)S(1)}, u32[]{:S(2)}, u32[]{:S(2)}) collective-permute-start(bf16[1024,256]{1,0:T(8,128)(2,1)S(1)} %collective-permute-done.2), channel_id=1, source_target_pairs={{0,16},{16,0},{1,17},{17,1},{2,18},{18,2},{3,19},{19,3},{4,20},{20... | collective-permute-start | bytes 1572872 | tf_op jit(solution)/shard_map/ppermute | solution.py:21
  37.5 14.2 %collective-permute-start.5 = (bf16[256,1024]{1,0:T(8,128)(2,1)S(1)}, bf16[256,1024]{1,0:T(8,128)(2,1)S(1)}, u32[]{:S(2)}, u32[]{:S(2)}) collective-permute-start(bf16[256,1024]{1,0:T(8,128)(2,1)S(1)} %collective-permute-done.4), channel_id=1, source_target_pairs={{0,16},{16,0},{1,17},{17,1},{2,18},{18,2},{3,19},{19,3},{4,20},{20... | collective-permute-start | bytes 1572872 | tf_op jit(solution)/shard_map/ppermute | solution.py:21
  58.8 3.1 %collective-permute-start.7 = (bf16[512,1024]{1,0:T(8,128)(2,1)}, bf16[512,1024]{1,0:T(8,128)(2,1)}, u32[]{:S(2)}, u32[]{:S(2)}) collective-permute-start(bf16[512,1024]{1,0:T(8,128)(2,1)} %pad_maximum_fusion.1), channel_id=1, source_target_pairs={{0,4},{4,0},{8,12},{12,8},{1,5},{5,1},{9,13},{13,9},{2,6},{6,2},{1... | collective-permute-start | bytes 3145736 | tf_op jit(solution)/shard_map/ppermute | solution.py:10
  58.9 4.5 %collective-permute-start.6 = (bf16[1024,512]{1,0:T(8,128)(2,1)}, bf16[1024,512]{1,0:T(8,128)(2,1)}, u32[]{:S(2)}, u32[]{:S(2)}) collective-permute-start(bf16[1024,512]{1,0:T(8,128)(2,1)} %pad_maximum_fusion), channel_id=1, source_target_pairs={{0,4},{4,0},{8,12},{12,8},{1,5},{5,1},{9,13},{13,9},{2,6},{6,2},{1... | collective-permute-start | bytes 3145736 | tf_op jit(solution)/shard_map/ppermute | solution.py:10
  72.0 43.3 %copy-start.4 = (f32[1024]{0:T(1024)S(1)}, f32[1024]{0:T(1024)}, u32[]{:S(2)}) copy-start(f32[1024]{0:T(1024)} %param.14) | copy-start | bytes 12292
  72.0 10.7 %collective-permute-start.10 = (bf16[128,1024]{1,0:T(8,128)(2,1)}, bf16[128,1024]{1,0:T(8,128)(2,1)S(1)}, u32[]{:S(2)}, u32[]{:S(2)}) collective-permute-start(bf16[128,1024]{1,0:T(8,128)(2,1)} %get-tuple-element.15), channel_id=1, source_target_pairs={{0,3},{1,0},{2,1},{3,2},{4,7},{5,4},{6,5},{7,6},{8,11},{9,8},{10,9... | collective-permute-start | bytes 786440 | tf_op jit(solution)/shard_map/ppermute | solution.py:106
  75.6 22.8 %collective-permute-start.9 = (bf16[128,1024]{1,0:T(8,128)(2,1)}, bf16[128,1024]{1,0:T(8,128)(2,1)S(1)}, u32[]{:S(2)}, u32[]{:S(2)}) collective-permute-start(bf16[128,1024]{1,0:T(8,128)(2,1)} %get-tuple-element.16), channel_id=1, source_target_pairs={{0,2},{1,3},{2,0},{3,1},{4,6},{5,7},{6,4},{7,5},{8,10},{9,11},{10,... | collective-permute-start | bytes 786440 | tf_op jit(solution)/shard_map/ppermute | solution.py:106
  75.6 22.8 %collective-permute-start.8 = (bf16[128,1024]{1,0:T(8,128)(2,1)S(1)}, bf16[128,1024]{1,0:T(8,128)(2,1)}, u32[]{:S(2)}, u32[]{:S(2)}) collective-permute-start(bf16[128,1024]{1,0:T(8,128)(2,1)S(1)} %get-tuple-element.14), channel_id=1, source_target_pairs={{0,1},{1,2},{2,3},{3,0},{4,5},{5,6},{6,7},{7,4},{8,9},{9,10},{10,1... | collective-permute-start | bytes 786440 | tf_op jit(solution)/shard_map/ppermute | solution.py:106
  115.2 1.0 copy-start.5
Sparse Core Ops, SparseCore 0:
  17.0 30.7 all-gather.1

commit v15 on v13

--- a/solution.py
+++ b/solution.py
@@ -72,32 +72,36 @@
     gathered = lax.all_gather(
         jnp.concatenate([normed, member_lanes], axis=1), "tp", axis=0, tiled=True
     )
-    gathered_rows = gathered[:, :feature_width]
-    gathered_member = gathered[:, feature_width].astype(jnp.int32)
+    tp_here = lax.axis_index("tp")
+    by_source = gathered.reshape(n_tp, rows_here, feature_width + 128)
+    shifts = list(range(1, n_tp)) + [0]
+    row_blocks = [
+        lax.dynamic_index_in_dim(by_source, (tp_here + shift) % n_tp, 0, keepdims=False)
+        for shift in shifts
+    ]
 
-    def apply_block(block_member, up_here, down_here):
-        keep = (gathered_member == block_member).astype(jnp.bfloat16)[:, None]
+    def apply_block(rows_block, block_member, up_here, down_here):
+        keep = (rows_block[:, feature_width].astype(jnp.int32) == block_member).astype(jnp.bfloat16)
         hidden = jax.nn.gelu(
-            jnp.dot(gathered_rows, up_here, preferred_element_type=jnp.float32)
-        ).astype(jnp.bfloat16) * keep
+            jnp.dot(rows_block[:, :feature_width], up_here, preferred_element_type=jnp.float32)
+        ).astype(jnp.bfloat16) * keep[:, None]
         return jnp.dot(hidden, down_here, preferred_element_type=jnp.float32)
 
-    def apply_pair(block_member, up_here, down_here):
+    def both_halves(block_member, up_here, down_here):
         both_up = jnp.concatenate([up_here, from_partner(up_here, "member", 0)], axis=1)
         both_down = jnp.concatenate([down_here, from_partner(down_here, "member", 0)], axis=0)
-        return apply_block(block_member, both_up, both_down)
+        return block_member, both_up, both_down
 
-    partial = apply_pair(*own_block)
+    own_pair = both_halves(*own_block)
+    totals = [apply_block(rows_block, *own_pair) for rows_block in row_blocks]
     for block_member, up_here, down_here in fetched:
-        partial, up_here, down_here = lax.optimization_barrier((partial, up_here, down_here))
-        partial = partial + apply_pair(block_member, up_here, down_here)
-    tp_here = lax.axis_index("tp")
-    by_target = partial.reshape(n_tp, rows_here, feature_width)
-    change = lax.dynamic_index_in_dim(by_target, tp_here, 0, keepdims=False)
-    for shift in range(1, n_tp):
-        outgoing = lax.dynamic_index_in_dim(by_target, (tp_here + shift) % n_tp, 0, keepdims=False)
+        totals, up_here, down_here = lax.optimization_barrier((totals, up_here, down_here))
+        pair = both_halves(block_member, up_here, down_here)
+        totals = [total + apply_block(rows_block, *pair) for total, rows_block in zip(totals, row_blocks)]
+    change = totals[-1]
+    for shift, total in zip(shifts[:-1], totals[:-1]):
         change = change + lax.ppermute(
-            outgoing.astype(PARTIAL_DTYPE),
+            total.astype(PARTIAL_DTYPE),
             "tp",
             [(i, (i + shift) % n_tp) for i in range(n_tp)],
         ).astype(jnp.float32)

time: 124 us -> 133 us (1.073)
  matrix products: 14.4 us -> 29.1 us
  waiting for transfers between devices: 53.3 us -> 42.4 us
  local copies, waits for them, and re-layouts: 2.8 us -> 7.66 us
    dot_general x2 -> x7, matrix products: 11.9 us -> 23.6 us  [apply_block(): return jnp.dot(hidden, down_here, preferred_element_type=jnp.float32)]
    ppermute x3, waiting for transfers between devices: 21.9 us -> 13.3 us  [local(): lax.ppermute(total.astype(PARTIAL_DTYPE), 'tp', [(i, (i + shift) % n_tp)...]
    convert_element_type x0 -> x3, other arithmetic: none -> 3.73 us  [local(): total.astype(PARTIAL_DTYPE)]
    unnamed x14 -> x34, local copies, waits for them, and re-layouts: 0.06 us -> 3.37 us
    add x1 -> x0, other arithmetic: 2.61 us -> none  [local(): partial = partial + apply_pair(block_member, up_here, down_here)]
    dynamic_slice x0 -> x5, local copies, waits for them, and re-layouts: none -> 2.18 us  [local(): lax.dynamic_index_in_dim(by_source, (tp_here + shift) % n_tp, 0, keepdims...]
    dot_general x1, matrix products: 1.34 us -> 2.79 us  [local(): jnp.dot(placer.astype(jnp.bfloat16), own_rows, preferred_element_type=jnp...]
    dot_general x0 -> x1, matrix products: none -> 1.41 us  [apply_block(): jnp.dot(rows_block[:, :feature_width], up_here, preferred_element_type=jn...]
  transfers between devices with their start and end apart: 12 -> 12, of which waited for: 8 -> 5; matrix products, arithmetic and copies ran while one was open for 7% -> 16% of each run, Pallas kernels for 0% -> 0%
where the time goes in v15:
time: 133 us; the launch traced here: 132 us
  waiting for transfers between devices  42.4 us (32%)
  matrix products  29.1 us (22%)
  blocking collectives  14.8 us (11%)
  between operations  14.4 us (11%)
  starting transfers between devices  13.4 us (10%)
  other arithmetic  10.7 us (8%)
  local copies, waits for them, and re-layouts  7.66 us (6%)
    dot_general x7, matrix products, apply_block(): return jnp.dot(hidden, down_here, preferred_element_type=jnp.float32)  23.6 us
    ppermute x2, waiting for transfers between devices, from_chip_behind(): lax.ppermute(value, axis, [(i, (i + 2 * chips_back) % size) for i in rang...  16.2 us
    all_to_all x1, blocking collectives, local(): lax.all_to_all(jnp.concatenate([packed, spot_lanes], axis=1).reshape(n_de...  14.8 us
    ppermute x3, waiting for transfers between devices, local(): lax.ppermute(total.astype(PARTIAL_DTYPE), 'tp', [(i, (i + shift) % n_tp)...  13.3 us
    ppermute x2, waiting for transfers between devices, swap_parts(): lax.ppermute(value, 'rep', [(i, (i + step) % n_rep) for i in range(n_rep)])  10.5 us
    ppermute x2, starting transfers between devices, from_chip_behind(): lax.ppermute(value, axis, [(i, (i + 2 * chips_back) % size) for i in rang...  4.84 us
    ppermute x3, starting transfers between devices, local(): lax.ppermute(total.astype(PARTIAL_DTYPE), 'tp', [(i, (i + shift) % n_tp)...  4.67 us
    convert_element_type x3, other arithmetic, local(): total.astype(PARTIAL_DTYPE)  3.73 us
  transfers between devices with their start and end apart: 12, of which 5 were waited for; matrix products, arithmetic and copies ran while one was open for 16% of the time, Pallas kernels for 0%

profile of v15, /device:TPU:0, one launch (start us, length us, event | category | flops | bytes accessed | tf_op | source)
XLA Modules:
  0.0 132.4 jit_solution(15513222292509934011)
XLA Ops:
  8.3 3.0 %collective-permute-start.2 = (bf16[1024,256]{1,0:T(8,128)(2,1)S(1)}, bf16[1024,256]{1,0:T(8,128)(2,1)S(1)}, u32[]{:S(2)}, u32[]{:S(2)}) collective-permute-start(bf16[1024,256]{1,0:T(8,128)(2,1)S(1)} %dynamic-slice_bitcast_fusion), channel_id=1, source_target_pairs={{0,8},{4,12},{8,0},{12,4},{1,9},{5,13},{9,1},{13,5},{2,10},{6,14},... | collective-permute-start | bytes 1572872 | tf_op jit(solution)/shard_map/ppermute | solution.py:15
  16.9 6.4 %collective-permute-done.2 = bf16[1024,256]{1,0:T(8,128)(2,1)S(1)} collective-permute-done((bf16[1024,256]{1,0:T(8,128)(2,1)S(1)}, bf16[1024,256]{1,0:T(8,128)(2,1)S(1)}, u32[]{:S(2)}, u32[]{:S(2)}) %collective-permute-start.2) | collective-permute-done | bytes 524320 | tf_op jit(solution)/shard_map/ppermute | solution.py:15
  23.3 1.8 %collective-permute-start.4 = (bf16[256,1024]{1,0:T(8,128)(2,1)S(1)}, bf16[256,1024]{1,0:T(8,128)(2,1)S(1)}, u32[]{:S(2)}, u32[]{:S(2)}) collective-permute-start(bf16[256,1024]{1,0:T(8,128)(2,1)S(1)} %constant_dynamic-slice_fusion), channel_id=1, source_target_pairs={{0,8},{4,12},{8,0},{12,4},{1,9},{5,13},{9,1},{13,5},{2,10},{6,14},... | collective-permute-start | bytes 1572872 | tf_op jit(solution)/shard_map/ppermute | solution.py:15
  25.1 1.5 %collective-permute-start.3 = (bf16[1024,256]{1,0:T(8,128)(2,1)S(1)}, bf16[1024,256]{1,0:T(8,128)(2,1)S(1)}, u32[]{:S(2)}, u32[]{:S(2)}) collective-permute-start(bf16[1024,256]{1,0:T(8,128)(2,1)S(1)} %collective-permute-done.2), channel_id=1, source_target_pairs={{0,16},{16,0},{1,17},{17,1},{2,18},{18,2},{3,19},{19,3},{4,20},{20... | collective-permute-start | bytes 1572872 | tf_op jit(solution)/shard_map/ppermute | solution.py:21
  26.6 9.9 %collective-permute-done.4 = bf16[256,1024]{1,0:T(8,128)(2,1)S(1)} collective-permute-done((bf16[256,1024]{1,0:T(8,128)(2,1)S(1)}, bf16[256,1024]{1,0:T(8,128)(2,1)S(1)}, u32[]{:S(2)}, u32[]{:S(2)}) %collective-permute-start.4) | collective-permute-done | bytes 524320 | tf_op jit(solution)/shard_map/ppermute | solution.py:15
  36.5 1.4 %collective-permute-start.5 = (bf16[256,1024]{1,0:T(8,128)(2,1)S(1)}, bf16[256,1024]{1,0:T(8,128)(2,1)}, u32[]{:S(2)}, u32[]{:S(2)}) collective-permute-start(bf16[256,1024]{1,0:T(8,128)(2,1)S(1)} %collective-permute-done.4), channel_id=1, source_target_pairs={{0,16},{16,0},{1,17},{17,1},{2,18},{18,2},{3,19},{19,3},{4,20},{20... | collective-permute-start | bytes 1572872 | tf_op jit(solution)/shard_map/ppermute | solution.py:21
  38.5 10.5 %collective-permute-done.5 = bf16[256,1024]{1,0:T(8,128)(2,1)} collective-permute-done((bf16[256,1024]{1,0:T(8,128)(2,1)S(1)}, bf16[256,1024]{1,0:T(8,128)(2,1)}, u32[]{:S(2)}, u32[]{:S(2)}) %collective-permute-start.5) | collective-permute-done | bytes 524320 | tf_op jit(solution)/shard_map/ppermute | solution.py:21
  49.0 2.1 %pad_maximum_fusion.3 = bf16[512,1024]{1,0:T(8,128)(2,1)} fusion(bf16[256,1024]{1,0:T(8,128)(2,1)} %collective-permute-done.5, bf16[256,1024]{1,0:T(8,128)(2,1)S(1)} %collective-permute-done.4), kind=kLoop, calls=%fused_computation.8 | loop fusion | flops 2097152 | bytes 2097152 | tf_op jit(solution)/shard_map/concatenate | solution.py:38
  51.1 1.3 constant_dynamic-slice_fusion.1
  53.3 4.0 %fusion.95 = f32[128,1024]{1,0:T(8,128)} fusion(bf16[128,1152]{0,1:T(8,128)(2,1)S(1)} %bitcast.44, bf16[128]{0:T(256)(128)(2,1)S(1)} %get-tuple-element.36, bf16[512,1024]{1,0:T(8,128)(2,1)} %collective-permute-done.1, bf16[512,1024]{1,0:T(8,128)(2,1)} %bitcast.58, bf16[1024,512]{1,0:T(8,128)(2,1)} %collective-permute-done, bf16[1024,512]{1,0:T(8,128)(2,1)} %bitcast.64), kind=kOutput, calls=%fused_computation.116 | convolution fusion | flops 546570240 | bytes 4981248 | tf_op jit(solution)/shard_map/dot_general | solution.py:88
  57.3 3.9 %fusion.93 = f32[128,1024]{1,0:T(8,128)} fusion(bf16[128,1152]{0,1:T(8,128)(2,1)S(1)} %bitcast.47, bf16[128]{0:T(256)(128)(2,1)S(1)} %get-tuple-element.27, bf16[512,1024]{1,0:T(8,128)(2,1)} %collective-permute-done.1, bf16[512,1024]{1,0:T(8,128)(2,1)} %bitcast.59, bf16[1024,512]{1,0:T(8,128)(2,1)} %collective-permute-done, bf16[1024,512]{1,0:T(8,128)(2,1)} %bitcast.65), kind=kOutput, calls=%fused_computation.114 | convolution fusion | flops 546570240 | bytes 4981248 | tf_op jit(solution)/shard_map/dot_general | solution.py:88
  61.3 3.9 %fusion.91 = f32[128,1024]{1,0:T(8,128)} fusion(bf16[128,1152]{0,1:T(8,128)(2,1)S(1)} %bitcast.50, bf16[128]{0:T(256)(128)(2,1)S(1)} %get-tuple-element.38, bf16[512,1024]{1,0:T(8,128)(2,1)} %collective-permute-done.1, bf16[512,1024]{1,0:T(8,128)(2,1)} %bitcast.60, bf16[1024,512]{1,0:T(8,128)(2,1)} %collective-permute-done, bf16[1024,512]{1,0:T(8,128)(2,1)} %bitcast.66), kind=kOutput, calls=%fused_computation.112 | convolution fusion | flops 546570240 | bytes 4981248 | tf_op jit(solution)/shard_map/dot_general | solution.py:88
  65.2 3.9 %fusion.89 = f32[128,1024]{1,0:T(8,128)} fusion(bf16[128,1152]{0,1:T(8,128)(2,1)S(1)} %bitcast.53, bf16[128]{0:T(256)(128)(2,1)S(1)} %get-tuple-element.23, bf16[512,1024]{1,0:T(8,128)(2,1)} %collective-permute-done.1, bf16[512,1024]{1,0:T(8,128)(2,1)} %bitcast.61, bf16[1024,512]{1,0:T(8,128)(2,1)} %collective-permute-done, bf16[1024,512]{1,0:T(8,128)(2,1)} %bitcast.67), kind=kOutput, calls=%fused_computation.110 | convolution fusion | flops 546570240 | bytes 4981248 | tf_op jit(solution)/shard_map/dot_general | solution.py:88
  69.6 1.3 constant_dynamic-update-slice_fusion.3
  71.1 2.4 %collective-permute-done.7 = bf16[512,1024]{1,0:T(8,128)(2,1)S(1)} collective-permute-done((bf16[512,1024]{1,0:T(8,128)(2,1)}, bf16[512,1024]{1,0:T(8,128)(2,1)S(1)}, u32[]{:S(2)}, u32[]{:S(2)}) %collective-permute-start.7) | collective-permute-done | bytes 1048608 | tf_op jit(solution)/shard_map/ppermute | solution.py:10
  74.8 2.7 %fusion.77 = f32[128,1024]{1,0:T(8,128)S(1)} fusion(bf16[1024,1024]{1,0:T(8,128)(2,1)} %copy-done.2, bf16[1024,1024]{1,0:T(8,128)(2,1)S(1)} %constant_dynamic-update-slice_fusion, bf16[128,1152]{0,1:T(8,128)(2,1)} %bitcast.51, bf16[128]{0:T(256)(128)(2,1)S(1)} %get-tuple-element.39), kind=kOutput, calls=%fused_computation.102 | convolution fusion | flops 538181632 | bytes 4980992 | tf_op jit(solution)/shard_map/dot_general | solution.py:88
  78.3 3.6 %collective-permute-start.10 = (bf16[128,1024]{1,0:T(8,128)(2,1)}, bf16[128,1024]{1,0:T(8,128)(2,1)}, u32[]{:S(2)}, u32[]{:S(2)}) collective-permute-start(bf16[128,1024]{1,0:T(8,128)(2,1)} %add_convert_fusion), channel_id=1, source_target_pairs={{0,3},{1,0},{2,1},{3,2},{4,7},{5,4},{6,5},{7,6},{8,11},{9,8},{10,9... | collective-permute-start | bytes 786440 | tf_op jit(solution)/shard_map/ppermute | solution.py:103
  81.9 2.7 %fusion.79 = f32[128,1024]{1,0:T(8,128)S(1)} fusion(bf16[1024,1024]{1,0:T(8,128)(2,1)} %copy-done.2, bf16[1024,1024]{1,0:T(8,128)(2,1)S(1)} %constant_dynamic-update-slice_fusion, bf16[128,1152]{0,1:T(8,128)(2,1)} %bitcast.48, bf16[128]{0:T(256)(128)(2,1)S(1)} %get-tuple-element.26), kind=kOutput, calls=%fused_computation.104 | convolution fusion | flops 538181632 | bytes 4980992 | tf_op jit(solution)/shard_map/dot_general | solution.py:88
  84.6 1.8 %add_convert_fusion.1 = bf16[128,1024]{1,0:T(8,128)(2,1)} fusion(f32[128,1024]{1,0:T(8,128)} %fusion.93, f32[128,1024]{1,0:T(8,128)S(1)} %fusion.79), kind=kLoop, calls=%fused_computation.94 | loop fusion | flops 262144 | bytes 1310720 | tf_op jit(solution)/shard_map/convert_element_type | solution.py:104
  86.4 2.5 %fusion.81 = f32[128,1024]{1,0:T(8,128)S(1)} fusion(bf16[1024,1024]{1,0:T(8,128)(2,1)} %copy-done.2, bf16[1024,1024]{1,0:T(8,128)(2,1)S(1)} %constant_dynamic-update-slice_fusion, bf16[128,1152]{0,1:T(8,128)(2,1)S(1)} %bitcast.45, bf16[128]{0:T(256)(128)(2,1)S(1)} %get-tuple-element.37), kind=kOutput, calls=%fused_computation.106 | convolution fusion | flops 538181632 | bytes 4981248 | tf_op jit(solution)/shard_map/dot_general | solution.py:88
  91.1 1.4 %fusion.133 = f32[128,1024]{1,0:T(8,128)S(1)} fusion(bf16[1024,1024]{1,0:T(8,128)(2,1)S(1)} %constant_dynamic-update-slice_fusion, bf16[128,1152]{0,1:T(8,128)(2,1)} %bitcast.54), kind=kOutput, calls=%fused_computation.142 | convolution fusion | flops 268435456 | bytes 2883584 | tf_op jit(solution)/shard_map/dot_general | solution.py:86
  92.6 13.2 %collective-permute-done.9 = bf16[128,1024]{1,0:T(8,128)(2,1)} collective-permute-done((bf16[128,1024]{1,0:T(8,128)(2,1)}, bf16[128,1024]{1,0:T(8,128)(2,1)}, u32[]{:S(2)}, u32[]{:S(2)}) %collective-permute-start.9) | collective-permute-done | bytes 262176 | tf_op jit(solution)/shard_map/ppermute | solution.py:103
  106.5 2.8 %convolution_convert_fusion.1 = bf16[128,1024]{1,0:T(8,128)(2,1)S(1)} fusion(bf16[128,1024]{1,0:T(8,128)(2,1)S(1)} %copy-done.4, bf16[128,1024]{1,0:T(8,128)(2,1)} %collective-permute-done.10, bf16[128,1024]{1,0:T(8,128)(2,1)} %collective-permute-done.9, bf16[128,1024]{1,0:T(8,128)(2,1)} %copy-done.11, f32[128,1024]{1,0:T(8,128)} %fusion.89, ...), kind=kOutput, calls=%fused_computation.4 | convolution fusion | flops 304758784 | bytes 4457216 | tf_op jit(solution)/shard_map/dot_general | solution.py:117
  109.4 14.8 %all_to_all.5 = bf16[16,8,1152]{2,1,0:T(8,128)(2,1)S(1)} all-to-all(bf16[16,8,1152]{2,1,0:T(8,128)(2,1)S(1)} %maximum_bitcast_fusion), channel_id=1, replica_groups=mesh['rep'=2,'member'=4,'tp'=4] {'member','tp'}, dimensions={0} | all-to-all | bytes 589824 | tf_op jit(solution)/shard_map/all_to_all | solution.py:124
  (82 shorter events, 15.2 us)
Async XLA Ops:
  7.2 117.5 %copy-start = (bf16[1024,128]{1,0:T(8,128)(2,1)S(1)}, bf16[1024,128]{1,0:T(8,128)(2,1)}, u32[]{:S(2)}) copy-start(bf16[1024,128]{1,0:T(8,128)(2,1)} %param.15) | copy-start | bytes 786436
  7.2 7.8 %copy-start.1 = (f32[2,1024]{1,0:T(2,128)S(1)}, f32[2,1024]{1,0:T(2,128)}, u32[]{:S(2)}) copy-start(f32[2,1024]{1,0:T(2,128)} %param.11) | copy-start | bytes 24580
  7.2 43.9 %all-gather.2.cloned.1.call-start = ((), (), s32[]{:S(2)}) async-start(), calls=%async_computation.1 | async-start | bytes 1474560 | tf_op jit(solution)/shard_map/all_gather | solution.py:72
  8.3 15.0 %collective-permute-start.2 = (bf16[1024,256]{1,0:T(8,128)(2,1)S(1)}, bf16[1024,256]{1,0:T(8,128)(2,1)S(1)}, u32[]{:S(2)}, u32[]{:S(2)}) collective-permute-start(bf16[1024,256]{1,0:T(8,128)(2,1)S(1)} %dynamic-slice_bitcast_fusion), channel_id=1, source_target_pairs={{0,8},{4,12},{8,0},{12,4},{1,9},{5,13},{9,1},{13,5},{2,10},{6,14},... | collective-permute-start | bytes 1572872 | tf_op jit(solution)/shard_map/ppermute | solution.py:15
  15.8 7.4 %copy-start.12 = (bf16[1,512,1024]{2,1,0:T(8,128)(2,1)S(1)}, bf16[1,512,1024]{2,1,0:T(8,128)(2,1)}, u32[]{:S(2)}) copy-start(bf16[1,512,1024]{2,1,0:T(8,128)(2,1)} %param.13) | copy-start | bytes 3145732
  23.3 13.2 %collective-permute-start.4 = (bf16[256,1024]{1,0:T(8,128)(2,1)S(1)}, bf16[256,1024]{1,0:T(8,128)(2,1)S(1)}, u32[]{:S(2)}, u32[]{:S(2)}) collective-permute-start(bf16[256,1024]{1,0:T(8,128)(2,1)S(1)} %constant_dynamic-slice_fusion), channel_id=1, source_target_pairs={{0,8},{4,12},{8,0},{12,4},{1,9},{5,13},{9,1},{13,5},{2,10},{6,14},... | collective-permute-start | bytes 1572872 | tf_op jit(solution)/shard_map/ppermute | solution.py:15
  25.1 13.3 %collective-permute-start.3 = (bf16[1024,256]{1,0:T(8,128)(2,1)S(1)}, bf16[1024,256]{1,0:T(8,128)(2,1)S(1)}, u32[]{:S(2)}, u32[]{:S(2)}) collective-permute-start(bf16[1024,256]{1,0:T(8,128)(2,1)S(1)} %collective-permute-done.2), channel_id=1, source_target_pairs={{0,16},{16,0},{1,17},{17,1},{2,18},{18,2},{3,19},{19,3},{4,20},{20... | collective-permute-start | bytes 1572872 | tf_op jit(solution)/shard_map/ppermute | solution.py:21
  36.5 12.5 %collective-permute-start.5 = (bf16[256,1024]{1,0:T(8,128)(2,1)S(1)}, bf16[256,1024]{1,0:T(8,128)(2,1)}, u32[]{:S(2)}, u32[]{:S(2)}) collective-permute-start(bf16[256,1024]{1,0:T(8,128)(2,1)S(1)} %collective-permute-done.4), channel_id=1, source_target_pairs={{0,16},{16,0},{1,17},{17,1},{2,18},{18,2},{3,19},{19,3},{4,20},{20... | collective-permute-start | bytes 1572872 | tf_op jit(solution)/shard_map/ppermute | solution.py:21
  37.9 15.4 %collective-permute-start.1 = (bf16[512,1024]{1,0:T(8,128)(2,1)}, bf16[512,1024]{1,0:T(8,128)(2,1)}, u32[]{:S(2)}, u32[]{:S(2)}) collective-permute-start(bf16[512,1024]{1,0:T(8,128)(2,1)} %bitcast.57), channel_id=1, source_target_pairs={{0,4},{4,0},{8,12},{12,8},{1,5},{5,1},{9,13},{13,9},{2,6},{6,2},{1... | collective-permute-start | bytes 3145736 | tf_op jit(solution)/shard_map/ppermute | solution.py:10
  37.9 15.4 %collective-permute-start = (bf16[1024,512]{1,0:T(8,128)(2,1)}, bf16[1024,512]{1,0:T(8,128)(2,1)}, u32[]{:S(2)}, u32[]{:S(2)}) collective-permute-start(bf16[1024,512]{1,0:T(8,128)(2,1)} %bitcast.63), channel_id=1, source_target_pairs={{0,4},{4,0},{8,12},{12,8},{1,5},{5,1},{9,13},{13,9},{2,6},{6,2},{1... | collective-permute-start | bytes 3145736 | tf_op jit(solution)/shard_map/ppermute | solution.py:10
  52.6 4.7 %copy-start.5 = (bf16[1,128,1152]{1,2,0:T(8,128)(2,1)}, bf16[1,128,1152]{1,2,0:T(8,128)(2,1)S(1)}, u32[]{:S(2)}) copy-start(bf16[1,128,1152]{1,2,0:T(8,128)(2,1)S(1)} %copy.19) | copy-start | bytes 884740
  52.8 12.4 %copy-start.9 = (bf16[1,128,1152]{1,2,0:T(8,128)(2,1)}, bf16[1,128,1152]{1,2,0:T(8,128)(2,1)S(1)}, u32[]{:S(2)}) copy-start(bf16[1,128,1152]{1,2,0:T(8,128)(2,1)S(1)} %copy.22) | copy-start | bytes 884740
  53.0 4.3 %copy-start.7 = (bf16[1,128,1152]{1,2,0:T(8,128)(2,1)}, bf16[1,128,1152]{1,2,0:T(8,128)(2,1)S(1)}, u32[]{:S(2)}) copy-start(bf16[1,128,1152]{1,2,0:T(8,128)(2,1)S(1)} %copy.20) | copy-start | bytes 884740
  53.3 8.0 %copy-start.8 = (bf16[1,128,1152]{1,2,0:T(8,128)(2,1)}, bf16[1,128,1152]{1,2,0:T(8,128)(2,1)S(1)}, u32[]{:S(2)}) copy-start(bf16[1,128,1152]{1,2,0:T(8,128)(2,1)S(1)} %copy.21) | copy-start | bytes 884740
  69.1 4.3 %collective-permute-start.7 = (bf16[512,1024]{1,0:T(8,128)(2,1)}, bf16[512,1024]{1,0:T(8,128)(2,1)S(1)}, u32[]{:S(2)}, u32[]{:S(2)}) collective-permute-start(bf16[512,1024]{1,0:T(8,128)(2,1)} %pad_maximum_fusion.3), channel_id=1, source_target_pairs={{0,4},{4,0},{8,12},{12,8},{1,5},{5,1},{9,13},{13,9},{2,6},{6,2},{1... | collective-permute-start | bytes 3145736 | tf_op jit(solution)/shard_map/ppermute | solution.py:10
  69.1 4.4 %collective-permute-start.6 = (bf16[1024,512]{1,0:T(8,128)(2,1)S(1)}, bf16[1024,512]{1,0:T(8,128)(2,1)S(1)}, u32[]{:S(2)}, u32[]{:S(2)}) collective-permute-start(bf16[1024,512]{1,0:T(8,128)(2,1)S(1)} %pad_maximum_fusion.2), channel_id=1, source_target_pairs={{0,4},{4,0},{8,12},{12,8},{1,5},{5,1},{9,13},{13,9},{2,6},{6,2},{1... | collective-permute-start | bytes 3145736 | tf_op jit(solution)/shard_map/ppermute | solution.py:10
  73.5 1.3 copy-start.2
  74.8 2.7 %copy-start.10 = (f32[128,1024]{1,0:T(8,128)S(1)}, f32[128,1024]{1,0:T(8,128)}, u32[]{:S(2)}) copy-start(f32[128,1024]{1,0:T(8,128)} %fusion.91) | copy-start | bytes 1572868
  78.3 14.3 %collective-permute-start.10 = (bf16[128,1024]{1,0:T(8,128)(2,1)}, bf16[128,1024]{1,0:T(8,128)(2,1)}, u32[]{:S(2)}, u32[]{:S(2)}) collective-permute-start(bf16[128,1024]{1,0:T(8,128)(2,1)} %add_convert_fusion), channel_id=1, source_target_pairs={{0,3},{1,0},{2,1},{3,2},{4,7},{5,4},{6,5},{7,6},{8,11},{9,8},{10,9... | collective-permute-start | bytes 786440 | tf_op jit(solution)/shard_map/ppermute | solution.py:103
  81.9 4.5 %copy-start.6 = (bf16[1,128,1152]{1,2,0:T(8,128)(2,1)S(1)}, bf16[1,128,1152]{1,2,0:T(8,128)(2,1)}, u32[]{:S(2)}) copy-start(bf16[1,128,1152]{1,2,0:T(8,128)(2,1)} %copy-done.5) | copy-start | bytes 884740
  86.4 19.4 %collective-permute-start.9 = (bf16[128,1024]{1,0:T(8,128)(2,1)}, bf16[128,1024]{1,0:T(8,128)(2,1)}, u32[]{:S(2)}, u32[]{:S(2)}) collective-permute-start(bf16[128,1024]{1,0:T(8,128)(2,1)} %add_convert_fusion.1), channel_id=1, source_target_pairs={{0,2},{1,3},{2,0},{3,1},{4,6},{5,7},{6,4},{7,5},{8,10},{9,11},{10,... | collective-permute-start | bytes 786440 | tf_op jit(solution)/shard_map/ppermute | solution.py:103
  88.9 17.6 %copy-start.4 = (bf16[128,1024]{1,0:T(8,128)(2,1)S(1)}, bf16[128,1024]{1,0:T(8,128)(2,1)}, u32[]{:S(2)}) copy-start(bf16[128,1024]{1,0:T(8,128)(2,1)} %param.8) | copy-start | bytes 786436
  90.1 15.7 %collective-permute-start.8 = (bf16[128,1024]{1,0:T(8,128)(2,1)S(1)}, bf16[128,1024]{1,0:T(8,128)(2,1)S(1)}, u32[]{:S(2)}, u32[]{:S(2)}) collective-permute-start(bf16[128,1024]{1,0:T(8,128)(2,1)S(1)} %add_convert_fusion.2), channel_id=1, source_target_pairs={{0,1},{1,2},{2,3},{3,0},{4,5},{5,6},{6,7},{7,4},{8,9},{9,10},{10,1... | collective-permute-start | bytes 786440 | tf_op jit(solution)/shard_map/ppermute | solution.py:103
  106.5 18.1 %copy-start.14 = (f32[1024]{0:T(1024)S(1)}, f32[1024]{0:T(1024)}, u32[]{:S(2)}) copy-start(f32[1024]{0:T(1024)} %param.14) | copy-start | bytes 12292
  (4 other events, 3.4 us)
Sparse Core Ops, SparseCore 0:
  17.0 30.7 all-gather.1

commit v16 on v14

--- a/solution.py
+++ b/solution.py
@@ -35,7 +35,13 @@
         lax.dynamic_slice_in_dim(down, rep_here * share, share, axis=0), "member", chips_back
     )
     up_parts = swap_parts(got_up)
-    return jnp.concatenate(up_parts, axis=1), jnp.concatenate(swap_parts(got_down), axis=0)
+    down_parts = swap_parts(got_down)
+    partner_up = [from_partner(part, "member", 0) for part in up_parts]
+    partner_down = [from_partner(part, "member", 0) for part in down_parts]
+    return (
+        jnp.concatenate(up_parts + partner_up, axis=1),
+        jnp.concatenate(down_parts + partner_down, axis=0),
+    )
 
 
 def rms_scale(values, gain):
@@ -90,7 +96,7 @@
     terms = [apply_pair(*own_block)]
     for block_member, up_here, down_here in fetched:
         terms, up_here, down_here = lax.optimization_barrier((terms, up_here, down_here))
-        terms = terms + [apply_pair(block_member, up_here, down_here)]
+        terms = terms + [apply_block(block_member, up_here, down_here)]
     tp_here = lax.axis_index("tp")
     by_target = [term.reshape(n_tp, rows_here, feature_width) for term in terms]
 

time: 123 us -> 121 us (0.984)
  waiting for transfers between devices: 53.3 us -> 48.5 us
  other arithmetic: 10.3 us -> 13.7 us
    ppermute x4 -> x6, waiting for transfers between devices: 4 us -> 0.02 us  [from_partner(): lax.ppermute(value, axis, [(i, i ^ 1 << distance) for i in range(lax.axis...]
    concatenate x2, other arithmetic: 2.11 us -> 5.49 us  [the longest x1 2.84 us: fetch_shared(): jnp.concatenate(down_parts + partner_down, axis=0)]
  transfers between devices with their start and end apart: 12 -> 14, of which waited for: 8 -> 5; matrix products, arithmetic and copies ran while one was open for 8% -> 12% of each run, Pallas kernels for 0% -> 0%
where the time goes in v16:
time: 121 us
  waiting for transfers between devices  48.5 us (40%)
  blocking collectives  15.2 us (13%)
  between operations  14.3 us (12%)
  matrix products  13.9 us (11%)
  other arithmetic  13.7 us (11%)
  starting transfers between devices  13.4 us (11%)
  local copies, waits for them, and re-layouts  1.97 us (2%)
    ppermute x3, waiting for transfers between devices, local(): lax.ppermute(slice_for((tp_here + shift) % n_tp).astype(PARTIAL_DTYPE), '...  22.2 us
    ppermute x2, waiting for transfers between devices, from_chip_behind(): lax.ppermute(value, axis, [(i, (i + 2 * chips_back) % size) for i in rang...  15.7 us
    all_to_all x1, blocking collectives, local(): lax.all_to_all(jnp.concatenate([packed, spot_lanes], axis=1).reshape(n_de...  15.2 us
    dot_general x2, matrix products, apply_block(): return jnp.dot(hidden, down_here, preferred_element_type=jnp.float32)  11.2 us
    ppermute x2, waiting for transfers between devices, swap_parts(): lax.ppermute(value, 'rep', [(i, (i + step) % n_rep) for i in range(n_rep)])  10.6 us
    ppermute x2, starting transfers between devices, from_chip_behind(): lax.ppermute(value, axis, [(i, (i + 2 * chips_back) % size) for i in rang...  4.84 us
    ppermute x3, starting transfers between devices, local(): lax.ppermute(slice_for((tp_here + shift) % n_tp).astype(PARTIAL_DTYPE), '...  4.61 us
    ppermute x2, starting transfers between devices, swap_parts(): lax.ppermute(value, 'rep', [(i, (i + step) % n_rep) for i in range(n_rep)])  2.88 us
  transfers between devices with their start and end apart: 14, of which 5 were waited for; matrix products, arithmetic and copies ran while one was open for 12% of the time, Pallas kernels for 0%

profile of v16, /device:TPU:0, one launch (start us, length us, event | category | flops | bytes accessed | tf_op | source)
XLA Modules:
  0.0 120.9 jit_solution(15835392867965463078)
XLA Ops:
  7.2 1.1 dynamic-slice_bitcast_fusion
  8.3 3.0 %collective-permute-start.2 = (bf16[1024,256]{1,0:T(8,128)(2,1)S(1)}, bf16[1024,256]{1,0:T(8,128)(2,1)S(1)}, u32[]{:S(2)}, u32[]{:S(2)}) collective-permute-start(bf16[1024,256]{1,0:T(8,128)(2,1)S(1)} %dynamic-slice_bitcast_fusion), channel_id=1, source_target_pairs={{0,8},{4,12},{8,0},{12,4},{1,9},{5,13},{9,1},{13,5},{2,10},{6,14},... | collective-permute-start | bytes 1572872 | tf_op jit(solution)/shard_map/ppermute | solution.py:15
  13.8 1.1 fusion.50
  15.1 0.8 gather_fusion
  16.2 0.7 pad_maximum_fusion.2
  16.9 6.4 %collective-permute-done.2 = bf16[1024,256]{1,0:T(8,128)(2,1)S(1)} collective-permute-done((bf16[1024,256]{1,0:T(8,128)(2,1)S(1)}, bf16[1024,256]{1,0:T(8,128)(2,1)S(1)}, u32[]{:S(2)}, u32[]{:S(2)}) %collective-permute-start.2) | collective-permute-done | bytes 524320 | tf_op jit(solution)/shard_map/ppermute | solution.py:15
  23.3 1.8 %collective-permute-start.6 = (bf16[256,1024]{1,0:T(8,128)(2,1)S(1)}, bf16[256,1024]{1,0:T(8,128)(2,1)S(1)}, u32[]{:S(2)}, u32[]{:S(2)}) collective-permute-start(bf16[256,1024]{1,0:T(8,128)(2,1)S(1)} %constant_dynamic-slice_fusion), channel_id=1, source_target_pairs={{0,8},{4,12},{8,0},{12,4},{1,9},{5,13},{9,1},{13,5},{2,10},{6,14},... | collective-permute-start | bytes 1572872 | tf_op jit(solution)/shard_map/ppermute | solution.py:15
  25.1 1.5 %collective-permute-start.3 = (bf16[1024,256]{1,0:T(8,128)(2,1)S(1)}, bf16[1024,256]{1,0:T(8,128)(2,1)S(1)}, u32[]{:S(2)}, u32[]{:S(2)}) collective-permute-start(bf16[1024,256]{1,0:T(8,128)(2,1)S(1)} %collective-permute-done.2), channel_id=1, source_target_pairs={{0,16},{16,0},{1,17},{17,1},{2,18},{18,2},{3,19},{19,3},{4,20},{20... | collective-permute-start | bytes 1572872 | tf_op jit(solution)/shard_map/ppermute | solution.py:21
  27.1 9.4 %collective-permute-done.6 = bf16[256,1024]{1,0:T(8,128)(2,1)S(1)} collective-permute-done((bf16[256,1024]{1,0:T(8,128)(2,1)S(1)}, bf16[256,1024]{1,0:T(8,128)(2,1)S(1)}, u32[]{:S(2)}, u32[]{:S(2)}) %collective-permute-start.6) | collective-permute-done | bytes 524320 | tf_op jit(solution)/shard_map/ppermute | solution.py:15
  36.5 1.4 %collective-permute-start.7 = (bf16[256,1024]{1,0:T(8,128)(2,1)S(1)}, bf16[256,1024]{1,0:T(8,128)(2,1)}, u32[]{:S(2)}, u32[]{:S(2)}) collective-permute-start(bf16[256,1024]{1,0:T(8,128)(2,1)S(1)} %collective-permute-done.6), channel_id=1, source_target_pairs={{0,16},{16,0},{1,17},{17,1},{2,18},{18,2},{3,19},{19,3},{4,20},{20... | collective-permute-start | bytes 1572872 | tf_op jit(solution)/shard_map/ppermute | solution.py:21
  38.4 10.6 %collective-permute-done.7 = bf16[256,1024]{1,0:T(8,128)(2,1)} collective-permute-done((bf16[256,1024]{1,0:T(8,128)(2,1)S(1)}, bf16[256,1024]{1,0:T(8,128)(2,1)}, u32[]{:S(2)}, u32[]{:S(2)}) %collective-permute-start.7) | collective-permute-done | bytes 524320 | tf_op jit(solution)/shard_map/ppermute | solution.py:21
  49.0 2.7 %pad_maximum_fusion = bf16[1024,1024]{1,0:T(8,128)(2,1)} fusion(bf16[1024,256]{1,0:T(8,128)(2,1)} %collective-permute-done.5, bf16[1024,256]{1,0:T(8,128)(2,1)S(1)} %collective-permute-done.4, bf16[1024,256]{1,0:T(8,128)(2,1)S(1)} %collective-permute-done.3, bf16[1024,256]{1,0:T(8,128)(2,1)S(1)} %collective-permute-done.2), kind=kLoop, calls=%fused_computation.27 | loop fusion | flops 8388608 | bytes 4194304 | tf_op jit(solution)/shard_map/concatenate | solution.py:42
  51.6 1.1 fusion.68
  52.8 4.9 %fusion.20 = f32[512,1024]{1,0:T(8,128)S(1)} fusion(bf16[512,1024]{1,0:T(8,128)(2,1)} %collective-permute-done.1, bf16[512,1024]{1,0:T(8,128)(2,1)} %bitcast.39, bf16[1024,512]{1,0:T(8,128)(2,1)} %collective-permute-done, bf16[1024,512]{1,0:T(8,128)(2,1)} %bitcast.42, bf16[512,1152]{1,0:T(8,128)(2,1)} %all-gather.2.cloned.1.call-done, ...), kind=kOutput, calls=%fused_computation.23 | convolution fusion | flops 2161115136 | bytes 7341056 | tf_op jit(solution)/shard_map/dot_general | solution.py:89
  57.7 2.8 %pad_maximum_fusion.1 = bf16[1024,1024]{1,0:T(8,128)(2,1)} fusion(bf16[256,1024]{1,0:T(8,128)(2,1)} %collective-permute-done.9, bf16[256,1024]{1,0:T(8,128)(2,1)} %collective-permute-done.8, bf16[256,1024]{1,0:T(8,128)(2,1)} %collective-permute-done.7, bf16[256,1024]{1,0:T(8,128)(2,1)S(1)} %collective-permute-done.6), kind=kLoop, calls=%fused_computation.28 | loop fusion | flops 8388608 | bytes 4194304 | tf_op jit(solution)/shard_map/concatenate | solution.py:43
  60.5 6.3 %fusion.30 = f32[512,1024]{1,0:T(8,128)} fusion(bf16[1024,1024]{1,0:T(8,128)(2,1)} %pad_maximum_fusion.1, bf16[1024,1024]{1,0:T(8,128)(2,1)} %pad_maximum_fusion, bf16[512,1152]{1,0:T(8,128)(2,1)} %all-gather.2.cloned.1.call-done, bf16[512]{0:T(512)(128)(2,1)S(1)} %get-tuple-element.12), kind=kOutput, calls=%fused_computation.34 | convolution fusion | flops 2152726528 | bytes 7341056 | tf_op jit(solution)/shard_map/dot_general | solution.py:89
  66.8 2.3 %fusion.58 = (bf16[128,1024]{1,0:T(8,128)(2,1)S(1)}, bf16[128,1024]{1,0:T(8,128)(2,1)}, bf16[128,1024]{1,0:T(8,128)(2,1)}) fusion(f32[4,128,1024]{2,1,0:T(8,128)} %bitcast.34, s32[]{:T(128)S(6)} %select_n.81, f32[4,128,1024]{2,1,0:T(8,128)S(1)} %bitcast.32, s32[]{:T(128)S(6)} %select_n.85, s32[]{:T(128)S(6)} %select_n.83), kind=kLoop, calls=%fused_computation.67 | loop fusion | flops 786432 | bytes 3932172 | tf_op jit(solution)/shard_map/convert_element_type | solution.py:113
  69.2 3.6 %collective-permute-start.12 = (bf16[128,1024]{1,0:T(8,128)(2,1)}, bf16[128,1024]{1,0:T(8,128)(2,1)S(1)}, u32[]{:S(2)}, u32[]{:S(2)}) collective-permute-start(bf16[128,1024]{1,0:T(8,128)(2,1)} %get-tuple-element.15), channel_id=1, source_target_pairs={{0,3},{1,0},{2,1},{3,2},{4,7},{5,4},{6,5},{7,6},{8,11},{9,8},{10,9... | collective-permute-start | bytes 786440 | tf_op jit(solution)/shard_map/ppermute | solution.py:112
  72.8 1.0 collective-permute-start.10
  73.8 6.0 %collective-permute-done.12 = bf16[128,1024]{1,0:T(8,128)(2,1)S(1)} collective-permute-done((bf16[128,1024]{1,0:T(8,128)(2,1)}, bf16[128,1024]{1,0:T(8,128)(2,1)S(1)}, u32[]{:S(2)}, u32[]{:S(2)}) %collective-permute-start.12) | collective-permute-done | bytes 262176 | tf_op jit(solution)/shard_map/ppermute | solution.py:112
  79.8 16.2 %collective-permute-done.11 = bf16[128,1024]{1,0:T(8,128)(2,1)S(1)} collective-permute-done((bf16[128,1024]{1,0:T(8,128)(2,1)}, bf16[128,1024]{1,0:T(8,128)(2,1)S(1)}, u32[]{:S(2)}, u32[]{:S(2)}) %collective-permute-start.11) | collective-permute-done | bytes 262176 | tf_op jit(solution)/shard_map/ppermute | solution.py:112
  96.0 1.4 %convolution_convert_fusion.1 = bf16[128,1024]{1,0:T(8,128)(2,1)S(1)} fusion(bf16[128,1024]{1,0:T(8,128)(2,1)S(1)} %copy-done.2, bf16[128,1024]{1,0:T(8,128)(2,1)S(1)} %collective-permute-done.12, bf16[128,1024]{1,0:T(8,128)(2,1)S(1)} %collective-permute-done.11, bf16[128,1024]{1,0:T(8,128)(2,1)} %collective-permute-done.10, f32[4,128,1024]{2,1,0:T(8,128)} %bitcast.35, ...), kind=kOutput, calls=%fused_computation.30 | convolution fusion | flops 35012608 | bytes 2359812 | tf_op jit(solution)/shard_map/dot_general | solution.py:126
  97.4 15.2 %all_to_all.5 = bf16[16,8,1152]{2,1,0:T(8,128)(2,1)S(1)} all-to-all(bf16[16,8,1152]{2,1,0:T(8,128)(2,1)S(1)} %maximum_bitcast_fusion), channel_id=1, replica_groups=mesh['rep'=2,'member'=4,'tp'=4] {'member','tp'}, dimensions={0} | all-to-all | bytes 589824 | tf_op jit(solution)/shard_map/all_to_all | solution.py:133
  113.1 0.9 fusion.24
  (50 shorter events, 4.4 us)
Async XLA Ops:
  7.2 105.9 %copy-start = (bf16[1024,128]{1,0:T(8,128)(2,1)S(1)}, bf16[1024,128]{1,0:T(8,128)(2,1)}, u32[]{:S(2)}) copy-start(bf16[1024,128]{1,0:T(8,128)(2,1)} %param.15) | copy-start | bytes 786436
  7.2 7.8 %copy-start.1 = (f32[2,1024]{1,0:T(2,128)S(1)}, f32[2,1024]{1,0:T(2,128)}, u32[]{:S(2)}) copy-start(f32[2,1024]{1,0:T(2,128)} %param.11) | copy-start | bytes 24580
  7.2 44.5 %all-gather.2.cloned.1.call-start = ((), (), s32[]{:S(2)}) async-start(), calls=%async_computation.1 | async-start | bytes 1474560 | tf_op jit(solution)/shard_map/all_gather | solution.py:78
  8.3 15.0 %collective-permute-start.2 = (bf16[1024,256]{1,0:T(8,128)(2,1)S(1)}, bf16[1024,256]{1,0:T(8,128)(2,1)S(1)}, u32[]{:S(2)}, u32[]{:S(2)}) collective-permute-start(bf16[1024,256]{1,0:T(8,128)(2,1)S(1)} %dynamic-slice_bitcast_fusion), channel_id=1, source_target_pairs={{0,8},{4,12},{8,0},{12,4},{1,9},{5,13},{9,1},{13,5},{2,10},{6,14},... | collective-permute-start | bytes 1572872 | tf_op jit(solution)/shard_map/ppermute | solution.py:15
  15.0 0.8 copy-start.4
  15.0 1.0 copy-start.2
  15.8 7.4 %copy-start.3 = (bf16[1,512,1024]{2,1,0:T(8,128)(2,1)S(1)}, bf16[1,512,1024]{2,1,0:T(8,128)(2,1)}, u32[]{:S(2)}) copy-start(bf16[1,512,1024]{2,1,0:T(8,128)(2,1)} %param.13) | copy-start | bytes 3145732
  23.3 13.2 %collective-permute-start.6 = (bf16[256,1024]{1,0:T(8,128)(2,1)S(1)}, bf16[256,1024]{1,0:T(8,128)(2,1)S(1)}, u32[]{:S(2)}, u32[]{:S(2)}) collective-permute-start(bf16[256,1024]{1,0:T(8,128)(2,1)S(1)} %constant_dynamic-slice_fusion), channel_id=1, source_target_pairs={{0,8},{4,12},{8,0},{12,4},{1,9},{5,13},{9,1},{13,5},{2,10},{6,14},... | collective-permute-start | bytes 1572872 | tf_op jit(solution)/shard_map/ppermute | solution.py:15
  25.1 12.8 %collective-permute-start.3 = (bf16[1024,256]{1,0:T(8,128)(2,1)S(1)}, bf16[1024,256]{1,0:T(8,128)(2,1)S(1)}, u32[]{:S(2)}, u32[]{:S(2)}) collective-permute-start(bf16[1024,256]{1,0:T(8,128)(2,1)S(1)} %collective-permute-done.2), channel_id=1, source_target_pairs={{0,16},{16,0},{1,17},{17,1},{2,18},{18,2},{3,19},{19,3},{4,20},{20... | collective-permute-start | bytes 1572872 | tf_op jit(solution)/shard_map/ppermute | solution.py:21
  26.6 26.1 %collective-permute-start.1 = (bf16[512,1024]{1,0:T(8,128)(2,1)}, bf16[512,1024]{1,0:T(8,128)(2,1)}, u32[]{:S(2)}, u32[]{:S(2)}) collective-permute-start(bf16[512,1024]{1,0:T(8,128)(2,1)} %bitcast.38), channel_id=1, source_target_pairs={{0,4},{4,0},{8,12},{12,8},{1,5},{5,1},{9,13},{13,9},{2,6},{6,2},{1... | collective-permute-start | bytes 3145736 | tf_op jit(solution)/shard_map/ppermute | solution.py:10
  26.6 26.1 %collective-permute-start = (bf16[1024,512]{1,0:T(8,128)(2,1)}, bf16[1024,512]{1,0:T(8,128)(2,1)}, u32[]{:S(2)}, u32[]{:S(2)}) collective-permute-start(bf16[1024,512]{1,0:T(8,128)(2,1)} %bitcast.41), channel_id=1, source_target_pairs={{0,4},{4,0},{8,12},{12,8},{1,5},{5,1},{9,13},{13,9},{2,6},{6,2},{1... | collective-permute-start | bytes 3145736 | tf_op jit(solution)/shard_map/ppermute | solution.py:10
  27.1 10.8 %collective-permute-start.4 = (bf16[1024,256]{1,0:T(8,128)(2,1)S(1)}, bf16[1024,256]{1,0:T(8,128)(2,1)S(1)}, u32[]{:S(2)}, u32[]{:S(2)}) collective-permute-start(bf16[1024,256]{1,0:T(8,128)(2,1)S(1)} %collective-permute-done.2), channel_id=1, source_target_pairs={{0,4},{4,0},{8,12},{12,8},{1,5},{5,1},{9,13},{13,9},{2,6},{6,2},{1... | collective-permute-start | bytes 1572872 | tf_op jit(solution)/shard_map/ppermute | solution.py:10
  36.5 12.5 %collective-permute-start.7 = (bf16[256,1024]{1,0:T(8,128)(2,1)S(1)}, bf16[256,1024]{1,0:T(8,128)(2,1)}, u32[]{:S(2)}, u32[]{:S(2)}) collective-permute-start(bf16[256,1024]{1,0:T(8,128)(2,1)S(1)} %collective-permute-done.6), channel_id=1, source_target_pairs={{0,16},{16,0},{1,17},{17,1},{2,18},{18,2},{3,19},{19,3},{4,20},{20... | collective-permute-start | bytes 1572872 | tf_op jit(solution)/shard_map/ppermute | solution.py:21
  37.9 11.1 %collective-permute-start.5 = (bf16[1024,256]{1,0:T(8,128)(2,1)S(1)}, bf16[1024,256]{1,0:T(8,128)(2,1)}, u32[]{:S(2)}, u32[]{:S(2)}) collective-permute-start(bf16[1024,256]{1,0:T(8,128)(2,1)S(1)} %collective-permute-done.3), channel_id=1, source_target_pairs={{0,4},{4,0},{8,12},{12,8},{1,5},{5,1},{9,13},{13,9},{2,6},{6,2},{1... | collective-permute-start | bytes 1572872 | tf_op jit(solution)/shard_map/ppermute | solution.py:10
  37.9 19.8 %collective-permute-start.8 = (bf16[256,1024]{1,0:T(8,128)(2,1)S(1)}, bf16[256,1024]{1,0:T(8,128)(2,1)}, u32[]{:S(2)}, u32[]{:S(2)}) collective-permute-start(bf16[256,1024]{1,0:T(8,128)(2,1)S(1)} %collective-permute-done.6), channel_id=1, source_target_pairs={{0,4},{4,0},{8,12},{12,8},{1,5},{5,1},{9,13},{13,9},{2,6},{6,2},{1... | collective-permute-start | bytes 1572872 | tf_op jit(solution)/shard_map/ppermute | solution.py:10
  49.0 8.7 %collective-permute-start.9 = (bf16[256,1024]{1,0:T(8,128)(2,1)}, bf16[256,1024]{1,0:T(8,128)(2,1)}, u32[]{:S(2)}, u32[]{:S(2)}) collective-permute-start(bf16[256,1024]{1,0:T(8,128)(2,1)} %collective-permute-done.7), channel_id=1, source_target_pairs={{0,4},{4,0},{8,12},{12,8},{1,5},{5,1},{9,13},{13,9},{2,6},{6,2},{1... | collective-permute-start | bytes 1572872 | tf_op jit(solution)/shard_map/ppermute | solution.py:10
  69.2 43.9 %copy-start.5 = (f32[1024]{0:T(1024)S(1)}, f32[1024]{0:T(1024)}, u32[]{:S(2)}) copy-start(f32[1024]{0:T(1024)} %param.14) | copy-start | bytes 12292
  69.2 10.6 %collective-permute-start.12 = (bf16[128,1024]{1,0:T(8,128)(2,1)}, bf16[128,1024]{1,0:T(8,128)(2,1)S(1)}, u32[]{:S(2)}, u32[]{:S(2)}) collective-permute-start(bf16[128,1024]{1,0:T(8,128)(2,1)} %get-tuple-element.15), channel_id=1, source_target_pairs={{0,3},{1,0},{2,1},{3,2},{4,7},{5,4},{6,5},{7,6},{8,11},{9,8},{10,9... | collective-permute-start | bytes 786440 | tf_op jit(solution)/shard_map/ppermute | solution.py:112
  72.8 23.2 %collective-permute-start.11 = (bf16[128,1024]{1,0:T(8,128)(2,1)}, bf16[128,1024]{1,0:T(8,128)(2,1)S(1)}, u32[]{:S(2)}, u32[]{:S(2)}) collective-permute-start(bf16[128,1024]{1,0:T(8,128)(2,1)} %get-tuple-element.16), channel_id=1, source_target_pairs={{0,2},{1,3},{2,0},{3,1},{4,6},{5,7},{6,4},{7,5},{8,10},{9,11},{10,... | collective-permute-start | bytes 786440 | tf_op jit(solution)/shard_map/ppermute | solution.py:112
  72.8 23.2 %collective-permute-start.10 = (bf16[128,1024]{1,0:T(8,128)(2,1)S(1)}, bf16[128,1024]{1,0:T(8,128)(2,1)}, u32[]{:S(2)}, u32[]{:S(2)}) collective-permute-start(bf16[128,1024]{1,0:T(8,128)(2,1)S(1)} %get-tuple-element.14), channel_id=1, source_target_pairs={{0,1},{1,2},{2,3},{3,0},{4,5},{5,6},{6,7},{7,4},{8,9},{9,10},{10,1... | collective-permute-start | bytes 786440 | tf_op jit(solution)/shard_map/ppermute | solution.py:112
  113.1 1.0 copy-start.6
Sparse Core Ops, SparseCore 0:
  17.0 30.7 all-gather.1

commit v17 on v16

--- a/solution.py
+++ b/solution.py
@@ -97,23 +97,12 @@
     for block_member, up_here, down_here in fetched:
         terms, up_here, down_here = lax.optimization_barrier((terms, up_here, down_here))
         terms = terms + [apply_block(block_member, up_here, down_here)]
-    tp_here = lax.axis_index("tp")
-    by_target = [term.reshape(n_tp, rows_here, feature_width) for term in terms]
-
-    def slice_for(target):
-        pieces = [lax.dynamic_index_in_dim(term, target, 0, keepdims=False) for term in by_target]
-        total = pieces[0]
-        for piece in pieces[1:]:
-            total = total + piece
-        return total
-
-    change = slice_for(tp_here)
-    for shift in range(1, n_tp):
-        change = change + lax.ppermute(
-            slice_for((tp_here + shift) % n_tp).astype(PARTIAL_DTYPE),
-            "tp",
-            [(i, (i + shift) % n_tp) for i in range(n_tp)],
-        ).astype(jnp.float32)
+    total = terms[0]
+    for term in terms[1:]:
+        total = total + term
+    change = lax.psum_scatter(
+        total.astype(PARTIAL_DTYPE), "tp", scatter_dimension=0, tiled=True
+    ).astype(jnp.float32)
     own_rows = (states.astype(jnp.float32) + change).astype(jnp.bfloat16)
     per_learner = rows_here // n_dev
     learner = place // rows_here

time: 121 us -> 124 us (1.025)
  waiting for transfers between devices: 48.5 us -> 54.7 us
  starting transfers between devices: 13.4 us -> 8.78 us
    reduce_scatter x0 -> x1, waiting for transfers between devices: none -> 28.3 us  [local(): lax.psum_scatter(total.astype(PARTIAL_DTYPE), 'tp', scatter_dimension=0,...]
    ppermute x3 -> x0, waiting for transfers between devices: 22.2 us -> none  [local(): lax.ppermute(slice_for((tp_here + shift) % n_tp).astype(PARTIAL_DTYPE), '...]
    ppermute x3 -> x0, starting transfers between devices: 4.61 us -> none  [local(): lax.ppermute(slice_for((tp_here + shift) % n_tp).astype(PARTIAL_DTYPE), '...]
    all_to_all x1, blocking collectives: 15.2 us -> 14 us  [local(): lax.all_to_all(jnp.concatenate([packed, spot_lanes], axis=1).reshape(n_de...]
  transfers between devices with their start and end apart: 14 -> 12, of which waited for: 5 -> 4; matrix products, arithmetic and copies ran while one was open for 12% -> 13% of each run, Pallas kernels for 0% -> 0%
where the time goes in v17:
time: 124 us; the launch traced here: 123 us
  waiting for transfers between devices  54.7 us (44%)
  matrix products  14.3 us (12%)
  between operations  14.3 us (12%)
  other arithmetic  14 us (11%)
  blocking collectives  14 us (11%)
  starting transfers between devices  8.78 us (7%)
  local copies, waits for them, and re-layouts  3.04 us (2%)
    reduce_scatter x1, waiting for transfers between devices, local(): lax.psum_scatter(total.astype(PARTIAL_DTYPE), 'tp', scatter_dimension=0,...  28.3 us
    ppermute x2, waiting for transfers between devices, from_chip_behind(): lax.ppermute(value, axis, [(i, (i + 2 * chips_back) % size) for i in rang...  15.8 us
    all_to_all x1, blocking collectives, local(): lax.all_to_all(jnp.concatenate([packed, spot_lanes], axis=1).reshape(n_de...  14 us
    dot_general x2, matrix products, apply_block(): return jnp.dot(hidden, down_here, preferred_element_type=jnp.float32)  11.9 us
    ppermute x2, waiting for transfers between devices, swap_parts(): lax.ppermute(value, 'rep', [(i, (i + step) % n_rep) for i in range(n_rep)])  10.6 us
    ppermute x2, starting transfers between devices, from_chip_behind(): lax.ppermute(value, axis, [(i, (i + 2 * chips_back) % size) for i in rang...  4.84 us
    convert_element_type x1, other arithmetic, local(): total.astype(PARTIAL_DTYPE)  3.53 us
    concatenate x1, other arithmetic, fetch_shared(): jnp.concatenate(down_parts + partner_down, axis=0)  2.99 us
  transfers between devices with their start and end apart: 12, of which 4 were waited for; matrix products, arithmetic and copies ran while one was open for 13% of the time, Pallas kernels for 0%

profile of v17, /device:TPU:0, one launch (start us, length us, event | category | flops | bytes accessed | tf_op | source)
XLA Modules:
  0.0 123.1 jit_solution(9574385348571906253)
XLA Ops:
  7.2 1.1 dynamic-slice_bitcast_fusion
  8.3 3.0 %collective-permute-start.2 = (bf16[1024,256]{1,0:T(8,128)(2,1)S(1)}, bf16[1024,256]{1,0:T(8,128)(2,1)S(1)}, u32[]{:S(2)}, u32[]{:S(2)}) collective-permute-start(bf16[1024,256]{1,0:T(8,128)(2,1)S(1)} %dynamic-slice_bitcast_fusion), channel_id=1, source_target_pairs={{0,8},{4,12},{8,0},{12,4},{1,9},{5,13},{9,1},{13,5},{2,10},{6,14},... | collective-permute-start | bytes 1572872 | tf_op jit(solution)/shard_map/ppermute | solution.py:15
  12.0 0.7 and_bitcast_fusion
  12.7 0.7 and_select_fusion.1
  13.8 1.1 fusion.50
  15.1 0.8 gather_fusion
  16.2 0.7 pad_maximum_fusion.2
  17.0 6.3 %collective-permute-done.2 = bf16[1024,256]{1,0:T(8,128)(2,1)S(1)} collective-permute-done((bf16[1024,256]{1,0:T(8,128)(2,1)S(1)}, bf16[1024,256]{1,0:T(8,128)(2,1)S(1)}, u32[]{:S(2)}, u32[]{:S(2)}) %collective-permute-start.2) | collective-permute-done | bytes 524320 | tf_op jit(solution)/shard_map/ppermute | solution.py:15
  23.3 1.1 constant_dynamic-slice_fusion
  24.4 1.8 %collective-permute-start.6 = (bf16[256,1024]{1,0:T(8,128)(2,1)S(1)}, bf16[256,1024]{1,0:T(8,128)(2,1)}, u32[]{:S(2)}, u32[]{:S(2)}) collective-permute-start(bf16[256,1024]{1,0:T(8,128)(2,1)S(1)} %constant_dynamic-slice_fusion), channel_id=1, source_target_pairs={{0,8},{4,12},{8,0},{12,4},{1,9},{5,13},{9,1},{13,5},{2,10},{6,14},... | collective-permute-start | bytes 1572872 | tf_op jit(solution)/shard_map/ppermute | solution.py:15
  26.2 1.5 %collective-permute-start.3 = (bf16[1024,256]{1,0:T(8,128)(2,1)S(1)}, bf16[1024,256]{1,0:T(8,128)(2,1)S(1)}, u32[]{:S(2)}, u32[]{:S(2)}) collective-permute-start(bf16[1024,256]{1,0:T(8,128)(2,1)S(1)} %collective-permute-done.2), channel_id=1, source_target_pairs={{0,16},{16,0},{1,17},{17,1},{2,18},{18,2},{3,19},{19,3},{4,20},{20... | collective-permute-start | bytes 1572872 | tf_op jit(solution)/shard_map/ppermute | solution.py:21
  28.2 9.4 %collective-permute-done.6 = bf16[256,1024]{1,0:T(8,128)(2,1)} collective-permute-done((bf16[256,1024]{1,0:T(8,128)(2,1)S(1)}, bf16[256,1024]{1,0:T(8,128)(2,1)}, u32[]{:S(2)}, u32[]{:S(2)}) %collective-permute-start.6) | collective-permute-done | bytes 524320 | tf_op jit(solution)/shard_map/ppermute | solution.py:15
  37.6 1.4 %collective-permute-start.7 = (bf16[256,1024]{1,0:T(8,128)(2,1)}, bf16[256,1024]{1,0:T(8,128)(2,1)}, u32[]{:S(2)}, u32[]{:S(2)}) collective-permute-start(bf16[256,1024]{1,0:T(8,128)(2,1)} %collective-permute-done.6), channel_id=1, source_target_pairs={{0,16},{16,0},{1,17},{17,1},{2,18},{18,2},{3,19},{19,3},{4,20},{20... | collective-permute-start | bytes 1572872 | tf_op jit(solution)/shard_map/ppermute | solution.py:21
  39.6 10.6 %collective-permute-done.7 = bf16[256,1024]{1,0:T(8,128)(2,1)} collective-permute-done((bf16[256,1024]{1,0:T(8,128)(2,1)}, bf16[256,1024]{1,0:T(8,128)(2,1)}, u32[]{:S(2)}, u32[]{:S(2)}) %collective-permute-start.7) | collective-permute-done | bytes 524320 | tf_op jit(solution)/shard_map/ppermute | solution.py:21
  50.1 1.7 %pad_maximum_fusion = bf16[1024,1024]{1,0:T(8,128)(2,1)S(1)} fusion(bf16[1024,256]{1,0:T(8,128)(2,1)} %collective-permute-done.5, bf16[1024,256]{1,0:T(8,128)(2,1)} %copy-done.4, bf16[1024,256]{1,0:T(8,128)(2,1)} %copy-done.3, bf16[1024,256]{1,0:T(8,128)(2,1)S(1)} %collective-permute-done.2), kind=kLoop, calls=%fused_computation.27 | loop fusion | flops 8388608 | bytes 4194304 | tf_op jit(solution)/shard_map/concatenate | solution.py:42
  51.8 1.1 fusion.63
  52.9 6.3 %fusion.20 = f32[512,1024]{1,0:T(8,128)} fusion(bf16[512,1024]{1,0:T(8,128)(2,1)} %collective-permute-done.1, bf16[512,1024]{1,0:T(8,128)(2,1)} %bitcast.4, bf16[1024,512]{1,0:T(8,128)(2,1)} %collective-permute-done, bf16[1024,512]{1,0:T(8,128)(2,1)} %bitcast.3, bf16[512,1152]{1,0:T(8,128)(2,1)} %all-gather.2.cloned.1.call-done, ...), kind=kOutput, calls=%fused_computation.23 | convolution fusion | flops 2161115136 | bytes 7341056 | tf_op jit(solution)/shard_map/dot_general | solution.py:89
  59.2 3.0 %pad_maximum_fusion.1 = bf16[1024,1024]{1,0:T(8,128)(2,1)} fusion(bf16[256,1024]{1,0:T(8,128)(2,1)} %collective-permute-done.9, bf16[256,1024]{1,0:T(8,128)(2,1)} %collective-permute-done.8, bf16[256,1024]{1,0:T(8,128)(2,1)} %collective-permute-done.7, bf16[256,1024]{1,0:T(8,128)(2,1)} %collective-permute-done.6), kind=kLoop, calls=%fused_computation.28 | loop fusion | flops 8388608 | bytes 4194304 | tf_op jit(solution)/shard_map/concatenate | solution.py:43
  62.2 5.7 %fusion.30 = f32[512,1024]{1,0:T(8,128)} fusion(bf16[1024,1024]{1,0:T(8,128)(2,1)} %pad_maximum_fusion.1, bf16[1024,1024]{1,0:T(8,128)(2,1)S(1)} %pad_maximum_fusion, bf16[512,1152]{1,0:T(8,128)(2,1)} %all-gather.2.cloned.1.call-done, bf16[512]{0:T(512)(128)(2,1)S(1)} %get-tuple-element.12), kind=kOutput, calls=%fused_computation.35 | convolution fusion | flops 2152726528 | bytes 7341056 | tf_op jit(solution)/shard_map/dot_general | solution.py:89
  67.9 3.5 %add_convert_fusion = bf16[512,1024]{1,0:T(8,128)(2,1)} fusion(f32[512,1024]{1,0:T(8,128)} %fusion.20, f32[512,1024]{1,0:T(8,128)} %fusion.30), kind=kLoop, calls=%fused_computation.29 | loop fusion | flops 1048576 | bytes 5242880 | tf_op jit(solution)/shard_map/convert_element_type | solution.py:104
  71.4 28.3 %reduce-scatter.2.cloned.1.call-done = bf16[128,1024]{1,0:T(8,128)(2,1)} async-done(((bf16[512,1024]{1,0:T(8,128)(2,1)}), bf16[128,1024]{1,0:T(8,128)(2,1)}) %reduce-scatter.2.cloned.1.call-update) | async-done | bytes 262160 | tf_op jit(solution)/shard_map/reduce_scatter | solution.py:103
  99.7 1.2 convolution_convert_fusion.1
  100.9 14.0 %all_to_all.5 = bf16[16,8,1152]{2,1,0:T(8,128)(2,1)S(1)} all-to-all(bf16[16,8,1152]{2,1,0:T(8,128)(2,1)S(1)} %maximum_bitcast_fusion), channel_id=1, replica_groups=mesh['rep'=2,'member'=4,'tp'=4] {'member','tp'}, dimensions={0} | all-to-all | bytes 589824 | tf_op jit(solution)/shard_map/all_to_all | solution.py:122
  115.3 0.9 fusion.24
  (49 shorter events, 3.1 us)
Async XLA Ops:
  7.2 108.1 %copy-start = (bf16[1024,128]{1,0:T(8,128)(2,1)S(1)}, bf16[1024,128]{1,0:T(8,128)(2,1)}, u32[]{:S(2)}) copy-start(bf16[1024,128]{1,0:T(8,128)(2,1)} %param.15) | copy-start | bytes 786436
  7.2 7.8 %copy-start.1 = (f32[2,1024]{1,0:T(2,128)S(1)}, f32[2,1024]{1,0:T(2,128)}, u32[]{:S(2)}) copy-start(f32[2,1024]{1,0:T(2,128)} %param.11) | copy-start | bytes 24580
  7.2 44.6 %all-gather.2.cloned.1.call-start = ((), (), s32[]{:S(2)}) async-start(), calls=%async_computation.2 | async-start | bytes 1474560 | tf_op jit(solution)/shard_map/all_gather | solution.py:78
  8.3 15.0 %collective-permute-start.2 = (bf16[1024,256]{1,0:T(8,128)(2,1)S(1)}, bf16[1024,256]{1,0:T(8,128)(2,1)S(1)}, u32[]{:S(2)}, u32[]{:S(2)}) collective-permute-start(bf16[1024,256]{1,0:T(8,128)(2,1)S(1)} %dynamic-slice_bitcast_fusion), channel_id=1, source_target_pairs={{0,8},{4,12},{8,0},{12,4},{1,9},{5,13},{9,1},{13,5},{2,10},{6,14},... | collective-permute-start | bytes 1572872 | tf_op jit(solution)/shard_map/ppermute | solution.py:15
  15.0 0.8 copy-start.5
  15.0 1.0 copy-start.2
  16.9 82.8 %reduce-scatter.2.cloned.1.call-start = ((), (), s32[]{:S(2)}) async-start(), calls=%async_computation.3 | async-start | bytes 1310720 | tf_op jit(solution)/shard_map/reduce_scatter | solution.py:103
  24.4 13.3 %collective-permute-start.6 = (bf16[256,1024]{1,0:T(8,128)(2,1)S(1)}, bf16[256,1024]{1,0:T(8,128)(2,1)}, u32[]{:S(2)}, u32[]{:S(2)}) collective-permute-start(bf16[256,1024]{1,0:T(8,128)(2,1)S(1)} %constant_dynamic-slice_fusion), channel_id=1, source_target_pairs={{0,8},{4,12},{8,0},{12,4},{1,9},{5,13},{9,1},{13,5},{2,10},{6,14},... | collective-permute-start | bytes 1572872 | tf_op jit(solution)/shard_map/ppermute | solution.py:15
  26.2 12.9 %collective-permute-start.3 = (bf16[1024,256]{1,0:T(8,128)(2,1)S(1)}, bf16[1024,256]{1,0:T(8,128)(2,1)S(1)}, u32[]{:S(2)}, u32[]{:S(2)}) collective-permute-start(bf16[1024,256]{1,0:T(8,128)(2,1)S(1)} %collective-permute-done.2), channel_id=1, source_target_pairs={{0,16},{16,0},{1,17},{17,1},{2,18},{18,2},{3,19},{19,3},{4,20},{20... | collective-permute-start | bytes 1572872 | tf_op jit(solution)/shard_map/ppermute | solution.py:21
  27.7 25.2 %collective-permute-start.1 = (bf16[512,1024]{1,0:T(8,128)(2,1)}, bf16[512,1024]{1,0:T(8,128)(2,1)}, u32[]{:S(2)}, u32[]{:S(2)}) collective-permute-start(bf16[512,1024]{1,0:T(8,128)(2,1)} %bitcast.4), channel_id=1, source_target_pairs={{0,4},{4,0},{8,12},{12,8},{1,5},{5,1},{9,13},{13,9},{2,6},{6,2},{1... | collective-permute-start | bytes 3145736 | tf_op jit(solution)/shard_map/ppermute | solution.py:10
  27.7 25.3 %collective-permute-start = (bf16[1024,512]{1,0:T(8,128)(2,1)}, bf16[1024,512]{1,0:T(8,128)(2,1)}, u32[]{:S(2)}, u32[]{:S(2)}) collective-permute-start(bf16[1024,512]{1,0:T(8,128)(2,1)} %bitcast.3), channel_id=1, source_target_pairs={{0,4},{4,0},{8,12},{12,8},{1,5},{5,1},{9,13},{13,9},{2,6},{6,2},{1... | collective-permute-start | bytes 3145736 | tf_op jit(solution)/shard_map/ppermute | solution.py:10
  28.2 10.9 %collective-permute-start.4 = (bf16[1024,256]{1,0:T(8,128)(2,1)S(1)}, bf16[1024,256]{1,0:T(8,128)(2,1)S(1)}, u32[]{:S(2)}, u32[]{:S(2)}) collective-permute-start(bf16[1024,256]{1,0:T(8,128)(2,1)S(1)} %collective-permute-done.2), channel_id=1, source_target_pairs={{0,4},{4,0},{8,12},{12,8},{1,5},{5,1},{9,13},{13,9},{2,6},{6,2},{1... | collective-permute-start | bytes 1572872 | tf_op jit(solution)/shard_map/ppermute | solution.py:10
  37.6 12.5 %collective-permute-start.7 = (bf16[256,1024]{1,0:T(8,128)(2,1)}, bf16[256,1024]{1,0:T(8,128)(2,1)}, u32[]{:S(2)}, u32[]{:S(2)}) collective-permute-start(bf16[256,1024]{1,0:T(8,128)(2,1)} %collective-permute-done.6), channel_id=1, source_target_pairs={{0,16},{16,0},{1,17},{17,1},{2,18},{18,2},{3,19},{19,3},{4,20},{20... | collective-permute-start | bytes 1572872 | tf_op jit(solution)/shard_map/ppermute | solution.py:21
  39.0 11.1 %copy-start.3 = (bf16[1024,256]{1,0:T(8,128)(2,1)}, bf16[1024,256]{1,0:T(8,128)(2,1)S(1)}, u32[]{:S(2)}) copy-start(bf16[1024,256]{1,0:T(8,128)(2,1)S(1)} %collective-permute-done.3) | copy-start | bytes 1572868
  39.0 11.1 %collective-permute-start.5 = (bf16[1024,256]{1,0:T(8,128)(2,1)S(1)}, bf16[1024,256]{1,0:T(8,128)(2,1)}, u32[]{:S(2)}, u32[]{:S(2)}) collective-permute-start(bf16[1024,256]{1,0:T(8,128)(2,1)S(1)} %collective-permute-done.3), channel_id=1, source_target_pairs={{0,4},{4,0},{8,12},{12,8},{1,5},{5,1},{9,13},{13,9},{2,6},{6,2},{1... | collective-permute-start | bytes 1572872 | tf_op jit(solution)/shard_map/ppermute | solution.py:10
  39.1 11.0 %copy-start.4 = (bf16[1024,256]{1,0:T(8,128)(2,1)}, bf16[1024,256]{1,0:T(8,128)(2,1)S(1)}, u32[]{:S(2)}) copy-start(bf16[1024,256]{1,0:T(8,128)(2,1)S(1)} %collective-permute-done.4) | copy-start | bytes 1572868
  39.1 20.1 %collective-permute-start.8 = (bf16[256,1024]{1,0:T(8,128)(2,1)}, bf16[256,1024]{1,0:T(8,128)(2,1)}, u32[]{:S(2)}, u32[]{:S(2)}) collective-permute-start(bf16[256,1024]{1,0:T(8,128)(2,1)} %collective-permute-done.6), channel_id=1, source_target_pairs={{0,4},{4,0},{8,12},{12,8},{1,5},{5,1},{9,13},{13,9},{2,6},{6,2},{1... | collective-permute-start | bytes 1572872 | tf_op jit(solution)/shard_map/ppermute | solution.py:10
  50.1 9.1 %collective-permute-start.9 = (bf16[256,1024]{1,0:T(8,128)(2,1)}, bf16[256,1024]{1,0:T(8,128)(2,1)}, u32[]{:S(2)}, u32[]{:S(2)}) collective-permute-start(bf16[256,1024]{1,0:T(8,128)(2,1)} %collective-permute-done.7), channel_id=1, source_target_pairs={{0,4},{4,0},{8,12},{12,8},{1,5},{5,1},{9,13},{13,9},{2,6},{6,2},{1... | collective-permute-start | bytes 1572872 | tf_op jit(solution)/shard_map/ppermute | solution.py:10
  71.4 43.9 %copy-start.6 = (f32[1024]{0:T(1024)S(1)}, f32[1024]{0:T(1024)}, u32[]{:S(2)}) copy-start(f32[1024]{0:T(1024)} %param.14) | copy-start | bytes 12292
  115.3 1.0 copy-start.7
Sparse Core Ops, SparseCore 0:
  17.0 30.7 all-gather.1
  71.5 28.1 reduce-scatter.1

commit v18 on v16

--- a/solution.py
+++ b/solution.py
@@ -127,24 +127,20 @@
         placer.astype(jnp.bfloat16), own_rows, preferred_element_type=jnp.float32
     ).astype(jnp.bfloat16)
     packed_spot = jnp.sum(placer.astype(jnp.int32) * spot_index[None, :], axis=1)
-    spot_lanes = jnp.where(
-        jnp.arange(128, dtype=jnp.int32)[None, :] == 0, packed_spot[:, None], 0
-    ).astype(jnp.bfloat16)
+    arrival_spots = lax.all_to_all(
+        packed_spot.reshape(n_dev, per_learner), ("member", "tp"), split_axis=0, concat_axis=0, tiled=True
+    ).reshape(n_dev * per_learner)
+    settle = (jnp.arange(rows_here, dtype=jnp.int32)[:, None] == arrival_spots[None, :]).astype(
+        jnp.bfloat16
+    )
     arrivals = lax.all_to_all(
-        jnp.concatenate([packed, spot_lanes], axis=1).reshape(n_dev, per_learner, feature_width + 128),
+        packed.reshape(n_dev, per_learner, feature_width),
         ("member", "tp"),
         split_axis=0,
         concat_axis=0,
         tiled=True,
-    )
-    arrivals = arrivals.reshape(n_dev * per_learner, feature_width + 128)
-    arrival_spots = arrivals[:, feature_width].astype(jnp.int32)
-    settle = (jnp.arange(rows_here, dtype=jnp.int32)[:, None] == arrival_spots[None, :]).astype(
-        jnp.bfloat16
-    )
-    imagined = jnp.dot(
-        settle, arrivals[:, :feature_width], preferred_element_type=jnp.float32
-    ).astype(jnp.bfloat16)
+    ).reshape(n_dev * per_learner, feature_width)
+    imagined = jnp.dot(settle, arrivals, preferred_element_type=jnp.float32).astype(jnp.bfloat16)
     policy_normed = rms_scale(imagined.astype(jnp.float32), policy_gain).astype(jnp.bfloat16)
     action = jnp.tanh(jnp.dot(policy_normed, w_policy, preferred_element_type=jnp.float32)).astype(
         jnp.bfloat16

time: 121 us -> 121 us (level)
  blocking collectives: 15.2 us -> 0 us
  starting transfers between devices: 13.4 us -> 23.2 us
  waiting for transfers between devices: 48.5 us -> 52 us
  local copies, waits for them, and re-layouts: 1.97 us -> 3.27 us
    all_to_all x1 -> x0, blocking collectives: 15.2 us -> none  [local(): lax.all_to_all(jnp.concatenate([packed, spot_lanes], axis=1).reshape(n_de...]
    all_to_all x0 -> x2, waiting for transfers between devices: none -> 12.5 us  [the longest x1 8.79 us: local(): lax.all_to_all(packed.reshape(n_dev, per_learner, feature_width), ('membe...]
    ppermute x3, waiting for transfers between devices: 22.2 us -> 12.5 us  [local(): lax.ppermute(slice_for((tp_here + shift) % n_tp).astype(PARTIAL_DTYPE), '...]
    all_to_all x0 -> x2, starting transfers between devices: none -> 8.8 us  [the longest x1 5.33 us: local(): lax.all_to_all(packed.reshape(n_dev, per_learner, feature_width), ('membe...]
    ppermute x2, waiting for transfers between devices: 15.7 us -> 17 us  [from_chip_behind(): lax.ppermute(value, axis, [(i, (i + 2 * chips_back) % size) for i in rang...]
    all_to_all x0 -> x2, local copies, waits for them, and re-layouts: none -> 1.21 us  [local(): lax.all_to_all(packed_spot.reshape(n_dev, per_learner), ('member', 'tp'),...]
  transfers between devices with their start and end apart: 14 -> 16, of which waited for: 5 -> 7; matrix products, arithmetic and copies ran while one was open for 12% -> 14% of each run, Pallas kernels for 0% -> 0%
where the time goes in v18:
time: 121 us
  waiting for transfers between devices  52 us (43%)
  starting transfers between devices  23.2 us (19%)
  matrix products  14.7 us (12%)
  between operations  14.3 us (12%)
  other arithmetic  13.5 us (11%)
  local copies, waits for them, and re-layouts  3.27 us (3%)
    ppermute x2, waiting for transfers between devices, from_chip_behind(): lax.ppermute(value, axis, [(i, (i + 2 * chips_back) % size) for i in rang...  17 us
    ppermute x3, waiting for transfers between devices, local(): lax.ppermute(slice_for((tp_here + shift) % n_tp).astype(PARTIAL_DTYPE), '...  12.5 us
    dot_general x2, matrix products, apply_block(): return jnp.dot(hidden, down_here, preferred_element_type=jnp.float32)  11.2 us
    ppermute x2, waiting for transfers between devices, swap_parts(): lax.ppermute(value, 'rep', [(i, (i + step) % n_rep) for i in range(n_rep)])  10 us
    all_to_all x1, waiting for transfers between devices, local(): lax.all_to_all(packed.reshape(n_dev, per_learner, feature_width), ('membe...  8.79 us
    ppermute x3, starting transfers between devices, local(): lax.ppermute(slice_for((tp_here + shift) % n_tp).astype(PARTIAL_DTYPE), '...  5.51 us
    all_to_all x1, starting transfers between devices, local(): lax.all_to_all(packed.reshape(n_dev, per_learner, feature_width), ('membe...  5.33 us
    ppermute x2, starting transfers between devices, from_chip_behind(): lax.ppermute(value, axis, [(i, (i + 2 * chips_back) % size) for i in rang...  4.84 us
  transfers between devices with their start and end apart: 16, of which 7 were waited for; matrix products, arithmetic and copies ran while one was open for 14% of the time, Pallas kernels for 0%

profile of v18, /device:TPU:0, one launch (start us, length us, event | category | flops | bytes accessed | tf_op | source)
XLA Modules:
  0.0 120.9 jit_solution(9023739973304615546)
XLA Ops:
  8.3 3.0 %collective-permute-start.2 = (bf16[1024,256]{1,0:T(8,128)(2,1)S(1)}, bf16[1024,256]{1,0:T(8,128)(2,1)S(1)}, u32[]{:S(2)}, u32[]{:S(2)}) collective-permute-start(bf16[1024,256]{1,0:T(8,128)(2,1)S(1)} %dynamic-slice_bitcast_fusion), channel_id=1, source_target_pairs={{0,8},{4,12},{8,0},{12,4},{1,9},{5,13},{9,1},{13,5},{2,10},{6,14},... | collective-permute-start | bytes 1572872 | tf_op jit(solution)/shard_map/ppermute | solution.py:15
  12.7 1.1 fusion.51
  15.7 7.6 %collective-permute-done.2 = bf16[1024,256]{1,0:T(8,128)(2,1)S(1)} collective-permute-done((bf16[1024,256]{1,0:T(8,128)(2,1)S(1)}, bf16[1024,256]{1,0:T(8,128)(2,1)S(1)}, u32[]{:S(2)}, u32[]{:S(2)}) %collective-permute-start.2) | collective-permute-done | bytes 524320 | tf_op jit(solution)/shard_map/ppermute | solution.py:15
  23.3 1.8 %collective-permute-start.6 = (bf16[256,1024]{1,0:T(8,128)(2,1)S(1)}, bf16[256,1024]{1,0:T(8,128)(2,1)S(1)}, u32[]{:S(2)}, u32[]{:S(2)}) collective-permute-start(bf16[256,1024]{1,0:T(8,128)(2,1)S(1)} %constant_dynamic-slice_fusion), channel_id=1, source_target_pairs={{0,8},{4,12},{8,0},{12,4},{1,9},{5,13},{9,1},{13,5},{2,10},{6,14},... | collective-permute-start | bytes 1572872 | tf_op jit(solution)/shard_map/ppermute | solution.py:15
  25.1 1.5 %collective-permute-start.3 = (bf16[1024,256]{1,0:T(8,128)(2,1)S(1)}, bf16[1024,256]{1,0:T(8,128)(2,1)S(1)}, u32[]{:S(2)}, u32[]{:S(2)}) collective-permute-start(bf16[1024,256]{1,0:T(8,128)(2,1)S(1)} %collective-permute-done.2), channel_id=1, source_target_pairs={{0,16},{16,0},{1,17},{17,1},{2,18},{18,2},{3,19},{19,3},{4,20},{20... | collective-permute-start | bytes 1572872 | tf_op jit(solution)/shard_map/ppermute | solution.py:21
  27.1 9.4 %collective-permute-done.6 = bf16[256,1024]{1,0:T(8,128)(2,1)S(1)} collective-permute-done((bf16[256,1024]{1,0:T(8,128)(2,1)S(1)}, bf16[256,1024]{1,0:T(8,128)(2,1)S(1)}, u32[]{:S(2)}, u32[]{:S(2)}) %collective-permute-start.6) | collective-permute-done | bytes 524320 | tf_op jit(solution)/shard_map/ppermute | solution.py:15
  36.5 1.4 %collective-permute-start.7 = (bf16[256,1024]{1,0:T(8,128)(2,1)S(1)}, bf16[256,1024]{1,0:T(8,128)(2,1)}, u32[]{:S(2)}, u32[]{:S(2)}) collective-permute-start(bf16[256,1024]{1,0:T(8,128)(2,1)S(1)} %collective-permute-done.6), channel_id=1, source_target_pairs={{0,16},{16,0},{1,17},{17,1},{2,18},{18,2},{3,19},{19,3},{4,20},{20... | collective-permute-start | bytes 1572872 | tf_op jit(solution)/shard_map/ppermute | solution.py:21
  39.0 10.0 %collective-permute-done.7 = bf16[256,1024]{1,0:T(8,128)(2,1)} collective-permute-done((bf16[256,1024]{1,0:T(8,128)(2,1)S(1)}, bf16[256,1024]{1,0:T(8,128)(2,1)}, u32[]{:S(2)}, u32[]{:S(2)}) %collective-permute-start.7) | collective-permute-done | bytes 524320 | tf_op jit(solution)/shard_map/ppermute | solution.py:21
  49.0 2.7 %pad_maximum_fusion = bf16[1024,1024]{1,0:T(8,128)(2,1)} fusion(bf16[1024,256]{1,0:T(8,128)(2,1)S(1)} %collective-permute-done.5, bf16[1024,256]{1,0:T(8,128)(2,1)} %collective-permute-done.4, bf16[1024,256]{1,0:T(8,128)(2,1)S(1)} %collective-permute-done.3, bf16[1024,256]{1,0:T(8,128)(2,1)S(1)} %collective-permute-done.2), kind=kLoop, calls=%fused_computation.27 | loop fusion | flops 8388608 | bytes 4194304 | tf_op jit(solution)/shard_map/concatenate | solution.py:42
  51.7 1.1 fusion.69
  52.8 4.9 %fusion.20 = f32[512,1024]{1,0:T(8,128)S(1)} fusion(bf16[512,1024]{1,0:T(8,128)(2,1)} %collective-permute-done.1, bf16[512,1024]{1,0:T(8,128)(2,1)} %bitcast.42, bf16[1024,512]{1,0:T(8,128)(2,1)} %collective-permute-done, bf16[1024,512]{1,0:T(8,128)(2,1)} %bitcast.45, bf16[512,1152]{1,0:T(8,128)(2,1)} %all-gather.2.cloned.1.call-done, ...), kind=kOutput, calls=%fused_computation.23 | convolution fusion | flops 2161115136 | bytes 7341056 | tf_op jit(solution)/shard_map/dot_general | solution.py:89
  57.7 2.8 %pad_maximum_fusion.1 = bf16[1024,1024]{1,0:T(8,128)(2,1)} fusion(bf16[256,1024]{1,0:T(8,128)(2,1)} %collective-permute-done.9, bf16[256,1024]{1,0:T(8,128)(2,1)} %collective-permute-done.8, bf16[256,1024]{1,0:T(8,128)(2,1)} %collective-permute-done.7, bf16[256,1024]{1,0:T(8,128)(2,1)S(1)} %collective-permute-done.6), kind=kLoop, calls=%fused_computation.28 | loop fusion | flops 8388608 | bytes 4194304 | tf_op jit(solution)/shard_map/concatenate | solution.py:43
  60.6 6.3 %fusion.31 = f32[512,1024]{1,0:T(8,128)} fusion(bf16[1024,1024]{1,0:T(8,128)(2,1)} %pad_maximum_fusion.1, bf16[1024,1024]{1,0:T(8,128)(2,1)} %pad_maximum_fusion, bf16[512,1152]{1,0:T(8,128)(2,1)} %all-gather.2.cloned.1.call-done, bf16[512]{0:T(512)(128)(2,1)S(1)} %get-tuple-element.12), kind=kOutput, calls=%fused_computation.35 | convolution fusion | flops 2152726528 | bytes 7341056 | tf_op jit(solution)/shard_map/dot_general | solution.py:89
  66.8 2.3 %fusion.59 = (bf16[128,1024]{1,0:T(8,128)(2,1)}, bf16[128,1024]{1,0:T(8,128)(2,1)S(1)}, bf16[128,1024]{1,0:T(8,128)(2,1)S(1)}) fusion(f32[4,128,1024]{2,1,0:T(8,128)} %bitcast.39, s32[]{:T(128)S(6)} %select_n.79, f32[4,128,1024]{2,1,0:T(8,128)S(1)} %bitcast.37, s32[]{:T(128)S(6)} %select_n.83, s32[]{:T(128)S(6)} %select_n.81), kind=kLoop, calls=%fused_computation.67 | loop fusion | flops 786432 | bytes 3932172 | tf_op jit(solution)/shard_map/convert_element_type | solution.py:113
  69.1 1.6 %collective-permute-start.10 = (bf16[128,1024]{1,0:T(8,128)(2,1)}, bf16[128,1024]{1,0:T(8,128)(2,1)S(1)}, u32[]{:S(2)}, u32[]{:S(2)}) collective-permute-start(bf16[128,1024]{1,0:T(8,128)(2,1)} %get-tuple-element.14), channel_id=1, source_target_pairs={{0,1},{1,2},{2,3},{3,0},{4,5},{5,6},{6,7},{7,4},{8,9},{9,10},{10,1... | collective-permute-start | bytes 786440 | tf_op jit(solution)/shard_map/ppermute | solution.py:112
  70.7 2.6 %collective-permute-start.11 = (bf16[128,1024]{1,0:T(8,128)(2,1)S(1)}, bf16[128,1024]{1,0:T(8,128)(2,1)}, u32[]{:S(2)}, u32[]{:S(2)}) collective-permute-start(bf16[128,1024]{1,0:T(8,128)(2,1)S(1)} %get-tuple-element.16), channel_id=1, source_target_pairs={{0,2},{1,3},{2,0},{3,1},{4,6},{5,7},{6,4},{7,5},{8,10},{9,11},{10,... | collective-permute-start | bytes 786440 | tf_op jit(solution)/shard_map/ppermute | solution.py:112
  73.3 1.4 %collective-permute-start.12 = (bf16[128,1024]{1,0:T(8,128)(2,1)S(1)}, bf16[128,1024]{1,0:T(8,128)(2,1)}, u32[]{:S(2)}, u32[]{:S(2)}) collective-permute-start(bf16[128,1024]{1,0:T(8,128)(2,1)S(1)} %get-tuple-element.15), channel_id=1, source_target_pairs={{0,3},{1,0},{2,1},{3,2},{4,7},{5,4},{6,5},{7,6},{8,11},{9,8},{10,9... | collective-permute-start | bytes 786440 | tf_op jit(solution)/shard_map/ppermute | solution.py:112
  75.4 3.5 %all-to-all-start = ((s32[16,1,8]{2,1,0:T(1,128)}), s32[16,1,8]{2,1,0:T(1,128)S(1)}, u32[]{:S(2)}, u32[]{:S(2)}) async-start(s32[16,1,8]{2,1,0:T(1,128)} %bitcast), calls=%async_computation | async-start | bytes 16384 | tf_op jit(solution)/shard_map/all_to_all | solution.py:130
  78.9 1.4 %collective-permute-done.10 = bf16[128,1024]{1,0:T(8,128)(2,1)S(1)} collective-permute-done((bf16[128,1024]{1,0:T(8,128)(2,1)}, bf16[128,1024]{1,0:T(8,128)(2,1)S(1)}, u32[]{:S(2)}, u32[]{:S(2)}) %collective-permute-start.10) | collective-permute-done | bytes 262176 | tf_op jit(solution)/shard_map/ppermute | solution.py:112
  80.3 11.0 %collective-permute-done.11 = bf16[128,1024]{1,0:T(8,128)(2,1)} collective-permute-done((bf16[128,1024]{1,0:T(8,128)(2,1)S(1)}, bf16[128,1024]{1,0:T(8,128)(2,1)}, u32[]{:S(2)}, u32[]{:S(2)}) %collective-permute-start.11) | collective-permute-done | bytes 262176 | tf_op jit(solution)/shard_map/ppermute | solution.py:112
  91.4 2.2 %fusion.24 = bf16[16,8,1024]{2,1,0:T(8,128)(2,1)} fusion(bf16[128,1024]{1,0:T(8,128)(2,1)S(1)} %copy-done.2, bf16[128,1024]{1,0:T(8,128)(2,1)} %collective-permute-done.12, bf16[128,1024]{1,0:T(8,128)(2,1)} %collective-permute-done.11, bf16[128,1024]{1,0:T(8,128)(2,1)S(1)} %collective-permute-done.10, f32[4,128,1024]{2,1,0:T(8,128)} %bitcast.40, ...), kind=kOutput, calls=%fused_computation.31 | convolution fusion | flops 35012608 | bytes 2359812 | tf_op jit(solution)/shard_map/dot_general | solution.py:126
  93.6 3.7 %all-to-all-done = s32[16,1,8]{2,1,0:T(1,128)S(1)} async-done(((s32[16,1,8]{2,1,0:T(1,128)}), s32[16,1,8]{2,1,0:T(1,128)S(1)}, u32[]{:S(2)}, u32[]{:S(2)}) %all-to-all-start) | async-done | bytes 544 | tf_op jit(solution)/shard_map/all_to_all | solution.py:130
  97.4 5.3 %all-to-all-start.1 = ((bf16[16,8,1024]{2,1,0:T(8,128)(2,1)}), bf16[16,8,1024]{2,1,0:T(8,128)(2,1)S(1)}, u32[]{:S(2)}, u32[]{:S(2)}) async-start(bf16[16,8,1024]{2,1,0:T(8,128)(2,1)} %fusion.24), calls=%async_computation.1 | async-start | bytes 524288 | tf_op jit(solution)/shard_map/all_to_all | solution.py:136
  104.0 8.8 %all-to-all-done.1 = bf16[16,8,1024]{2,1,0:T(8,128)(2,1)S(1)} async-done(((bf16[16,8,1024]{2,1,0:T(8,128)(2,1)}), bf16[16,8,1024]{2,1,0:T(8,128)(2,1)S(1)}, u32[]{:S(2)}, u32[]{:S(2)}) %all-to-all-start.1) | async-done | bytes 262176 | tf_op jit(solution)/shard_map/all_to_all | solution.py:136
  (57 shorter events, 9.2 us)
Async XLA Ops:
  7.2 105.9 %copy-start = (bf16[1024,128]{1,0:T(8,128)(2,1)S(1)}, bf16[1024,128]{1,0:T(8,128)(2,1)}, u32[]{:S(2)}) copy-start(bf16[1024,128]{1,0:T(8,128)(2,1)} %param.15) | copy-start | bytes 786436
  7.2 6.6 %copy-start.1 = (f32[2,1024]{1,0:T(2,128)S(1)}, f32[2,1024]{1,0:T(2,128)}, u32[]{:S(2)}) copy-start(f32[2,1024]{1,0:T(2,128)} %param.11) | copy-start | bytes 24580
  7.2 44.5 %all-gather.2.cloned.1.call-start = ((), (), s32[]{:S(2)}) async-start(), calls=%async_computation.2 | async-start | bytes 1474560 | tf_op jit(solution)/shard_map/all_gather | solution.py:78
  8.3 15.0 %collective-permute-start.2 = (bf16[1024,256]{1,0:T(8,128)(2,1)S(1)}, bf16[1024,256]{1,0:T(8,128)(2,1)S(1)}, u32[]{:S(2)}, u32[]{:S(2)}) collective-permute-start(bf16[1024,256]{1,0:T(8,128)(2,1)S(1)} %dynamic-slice_bitcast_fusion), channel_id=1, source_target_pairs={{0,8},{4,12},{8,0},{12,4},{1,9},{5,13},{9,1},{13,5},{2,10},{6,14},... | collective-permute-start | bytes 1572872 | tf_op jit(solution)/shard_map/ppermute | solution.py:15
  13.8 0.8 copy-start.5
  13.8 1.0 copy-start.2
  14.6 8.7 %copy-start.4 = (bf16[1,512,1024]{2,1,0:T(8,128)(2,1)S(1)}, bf16[1,512,1024]{2,1,0:T(8,128)(2,1)}, u32[]{:S(2)}) copy-start(bf16[1,512,1024]{2,1,0:T(8,128)(2,1)} %param.13) | copy-start | bytes 3145732
  14.6 23.3 %copy-start.7 = (s32[128]{0:T(128)S(1)}, s32[128]{0:T(128)}, u32[]{:S(2)}) copy-start(s32[128]{0:T(128)} %param.10) | copy-start | bytes 1540
  23.3 13.2 %collective-permute-start.6 = (bf16[256,1024]{1,0:T(8,128)(2,1)S(1)}, bf16[256,1024]{1,0:T(8,128)(2,1)S(1)}, u32[]{:S(2)}, u32[]{:S(2)}) collective-permute-start(bf16[256,1024]{1,0:T(8,128)(2,1)S(1)} %constant_dynamic-slice_fusion), channel_id=1, source_target_pairs={{0,8},{4,12},{8,0},{12,4},{1,9},{5,13},{9,1},{13,5},{2,10},{6,14},... | collective-permute-start | bytes 1572872 | tf_op jit(solution)/shard_map/ppermute | solution.py:15
  25.1 12.8 %collective-permute-start.3 = (bf16[1024,256]{1,0:T(8,128)(2,1)S(1)}, bf16[1024,256]{1,0:T(8,128)(2,1)S(1)}, u32[]{:S(2)}, u32[]{:S(2)}) collective-permute-start(bf16[1024,256]{1,0:T(8,128)(2,1)S(1)} %collective-permute-done.2), channel_id=1, source_target_pairs={{0,16},{16,0},{1,17},{17,1},{2,18},{18,2},{3,19},{19,3},{4,20},{20... | collective-permute-start | bytes 1572872 | tf_op jit(solution)/shard_map/ppermute | solution.py:21
  26.6 26.1 %collective-permute-start.1 = (bf16[512,1024]{1,0:T(8,128)(2,1)}, bf16[512,1024]{1,0:T(8,128)(2,1)}, u32[]{:S(2)}, u32[]{:S(2)}) collective-permute-start(bf16[512,1024]{1,0:T(8,128)(2,1)} %bitcast.41), channel_id=1, source_target_pairs={{0,4},{4,0},{8,12},{12,8},{1,5},{5,1},{9,13},{13,9},{2,6},{6,2},{1... | collective-permute-start | bytes 3145736 | tf_op jit(solution)/shard_map/ppermute | solution.py:10
  26.6 26.1 %collective-permute-start = (bf16[1024,512]{1,0:T(8,128)(2,1)}, bf16[1024,512]{1,0:T(8,128)(2,1)}, u32[]{:S(2)}, u32[]{:S(2)}) collective-permute-start(bf16[1024,512]{1,0:T(8,128)(2,1)} %bitcast.44), channel_id=1, source_target_pairs={{0,4},{4,0},{8,12},{12,8},{1,5},{5,1},{9,13},{13,9},{2,6},{6,2},{1... | collective-permute-start | bytes 3145736 | tf_op jit(solution)/shard_map/ppermute | solution.py:10
  27.1 11.2 %collective-permute-start.4 = (bf16[1024,256]{1,0:T(8,128)(2,1)S(1)}, bf16[1024,256]{1,0:T(8,128)(2,1)}, u32[]{:S(2)}, u32[]{:S(2)}) collective-permute-start(bf16[1024,256]{1,0:T(8,128)(2,1)S(1)} %collective-permute-done.2), channel_id=1, source_target_pairs={{0,4},{4,0},{8,12},{12,8},{1,5},{5,1},{9,13},{13,9},{2,6},{6,2},{1... | collective-permute-start | bytes 1572872 | tf_op jit(solution)/shard_map/ppermute | solution.py:10
  36.5 12.5 %collective-permute-start.7 = (bf16[256,1024]{1,0:T(8,128)(2,1)S(1)}, bf16[256,1024]{1,0:T(8,128)(2,1)}, u32[]{:S(2)}, u32[]{:S(2)}) collective-permute-start(bf16[256,1024]{1,0:T(8,128)(2,1)S(1)} %collective-permute-done.6), channel_id=1, source_target_pairs={{0,16},{16,0},{1,17},{17,1},{2,18},{18,2},{3,19},{19,3},{4,20},{20... | collective-permute-start | bytes 1572872 | tf_op jit(solution)/shard_map/ppermute | solution.py:21
  37.9 11.1 %collective-permute-start.5 = (bf16[1024,256]{1,0:T(8,128)(2,1)S(1)}, bf16[1024,256]{1,0:T(8,128)(2,1)S(1)}, u32[]{:S(2)}, u32[]{:S(2)}) collective-permute-start(bf16[1024,256]{1,0:T(8,128)(2,1)S(1)} %collective-permute-done.3), channel_id=1, source_target_pairs={{0,4},{4,0},{8,12},{12,8},{1,5},{5,1},{9,13},{13,9},{2,6},{6,2},{1... | collective-permute-start | bytes 1572872 | tf_op jit(solution)/shard_map/ppermute | solution.py:10
  38.4 19.3 %collective-permute-start.8 = (bf16[256,1024]{1,0:T(8,128)(2,1)S(1)}, bf16[256,1024]{1,0:T(8,128)(2,1)}, u32[]{:S(2)}, u32[]{:S(2)}) collective-permute-start(bf16[256,1024]{1,0:T(8,128)(2,1)S(1)} %collective-permute-done.6), channel_id=1, source_target_pairs={{0,4},{4,0},{8,12},{12,8},{1,5},{5,1},{9,13},{13,9},{2,6},{6,2},{1... | collective-permute-start | bytes 1572872 | tf_op jit(solution)/shard_map/ppermute | solution.py:10
  49.0 8.7 %collective-permute-start.9 = (bf16[256,1024]{1,0:T(8,128)(2,1)}, bf16[256,1024]{1,0:T(8,128)(2,1)}, u32[]{:S(2)}, u32[]{:S(2)}) collective-permute-start(bf16[256,1024]{1,0:T(8,128)(2,1)} %collective-permute-done.7), channel_id=1, source_target_pairs={{0,4},{4,0},{8,12},{12,8},{1,5},{5,1},{9,13},{13,9},{2,6},{6,2},{1... | collective-permute-start | bytes 1572872 | tf_op jit(solution)/shard_map/ppermute | solution.py:10
  69.1 44.0 %copy-start.6 = (f32[1024]{0:T(1024)S(1)}, f32[1024]{0:T(1024)}, u32[]{:S(2)}) copy-start(f32[1024]{0:T(1024)} %param.14) | copy-start | bytes 12292
  69.1 11.2 %collective-permute-start.10 = (bf16[128,1024]{1,0:T(8,128)(2,1)}, bf16[128,1024]{1,0:T(8,128)(2,1)S(1)}, u32[]{:S(2)}, u32[]{:S(2)}) collective-permute-start(bf16[128,1024]{1,0:T(8,128)(2,1)} %get-tuple-element.14), channel_id=1, source_target_pairs={{0,1},{1,2},{2,3},{3,0},{4,5},{5,6},{6,7},{7,4},{8,9},{9,10},{10,1... | collective-permute-start | bytes 786440 | tf_op jit(solution)/shard_map/ppermute | solution.py:112
  70.7 20.7 %collective-permute-start.11 = (bf16[128,1024]{1,0:T(8,128)(2,1)S(1)}, bf16[128,1024]{1,0:T(8,128)(2,1)}, u32[]{:S(2)}, u32[]{:S(2)}) collective-permute-start(bf16[128,1024]{1,0:T(8,128)(2,1)S(1)} %get-tuple-element.16), channel_id=1, source_target_pairs={{0,2},{1,3},{2,0},{3,1},{4,6},{5,7},{6,4},{7,5},{8,10},{9,11},{10,... | collective-permute-start | bytes 786440 | tf_op jit(solution)/shard_map/ppermute | solution.py:112
  73.3 18.1 %collective-permute-start.12 = (bf16[128,1024]{1,0:T(8,128)(2,1)S(1)}, bf16[128,1024]{1,0:T(8,128)(2,1)}, u32[]{:S(2)}, u32[]{:S(2)}) collective-permute-start(bf16[128,1024]{1,0:T(8,128)(2,1)S(1)} %get-tuple-element.15), channel_id=1, source_target_pairs={{0,3},{1,0},{2,1},{3,2},{4,7},{5,4},{6,5},{7,6},{8,11},{9,8},{10,9... | collective-permute-start | bytes 786440 | tf_op jit(solution)/shard_map/ppermute | solution.py:112
  75.4 21.9 %all-to-all-start = ((s32[16,1,8]{2,1,0:T(1,128)}), s32[16,1,8]{2,1,0:T(1,128)S(1)}, u32[]{:S(2)}, u32[]{:S(2)}) async-start(s32[16,1,8]{2,1,0:T(1,128)} %bitcast), calls=%async_computation | async-start | bytes 16384 | tf_op jit(solution)/shard_map/all_to_all | solution.py:130
  97.4 15.4 %all-to-all-start.1 = ((bf16[16,8,1024]{2,1,0:T(8,128)(2,1)}), bf16[16,8,1024]{2,1,0:T(8,128)(2,1)S(1)}, u32[]{:S(2)}, u32[]{:S(2)}) async-start(bf16[16,8,1024]{2,1,0:T(8,128)(2,1)} %fusion.24), calls=%async_computation.1 | async-start | bytes 524288 | tf_op jit(solution)/shard_map/all_to_all | solution.py:136
  113.1 1.0 copy-start.3
Sparse Core Ops, SparseCore 0:
  15.8 30.7 all-gather.1

commit v19 on v16

--- a/solution.py
+++ b/solution.py
@@ -38,10 +38,7 @@
     down_parts = swap_parts(got_down)
     partner_up = [from_partner(part, "member", 0) for part in up_parts]
     partner_down = [from_partner(part, "member", 0) for part in down_parts]
-    return (
-        jnp.concatenate(up_parts + partner_up, axis=1),
-        jnp.concatenate(down_parts + partner_down, axis=0),
-    )
+    return up_parts + partner_up, down_parts + partner_down
 
 
 def rms_scale(values, gain):
@@ -96,7 +93,11 @@
     terms = [apply_pair(*own_block)]
     for block_member, up_here, down_here in fetched:
         terms, up_here, down_here = lax.optimization_barrier((terms, up_here, down_here))
-        terms = terms + [apply_block(block_member, up_here, down_here)]
+        terms = terms + [
+            apply_block(
+                block_member, jnp.concatenate(up_here, axis=1), jnp.concatenate(down_here, axis=0)
+            )
+        ]
     tp_here = lax.axis_index("tp")
     by_target = [term.reshape(n_tp, rows_here, feature_width) for term in terms]
 

time: 121 us -> 120 us (level)
  waiting for transfers between devices: 48.5 us -> 55.2 us
  other arithmetic: 13.7 us -> 8.21 us
    ppermute x2, waiting for transfers between devices: 15.7 us -> 22 us  [from_chip_behind(): lax.ppermute(value, axis, [(i, (i + 2 * chips_back) % size) for i in rang...]
    concatenate x2 -> x0, other arithmetic: 5.49 us -> none  [the longest x1 2.84 us: fetch_shared(): jnp.concatenate(down_parts + partner_down, axis=0)]
    all_gather x1, waiting for transfers between devices: 0.01 us -> 3.45 us  [local(): lax.all_gather(jnp.concatenate([normed, member_lanes], axis=1), 'tp', axi...]
    ppermute x2, waiting for transfers between devices: 10.6 us -> 7.58 us  [swap_parts(): lax.ppermute(value, 'rep', [(i, (i + step) % n_rep) for i in range(n_rep)])]
  transfers between devices with their start and end apart: 14 -> 14, of which waited for: 5 -> 6; matrix products, arithmetic and copies ran while one was open for 12% -> 5% of each run, Pallas kernels for 0% -> 0%
where the time goes in v19:
time: 120 us
  waiting for transfers between devices  55.2 us (46%)
  blocking collectives  14.9 us (12%)
  between operations  14.3 us (12%)
  matrix products  13.6 us (11%)
  starting transfers between devices  13 us (11%)
  other arithmetic  8.21 us (7%)
    ppermute x3, waiting for transfers between devices, local(): lax.ppermute(slice_for((tp_here + shift) % n_tp).astype(PARTIAL_DTYPE), '...  22.2 us
    ppermute x2, waiting for transfers between devices, from_chip_behind(): lax.ppermute(value, axis, [(i, (i + 2 * chips_back) % size) for i in rang...  22 us
    all_to_all x1, blocking collectives, local(): lax.all_to_all(jnp.concatenate([packed, spot_lanes], axis=1).reshape(n_de...  14.9 us
    dot_general x2, matrix products, apply_block(): return jnp.dot(hidden, down_here, preferred_element_type=jnp.float32)  10.9 us
    ppermute x2, waiting for transfers between devices, swap_parts(): lax.ppermute(value, 'rep', [(i, (i + step) % n_rep) for i in range(n_rep)])  7.58 us
    ppermute x2, starting transfers between devices, from_chip_behind(): lax.ppermute(value, axis, [(i, (i + 2 * chips_back) % size) for i in rang...  4.84 us
    ppermute x3, starting transfers between devices, local(): lax.ppermute(slice_for((tp_here + shift) % n_tp).astype(PARTIAL_DTYPE), '...  4.62 us
    all_gather x1, waiting for transfers between devices, local(): lax.all_gather(jnp.concatenate([normed, member_lanes], axis=1), 'tp', axi...  3.45 us
  transfers between devices with their start and end apart: 14, of which 6 were waited for; matrix products, arithmetic and copies ran while one was open for 5% of the time, Pallas kernels for 0%

profile of v19, /device:TPU:0, one launch (start us, length us, event | category | flops | bytes accessed | tf_op | source)
XLA Modules:
  0.0 120.1 jit_solution(16124710058323234987)
XLA Ops:
  7.9 0.7 and_bitcast_fusion
  8.6 0.7 and_select_fusion.1
  9.7 1.1 fusion.68
  11.0 0.8 gather_fusion
  12.0 0.8 pad_maximum_fusion
  12.9 3.0 %collective-permute-start.2 = (bf16[1024,256]{1,0:T(8,128)(2,1)S(1)}, bf16[1024,256]{1,0:T(8,128)(2,1)S(1)}, u32[]{:S(2)}, u32[]{:S(2)}) collective-permute-start(bf16[1024,256]{1,0:T(8,128)(2,1)S(1)} %dynamic-slice_bitcast_fusion), channel_id=1, source_target_pairs={{0,8},{4,12},{8,0},{12,4},{1,9},{5,13},{9,1},{13,5},{2,10},{6,14},... | collective-permute-start | bytes 1572872 | tf_op jit(solution)/shard_map/ppermute | solution.py:15
  15.9 11.9 %collective-permute-done.2 = bf16[1024,256]{1,0:T(8,128)(2,1)S(1)} collective-permute-done((bf16[1024,256]{1,0:T(8,128)(2,1)S(1)}, bf16[1024,256]{1,0:T(8,128)(2,1)S(1)}, u32[]{:S(2)}, u32[]{:S(2)}) %collective-permute-start.2) | collective-permute-done | bytes 524320 | tf_op jit(solution)/shard_map/ppermute | solution.py:15
  27.9 1.8 %collective-permute-start.6 = (bf16[256,1024]{1,0:T(8,128)(2,1)S(1)}, bf16[256,1024]{1,0:T(8,128)(2,1)}, u32[]{:S(2)}, u32[]{:S(2)}) collective-permute-start(bf16[256,1024]{1,0:T(8,128)(2,1)S(1)} %constant_dynamic-slice_fusion), channel_id=1, source_target_pairs={{0,8},{4,12},{8,0},{12,4},{1,9},{5,13},{9,1},{13,5},{2,10},{6,14},... | collective-permute-start | bytes 1572872 | tf_op jit(solution)/shard_map/ppermute | solution.py:15
  29.7 1.5 %collective-permute-start.3 = (bf16[1024,256]{1,0:T(8,128)(2,1)S(1)}, bf16[1024,256]{1,0:T(8,128)(2,1)}, u32[]{:S(2)}, u32[]{:S(2)}) collective-permute-start(bf16[1024,256]{1,0:T(8,128)(2,1)S(1)} %collective-permute-done.2), channel_id=1, source_target_pairs={{0,16},{16,0},{1,17},{17,1},{2,18},{18,2},{3,19},{19,3},{4,20},{20... | collective-permute-start | bytes 1572872 | tf_op jit(solution)/shard_map/ppermute | solution.py:21
  31.2 10.0 %collective-permute-done.6 = bf16[256,1024]{1,0:T(8,128)(2,1)} collective-permute-done((bf16[256,1024]{1,0:T(8,128)(2,1)S(1)}, bf16[256,1024]{1,0:T(8,128)(2,1)}, u32[]{:S(2)}, u32[]{:S(2)}) %collective-permute-start.6) | collective-permute-done | bytes 524320 | tf_op jit(solution)/shard_map/ppermute | solution.py:15
  41.2 1.4 %collective-permute-start.7 = (bf16[256,1024]{1,0:T(8,128)(2,1)}, bf16[256,1024]{1,0:T(8,128)(2,1)}, u32[]{:S(2)}, u32[]{:S(2)}) collective-permute-start(bf16[256,1024]{1,0:T(8,128)(2,1)} %collective-permute-done.6), channel_id=1, source_target_pairs={{0,16},{16,0},{1,17},{17,1},{2,18},{18,2},{3,19},{19,3},{4,20},{20... | collective-permute-start | bytes 1572872 | tf_op jit(solution)/shard_map/ppermute | solution.py:21
  42.7 3.5 %all-gather.2.cloned.1.call-done = bf16[512,1152]{1,0:T(8,128)(2,1)} async-done(((bf16[128,1152]{1,0:T(8,128)(2,1)}), bf16[512,1152]{1,0:T(8,128)(2,1)}) %all-gather.2.cloned.1.call-update) | async-done | bytes 1179664 | tf_op jit(solution)/shard_map/all_gather | solution.py:75
  46.1 1.1 fusion.86
  47.8 7.6 %collective-permute-done.7 = bf16[256,1024]{1,0:T(8,128)(2,1)} collective-permute-done((bf16[256,1024]{1,0:T(8,128)(2,1)}, bf16[256,1024]{1,0:T(8,128)(2,1)}, u32[]{:S(2)}, u32[]{:S(2)}) %collective-permute-start.7) | collective-permute-done | bytes 524320 | tf_op jit(solution)/shard_map/ppermute | solution.py:21
  55.4 4.9 %fusion.20 = f32[512,1024]{1,0:T(8,128)S(1)} fusion(bf16[512,1024]{1,0:T(8,128)(2,1)} %collective-permute-done.1, bf16[512,1024]{1,0:T(8,128)(2,1)} %bitcast.36, bf16[1024,512]{1,0:T(8,128)(2,1)} %collective-permute-done, bf16[1024,512]{1,0:T(8,128)(2,1)} %bitcast.39, bf16[512,1152]{1,0:T(8,128)(2,1)} %all-gather.2.cloned.1.call-done, ...), kind=kOutput, calls=%fused_computation.23 | convolution fusion | flops 2161115136 | bytes 7341056 | tf_op jit(solution)/shard_map/dot_general | solution.py:86
  60.3 6.0 %fusion.32 = f32[512,1024]{1,0:T(8,128)} fusion(bf16[256,1024]{1,0:T(8,128)(2,1)} %collective-permute-done.9, bf16[256,1024]{1,0:T(8,128)(2,1)} %collective-permute-done.8, bf16[256,1024]{1,0:T(8,128)(2,1)} %collective-permute-done.7, bf16[256,1024]{1,0:T(8,128)(2,1)} %collective-permute-done.6, bf16[1024,256]{1,0:T(8,128)(2,1)} %collective-permute-done.5, ...), kind=kOutput, calls=%fused_computation.35 | convolution fusion | flops 2169503744 | bytes 7341056 | tf_op jit(solution)/shard_map/dot_general | solution.py:86
  66.4 2.4 %fusion.76 = (bf16[128,1024]{1,0:T(8,128)(2,1)S(1)}, bf16[128,1024]{1,0:T(8,128)(2,1)}, bf16[128,1024]{1,0:T(8,128)(2,1)}) fusion(f32[4,128,1024]{2,1,0:T(8,128)} %bitcast.32, s32[]{:T(128)S(6)} %select_n.81, f32[4,128,1024]{2,1,0:T(8,128)S(1)} %bitcast.30, s32[]{:T(128)S(6)} %select_n.85, s32[]{:T(128)S(6)} %select_n.83), kind=kLoop, calls=%fused_computation.79 | loop fusion | flops 786432 | bytes 3932172 | tf_op jit(solution)/shard_map/convert_element_type | solution.py:114
  68.7 3.6 %collective-permute-start.12 = (bf16[128,1024]{1,0:T(8,128)(2,1)}, bf16[128,1024]{1,0:T(8,128)(2,1)S(1)}, u32[]{:S(2)}, u32[]{:S(2)}) collective-permute-start(bf16[128,1024]{1,0:T(8,128)(2,1)} %get-tuple-element.27), channel_id=1, source_target_pairs={{0,3},{1,0},{2,1},{3,2},{4,7},{5,4},{6,5},{7,6},{8,11},{9,8},{10,9... | collective-permute-start | bytes 786440 | tf_op jit(solution)/shard_map/ppermute | solution.py:113
  72.3 1.0 collective-permute-start.10
  73.3 6.0 %collective-permute-done.12 = bf16[128,1024]{1,0:T(8,128)(2,1)S(1)} collective-permute-done((bf16[128,1024]{1,0:T(8,128)(2,1)}, bf16[128,1024]{1,0:T(8,128)(2,1)S(1)}, u32[]{:S(2)}, u32[]{:S(2)}) %collective-permute-start.12) | collective-permute-done | bytes 262176 | tf_op jit(solution)/shard_map/ppermute | solution.py:113
  79.3 16.2 %collective-permute-done.11 = bf16[128,1024]{1,0:T(8,128)(2,1)S(1)} collective-permute-done((bf16[128,1024]{1,0:T(8,128)(2,1)}, bf16[128,1024]{1,0:T(8,128)(2,1)S(1)}, u32[]{:S(2)}, u32[]{:S(2)}) %collective-permute-start.11) | collective-permute-done | bytes 262176 | tf_op jit(solution)/shard_map/ppermute | solution.py:113
  95.5 1.5 %convolution_convert_fusion.1 = bf16[128,1024]{1,0:T(8,128)(2,1)S(1)} fusion(bf16[128,1024]{1,0:T(8,128)(2,1)S(1)} %copy-done.2, bf16[128,1024]{1,0:T(8,128)(2,1)S(1)} %collective-permute-done.12, bf16[128,1024]{1,0:T(8,128)(2,1)S(1)} %collective-permute-done.11, bf16[128,1024]{1,0:T(8,128)(2,1)} %collective-permute-done.10, f32[4,128,1024]{2,1,0:T(8,128)} %bitcast.33, ...), kind=kOutput, calls=%fused_computation.44 | convolution fusion | flops 35012608 | bytes 2359812 | tf_op jit(solution)/shard_map/dot_general | solution.py:127
  97.0 14.9 %all_to_all.5 = bf16[16,8,1152]{2,1,0:T(8,128)(2,1)S(1)} all-to-all(bf16[16,8,1152]{2,1,0:T(8,128)(2,1)S(1)} %maximum_bitcast_fusion), channel_id=1, replica_groups=mesh['rep'=2,'member'=4,'tp'=4] {'member','tp'}, dimensions={0} | all-to-all | bytes 589824 | tf_op jit(solution)/shard_map/all_to_all | solution.py:134
  112.3 0.9 fusion.40
  (50 shorter events, 2.7 us)
Async XLA Ops:
  7.2 105.2 %copy-start = (bf16[1024,128]{1,0:T(8,128)(2,1)S(1)}, bf16[1024,128]{1,0:T(8,128)(2,1)}, u32[]{:S(2)}) copy-start(bf16[1024,128]{1,0:T(8,128)(2,1)} %param.15) | copy-start | bytes 786436
  7.2 3.7 %copy-start.1 = (f32[2,1024]{1,0:T(2,128)S(1)}, f32[2,1024]{1,0:T(2,128)}, u32[]{:S(2)}) copy-start(f32[2,1024]{1,0:T(2,128)} %param.11) | copy-start | bytes 24580
  7.2 38.9 %all-gather.2.cloned.1.call-start = ((), (), s32[]{:S(2)}) async-start(), calls=%async_computation.1 | async-start | bytes 1474560 | tf_op jit(solution)/shard_map/all_gather | solution.py:75
  10.9 0.8 copy-start.5
  10.9 1.0 copy-start.2
  10.9 1.9 %copy-start.4 = (bf16[1,1024,512]{2,1,0:T(8,128)(2,1)S(1)}, bf16[1,1024,512]{2,1,0:T(8,128)(2,1)}, u32[]{:S(2)}) copy-start(bf16[1,1024,512]{2,1,0:T(8,128)(2,1)} %param.12) | copy-start | bytes 3145732
  11.7 4.2 %copy-start.3 = (bf16[1,512,1024]{2,1,0:T(8,128)(2,1)S(1)}, bf16[1,512,1024]{2,1,0:T(8,128)(2,1)}, u32[]{:S(2)}) copy-start(bf16[1,512,1024]{2,1,0:T(8,128)(2,1)} %param.13) | copy-start | bytes 3145732
  12.9 15.0 %collective-permute-start.2 = (bf16[1024,256]{1,0:T(8,128)(2,1)S(1)}, bf16[1024,256]{1,0:T(8,128)(2,1)S(1)}, u32[]{:S(2)}, u32[]{:S(2)}) collective-permute-start(bf16[1024,256]{1,0:T(8,128)(2,1)S(1)} %dynamic-slice_bitcast_fusion), channel_id=1, source_target_pairs={{0,8},{4,12},{8,0},{12,4},{1,9},{5,13},{9,1},{13,5},{2,10},{6,14},... | collective-permute-start | bytes 1572872 | tf_op jit(solution)/shard_map/ppermute | solution.py:15
  15.9 31.3 %collective-permute-start.1 = (bf16[512,1024]{1,0:T(8,128)(2,1)S(1)}, bf16[512,1024]{1,0:T(8,128)(2,1)}, u32[]{:S(2)}, u32[]{:S(2)}) collective-permute-start(bf16[512,1024]{1,0:T(8,128)(2,1)S(1)} %bitcast.37), channel_id=1, source_target_pairs={{0,4},{4,0},{8,12},{12,8},{1,5},{5,1},{9,13},{13,9},{2,6},{6,2},{1... | collective-permute-start | bytes 3145736 | tf_op jit(solution)/shard_map/ppermute | solution.py:10
  27.9 13.3 %collective-permute-start.6 = (bf16[256,1024]{1,0:T(8,128)(2,1)S(1)}, bf16[256,1024]{1,0:T(8,128)(2,1)}, u32[]{:S(2)}, u32[]{:S(2)}) collective-permute-start(bf16[256,1024]{1,0:T(8,128)(2,1)S(1)} %constant_dynamic-slice_fusion), channel_id=1, source_target_pairs={{0,8},{4,12},{8,0},{12,4},{1,9},{5,13},{9,1},{13,5},{2,10},{6,14},... | collective-permute-start | bytes 1572872 | tf_op jit(solution)/shard_map/ppermute | solution.py:15
  29.7 25.7 %collective-permute-start = (bf16[1024,512]{1,0:T(8,128)(2,1)S(1)}, bf16[1024,512]{1,0:T(8,128)(2,1)}, u32[]{:S(2)}, u32[]{:S(2)}) collective-permute-start(bf16[1024,512]{1,0:T(8,128)(2,1)S(1)} %bitcast.40), channel_id=1, source_target_pairs={{0,4},{4,0},{8,12},{12,8},{1,5},{5,1},{9,13},{13,9},{2,6},{6,2},{1... | collective-permute-start | bytes 3145736 | tf_op jit(solution)/shard_map/ppermute | solution.py:10
  29.7 17.6 %collective-permute-start.3 = (bf16[1024,256]{1,0:T(8,128)(2,1)S(1)}, bf16[1024,256]{1,0:T(8,128)(2,1)}, u32[]{:S(2)}, u32[]{:S(2)}) collective-permute-start(bf16[1024,256]{1,0:T(8,128)(2,1)S(1)} %collective-permute-done.2), channel_id=1, source_target_pairs={{0,16},{16,0},{1,17},{17,1},{2,18},{18,2},{3,19},{19,3},{4,20},{20... | collective-permute-start | bytes 1572872 | tf_op jit(solution)/shard_map/ppermute | solution.py:21
  41.2 14.1 %collective-permute-start.7 = (bf16[256,1024]{1,0:T(8,128)(2,1)}, bf16[256,1024]{1,0:T(8,128)(2,1)}, u32[]{:S(2)}, u32[]{:S(2)}) collective-permute-start(bf16[256,1024]{1,0:T(8,128)(2,1)} %collective-permute-done.6), channel_id=1, source_target_pairs={{0,16},{16,0},{1,17},{17,1},{2,18},{18,2},{3,19},{19,3},{4,20},{20... | collective-permute-start | bytes 1572872 | tf_op jit(solution)/shard_map/ppermute | solution.py:21
  42.7 17.6 %collective-permute-start.4 = (bf16[1024,256]{1,0:T(8,128)(2,1)S(1)}, bf16[1024,256]{1,0:T(8,128)(2,1)}, u32[]{:S(2)}, u32[]{:S(2)}) collective-permute-start(bf16[1024,256]{1,0:T(8,128)(2,1)S(1)} %collective-permute-done.2), channel_id=1, source_target_pairs={{0,4},{4,0},{8,12},{12,8},{1,5},{5,1},{9,13},{13,9},{2,6},{6,2},{1... | collective-permute-start | bytes 1572872 | tf_op jit(solution)/shard_map/ppermute | solution.py:10
  47.2 13.1 %collective-permute-start.8 = (bf16[256,1024]{1,0:T(8,128)(2,1)}, bf16[256,1024]{1,0:T(8,128)(2,1)}, u32[]{:S(2)}, u32[]{:S(2)}) collective-permute-start(bf16[256,1024]{1,0:T(8,128)(2,1)} %collective-permute-done.6), channel_id=1, source_target_pairs={{0,4},{4,0},{8,12},{12,8},{1,5},{5,1},{9,13},{13,9},{2,6},{6,2},{1... | collective-permute-start | bytes 1572872 | tf_op jit(solution)/shard_map/ppermute | solution.py:10
  47.3 13.0 %collective-permute-start.5 = (bf16[1024,256]{1,0:T(8,128)(2,1)}, bf16[1024,256]{1,0:T(8,128)(2,1)}, u32[]{:S(2)}, u32[]{:S(2)}) collective-permute-start(bf16[1024,256]{1,0:T(8,128)(2,1)} %collective-permute-done.3), channel_id=1, source_target_pairs={{0,4},{4,0},{8,12},{12,8},{1,5},{5,1},{9,13},{13,9},{2,6},{6,2},{1... | collective-permute-start | bytes 1572872 | tf_op jit(solution)/shard_map/ppermute | solution.py:10
  55.4 5.0 %collective-permute-start.9 = (bf16[256,1024]{1,0:T(8,128)(2,1)}, bf16[256,1024]{1,0:T(8,128)(2,1)}, u32[]{:S(2)}, u32[]{:S(2)}) collective-permute-start(bf16[256,1024]{1,0:T(8,128)(2,1)} %collective-permute-done.7), channel_id=1, source_target_pairs={{0,4},{4,0},{8,12},{12,8},{1,5},{5,1},{9,13},{13,9},{2,6},{6,2},{1... | collective-permute-start | bytes 1572872 | tf_op jit(solution)/shard_map/ppermute | solution.py:10
  68.7 43.6 %copy-start.6 = (f32[1024]{0:T(1024)S(1)}, f32[1024]{0:T(1024)}, u32[]{:S(2)}) copy-start(f32[1024]{0:T(1024)} %param.14) | copy-start | bytes 12292
  68.7 10.6 %collective-permute-start.12 = (bf16[128,1024]{1,0:T(8,128)(2,1)}, bf16[128,1024]{1,0:T(8,128)(2,1)S(1)}, u32[]{:S(2)}, u32[]{:S(2)}) collective-permute-start(bf16[128,1024]{1,0:T(8,128)(2,1)} %get-tuple-element.27), channel_id=1, source_target_pairs={{0,3},{1,0},{2,1},{3,2},{4,7},{5,4},{6,5},{7,6},{8,11},{9,8},{10,9... | collective-permute-start | bytes 786440 | tf_op jit(solution)/shard_map/ppermute | solution.py:113
  72.3 23.2 %collective-permute-start.11 = (bf16[128,1024]{1,0:T(8,128)(2,1)}, bf16[128,1024]{1,0:T(8,128)(2,1)S(1)}, u32[]{:S(2)}, u32[]{:S(2)}) collective-permute-start(bf16[128,1024]{1,0:T(8,128)(2,1)} %get-tuple-element.28), channel_id=1, source_target_pairs={{0,2},{1,3},{2,0},{3,1},{4,6},{5,7},{6,4},{7,5},{8,10},{9,11},{10,... | collective-permute-start | bytes 786440 | tf_op jit(solution)/shard_map/ppermute | solution.py:113
  72.3 23.2 %collective-permute-start.10 = (bf16[128,1024]{1,0:T(8,128)(2,1)S(1)}, bf16[128,1024]{1,0:T(8,128)(2,1)}, u32[]{:S(2)}, u32[]{:S(2)}) collective-permute-start(bf16[128,1024]{1,0:T(8,128)(2,1)S(1)} %get-tuple-element.26), channel_id=1, source_target_pairs={{0,1},{1,2},{2,3},{3,0},{4,5},{5,6},{6,7},{7,4},{8,9},{9,10},{10,1... | collective-permute-start | bytes 786440 | tf_op jit(solution)/shard_map/ppermute | solution.py:113
  112.3 1.0 copy-start.7
Sparse Core Ops, SparseCore 0:
  12.9 33.1 all-gather.1

commit v20 on v19

--- a/solution.py
+++ b/solution.py
@@ -72,9 +72,10 @@
     member_lanes = jnp.where(
         jnp.arange(128, dtype=jnp.int32)[None, :] == 0, member[:, None], 0
     ).astype(jnp.bfloat16)
-    gathered = lax.all_gather(
-        jnp.concatenate([normed, member_lanes], axis=1), "tp", axis=0, tiled=True
-    )
+    to_gather = jnp.concatenate([normed, member_lanes], axis=1)
+    if fetched:
+        to_gather, _ = lax.optimization_barrier((to_gather, fetched[0][1][0]))
+    gathered = lax.all_gather(to_gather, "tp", axis=0, tiled=True)
     gathered_rows = gathered[:, :feature_width]
     gathered_member = gathered[:, feature_width].astype(jnp.int32)
 

time: 120 us -> 122 us (1.017)
  local copies, waits for them, and re-layouts: 0.92 us -> 2.41 us
    all_gather x1, waiting for transfers between devices: 3.45 us -> 15.7 us  [local(): gathered = lax.all_gather(to_gather, 'tp', axis=0, tiled=True)]
    ppermute x2, waiting for transfers between devices: 7.58 us -> 0.01 us  [swap_parts(): lax.ppermute(value, 'rep', [(i, (i + step) % n_rep) for i in range(n_rep)])]
    ppermute x2, waiting for transfers between devices: 22 us -> 16.6 us  [from_chip_behind(): lax.ppermute(value, axis, [(i, (i + 2 * chips_back) % size) for i in rang...]
  transfers between devices with their start and end apart: 14 -> 14, of which waited for: 6 -> 5; matrix products, arithmetic and copies ran while one was open for 5% -> 10% of each run, Pallas kernels for 0% -> 0%
where the time goes in v20:
time: 122 us; the launch traced here: 121 us
  waiting for transfers between devices  54.6 us (45%)
  blocking collectives  15 us (12%)
  between operations  14.3 us (12%)
  matrix products  13.6 us (11%)
  starting transfers between devices  12.6 us (10%)
  other arithmetic  8.83 us (7%)
  local copies, waits for them, and re-layouts  2.41 us (2%)
    ppermute x3, waiting for transfers between devices, local(): lax.ppermute(slice_for((tp_here + shift) % n_tp).astype(PARTIAL_DTYPE), '...  22.2 us
    ppermute x2, waiting for transfers between devices, from_chip_behind(): lax.ppermute(value, axis, [(i, (i + 2 * chips_back) % size) for i in rang...  16.6 us
    all_gather x1, waiting for transfers between devices, local(): gathered = lax.all_gather(to_gather, 'tp', axis=0, tiled=True)  15.7 us
    all_to_all x1, blocking collectives, local(): lax.all_to_all(jnp.concatenate([packed, spot_lanes], axis=1).reshape(n_de...  15 us
    dot_general x2, matrix products, apply_block(): return jnp.dot(hidden, down_here, preferred_element_type=jnp.float32)  10.9 us
    ppermute x2, starting transfers between devices, from_chip_behind(): lax.ppermute(value, axis, [(i, (i + 2 * chips_back) % size) for i in rang...  4.84 us
    ppermute x3, starting transfers between devices, local(): lax.ppermute(slice_for((tp_here + shift) % n_tp).astype(PARTIAL_DTYPE), '...  3.57 us
    ppermute x2, starting transfers between devices, swap_parts(): lax.ppermute(value, 'rep', [(i, (i + step) % n_rep) for i in range(n_rep)])  3.2 us
  transfers between devices with their start and end apart: 14, of which 5 were waited for; matrix products, arithmetic and copies ran while one was open for 10% of the time, Pallas kernels for 0%

profile of v20, /device:TPU:0, one launch (start us, length us, event | category | flops | bytes accessed | tf_op | source)
XLA Modules:
  0.0 121.3 jit_solution(6485306867811750632)
XLA Ops:
  7.2 1.1 dynamic-slice_bitcast_fusion
  8.3 3.0 %collective-permute-start = (bf16[1024,256]{1,0:T(8,128)(2,1)S(1)}, bf16[1024,256]{1,0:T(8,128)(2,1)S(1)}, u32[]{:S(2)}, u32[]{:S(2)}) collective-permute-start(bf16[1024,256]{1,0:T(8,128)(2,1)S(1)} %dynamic-slice_bitcast_fusion), channel_id=1, source_target_pairs={{0,8},{4,12},{8,0},{12,4},{1,9},{5,13},{9,1},{13,5},{2,10},{6,14},... | collective-permute-start | bytes 1572872 | tf_op jit(solution)/shard_map/ppermute | solution.py:15
  13.8 1.1 fusion.68
  15.0 0.8 select_convert_fusion.1
  15.8 0.8 gather_fusion
  16.9 0.7 pad_maximum_fusion
  17.7 5.6 %collective-permute-done = bf16[1024,256]{1,0:T(8,128)(2,1)S(1)} collective-permute-done((bf16[1024,256]{1,0:T(8,128)(2,1)S(1)}, bf16[1024,256]{1,0:T(8,128)(2,1)S(1)}, u32[]{:S(2)}, u32[]{:S(2)}) %collective-permute-start) | collective-permute-done | bytes 524320 | tf_op jit(solution)/shard_map/ppermute | solution.py:15
  23.4 1.8 %collective-permute-start.6 = (bf16[256,1024]{1,0:T(8,128)(2,1)S(1)}, bf16[256,1024]{1,0:T(8,128)(2,1)}, u32[]{:S(2)}, u32[]{:S(2)}) collective-permute-start(bf16[256,1024]{1,0:T(8,128)(2,1)S(1)} %constant_dynamic-slice_fusion), channel_id=1, source_target_pairs={{0,8},{4,12},{8,0},{12,4},{1,9},{5,13},{9,1},{13,5},{2,10},{6,14},... | collective-permute-start | bytes 1572872 | tf_op jit(solution)/shard_map/ppermute | solution.py:15
  25.5 1.5 %collective-permute-start.3 = (bf16[1024,256]{1,0:T(8,128)(2,1)S(1)}, bf16[1024,256]{1,0:T(8,128)(2,1)}, u32[]{:S(2)}, u32[]{:S(2)}) collective-permute-start(bf16[1024,256]{1,0:T(8,128)(2,1)S(1)} %collective-permute-done), channel_id=1, source_target_pairs={{0,16},{16,0},{1,17},{17,1},{2,18},{18,2},{3,19},{19,3},{4,20},{20... | collective-permute-start | bytes 1572872 | tf_op jit(solution)/shard_map/ppermute | solution.py:21
  26.9 11.0 %collective-permute-done.6 = bf16[256,1024]{1,0:T(8,128)(2,1)} collective-permute-done((bf16[256,1024]{1,0:T(8,128)(2,1)S(1)}, bf16[256,1024]{1,0:T(8,128)(2,1)}, u32[]{:S(2)}, u32[]{:S(2)}) %collective-permute-start.6) | collective-permute-done | bytes 524320 | tf_op jit(solution)/shard_map/ppermute | solution.py:15
  37.9 1.7 %collective-permute-start.7 = (bf16[256,1024]{1,0:T(8,128)(2,1)}, bf16[256,1024]{1,0:T(8,128)(2,1)}, u32[]{:S(2)}, u32[]{:S(2)}) collective-permute-start(bf16[256,1024]{1,0:T(8,128)(2,1)} %collective-permute-done.6), channel_id=1, source_target_pairs={{0,16},{16,0},{1,17},{17,1},{2,18},{18,2},{3,19},{19,3},{4,20},{20... | collective-permute-start | bytes 1572872 | tf_op jit(solution)/shard_map/ppermute | solution.py:21
  39.6 15.7 %all-gather.2.cloned.1.call-done = bf16[512,1152]{1,0:T(8,128)(2,1)} async-done(((bf16[128,1152]{1,0:T(8,128)(2,1)}), bf16[512,1152]{1,0:T(8,128)(2,1)}) %all-gather.2.cloned.1.call-update) | async-done | bytes 1179664 | tf_op jit(solution)/shard_map/all_gather | solution.py:78
  55.4 1.1 fusion.86
  57.5 4.9 %fusion.20 = f32[512,1024]{1,0:T(8,128)S(1)} fusion(bf16[512,1024]{1,0:T(8,128)(2,1)} %copy-done.4, bf16[512,1024]{1,0:T(8,128)(2,1)} %bitcast.36, bf16[1024,512]{1,0:T(8,128)(2,1)} %collective-permute-done.1, bf16[1024,512]{1,0:T(8,128)(2,1)} %bitcast.40, bf16[512,1152]{1,0:T(8,128)(2,1)} %all-gather.2.cloned.1.call-done, ...), kind=kOutput, calls=%fused_computation.23 | convolution fusion | flops 2161115136 | bytes 7341056 | tf_op jit(solution)/shard_map/dot_general | solution.py:87
  62.4 6.0 %fusion.32 = f32[512,1024]{1,0:T(8,128)} fusion(bf16[256,1024]{1,0:T(8,128)(2,1)} %collective-permute-done.9, bf16[256,1024]{1,0:T(8,128)(2,1)} %collective-permute-done.8, bf16[256,1024]{1,0:T(8,128)(2,1)} %collective-permute-done.7, bf16[256,1024]{1,0:T(8,128)(2,1)} %collective-permute-done.6, bf16[1024,256]{1,0:T(8,128)(2,1)} %collective-permute-done.5, ...), kind=kOutput, calls=%fused_computation.35 | convolution fusion | flops 2169503744 | bytes 7341056 | tf_op jit(solution)/shard_map/dot_general | solution.py:87
  68.5 2.3 %fusion.76 = (bf16[128,1024]{1,0:T(8,128)(2,1)S(1)}, bf16[128,1024]{1,0:T(8,128)(2,1)}, bf16[128,1024]{1,0:T(8,128)(2,1)}) fusion(f32[4,128,1024]{2,1,0:T(8,128)} %bitcast.32, s32[]{:T(128)S(6)} %select_n.81, f32[4,128,1024]{2,1,0:T(8,128)S(1)} %bitcast.30, s32[]{:T(128)S(6)} %select_n.85, s32[]{:T(128)S(6)} %select_n.83), kind=kLoop, calls=%fused_computation.79 | loop fusion | flops 786432 | bytes 3932172 | tf_op jit(solution)/shard_map/convert_element_type | solution.py:115
  70.8 1.5 %collective-permute-start.12 = (bf16[128,1024]{1,0:T(8,128)(2,1)}, bf16[128,1024]{1,0:T(8,128)(2,1)S(1)}, u32[]{:S(2)}, u32[]{:S(2)}) collective-permute-start(bf16[128,1024]{1,0:T(8,128)(2,1)} %get-tuple-element.29), channel_id=1, source_target_pairs={{0,3},{1,0},{2,1},{3,2},{4,7},{5,4},{6,5},{7,6},{8,11},{9,8},{10,9... | collective-permute-start | bytes 786440 | tf_op jit(solution)/shard_map/ppermute | solution.py:114
  72.3 0.9 collective-permute-start.11
  73.2 1.1 collective-permute-start.10
  74.4 5.3 %collective-permute-done.12 = bf16[128,1024]{1,0:T(8,128)(2,1)S(1)} collective-permute-done((bf16[128,1024]{1,0:T(8,128)(2,1)}, bf16[128,1024]{1,0:T(8,128)(2,1)S(1)}, u32[]{:S(2)}, u32[]{:S(2)}) %collective-permute-start.12) | collective-permute-done | bytes 262176 | tf_op jit(solution)/shard_map/ppermute | solution.py:114
  79.6 17.0 %collective-permute-done.11 = bf16[128,1024]{1,0:T(8,128)(2,1)S(1)} collective-permute-done((bf16[128,1024]{1,0:T(8,128)(2,1)}, bf16[128,1024]{1,0:T(8,128)(2,1)S(1)}, u32[]{:S(2)}, u32[]{:S(2)}) %collective-permute-start.11) | collective-permute-done | bytes 262176 | tf_op jit(solution)/shard_map/ppermute | solution.py:114
  96.6 1.4 %convolution_convert_fusion.1 = bf16[128,1024]{1,0:T(8,128)(2,1)S(1)} fusion(bf16[128,1024]{1,0:T(8,128)(2,1)S(1)} %copy-done.2, bf16[128,1024]{1,0:T(8,128)(2,1)S(1)} %collective-permute-done.12, bf16[128,1024]{1,0:T(8,128)(2,1)S(1)} %collective-permute-done.11, bf16[128,1024]{1,0:T(8,128)(2,1)} %collective-permute-done.10, f32[4,128,1024]{2,1,0:T(8,128)} %bitcast.33, ...), kind=kOutput, calls=%fused_computation.44 | convolution fusion | flops 35012608 | bytes 2359812 | tf_op jit(solution)/shard_map/dot_general | solution.py:128
  98.1 15.0 %all_to_all.5 = bf16[16,8,1152]{2,1,0:T(8,128)(2,1)S(1)} all-to-all(bf16[16,8,1152]{2,1,0:T(8,128)(2,1)S(1)} %maximum_bitcast_fusion), channel_id=1, replica_groups=mesh['rep'=2,'member'=4,'tp'=4] {'member','tp'}, dimensions={0} | all-to-all | bytes 589824 | tf_op jit(solution)/shard_map/all_to_all | solution.py:135
  113.5 0.9 fusion.40
  (48 shorter events, 4.7 us)
Async XLA Ops:
  7.2 106.4 %copy-start = (bf16[1024,128]{1,0:T(8,128)(2,1)S(1)}, bf16[1024,128]{1,0:T(8,128)(2,1)}, u32[]{:S(2)}) copy-start(bf16[1024,128]{1,0:T(8,128)(2,1)} %param.15) | copy-start | bytes 786436
  7.2 8.6 %copy-start.1 = (f32[2,1024]{1,0:T(2,128)S(1)}, f32[2,1024]{1,0:T(2,128)}, u32[]{:S(2)}) copy-start(f32[2,1024]{1,0:T(2,128)} %param.11) | copy-start | bytes 24580
  7.2 48.2 %all-gather.2.cloned.1.call-start = ((), (), s32[]{:S(2)}) async-start(), calls=%async_computation.1 | async-start | bytes 1474560 | tf_op jit(solution)/shard_map/all_gather | solution.py:78
  8.3 15.0 %collective-permute-start = (bf16[1024,256]{1,0:T(8,128)(2,1)S(1)}, bf16[1024,256]{1,0:T(8,128)(2,1)S(1)}, u32[]{:S(2)}, u32[]{:S(2)}) collective-permute-start(bf16[1024,256]{1,0:T(8,128)(2,1)S(1)} %dynamic-slice_bitcast_fusion), channel_id=1, source_target_pairs={{0,8},{4,12},{8,0},{12,4},{1,9},{5,13},{9,1},{13,5},{2,10},{6,14},... | collective-permute-start | bytes 1572872 | tf_op jit(solution)/shard_map/ppermute | solution.py:15
  15.8 1.0 copy-start.2
  15.8 7.5 %copy-start.3 = (bf16[1,512,1024]{2,1,0:T(8,128)(2,1)S(1)}, bf16[1,512,1024]{2,1,0:T(8,128)(2,1)}, u32[]{:S(2)}) copy-start(bf16[1,512,1024]{2,1,0:T(8,128)(2,1)} %param.13) | copy-start | bytes 3145732
  23.3 33.1 %collective-permute-start.2 = (bf16[512,1024]{1,0:T(8,128)(2,1)S(1)}, bf16[512,1024]{1,0:T(8,128)(2,1)S(1)}, u32[]{:S(2)}, u32[]{:S(2)}) collective-permute-start(bf16[512,1024]{1,0:T(8,128)(2,1)S(1)} %bitcast.37), channel_id=1, source_target_pairs={{0,4},{4,0},{8,12},{12,8},{1,5},{5,1},{9,13},{13,9},{2,6},{6,2},{1... | collective-permute-start | bytes 3145736 | tf_op jit(solution)/shard_map/ppermute | solution.py:10
  23.4 14.5 %collective-permute-start.6 = (bf16[256,1024]{1,0:T(8,128)(2,1)S(1)}, bf16[256,1024]{1,0:T(8,128)(2,1)}, u32[]{:S(2)}, u32[]{:S(2)}) collective-permute-start(bf16[256,1024]{1,0:T(8,128)(2,1)S(1)} %constant_dynamic-slice_fusion), channel_id=1, source_target_pairs={{0,8},{4,12},{8,0},{12,4},{1,9},{5,13},{9,1},{13,5},{2,10},{6,14},... | collective-permute-start | bytes 1572872 | tf_op jit(solution)/shard_map/ppermute | solution.py:15
  25.3 31.9 %collective-permute-start.1 = (bf16[1024,512]{1,0:T(8,128)(2,1)}, bf16[1024,512]{1,0:T(8,128)(2,1)}, u32[]{:S(2)}, u32[]{:S(2)}) collective-permute-start(bf16[1024,512]{1,0:T(8,128)(2,1)} %bitcast.39), channel_id=1, source_target_pairs={{0,4},{4,0},{8,12},{12,8},{1,5},{5,1},{9,13},{13,9},{2,6},{6,2},{1... | collective-permute-start | bytes 3145736 | tf_op jit(solution)/shard_map/ppermute | solution.py:10
  25.5 31.1 %collective-permute-start.3 = (bf16[1024,256]{1,0:T(8,128)(2,1)S(1)}, bf16[1024,256]{1,0:T(8,128)(2,1)}, u32[]{:S(2)}, u32[]{:S(2)}) collective-permute-start(bf16[1024,256]{1,0:T(8,128)(2,1)S(1)} %collective-permute-done), channel_id=1, source_target_pairs={{0,16},{16,0},{1,17},{17,1},{2,18},{18,2},{3,19},{19,3},{4,20},{20... | collective-permute-start | bytes 1572872 | tf_op jit(solution)/shard_map/ppermute | solution.py:21
  37.9 19.1 %collective-permute-start.7 = (bf16[256,1024]{1,0:T(8,128)(2,1)}, bf16[256,1024]{1,0:T(8,128)(2,1)}, u32[]{:S(2)}, u32[]{:S(2)}) collective-permute-start(bf16[256,1024]{1,0:T(8,128)(2,1)} %collective-permute-done.6), channel_id=1, source_target_pairs={{0,16},{16,0},{1,17},{17,1},{2,18},{18,2},{3,19},{19,3},{4,20},{20... | collective-permute-start | bytes 1572872 | tf_op jit(solution)/shard_map/ppermute | solution.py:21
  39.6 22.8 %collective-permute-start.4 = (bf16[1024,256]{1,0:T(8,128)(2,1)S(1)}, bf16[1024,256]{1,0:T(8,128)(2,1)}, u32[]{:S(2)}, u32[]{:S(2)}) collective-permute-start(bf16[1024,256]{1,0:T(8,128)(2,1)S(1)} %collective-permute-done), channel_id=1, source_target_pairs={{0,4},{4,0},{8,12},{12,8},{1,5},{5,1},{9,13},{13,9},{2,6},{6,2},{1... | collective-permute-start | bytes 1572872 | tf_op jit(solution)/shard_map/ppermute | solution.py:10
  56.5 1.0 copy-start.4
  56.5 5.9 %collective-permute-start.8 = (bf16[256,1024]{1,0:T(8,128)(2,1)}, bf16[256,1024]{1,0:T(8,128)(2,1)}, u32[]{:S(2)}, u32[]{:S(2)}) collective-permute-start(bf16[256,1024]{1,0:T(8,128)(2,1)} %collective-permute-done.6), channel_id=1, source_target_pairs={{0,4},{4,0},{8,12},{12,8},{1,5},{5,1},{9,13},{13,9},{2,6},{6,2},{1... | collective-permute-start | bytes 1572872 | tf_op jit(solution)/shard_map/ppermute | solution.py:10
  56.6 5.8 %collective-permute-start.5 = (bf16[1024,256]{1,0:T(8,128)(2,1)}, bf16[1024,256]{1,0:T(8,128)(2,1)}, u32[]{:S(2)}, u32[]{:S(2)}) collective-permute-start(bf16[1024,256]{1,0:T(8,128)(2,1)} %collective-permute-done.3), channel_id=1, source_target_pairs={{0,4},{4,0},{8,12},{12,8},{1,5},{5,1},{9,13},{13,9},{2,6},{6,2},{1... | collective-permute-start | bytes 1572872 | tf_op jit(solution)/shard_map/ppermute | solution.py:10
  57.1 5.4 %collective-permute-start.9 = (bf16[256,1024]{1,0:T(8,128)(2,1)}, bf16[256,1024]{1,0:T(8,128)(2,1)}, u32[]{:S(2)}, u32[]{:S(2)}) collective-permute-start(bf16[256,1024]{1,0:T(8,128)(2,1)} %collective-permute-done.7), channel_id=1, source_target_pairs={{0,4},{4,0},{8,12},{12,8},{1,5},{5,1},{9,13},{13,9},{2,6},{6,2},{1... | collective-permute-start | bytes 1572872 | tf_op jit(solution)/shard_map/ppermute | solution.py:10
  70.8 42.7 %copy-start.5 = (f32[1024]{0:T(1024)S(1)}, f32[1024]{0:T(1024)}, u32[]{:S(2)}) copy-start(f32[1024]{0:T(1024)} %param.14) | copy-start | bytes 12292
  70.8 8.8 %collective-permute-start.12 = (bf16[128,1024]{1,0:T(8,128)(2,1)}, bf16[128,1024]{1,0:T(8,128)(2,1)S(1)}, u32[]{:S(2)}, u32[]{:S(2)}) collective-permute-start(bf16[128,1024]{1,0:T(8,128)(2,1)} %get-tuple-element.29), channel_id=1, source_target_pairs={{0,3},{1,0},{2,1},{3,2},{4,7},{5,4},{6,5},{7,6},{8,11},{9,8},{10,9... | collective-permute-start | bytes 786440 | tf_op jit(solution)/shard_map/ppermute | solution.py:114
  72.3 24.3 %collective-permute-start.11 = (bf16[128,1024]{1,0:T(8,128)(2,1)}, bf16[128,1024]{1,0:T(8,128)(2,1)S(1)}, u32[]{:S(2)}, u32[]{:S(2)}) collective-permute-start(bf16[128,1024]{1,0:T(8,128)(2,1)} %get-tuple-element.30), channel_id=1, source_target_pairs={{0,2},{1,3},{2,0},{3,1},{4,6},{5,7},{6,4},{7,5},{8,10},{9,11},{10,... | collective-permute-start | bytes 786440 | tf_op jit(solution)/shard_map/ppermute | solution.py:114
  73.2 23.4 %collective-permute-start.10 = (bf16[128,1024]{1,0:T(8,128)(2,1)S(1)}, bf16[128,1024]{1,0:T(8,128)(2,1)}, u32[]{:S(2)}, u32[]{:S(2)}) collective-permute-start(bf16[128,1024]{1,0:T(8,128)(2,1)S(1)} %get-tuple-element.28), channel_id=1, source_target_pairs={{0,1},{1,2},{2,3},{3,0},{4,5},{5,6},{6,7},{7,4},{8,9},{9,10},{10,1... | collective-permute-start | bytes 786440 | tf_op jit(solution)/shard_map/ppermute | solution.py:114
  113.5 1.0 copy-start.6
Sparse Core Ops, SparseCore 0:
  23.4 31.9 all-gather.1

commit v21 on v19

--- a/solution.py
+++ b/solution.py
@@ -66,7 +66,18 @@
         )
         for back in range(1, member_total)
     ]
-    member = member_of[:, 0]
+    per_learner = rows_here // n_dev
+    learner = place // rows_here
+    learner_hits = (learner[:, None] == jnp.arange(n_dev, dtype=jnp.int32)[None, :]).astype(
+        jnp.int32
+    )
+    lane_index = learner * per_learner + running_rank(learner_hits)
+    placer = jnp.arange(rows_here, dtype=jnp.int32)[:, None] == lane_index[None, :]
+    states = jnp.dot(
+        placer.astype(jnp.bfloat16), states, preferred_element_type=jnp.float32
+    ).astype(jnp.bfloat16)
+    member = jnp.sum(placer.astype(jnp.int32) * member_of[:, 0][None, :], axis=1)
+    packed_spot = jnp.sum(placer.astype(jnp.int32) * (place % rows_here)[None, :], axis=1)
     gain_rows = jnp.take(norm_gain, member, axis=0)
     normed = rms_scale(states.astype(jnp.float32), gain_rows).astype(jnp.bfloat16)
     member_lanes = jnp.where(
@@ -115,19 +126,7 @@
             "tp",
             [(i, (i + shift) % n_tp) for i in range(n_tp)],
         ).astype(jnp.float32)
-    own_rows = (states.astype(jnp.float32) + change).astype(jnp.bfloat16)
-    per_learner = rows_here // n_dev
-    learner = place // rows_here
-    learner_hits = (learner[:, None] == jnp.arange(n_dev, dtype=jnp.int32)[None, :]).astype(
-        jnp.int32
-    )
-    lane_index = learner * per_learner + running_rank(learner_hits)
-    placer = jnp.arange(rows_here, dtype=jnp.int32)[:, None] == lane_index[None, :]
-    spot_index = place % rows_here
-    packed = jnp.dot(
-        placer.astype(jnp.bfloat16), own_rows, preferred_element_type=jnp.float32
-    ).astype(jnp.bfloat16)
-    packed_spot = jnp.sum(placer.astype(jnp.int32) * spot_index[None, :], axis=1)
+    packed = (states.astype(jnp.float32) + change).astype(jnp.bfloat16)
     spot_lanes = jnp.where(
         jnp.arange(128, dtype=jnp.int32)[None, :] == 0, packed_spot[:, None], 0
     ).astype(jnp.bfloat16)

time: 120 us -> 119 us (level)
    convert_element_type x0 -> x1, other arithmetic: none -> 1.5 us  [local(): packed = (states.astype(jnp.float32) + change).astype(jnp.bfloat16)]
where the time goes in v21:
time: 119 us
  waiting for transfers between devices  55.4 us (47%)
  blocking collectives  14.5 us (12%)
  between operations  14.3 us (12%)
  starting transfers between devices  12.9 us (11%)
  matrix products  12.5 us (11%)
  other arithmetic  7.9 us (7%)
  local copies, waits for them, and re-layouts  1.27 us (1%)
    ppermute x3, waiting for transfers between devices, local(): lax.ppermute(slice_for((tp_here + shift) % n_tp).astype(PARTIAL_DTYPE), '...  22.3 us
    ppermute x2, waiting for transfers between devices, from_chip_behind(): lax.ppermute(value, axis, [(i, (i + 2 * chips_back) % size) for i in rang...  22 us
    all_to_all x1, blocking collectives, local(): lax.all_to_all(jnp.concatenate([packed, spot_lanes], axis=1).reshape(n_de...  14.5 us
    dot_general x2, matrix products, apply_block(): return jnp.dot(hidden, down_here, preferred_element_type=jnp.float32)  10.9 us
    ppermute x2, waiting for transfers between devices, swap_parts(): lax.ppermute(value, 'rep', [(i, (i + step) % n_rep) for i in range(n_rep)])  7.94 us
    ppermute x2, starting transfers between devices, from_chip_behind(): lax.ppermute(value, axis, [(i, (i + 2 * chips_back) % size) for i in rang...  4.84 us
    ppermute x3, starting transfers between devices, local(): lax.ppermute(slice_for((tp_here + shift) % n_tp).astype(PARTIAL_DTYPE), '...  4.61 us
    all_gather x1, waiting for transfers between devices, local(): lax.all_gather(jnp.concatenate([normed, member_lanes], axis=1), 'tp', axi...  3.1 us
  transfers between devices with their start and end apart: 14, of which 6 were waited for; matrix products, arithmetic and copies ran while one was open for 5% of the time, Pallas kernels for 0%

profile of v21, /device:TPU:0, one launch (start us, length us, event | category | flops | bytes accessed | tf_op | source)
XLA Modules:
  0.0 118.7 jit_solution(594228416031735746)
XLA Ops:
  7.2 0.7 and_select_fusion
  8.4 0.8 select_reduce_fusion.1
  9.6 0.8 gather_fusion
  10.6 0.8 pad_maximum_fusion
  11.8 3.0 %collective-permute-start.2 = (bf16[1024,256]{1,0:T(8,128)(2,1)S(1)}, bf16[1024,256]{1,0:T(8,128)(2,1)S(1)}, u32[]{:S(2)}, u32[]{:S(2)}) collective-permute-start(bf16[1024,256]{1,0:T(8,128)(2,1)S(1)} %dynamic-slice_bitcast_fusion), channel_id=1, source_target_pairs={{0,8},{4,12},{8,0},{12,4},{1,9},{5,13},{9,1},{13,5},{2,10},{6,14},... | collective-permute-start | bytes 1572872 | tf_op jit(solution)/shard_map/ppermute | solution.py:15
  14.8 11.9 %collective-permute-done.2 = bf16[1024,256]{1,0:T(8,128)(2,1)S(1)} collective-permute-done((bf16[1024,256]{1,0:T(8,128)(2,1)S(1)}, bf16[1024,256]{1,0:T(8,128)(2,1)S(1)}, u32[]{:S(2)}, u32[]{:S(2)}) %collective-permute-start.2) | collective-permute-done | bytes 524320 | tf_op jit(solution)/shard_map/ppermute | solution.py:15
  26.8 1.8 %collective-permute-start.6 = (bf16[256,1024]{1,0:T(8,128)(2,1)S(1)}, bf16[256,1024]{1,0:T(8,128)(2,1)}, u32[]{:S(2)}, u32[]{:S(2)}) collective-permute-start(bf16[256,1024]{1,0:T(8,128)(2,1)S(1)} %constant_dynamic-slice_fusion), channel_id=1, source_target_pairs={{0,8},{4,12},{8,0},{12,4},{1,9},{5,13},{9,1},{13,5},{2,10},{6,14},... | collective-permute-start | bytes 1572872 | tf_op jit(solution)/shard_map/ppermute | solution.py:15
  28.6 1.5 %collective-permute-start.3 = (bf16[1024,256]{1,0:T(8,128)(2,1)S(1)}, bf16[1024,256]{1,0:T(8,128)(2,1)}, u32[]{:S(2)}, u32[]{:S(2)}) collective-permute-start(bf16[1024,256]{1,0:T(8,128)(2,1)S(1)} %collective-permute-done.2), channel_id=1, source_target_pairs={{0,16},{16,0},{1,17},{17,1},{2,18},{18,2},{3,19},{19,3},{4,20},{20... | collective-permute-start | bytes 1572872 | tf_op jit(solution)/shard_map/ppermute | solution.py:21
  30.1 10.1 %collective-permute-done.6 = bf16[256,1024]{1,0:T(8,128)(2,1)} collective-permute-done((bf16[256,1024]{1,0:T(8,128)(2,1)S(1)}, bf16[256,1024]{1,0:T(8,128)(2,1)}, u32[]{:S(2)}, u32[]{:S(2)}) %collective-permute-start.6) | collective-permute-done | bytes 524320 | tf_op jit(solution)/shard_map/ppermute | solution.py:15
  40.2 1.4 %collective-permute-start.7 = (bf16[256,1024]{1,0:T(8,128)(2,1)}, bf16[256,1024]{1,0:T(8,128)(2,1)}, u32[]{:S(2)}, u32[]{:S(2)}) collective-permute-start(bf16[256,1024]{1,0:T(8,128)(2,1)} %collective-permute-done.6), channel_id=1, source_target_pairs={{0,16},{16,0},{1,17},{17,1},{2,18},{18,2},{3,19},{19,3},{4,20},{20... | collective-permute-start | bytes 1572872 | tf_op jit(solution)/shard_map/ppermute | solution.py:21
  41.6 3.1 %all-gather.2.cloned.1.call-done = bf16[512,1152]{1,0:T(8,128)(2,1)} async-done(((bf16[128,1152]{1,0:T(8,128)(2,1)}), bf16[512,1152]{1,0:T(8,128)(2,1)}) %all-gather.2.cloned.1.call-update) | async-done | bytes 1179664 | tf_op jit(solution)/shard_map/all_gather | solution.py:86
  44.7 1.1 fusion.84
  45.8 0.5 collective-permute-start.5
  46.3 7.9 %collective-permute-done.7 = bf16[256,1024]{1,0:T(8,128)(2,1)} collective-permute-done((bf16[256,1024]{1,0:T(8,128)(2,1)}, bf16[256,1024]{1,0:T(8,128)(2,1)}, u32[]{:S(2)}, u32[]{:S(2)}) %collective-permute-start.7) | collective-permute-done | bytes 524320 | tf_op jit(solution)/shard_map/ppermute | solution.py:21
  54.3 4.9 %fusion.20 = f32[512,1024]{1,0:T(8,128)S(1)} fusion(bf16[512,1024]{1,0:T(8,128)(2,1)} %collective-permute-done.1, bf16[512,1024]{1,0:T(8,128)(2,1)} %bitcast.38, bf16[1024,512]{1,0:T(8,128)(2,1)} %collective-permute-done, bf16[1024,512]{1,0:T(8,128)(2,1)} %bitcast.41, bf16[512,1152]{1,0:T(8,128)(2,1)} %all-gather.2.cloned.1.call-done, ...), kind=kOutput, calls=%fused_computation.23 | convolution fusion | flops 2161115136 | bytes 7341056 | tf_op jit(solution)/shard_map/dot_general | solution.py:97
  59.2 6.0 %fusion.32 = f32[512,1024]{1,0:T(8,128)} fusion(bf16[256,1024]{1,0:T(8,128)(2,1)} %collective-permute-done.9, bf16[256,1024]{1,0:T(8,128)(2,1)} %collective-permute-done.8, bf16[256,1024]{1,0:T(8,128)(2,1)} %collective-permute-done.7, bf16[256,1024]{1,0:T(8,128)(2,1)} %collective-permute-done.6, bf16[1024,256]{1,0:T(8,128)(2,1)} %collective-permute-done.5, ...), kind=kOutput, calls=%fused_computation.35 | convolution fusion | flops 2169503744 | bytes 7341056 | tf_op jit(solution)/shard_map/dot_general | solution.py:97
  65.3 2.3 %fusion.75 = (bf16[128,1024]{1,0:T(8,128)(2,1)S(1)}, bf16[128,1024]{1,0:T(8,128)(2,1)}, bf16[128,1024]{1,0:T(8,128)(2,1)S(1)}) fusion(f32[4,128,1024]{2,1,0:T(8,128)} %bitcast.34, s32[]{:T(128)S(6)} %select_n.91, f32[4,128,1024]{2,1,0:T(8,128)S(1)} %bitcast.32, s32[]{:T(128)S(6)} %select_n.95, s32[]{:T(128)S(6)} %select_n.93), kind=kLoop, calls=%fused_computation.77 | loop fusion | flops 786432 | bytes 3932172 | tf_op jit(solution)/shard_map/convert_element_type | solution.py:125
  67.5 3.6 %collective-permute-start.12 = (bf16[128,1024]{1,0:T(8,128)(2,1)}, bf16[128,1024]{1,0:T(8,128)(2,1)}, u32[]{:S(2)}, u32[]{:S(2)}) collective-permute-start(bf16[128,1024]{1,0:T(8,128)(2,1)} %get-tuple-element.29), channel_id=1, source_target_pairs={{0,3},{1,0},{2,1},{3,2},{4,7},{5,4},{6,5},{7,6},{8,11},{9,8},{10,9... | collective-permute-start | bytes 786440 | tf_op jit(solution)/shard_map/ppermute | solution.py:124
  71.1 1.0 collective-permute-start.10
  72.2 6.0 %collective-permute-done.12 = bf16[128,1024]{1,0:T(8,128)(2,1)} collective-permute-done((bf16[128,1024]{1,0:T(8,128)(2,1)}, bf16[128,1024]{1,0:T(8,128)(2,1)}, u32[]{:S(2)}, u32[]{:S(2)}) %collective-permute-start.12) | collective-permute-done | bytes 262176 | tf_op jit(solution)/shard_map/ppermute | solution.py:124
  78.2 16.3 %collective-permute-done.11 = bf16[128,1024]{1,0:T(8,128)(2,1)} collective-permute-done((bf16[128,1024]{1,0:T(8,128)(2,1)S(1)}, bf16[128,1024]{1,0:T(8,128)(2,1)}, u32[]{:S(2)}, u32[]{:S(2)}) %collective-permute-start.11) | collective-permute-done | bytes 262176 | tf_op jit(solution)/shard_map/ppermute | solution.py:124
  94.5 1.5 %fusion.72 = bf16[128,1024]{1,0:T(8,128)(2,1)S(1)} fusion(f32[128,1024]{1,0:T(8,128)S(1)} %get-tuple-element.36, bf16[128,1024]{1,0:T(8,128)(2,1)} %collective-permute-done.12, bf16[128,1024]{1,0:T(8,128)(2,1)} %collective-permute-done.11, bf16[128,1024]{1,0:T(8,128)(2,1)} %collective-permute-done.10, f32[4,128,1024]{2,1,0:T(8,128)} %bitcast.35, ...), kind=kLoop, calls=%fused_computation.64 | loop fusion | flops 1179648 | bytes 2621444 | tf_op jit(solution)/shard_map/convert_element_type | solution.py:129
  96.0 14.5 %all_to_all.5 = bf16[16,8,1152]{2,1,0:T(8,128)(2,1)S(1)} all-to-all(bf16[16,8,1152]{2,1,0:T(8,128)(2,1)S(1)} %maximum_bitcast_fusion), channel_id=1, replica_groups=mesh['rep'=2,'member'=4,'tp'=4] {'member','tp'}, dimensions={0} | all-to-all | bytes 589824 | tf_op jit(solution)/shard_map/all_to_all | solution.py:133
  111.0 0.9 fusion.41
  (47 shorter events, 2.1 us)
Async XLA Ops:
  7.2 2.0 %copy-start = (bf16[128,1024]{1,0:T(8,128)(2,1)S(1)}, bf16[128,1024]{1,0:T(8,128)(2,1)}, u32[]{:S(2)}) copy-start(bf16[128,1024]{1,0:T(8,128)(2,1)} %param.8) | copy-start | bytes 786436
  7.2 2.4 %copy-start.1 = (f32[2,1024]{1,0:T(2,128)S(1)}, f32[2,1024]{1,0:T(2,128)}, u32[]{:S(2)}) copy-start(f32[2,1024]{1,0:T(2,128)} %param.11) | copy-start | bytes 24580
  7.2 37.5 %all-gather.2.cloned.1.call-start = ((), (), s32[]{:S(2)}) async-start(), calls=%async_computation.1 | async-start | bytes 1474560 | tf_op jit(solution)/shard_map/all_gather | solution.py:86
  10.4 1.3 %copy-start.3 = (bf16[1,1024,512]{2,1,0:T(8,128)(2,1)S(1)}, bf16[1,1024,512]{2,1,0:T(8,128)(2,1)}, u32[]{:S(2)}) copy-start(bf16[1,1024,512]{2,1,0:T(8,128)(2,1)} %param.12) | copy-start | bytes 3145732
  10.4 4.4 %copy-start.2 = (bf16[1,512,1024]{2,1,0:T(8,128)(2,1)S(1)}, bf16[1,512,1024]{2,1,0:T(8,128)(2,1)}, u32[]{:S(2)}) copy-start(bf16[1,512,1024]{2,1,0:T(8,128)(2,1)} %param.13) | copy-start | bytes 3145732
  11.8 15.0 %collective-permute-start.2 = (bf16[1024,256]{1,0:T(8,128)(2,1)S(1)}, bf16[1024,256]{1,0:T(8,128)(2,1)S(1)}, u32[]{:S(2)}, u32[]{:S(2)}) collective-permute-start(bf16[1024,256]{1,0:T(8,128)(2,1)S(1)} %dynamic-slice_bitcast_fusion), channel_id=1, source_target_pairs={{0,8},{4,12},{8,0},{12,4},{1,9},{5,13},{9,1},{13,5},{2,10},{6,14},... | collective-permute-start | bytes 1572872 | tf_op jit(solution)/shard_map/ppermute | solution.py:15
  14.8 30.9 %collective-permute-start.1 = (bf16[512,1024]{1,0:T(8,128)(2,1)S(1)}, bf16[512,1024]{1,0:T(8,128)(2,1)}, u32[]{:S(2)}, u32[]{:S(2)}) collective-permute-start(bf16[512,1024]{1,0:T(8,128)(2,1)S(1)} %bitcast.39), channel_id=1, source_target_pairs={{0,4},{4,0},{8,12},{12,8},{1,5},{5,1},{9,13},{13,9},{2,6},{6,2},{1... | collective-permute-start | bytes 3145736 | tf_op jit(solution)/shard_map/ppermute | solution.py:10
  26.8 13.4 %collective-permute-start.6 = (bf16[256,1024]{1,0:T(8,128)(2,1)S(1)}, bf16[256,1024]{1,0:T(8,128)(2,1)}, u32[]{:S(2)}, u32[]{:S(2)}) collective-permute-start(bf16[256,1024]{1,0:T(8,128)(2,1)S(1)} %constant_dynamic-slice_fusion), channel_id=1, source_target_pairs={{0,8},{4,12},{8,0},{12,4},{1,9},{5,13},{9,1},{13,5},{2,10},{6,14},... | collective-permute-start | bytes 1572872 | tf_op jit(solution)/shard_map/ppermute | solution.py:15
  28.6 25.7 %collective-permute-start = (bf16[1024,512]{1,0:T(8,128)(2,1)S(1)}, bf16[1024,512]{1,0:T(8,128)(2,1)}, u32[]{:S(2)}, u32[]{:S(2)}) collective-permute-start(bf16[1024,512]{1,0:T(8,128)(2,1)S(1)} %bitcast.42), channel_id=1, source_target_pairs={{0,4},{4,0},{8,12},{12,8},{1,5},{5,1},{9,13},{13,9},{2,6},{6,2},{1... | collective-permute-start | bytes 3145736 | tf_op jit(solution)/shard_map/ppermute | solution.py:10
  28.6 17.2 %collective-permute-start.3 = (bf16[1024,256]{1,0:T(8,128)(2,1)S(1)}, bf16[1024,256]{1,0:T(8,128)(2,1)}, u32[]{:S(2)}, u32[]{:S(2)}) collective-permute-start(bf16[1024,256]{1,0:T(8,128)(2,1)S(1)} %collective-permute-done.2), channel_id=1, source_target_pairs={{0,16},{16,0},{1,17},{17,1},{2,18},{18,2},{3,19},{19,3},{4,20},{20... | collective-permute-start | bytes 1572872 | tf_op jit(solution)/shard_map/ppermute | solution.py:21
  40.2 14.1 %collective-permute-start.7 = (bf16[256,1024]{1,0:T(8,128)(2,1)}, bf16[256,1024]{1,0:T(8,128)(2,1)}, u32[]{:S(2)}, u32[]{:S(2)}) collective-permute-start(bf16[256,1024]{1,0:T(8,128)(2,1)} %collective-permute-done.6), channel_id=1, source_target_pairs={{0,16},{16,0},{1,17},{17,1},{2,18},{18,2},{3,19},{19,3},{4,20},{20... | collective-permute-start | bytes 1572872 | tf_op jit(solution)/shard_map/ppermute | solution.py:21
  41.6 17.6 %collective-permute-start.4 = (bf16[1024,256]{1,0:T(8,128)(2,1)S(1)}, bf16[1024,256]{1,0:T(8,128)(2,1)}, u32[]{:S(2)}, u32[]{:S(2)}) collective-permute-start(bf16[1024,256]{1,0:T(8,128)(2,1)S(1)} %collective-permute-done.2), channel_id=1, source_target_pairs={{0,4},{4,0},{8,12},{12,8},{1,5},{5,1},{9,13},{13,9},{2,6},{6,2},{1... | collective-permute-start | bytes 1572872 | tf_op jit(solution)/shard_map/ppermute | solution.py:10
  45.8 13.5 %collective-permute-start.8 = (bf16[256,1024]{1,0:T(8,128)(2,1)}, bf16[256,1024]{1,0:T(8,128)(2,1)}, u32[]{:S(2)}, u32[]{:S(2)}) collective-permute-start(bf16[256,1024]{1,0:T(8,128)(2,1)} %collective-permute-done.6), channel_id=1, source_target_pairs={{0,4},{4,0},{8,12},{12,8},{1,5},{5,1},{9,13},{13,9},{2,6},{6,2},{1... | collective-permute-start | bytes 1572872 | tf_op jit(solution)/shard_map/ppermute | solution.py:10
  45.8 13.4 %collective-permute-start.5 = (bf16[1024,256]{1,0:T(8,128)(2,1)}, bf16[1024,256]{1,0:T(8,128)(2,1)}, u32[]{:S(2)}, u32[]{:S(2)}) collective-permute-start(bf16[1024,256]{1,0:T(8,128)(2,1)} %collective-permute-done.3), channel_id=1, source_target_pairs={{0,4},{4,0},{8,12},{12,8},{1,5},{5,1},{9,13},{13,9},{2,6},{6,2},{1... | collective-permute-start | bytes 1572872 | tf_op jit(solution)/shard_map/ppermute | solution.py:10
  54.3 5.0 %collective-permute-start.9 = (bf16[256,1024]{1,0:T(8,128)(2,1)}, bf16[256,1024]{1,0:T(8,128)(2,1)}, u32[]{:S(2)}, u32[]{:S(2)}) collective-permute-start(bf16[256,1024]{1,0:T(8,128)(2,1)} %collective-permute-done.7), channel_id=1, source_target_pairs={{0,4},{4,0},{8,12},{12,8},{1,5},{5,1},{9,13},{13,9},{2,6},{6,2},{1... | collective-permute-start | bytes 1572872 | tf_op jit(solution)/shard_map/ppermute | solution.py:10
  67.5 10.6 %collective-permute-start.12 = (bf16[128,1024]{1,0:T(8,128)(2,1)}, bf16[128,1024]{1,0:T(8,128)(2,1)}, u32[]{:S(2)}, u32[]{:S(2)}) collective-permute-start(bf16[128,1024]{1,0:T(8,128)(2,1)} %get-tuple-element.29), channel_id=1, source_target_pairs={{0,3},{1,0},{2,1},{3,2},{4,7},{5,4},{6,5},{7,6},{8,11},{9,8},{10,9... | collective-permute-start | bytes 786440 | tf_op jit(solution)/shard_map/ppermute | solution.py:124
  71.1 23.3 %collective-permute-start.11 = (bf16[128,1024]{1,0:T(8,128)(2,1)S(1)}, bf16[128,1024]{1,0:T(8,128)(2,1)}, u32[]{:S(2)}, u32[]{:S(2)}) collective-permute-start(bf16[128,1024]{1,0:T(8,128)(2,1)S(1)} %get-tuple-element.30), channel_id=1, source_target_pairs={{0,2},{1,3},{2,0},{3,1},{4,6},{5,7},{6,4},{7,5},{8,10},{9,11},{10,... | collective-permute-start | bytes 786440 | tf_op jit(solution)/shard_map/ppermute | solution.py:124
  71.1 23.3 %collective-permute-start.10 = (bf16[128,1024]{1,0:T(8,128)(2,1)S(1)}, bf16[128,1024]{1,0:T(8,128)(2,1)}, u32[]{:S(2)}, u32[]{:S(2)}) collective-permute-start(bf16[128,1024]{1,0:T(8,128)(2,1)S(1)} %get-tuple-element.28), channel_id=1, source_target_pairs={{0,1},{1,2},{2,3},{3,0},{4,5},{5,6},{6,7},{7,4},{8,9},{9,10},{10,1... | collective-permute-start | bytes 786440 | tf_op jit(solution)/shard_map/ppermute | solution.py:124
  72.2 38.8 %copy-start.4 = (bf16[1024,128]{1,0:T(8,128)(2,1)S(1)}, bf16[1024,128]{1,0:T(8,128)(2,1)}, u32[]{:S(2)}) copy-start(bf16[1024,128]{1,0:T(8,128)(2,1)} %param.15) | copy-start | bytes 786436
  72.2 38.8 %copy-start.5 = (f32[1024]{0:T(1024)S(1)}, f32[1024]{0:T(1024)}, u32[]{:S(2)}) copy-start(f32[1024]{0:T(1024)} %param.14) | copy-start | bytes 12292
  110.9 1.0 copy-start.6
Sparse Core Ops, SparseCore 0:
  11.5 33.1 all-gather.1

commit v22 on v21

--- a/solution.py
+++ b/solution.py
@@ -78,14 +78,18 @@
     ).astype(jnp.bfloat16)
     member = jnp.sum(placer.astype(jnp.int32) * member_of[:, 0][None, :], axis=1)
     packed_spot = jnp.sum(placer.astype(jnp.int32) * (place % rows_here)[None, :], axis=1)
+    arrival_spots = lax.all_to_all(
+        packed_spot.reshape(n_dev, per_learner), ("member", "tp"), split_axis=0, concat_axis=0, tiled=True
+    ).reshape(n_dev * per_learner)
     gain_rows = jnp.take(norm_gain, member, axis=0)
     normed = rms_scale(states.astype(jnp.float32), gain_rows).astype(jnp.bfloat16)
     member_lanes = jnp.where(
         jnp.arange(128, dtype=jnp.int32)[None, :] == 0, member[:, None], 0
     ).astype(jnp.bfloat16)
-    gathered = lax.all_gather(
-        jnp.concatenate([normed, member_lanes], axis=1), "tp", axis=0, tiled=True
+    to_gather, arrival_spots = lax.optimization_barrier(
+        (jnp.concatenate([normed, member_lanes], axis=1), arrival_spots)
     )
+    gathered = lax.all_gather(to_gather, "tp", axis=0, tiled=True)
     gathered_rows = gathered[:, :feature_width]
     gathered_member = gathered[:, feature_width].astype(jnp.int32)
 
@@ -127,24 +131,17 @@
             [(i, (i + shift) % n_tp) for i in range(n_tp)],
         ).astype(jnp.float32)
     packed = (states.astype(jnp.float32) + change).astype(jnp.bfloat16)
-    spot_lanes = jnp.where(
-        jnp.arange(128, dtype=jnp.int32)[None, :] == 0, packed_spot[:, None], 0
-    ).astype(jnp.bfloat16)
     arrivals = lax.all_to_all(
-        jnp.concatenate([packed, spot_lanes], axis=1).reshape(n_dev, per_learner, feature_width + 128),
+        packed.reshape(n_dev, per_learner, feature_width),
         ("member", "tp"),
         split_axis=0,
         concat_axis=0,
         tiled=True,
-    )
-    arrivals = arrivals.reshape(n_dev * per_learner, feature_width + 128)
-    arrival_spots = arrivals[:, feature_width].astype(jnp.int32)
+    ).reshape(n_dev * per_learner, feature_width)
     settle = (jnp.arange(rows_here, dtype=jnp.int32)[:, None] == arrival_spots[None, :]).astype(
         jnp.bfloat16
     )
-    imagined = jnp.dot(
-        settle, arrivals[:, :feature_width], preferred_element_type=jnp.float32
-    ).astype(jnp.bfloat16)
+    imagined = jnp.dot(settle, arrivals, preferred_element_type=jnp.float32).astype(jnp.bfloat16)
     policy_normed = rms_scale(imagined.astype(jnp.float32), policy_gain).astype(jnp.bfloat16)
     action = jnp.tanh(jnp.dot(policy_normed, w_policy, preferred_element_type=jnp.float32)).astype(
         jnp.bfloat16

time: 119 us -> 128 us (1.076)
  starting transfers between devices: 12.9 us -> 16.2 us
  blocking collectives: 14.5 us -> 17.6 us
    all_to_all x0 -> x1, starting transfers between devices: none -> 7.39 us  [local(): lax.all_to_all(packed_spot.reshape(n_dev, per_learner), ('member', 'tp'),...]
    ppermute x3, waiting for transfers between devices: 22.3 us -> 18.2 us  [local(): lax.ppermute(slice_for((tp_here + shift) % n_tp).astype(PARTIAL_DTYPE), '...]
    all_to_all x0 -> x1, waiting for transfers between devices: none -> 4.06 us  [local(): lax.all_to_all(packed_spot.reshape(n_dev, per_learner), ('member', 'tp'),...]
    ppermute x2, starting transfers between devices: 4.84 us -> 1.28 us  [from_chip_behind(): lax.ppermute(value, axis, [(i, (i + 2 * chips_back) % size) for i in rang...]
    all_gather x1, waiting for transfers between devices: 3.1 us -> 0.01 us  [local(): gathered = lax.all_gather(to_gather, 'tp', axis=0, tiled=True)]
    all_to_all x1, blocking collectives: 14.5 us -> 17.6 us  [local(): lax.all_to_all(packed.reshape(n_dev, per_learner, feature_width), ('membe...]
    ppermute x2, waiting for transfers between devices: 7.94 us -> 10.3 us  [swap_parts(): lax.ppermute(value, 'rep', [(i, (i + step) % n_rep) for i in range(n_rep)])]
    ppermute x2, waiting for transfers between devices: 22 us -> 24 us  [from_chip_behind(): lax.ppermute(value, axis, [(i, (i + 2 * chips_back) % size) for i in rang...]
  transfers between devices with their start and end apart: 14 -> 15, of which waited for: 6 -> 6; matrix products, arithmetic and copies ran while one was open for 5% -> 6% of each run, Pallas kernels for 0% -> 0%
where the time goes in v22:
time: 128 us
  waiting for transfers between devices  56.6 us (44%)
  blocking collectives  17.6 us (14%)
  starting transfers between devices  16.2 us (13%)
  between operations  14.3 us (11%)
  matrix products  12.6 us (10%)
  other arithmetic  8.44 us (7%)
  local copies, waits for them, and re-layouts  2.19 us (2%)
    ppermute x2, waiting for transfers between devices, from_chip_behind(): lax.ppermute(value, axis, [(i, (i + 2 * chips_back) % size) for i in rang...  24 us
    ppermute x3, waiting for transfers between devices, local(): lax.ppermute(slice_for((tp_here + shift) % n_tp).astype(PARTIAL_DTYPE), '...  18.2 us
    all_to_all x1, blocking collectives, local(): lax.all_to_all(packed.reshape(n_dev, per_learner, feature_width), ('membe...  17.6 us
    dot_general x2, matrix products, apply_block(): return jnp.dot(hidden, down_here, preferred_element_type=jnp.float32)  11.1 us
    ppermute x2, waiting for transfers between devices, swap_parts(): lax.ppermute(value, 'rep', [(i, (i + step) % n_rep) for i in range(n_rep)])  10.3 us
    all_to_all x1, starting transfers between devices, local(): lax.all_to_all(packed_spot.reshape(n_dev, per_learner), ('member', 'tp'),...  7.39 us
    all_to_all x1, waiting for transfers between devices, local(): lax.all_to_all(packed_spot.reshape(n_dev, per_learner), ('member', 'tp'),...  4.06 us
    ppermute x3, starting transfers between devices, local(): lax.ppermute(slice_for((tp_here + shift) % n_tp).astype(PARTIAL_DTYPE), '...  3.83 us
  transfers between devices with their start and end apart: 15, of which 6 were waited for; matrix products, arithmetic and copies ran while one was open for 6% of the time, Pallas kernels for 0%

profile of v22, /device:TPU:0, one launch (start us, length us, event | category | flops | bytes accessed | tf_op | source)
XLA Modules:
  0.0 127.9 jit_solution(15633452063088852447)
XLA Ops:
  7.2 0.7 and_select_fusion
  8.3 0.8 select_reduce_fusion
  9.1 0.7 all_to_all.9
  9.8 7.4 %all-to-all-start = ((s32[16,1,8]{2,1,0:T(1,128)}), s32[16,1,8]{2,1,0:T(1,128)S(1)}, u32[]{:S(2)}, u32[]{:S(2)}) async-start(s32[16,1,8]{2,1,0:T(1,128)} %bitcast.3), calls=%async_computation | async-start | bytes 16384 | tf_op jit(solution)/shard_map/all_to_all | solution.py:81
  17.7 0.8 gather_fusion
  18.7 0.7 pad_maximum_fusion
  19.4 4.1 %all-to-all-done = s32[16,1,8]{2,1,0:T(1,128)S(1)} async-done(((s32[16,1,8]{2,1,0:T(1,128)}), s32[16,1,8]{2,1,0:T(1,128)S(1)}, u32[]{:S(2)}, u32[]{:S(2)}) %all-to-all-start) | async-done | bytes 544 | tf_op jit(solution)/shard_map/all_to_all | solution.py:81
  24.0 0.7 reduce.7
  25.5 13.2 %collective-permute-done.2 = bf16[1024,256]{1,0:T(8,128)(2,1)} collective-permute-done((bf16[1024,256]{1,0:T(8,128)(2,1)S(1)}, bf16[1024,256]{1,0:T(8,128)(2,1)}, u32[]{:S(2)}, u32[]{:S(2)}) %collective-permute-start.2) | collective-permute-done | bytes 524320 | tf_op jit(solution)/shard_map/ppermute | solution.py:15
  39.4 1.5 %collective-permute-start.3 = (bf16[1024,256]{1,0:T(8,128)(2,1)}, bf16[1024,256]{1,0:T(8,128)(2,1)}, u32[]{:S(2)}, u32[]{:S(2)}) collective-permute-start(bf16[1024,256]{1,0:T(8,128)(2,1)} %collective-permute-done.2), channel_id=1, source_target_pairs={{0,16},{16,0},{1,17},{17,1},{2,18},{18,2},{3,19},{19,3},{4,20},{20... | collective-permute-start | bytes 1572872 | tf_op jit(solution)/shard_map/ppermute | solution.py:21
  40.9 10.8 %collective-permute-done.6 = bf16[256,1024]{1,0:T(8,128)(2,1)} collective-permute-done((bf16[256,1024]{1,0:T(8,128)(2,1)S(1)}, bf16[256,1024]{1,0:T(8,128)(2,1)}, u32[]{:S(2)}, u32[]{:S(2)}) %collective-permute-start.6) | collective-permute-done | bytes 524320 | tf_op jit(solution)/shard_map/ppermute | solution.py:15
  51.7 1.5 %collective-permute-start.7 = (bf16[256,1024]{1,0:T(8,128)(2,1)}, bf16[256,1024]{1,0:T(8,128)(2,1)}, u32[]{:S(2)}, u32[]{:S(2)}) collective-permute-start(bf16[256,1024]{1,0:T(8,128)(2,1)} %collective-permute-done.6), channel_id=1, source_target_pairs={{0,16},{16,0},{1,17},{17,1},{2,18},{18,2},{3,19},{19,3},{4,20},{20... | collective-permute-start | bytes 1572872 | tf_op jit(solution)/shard_map/ppermute | solution.py:21
  53.2 1.1 fusion.85
  55.0 10.3 %collective-permute-done.7 = bf16[256,1024]{1,0:T(8,128)(2,1)} collective-permute-done((bf16[256,1024]{1,0:T(8,128)(2,1)}, bf16[256,1024]{1,0:T(8,128)(2,1)}, u32[]{:S(2)}, u32[]{:S(2)}) %collective-permute-start.7) | collective-permute-done | bytes 524320 | tf_op jit(solution)/shard_map/ppermute | solution.py:21
  65.3 4.9 %fusion.20 = f32[512,1024]{1,0:T(8,128)S(1)} fusion(bf16[512,1024]{1,0:T(8,128)(2,1)} %collective-permute-done.1, bf16[512,1024]{1,0:T(8,128)(2,1)} %bitcast.43, bf16[1024,512]{1,0:T(8,128)(2,1)} %collective-permute-done, bf16[1024,512]{1,0:T(8,128)(2,1)} %bitcast.46, bf16[512,1152]{1,0:T(8,128)(2,1)} %all-gather.2.cloned.1.call-done, ...), kind=kOutput, calls=%fused_computation.23 | convolution fusion | flops 2161115136 | bytes 7341056 | tf_op jit(solution)/shard_map/dot_general | solution.py:101
  70.2 6.2 %fusion.32 = f32[512,1024]{1,0:T(8,128)} fusion(bf16[256,1024]{1,0:T(8,128)(2,1)} %collective-permute-done.9, bf16[256,1024]{1,0:T(8,128)(2,1)} %collective-permute-done.8, bf16[256,1024]{1,0:T(8,128)(2,1)} %collective-permute-done.7, bf16[256,1024]{1,0:T(8,128)(2,1)} %collective-permute-done.6, bf16[1024,256]{1,0:T(8,128)(2,1)} %collective-permute-done.5, ...), kind=kOutput, calls=%fused_computation.35 | convolution fusion | flops 2169503744 | bytes 7341056 | tf_op jit(solution)/shard_map/dot_general | solution.py:101
  76.4 2.3 %fusion.75 = (bf16[128,1024]{1,0:T(8,128)(2,1)}, bf16[128,1024]{1,0:T(8,128)(2,1)S(1)}, bf16[128,1024]{1,0:T(8,128)(2,1)S(1)}) fusion(f32[4,128,1024]{2,1,0:T(8,128)} %bitcast.41, s32[]{:T(128)S(6)} %select_n.89, f32[4,128,1024]{2,1,0:T(8,128)S(1)} %bitcast.39, s32[]{:T(128)S(6)} %select_n.93, s32[]{:T(128)S(6)} %select_n.91), kind=kLoop, calls=%fused_computation.76 | loop fusion | flops 786432 | bytes 3932172 | tf_op jit(solution)/shard_map/convert_element_type | solution.py:129
  79.3 0.9 collective-permute-start.11
  80.1 2.4 %collective-permute-start.12 = (bf16[128,1024]{1,0:T(8,128)(2,1)S(1)}, bf16[128,1024]{1,0:T(8,128)(2,1)}, u32[]{:S(2)}, u32[]{:S(2)}) collective-permute-start(bf16[128,1024]{1,0:T(8,128)(2,1)S(1)} %get-tuple-element.33), channel_id=1, source_target_pairs={{0,3},{1,0},{2,1},{3,2},{4,7},{5,4},{6,5},{7,6},{8,11},{9,8},{10,9... | collective-permute-start | bytes 786440 | tf_op jit(solution)/shard_map/ppermute | solution.py:128
  82.5 7.5 %collective-permute-done.10 = bf16[128,1024]{1,0:T(8,128)(2,1)} collective-permute-done((bf16[128,1024]{1,0:T(8,128)(2,1)}, bf16[128,1024]{1,0:T(8,128)(2,1)}, u32[]{:S(2)}, u32[]{:S(2)}) %collective-permute-start.10) | collective-permute-done | bytes 262176 | tf_op jit(solution)/shard_map/ppermute | solution.py:128
  90.0 10.6 %collective-permute-done.11 = bf16[128,1024]{1,0:T(8,128)(2,1)} collective-permute-done((bf16[128,1024]{1,0:T(8,128)(2,1)S(1)}, bf16[128,1024]{1,0:T(8,128)(2,1)}, u32[]{:S(2)}, u32[]{:S(2)}) %collective-permute-start.11) | collective-permute-done | bytes 262176 | tf_op jit(solution)/shard_map/ppermute | solution.py:128
  100.7 1.5 %fusion.78 = bf16[16,8,1024]{2,1,0:T(8,128)(2,1)S(1)} fusion(f32[128,1024]{1,0:T(8,128)S(1)} %get-tuple-element.38, bf16[128,1024]{1,0:T(8,128)(2,1)} %collective-permute-done.12, bf16[128,1024]{1,0:T(8,128)(2,1)} %collective-permute-done.11, bf16[128,1024]{1,0:T(8,128)(2,1)} %collective-permute-done.10, f32[4,128,1024]{2,1,0:T(8,128)} %bitcast.42, ...), kind=kLoop, calls=%fused_computation.79 | loop fusion | flops 1179648 | bytes 2621444 | tf_op jit(solution)/shard_map/reshape | solution.py:135
  102.2 17.6 %all_to_all.14 = bf16[16,8,1024]{2,1,0:T(8,128)(2,1)S(1)} all-to-all(bf16[16,8,1024]{2,1,0:T(8,128)(2,1)S(1)} %fusion.78), channel_id=1, replica_groups=mesh['rep'=2,'member'=4,'tp'=4] {'member','tp'}, dimensions={0} | all-to-all | bytes 524288 | tf_op jit(solution)/shard_map/all_to_all | solution.py:134
  120.1 0.9 fusion.41
  (52 shorter events, 4.6 us)
Async XLA Ops:
  7.2 10.1 %copy-start = (bf16[128,1024]{1,0:T(8,128)(2,1)S(1)}, bf16[128,1024]{1,0:T(8,128)(2,1)}, u32[]{:S(2)}) copy-start(bf16[128,1024]{1,0:T(8,128)(2,1)} %param.8) | copy-start | bytes 786436
  7.2 10.6 %copy-start.1 = (f32[2,1024]{1,0:T(2,128)S(1)}, f32[2,1024]{1,0:T(2,128)}, u32[]{:S(2)}) copy-start(f32[2,1024]{1,0:T(2,128)} %param.11) | copy-start | bytes 24580
  9.8 13.7 %all-to-all-start = ((s32[16,1,8]{2,1,0:T(1,128)}), s32[16,1,8]{2,1,0:T(1,128)S(1)}, u32[]{:S(2)}, u32[]{:S(2)}) async-start(s32[16,1,8]{2,1,0:T(1,128)} %bitcast.3), calls=%async_computation | async-start | bytes 16384 | tf_op jit(solution)/shard_map/all_to_all | solution.py:81
  17.2 36.0 %all-gather.2.cloned.1.call-start = ((), (), s32[]{:S(2)}) async-start(), calls=%async_computation.2 | async-start | bytes 1474560 | tf_op jit(solution)/shard_map/all_gather | solution.py:92
  18.5 6.3 %copy-start.4 = (bf16[1,1024,512]{2,1,0:T(8,128)(2,1)S(1)}, bf16[1,1024,512]{2,1,0:T(8,128)(2,1)}, u32[]{:S(2)}) copy-start(bf16[1,1024,512]{2,1,0:T(8,128)(2,1)} %param.12) | copy-start | bytes 3145732
  18.5 7.0 %copy-start.3 = (bf16[1,512,1024]{2,1,0:T(8,128)(2,1)S(1)}, bf16[1,512,1024]{2,1,0:T(8,128)(2,1)}, u32[]{:S(2)}) copy-start(bf16[1,512,1024]{2,1,0:T(8,128)(2,1)} %param.13) | copy-start | bytes 3145732
  24.9 13.8 %collective-permute-start.2 = (bf16[1024,256]{1,0:T(8,128)(2,1)S(1)}, bf16[1024,256]{1,0:T(8,128)(2,1)}, u32[]{:S(2)}, u32[]{:S(2)}) collective-permute-start(bf16[1024,256]{1,0:T(8,128)(2,1)S(1)} %dynamic-slice_bitcast_fusion), channel_id=1, source_target_pairs={{0,8},{4,12},{8,0},{12,4},{1,9},{5,13},{9,1},{13,5},{2,10},{6,14},... | collective-permute-start | bytes 1572872 | tf_op jit(solution)/shard_map/ppermute | solution.py:15
  25.5 28.8 %collective-permute-start.1 = (bf16[512,1024]{1,0:T(8,128)(2,1)S(1)}, bf16[512,1024]{1,0:T(8,128)(2,1)}, u32[]{:S(2)}, u32[]{:S(2)}) collective-permute-start(bf16[512,1024]{1,0:T(8,128)(2,1)S(1)} %bitcast.44), channel_id=1, source_target_pairs={{0,4},{4,0},{8,12},{12,8},{1,5},{5,1},{9,13},{13,9},{2,6},{6,2},{1... | collective-permute-start | bytes 3145736 | tf_op jit(solution)/shard_map/ppermute | solution.py:10
  38.7 13.0 %collective-permute-start.6 = (bf16[256,1024]{1,0:T(8,128)(2,1)S(1)}, bf16[256,1024]{1,0:T(8,128)(2,1)}, u32[]{:S(2)}, u32[]{:S(2)}) collective-permute-start(bf16[256,1024]{1,0:T(8,128)(2,1)S(1)} %constant_dynamic-slice_fusion), channel_id=1, source_target_pairs={{0,8},{4,12},{8,0},{12,4},{1,9},{5,13},{9,1},{13,5},{2,10},{6,14},... | collective-permute-start | bytes 1572872 | tf_op jit(solution)/shard_map/ppermute | solution.py:15
  39.4 25.9 %collective-permute-start = (bf16[1024,512]{1,0:T(8,128)(2,1)S(1)}, bf16[1024,512]{1,0:T(8,128)(2,1)}, u32[]{:S(2)}, u32[]{:S(2)}) collective-permute-start(bf16[1024,512]{1,0:T(8,128)(2,1)S(1)} %bitcast.47), channel_id=1, source_target_pairs={{0,4},{4,0},{8,12},{12,8},{1,5},{5,1},{9,13},{13,9},{2,6},{6,2},{1... | collective-permute-start | bytes 3145736 | tf_op jit(solution)/shard_map/ppermute | solution.py:10
  39.4 15.5 %collective-permute-start.3 = (bf16[1024,256]{1,0:T(8,128)(2,1)}, bf16[1024,256]{1,0:T(8,128)(2,1)}, u32[]{:S(2)}, u32[]{:S(2)}) collective-permute-start(bf16[1024,256]{1,0:T(8,128)(2,1)} %collective-permute-done.2), channel_id=1, source_target_pairs={{0,16},{16,0},{1,17},{17,1},{2,18},{18,2},{3,19},{19,3},{4,20},{20... | collective-permute-start | bytes 1572872 | tf_op jit(solution)/shard_map/ppermute | solution.py:21
  51.7 13.6 %collective-permute-start.7 = (bf16[256,1024]{1,0:T(8,128)(2,1)}, bf16[256,1024]{1,0:T(8,128)(2,1)}, u32[]{:S(2)}, u32[]{:S(2)}) collective-permute-start(bf16[256,1024]{1,0:T(8,128)(2,1)} %collective-permute-done.6), channel_id=1, source_target_pairs={{0,16},{16,0},{1,17},{17,1},{2,18},{18,2},{3,19},{19,3},{4,20},{20... | collective-permute-start | bytes 1572872 | tf_op jit(solution)/shard_map/ppermute | solution.py:21
  53.2 17.0 %collective-permute-start.4 = (bf16[1024,256]{1,0:T(8,128)(2,1)}, bf16[1024,256]{1,0:T(8,128)(2,1)}, u32[]{:S(2)}, u32[]{:S(2)}) collective-permute-start(bf16[1024,256]{1,0:T(8,128)(2,1)} %collective-permute-done.2), channel_id=1, source_target_pairs={{0,4},{4,0},{8,12},{12,8},{1,5},{5,1},{9,13},{13,9},{2,6},{6,2},{1... | collective-permute-start | bytes 1572872 | tf_op jit(solution)/shard_map/ppermute | solution.py:10
  54.3 15.9 %collective-permute-start.8 = (bf16[256,1024]{1,0:T(8,128)(2,1)}, bf16[256,1024]{1,0:T(8,128)(2,1)}, u32[]{:S(2)}, u32[]{:S(2)}) collective-permute-start(bf16[256,1024]{1,0:T(8,128)(2,1)} %collective-permute-done.6), channel_id=1, source_target_pairs={{0,4},{4,0},{8,12},{12,8},{1,5},{5,1},{9,13},{13,9},{2,6},{6,2},{1... | collective-permute-start | bytes 1572872 | tf_op jit(solution)/shard_map/ppermute | solution.py:10
  54.9 15.3 %collective-permute-start.5 = (bf16[1024,256]{1,0:T(8,128)(2,1)}, bf16[1024,256]{1,0:T(8,128)(2,1)}, u32[]{:S(2)}, u32[]{:S(2)}) collective-permute-start(bf16[1024,256]{1,0:T(8,128)(2,1)} %collective-permute-done.3), channel_id=1, source_target_pairs={{0,4},{4,0},{8,12},{12,8},{1,5},{5,1},{9,13},{13,9},{2,6},{6,2},{1... | collective-permute-start | bytes 1572872 | tf_op jit(solution)/shard_map/ppermute | solution.py:10
  65.3 5.0 %collective-permute-start.9 = (bf16[256,1024]{1,0:T(8,128)(2,1)}, bf16[256,1024]{1,0:T(8,128)(2,1)}, u32[]{:S(2)}, u32[]{:S(2)}) collective-permute-start(bf16[256,1024]{1,0:T(8,128)(2,1)} %collective-permute-done.7), channel_id=1, source_target_pairs={{0,4},{4,0},{8,12},{12,8},{1,5},{5,1},{9,13},{13,9},{2,6},{6,2},{1... | collective-permute-start | bytes 1572872 | tf_op jit(solution)/shard_map/ppermute | solution.py:10
  78.7 41.4 %copy-start.6 = (f32[1024]{0:T(1024)S(1)}, f32[1024]{0:T(1024)}, u32[]{:S(2)}) copy-start(f32[1024]{0:T(1024)} %param.14) | copy-start | bytes 12292
  78.7 11.4 %collective-permute-start.10 = (bf16[128,1024]{1,0:T(8,128)(2,1)}, bf16[128,1024]{1,0:T(8,128)(2,1)}, u32[]{:S(2)}, u32[]{:S(2)}) collective-permute-start(bf16[128,1024]{1,0:T(8,128)(2,1)} %get-tuple-element.32), channel_id=1, source_target_pairs={{0,1},{1,2},{2,3},{3,0},{4,5},{5,6},{6,7},{7,4},{8,9},{9,10},{10,1... | collective-permute-start | bytes 786440 | tf_op jit(solution)/shard_map/ppermute | solution.py:128
  79.3 21.4 %collective-permute-start.11 = (bf16[128,1024]{1,0:T(8,128)(2,1)S(1)}, bf16[128,1024]{1,0:T(8,128)(2,1)}, u32[]{:S(2)}, u32[]{:S(2)}) collective-permute-start(bf16[128,1024]{1,0:T(8,128)(2,1)S(1)} %get-tuple-element.34), channel_id=1, source_target_pairs={{0,2},{1,3},{2,0},{3,1},{4,6},{5,7},{6,4},{7,5},{8,10},{9,11},{10,... | collective-permute-start | bytes 786440 | tf_op jit(solution)/shard_map/ppermute | solution.py:128
  80.1 20.6 %collective-permute-start.12 = (bf16[128,1024]{1,0:T(8,128)(2,1)S(1)}, bf16[128,1024]{1,0:T(8,128)(2,1)}, u32[]{:S(2)}, u32[]{:S(2)}) collective-permute-start(bf16[128,1024]{1,0:T(8,128)(2,1)S(1)} %get-tuple-element.33), channel_id=1, source_target_pairs={{0,3},{1,0},{2,1},{3,2},{4,7},{5,4},{6,5},{7,6},{8,11},{9,8},{10,9... | collective-permute-start | bytes 786440 | tf_op jit(solution)/shard_map/ppermute | solution.py:128
  82.5 37.6 %copy-start.5 = (bf16[1024,128]{1,0:T(8,128)(2,1)S(1)}, bf16[1024,128]{1,0:T(8,128)(2,1)}, u32[]{:S(2)}) copy-start(bf16[1024,128]{1,0:T(8,128)(2,1)} %param.15) | copy-start | bytes 786436
  120.1 1.0 copy-start.2
Sparse Core Ops, SparseCore 0:
  24.9 27.7 all-gather.1
